TPU v7x, 32 devices: a whole 2x2x4 slice. The times are simulated.
32 devices in a mesh: groups: 2 (over y), frame: 4 (over x, core), row: 4 (over z).
Axes of the slice: x: 2, y: 2, z: 4, core: 2. Of those that a mesh axis runs over, the one named last changes fastest.
Arguments:
- query_in: bfloat16 [8, 4, 64, 2240], P(('groups', 'frame'), 'row'), parts along dimension 0, may hold values from -6 to 6
- key_in: bfloat16 [8, 4, 64, 2240], P(('groups', 'frame'), 'row'), parts along dimension 0, may hold values from -216 to 216
- value_in: bfloat16 [8, 4, 64, 2240], P(('groups', 'frame'), 'row'), parts along dimension 0, may hold values from -6 to 6
- stream_in: bfloat16 [8, 4, 64, 2240], P(('groups', 'frame'), 'row'), parts along dimension 0, may hold values from -6 to 6
- attn_gain: bfloat16 [2240], replicated, may hold values from 0.5 to 1.5
- ffn_gain: bfloat16 [2240], replicated, may hold values from 0.5 to 1.5
- in_weight: bfloat16 [2240, 2, 3360], P('row', None, 'frame'), may hold values from -0.125 to 0.125
- conv_weight: bfloat16 [9, 2, 3360], P(None, None, 'frame'), may hold values from -3.5 to 3.5
- out_weight: bfloat16 [3360, 2240], P('frame'), may hold values from -0.109375 to 0.109375
Outputs:
- stream_out: bfloat16 [8, 4, 64, 2240], P(('groups', 'frame'), 'row'), parts along dimension 0
- block_out: bfloat16 [8, 4, 64, 2240], P(('groups', 'frame'), 'row'), parts along dimension 0
There are 2 independent parts, one for each index of `groups`. A program takes and returns all parts, laid end to end along the dimension named above; an argument that names none is the same for every part. Nothing has to cross between parts.
All inputs are finite; a program needn't handle non-finite values.
Results may differ from a plain program's by a relative error of at most 0.01.
Values may be sent and summed in bfloat16 or wider, within the bound.
No kernel may reach another device: no remote copies, remote signals or barrier semaphores. Data moves between devices by JAX's collectives and lax.ppermute only.
A program may use at most 64 MiB of HBM per device.

v0:
```python
import jax
import jax.numpy as jnp
from jax import lax
from jax.sharding import PartitionSpec as P

HEADS = 20
HEAD_DIM = 112


NORM_EPS = 1e-06
SHARE_EPS = 1e-06


def padded_2(cells, sides, width):
    for axis, dim in sides:
        count = lax.axis_size(axis)
        ends = count - 1
        head = lax.slice_in_dim(cells, 0, width, axis=dim)
        tail = lax.slice_in_dim(cells, cells.shape[dim] - width, cells.shape[dim], axis=dim)
        cells = jnp.concatenate(
            [
                lax.ppermute(tail, axis, [(i, (i + 1) % count) for i in range(ends)]),
                cells,
                lax.ppermute(head, axis, [((i + 1) % count, i) for i in range(ends)]),
            ],
            axis=dim,
        )
    return cells


def rms_norm(features):
    return features * lax.rsqrt(jnp.mean(features * features, axis=-1, keepdims=True) + NORM_EPS)


def depthwise(padded, conv_taps, row_count, col_count, half_width):
    widened = jnp.pad(padded, ((0, 0), (0, 0), (1, 1), (0, 0)))
    summed = jnp.zeros((padded.shape[0], row_count, col_count, padded.shape[3]), jnp.float32)
    for row_off in range(3):
        for col_off in range(3):
            window = widened[
                :, row_off : row_off + row_count, col_off : col_off + col_count, :
            ].astype(jnp.float32)
            summed = summed + window * conv_taps[row_off * 3 + col_off]
    return (summed[..., :half_width] * jax.nn.silu(summed[..., half_width:])).astype(jnp.bfloat16)


def local(
    query_in, key_in, value_in, stream_in, attn_gain, ffn_gain, in_weight, conv_weight, out_weight
):
    frame_count, row_count, col_count, model_width = query_in.shape
    token_count = frame_count * row_count * col_count
    local_gated = in_weight.shape[2]
    highest = lax.Precision.HIGHEST
    key_pos = jnp.maximum(key_in, 0).reshape(token_count, HEADS, HEAD_DIM)
    value_heads = value_in.reshape(token_count, HEADS, HEAD_DIM)
    local_state = jnp.einsum(
        "thi,thj->ihj", key_pos, value_heads, preferred_element_type=jnp.float32
    ).reshape(HEAD_DIM, model_width)
    local_total = jnp.sum(key_pos.reshape(token_count, model_width), axis=0, dtype=jnp.float32)
    state_share, total_share = (
        lax.psum_scatter(
            local_state.astype(jnp.bfloat16), "row", scatter_dimension=1, tiled=True
        ).astype(jnp.float32),
        lax.psum_scatter(
            local_total.astype(jnp.bfloat16), "row", scatter_dimension=0, tiled=True
        ).astype(jnp.float32),
    )
    state_share, total_share = lax.psum((state_share, total_share), "frame")
    kv_state, key_total = (
        lax.all_gather(state_share, "row", axis=1, tiled=True),
        lax.all_gather(total_share, "row", axis=0, tiled=True),
    )
    query_pos = jnp.maximum(query_in, 0).reshape(token_count, HEADS, HEAD_DIM).astype(jnp.float32)
    numerator = jnp.einsum(
        "thi,ihj->thj", query_pos, kv_state.reshape(HEAD_DIM, HEADS, HEAD_DIM), precision=highest
    )
    denominator = jnp.einsum(
        "thi,hi->th", query_pos, key_total.reshape(HEADS, HEAD_DIM), precision=highest
    )
    attended = (numerator / (denominator[:, :, None] + SHARE_EPS)).reshape(token_count, model_width)
    stream_flat = stream_in.reshape(token_count, model_width).astype(jnp.float32)
    stream_out = (stream_flat + attn_gain.astype(jnp.float32) * rms_norm(attended)).astype(
        jnp.bfloat16
    )
    normed = (rms_norm(stream_out.astype(jnp.float32)) * ffn_gain.astype(jnp.float32)).astype(
        jnp.bfloat16
    )
    normed_grid = normed.reshape(frame_count, row_count, col_count, model_width)
    in_full = lax.all_gather(in_weight, "row", axis=0, tiled=True).reshape(
        model_width, 2 * local_gated
    )
    conv_taps = conv_weight.reshape(9, 2 * local_gated).astype(jnp.float32)
    frame_piece = lax.all_gather(normed_grid, "frame", axis=0, tiled=True)
    piece_frames = frame_piece.shape[0]
    piece_rows = frame_piece.shape[1]
    projected = jnp.dot(
        frame_piece.reshape(piece_frames * piece_rows * col_count, model_width),
        in_full,
        preferred_element_type=jnp.float32,
    )
    expanded = (
        jax.nn.silu(projected)
        .astype(jnp.bfloat16)
        .reshape(piece_frames, piece_rows, col_count, 2 * local_gated)
    )
    padded_expanded = padded_2(expanded, (("row", 1),), 1)
    hidden = depthwise(padded_expanded, conv_taps, row_count, col_count, local_gated)
    hidden_flat = hidden.reshape(-1, local_gated)
    ffn_rows = lax.psum_scatter(
        jnp.dot(hidden_flat, out_weight, preferred_element_type=jnp.float32).astype(jnp.bfloat16),
        "frame",
        scatter_dimension=0,
        tiled=True,
    ).astype(jnp.float32)
    block_out = (stream_out.astype(jnp.float32) + ffn_rows).astype(jnp.bfloat16)
    grid_shape = (frame_count, row_count, col_count, model_width)
    return (stream_out.reshape(grid_shape), block_out.reshape(grid_shape))


def solution(mesh):
    in_specs = (
        P(("groups", "frame"), "row", None, None),
        P(("groups", "frame"), "row", None, None),
        P(("groups", "frame"), "row", None, None),
        P(("groups", "frame"), "row", None, None),
        P(),
        P(),
        P("row", None, "frame"),
        P(None, None, "frame"),
        P("frame", None),
    )
    out_specs = (
        P(("groups", "frame"), "row", None, None),
        P(("groups", "frame"), "row", None, None),
    )
    return jax.shard_map(local, mesh=mesh, in_specs=in_specs, out_specs=out_specs, check_vma=False)
```

profile of v0, /device:TPU:2, one launch (start us, length us, event | category | flops | bytes accessed | tf_op | source)
XLA Modules:
  0.0 291.0 jit_solution(11495132540162727477)
XLA Ops:
  7.2 1.1 fusion.21
  8.3 0.4 reshape.204
  8.7 1.4 reshape.205
  10.1 0.4 fusion.7
  10.5 1.1 copy.25
  11.6 0.7 all-gather.5.cloned.1.call-update
  12.5 0.4 reshape.207
  12.9 0.6 fusion.25
  14.8 12.8 %all-reduce.2 = bf16[2240]{0:T(1024)(128)(2,1)S(1)} all-reduce(bf16[2240]{0:T(1024)(128)(2,1)S(1)} %get-tuple-element.8), channel_id=3, replica_groups=mesh['groups'=2,'frame'=4,'row'=4] {'row'}, use_global_device_ids=true, to_apply=%region_3.0.clone | all-reduce | flops 2240 | bytes 8960
  27.7 7.2 %reduce-scatter.3.cloned.1.call-done = bf16[112,560]{0,1:T(8,128)(2,1)} async-done(((bf16[112,2240]{0,1:T(8,128)(2,1)}), bf16[112,560]{0,1:T(8,128)(2,1)}) %reduce-scatter.3.cloned.1.call-update) | async-done | bytes 125456 | tf_op jit(solution)/shard_map/reduce_scatter | solution.py:61
  34.9 14.8 %all-reduce.5 = (f32[112,560]{0,1:T(8,128)S(1)}, f32[560]{0:T(1024)S(1)}) all-reduce(bf16[112,560]{0,1:T(8,128)(2,1)} %reduce-scatter.3.cloned.1.call-done, f32[560]{0:T(1024)S(1)} %dynamic-slice_convert_fusion), channel_id=1, replica_groups=mesh['groups'=2,'frame'=4,'row'=4] {'frame'}, use_global_device_ids=true, to_apply=%region_1.0 | all-reduce | flops 63280 | bytes 380800 | tf_op jit(solution)/shard_map/psum | solution.py:68
  49.7 0.3 dynamic-update-slice
  50.0 18.8 %all-reduce.1 = f32[2240]{0:T(1024)S(1)} all-reduce(f32[2240]{0:T(1024)S(1)} %dynamic-update-slice), channel_id=1, replica_groups=mesh['groups'=2,'frame'=4,'row'=4] {'row'}, use_global_device_ids=true, to_apply=%add.1 | all-reduce | flops 2240 | bytes 17920
  68.9 0.6 fusion.17
  69.5 39.5 %all_gather.12 = f32[112,2240]{0,1:T(8,128)S(1)} all-gather(f32[112,560]{0,1:T(8,128)S(1)} %get-tuple-element.2), channel_id=1, replica_groups=mesh['groups'=2,'frame'=4,'row'=4] {'row'}, dimensions={1}, use_global_device_ids=true | all-gather | bytes 1254400 | tf_op jit(solution)/shard_map/all_gather | solution.py:70
  109.0 1.4 multiply_reduce_fusion
  110.4 0.4 copy.28
  111.7 1.0 multiply_convert_fusion.1
  112.8 84.7 %all-gather.5.cloned.1.call-done = bf16[2240,2,840]{2,1,0:T(2,128)(2,1)} async-done(((bf16[560,2,840]{2,1,0:T(2,128)(2,1)}), bf16[2240,2,840]{2,1,0:T(2,128)(2,1)}) %all-gather.5.cloned.1.call-update) | async-done | bytes 7526416 | tf_op jit(solution)/shard_map/all_gather | solution.py:89
  197.5 22.9 %copy.30 = bf16[2240,2,840]{0,2,1:T(8,128)(2,1)} copy(bf16[2240,2,840]{2,1,0:T(2,128)(2,1)} %all-gather.5.cloned.1.call-done) | data formatting | bytes 15052800 | tf_op jit(solution)/shard_map/all_gather | solution.py:89
  220.5 5.8 %multiply_convert_fusion = bf16[256,1680]{0,1:T(8,128)(2,1)S(1)} fusion(bf16[256,2240]{1,0:T(8,128)(2,1)} %bitcast.49, bf16[2240,1680]{0,1:T(8,128)(2,1)} %bitcast.45), kind=kOutput, calls=%fused_computation.10 | convolution fusion | flops 1928908800 | bytes 9533440 | tf_op jit(solution)/shard_map/dot_general | solution.py:96
  226.3 0.6 copy.31
  226.9 1.3 collective-permute-start.1
  228.2 4.8 %collective-permute-start = (bf16[4,1,64,1680]{3,2,0,1:T(8,128)(2,1)S(1)}, bf16[4,1,64,1680]{3,2,0,1:T(8,128)(2,1)S(1)}, u32[]{:S(2)}, u32[]{:S(2)}) collective-permute-start(bf16[4,1,64,1680]{3,2,0,1:T(8,128)(2,1)S(1)} %bitcast.42), channel_id=1, source_target_pairs={{0,1},{1,2},{2,3},{4,5},{5,6},{6,7},{8,9},{9,10},{10,11},{12,13},{... | collective-permute-start | bytes 2580488 | tf_op jit(solution)/shard_map/ppermute | solution.py:22
  233.8 17.4 %collective-permute-done.1 = bf16[4,1,64,1680]{3,2,0,1:T(8,128)(2,1)S(1)} collective-permute-done((bf16[4,1,64,1680]{3,2,0,1:T(8,128)(2,1)S(1)}, bf16[4,1,64,1680]{3,2,0,1:T(8,128)(2,1)S(1)}, u32[]{:S(2)}, u32[]{:S(2)}) %collective-permute-start.1) | collective-permute-done | bytes 860192 | tf_op jit(solution)/shard_map/ppermute | solution.py:24
  251.1 1.2 collective-permute-done
  252.3 1.1 fusion.5
  253.4 1.8 multiply_add_fusion
  255.2 0.3 fusion.8
  255.5 2.4 convolution_convert_fusion
  258.0 24.8 %reduce-scatter.5.cloned.1.call-done = bf16[64,2240]{1,0:T(8,128)(2,1)} async-done(((bf16[256,2240]{1,0:T(8,128)(2,1)}), bf16[64,2240]{1,0:T(8,128)(2,1)}) %reduce-scatter.5.cloned.1.call-update) | async-done | bytes 286736 | tf_op jit(solution)/shard_map/reduce_scatter | solution.py:109
  282.7 1.7 fusion.16
  (44 shorter events, 2.0 us)
Async XLA Ops:
  7.2 27.7 %reduce-scatter.3.cloned.1.call-start = ((), (), s32[]{:S(2)}) async-start(), calls=%async_computation.2 | async-start | bytes 716800 | tf_op jit(solution)/shard_map/reduce_scatter | solution.py:61
  10.4 2.0 copy-start.3
  10.5 2.0 copy-start.4
  10.5 2.0 copy-start.1
  11.6 1.4 copy-start.5
  11.6 185.9 %all-gather.5.cloned.1.call-start = ((), (), s32[]{:S(2)}) async-start(), calls=%async_computation.4 | async-start | bytes 10035200 | tf_op jit(solution)/shard_map/all_gather | solution.py:89
  12.4 208.1 %all-gather.3.cloned.1.call-start = ((), (), s32[]{:S(2)}) async-start(), calls=%async_computation.3 | async-start | bytes 1474560 | tf_op jit(solution)/shard_map/all_gather | solution.py:93
  110.4 1.0 copy-start
  112.8 170.0 %reduce-scatter.5.cloned.1.call-start = ((), (), s32[]{:S(2)}) async-start(), calls=%async_computation.5 | async-start | bytes 1474560 | tf_op jit(solution)/shard_map/reduce_scatter | solution.py:109
  220.5 12.6 %copy-start.2 = (bf16[9,2,840]{2,1,0:T(2,128)(2,1)S(1)}, bf16[9,2,840]{2,1,0:T(2,128)(2,1)}, u32[]{:S(2)}) copy-start(bf16[9,2,840]{2,1,0:T(2,128)(2,1)} %param.16) | copy-start | bytes 90724
  226.9 24.2 %collective-permute-start.1 = (bf16[4,1,64,1680]{3,2,0,1:T(8,128)(2,1)S(1)}, bf16[4,1,64,1680]{3,2,0,1:T(8,128)(2,1)S(1)}, u32[]{:S(2)}, u32[]{:S(2)}) collective-permute-start(bf16[4,1,64,1680]{3,2,0,1:T(8,128)(2,1)S(1)} %bitcast.41), channel_id=1, source_target_pairs={{1,0},{2,1},{3,2},{5,4},{6,5},{7,6},{9,8},{10,9},{11,10},{13,12},{... | collective-permute-start | bytes 2580488 | tf_op jit(solution)/shard_map/ppermute | solution.py:24
  228.2 24.1 %collective-permute-start = (bf16[4,1,64,1680]{3,2,0,1:T(8,128)(2,1)S(1)}, bf16[4,1,64,1680]{3,2,0,1:T(8,128)(2,1)S(1)}, u32[]{:S(2)}, u32[]{:S(2)}) collective-permute-start(bf16[4,1,64,1680]{3,2,0,1:T(8,128)(2,1)S(1)} %bitcast.42), channel_id=1, source_target_pairs={{0,1},{1,2},{2,3},{4,5},{5,6},{6,7},{8,9},{9,10},{10,11},{12,13},{... | collective-permute-start | bytes 2580488 | tf_op jit(solution)/shard_map/ppermute | solution.py:22
  253.4 2.1 copy-start.6
Sparse Core Ops, SparseCore 0:
  11.7 23.1 reduce-scatter.2
  36.5 161.0 all-gather.4
  199.7 14.5 all-gather.2
  258.1 24.6 reduce-scatter.4
where the time goes:
time: 295 us; the launch traced here: 291 us
  waiting for transfers between devices  136 us (46%)
  blocking collectives  85.9 us (29%)
  local copies, waits for them, and re-layouts  29.5 us (10%)
  between operations  15.4 us (5%)
  matrix products  10.6 us (4%)
  other arithmetic  7.42 us (3%)
  starting transfers between devices  6.24 us (2%)
    all_gather x1, waiting for transfers between devices, local(): lax.all_gather(in_weight, 'row', axis=0, tiled=True)  84.7 us
    all_gather x1, blocking collectives, local(): lax.all_gather(state_share, 'row', axis=1, tiled=True)  39.5 us
    unnamed x2, blocking collectives  31.6 us
    reduce_scatter x1, waiting for transfers between devices, local(): lax.psum_scatter(jnp.dot(hidden_flat, out_weight, preferred_element_type=...  24.8 us
    all_gather x1, local copies, waits for them, and re-layouts, local(): lax.all_gather(in_weight, 'row', axis=0, tiled=True)  22.9 us
    ppermute x1, waiting for transfers between devices, padded_2(): lax.ppermute(head, axis, [((i + 1) % count, i) for i in range(ends)])  17.4 us
    psum x1, blocking collectives, local(): state_share, total_share = lax.psum((state_share, total_share), 'frame')  14.8 us
    reduce_scatter x1, waiting for transfers between devices, local(): lax.psum_scatter(local_state.astype(jnp.bfloat16), 'row', scatter_dimensi...  7.2 us
  transfers between devices with their start and end apart: 6, of which 5 were waited for; matrix products, arithmetic and copies ran while one was open for 10% of the time, Pallas kernels for 0%

commit v1 on v0

--- a/solution.py
+++ b/solution.py
@@ -57,19 +57,11 @@
         "thi,thj->ihj", key_pos, value_heads, preferred_element_type=jnp.float32
     ).reshape(HEAD_DIM, model_width)
     local_total = jnp.sum(key_pos.reshape(token_count, model_width), axis=0, dtype=jnp.float32)
-    state_share, total_share = (
-        lax.psum_scatter(
-            local_state.astype(jnp.bfloat16), "row", scatter_dimension=1, tiled=True
-        ).astype(jnp.float32),
-        lax.psum_scatter(
-            local_total.astype(jnp.bfloat16), "row", scatter_dimension=0, tiled=True
-        ).astype(jnp.float32),
-    )
-    state_share, total_share = lax.psum((state_share, total_share), "frame")
-    kv_state, key_total = (
-        lax.all_gather(state_share, "row", axis=1, tiled=True),
-        lax.all_gather(total_share, "row", axis=0, tiled=True),
-    )
+    stats = jnp.concatenate([local_state, local_total[None, :]], axis=0)
+    stats = lax.psum_scatter(stats, "frame", scatter_dimension=1, tiled=True)
+    stats = lax.psum(stats, "row")
+    stats = lax.all_gather(stats, "frame", axis=1, tiled=True)
+    kv_state, key_total = stats[:HEAD_DIM], stats[HEAD_DIM]
     query_pos = jnp.maximum(query_in, 0).reshape(token_count, HEADS, HEAD_DIM).astype(jnp.float32)
     numerator = jnp.einsum(
         "thi,ihj->thj", query_pos, kv_state.reshape(HEAD_DIM, HEADS, HEAD_DIM), precision=highest
@@ -86,23 +78,24 @@
         jnp.bfloat16
     )
     normed_grid = normed.reshape(frame_count, row_count, col_count, model_width)
-    in_full = lax.all_gather(in_weight, "row", axis=0, tiled=True).reshape(
-        model_width, 2 * local_gated
+    conv_taps = conv_weight.reshape(9, 2 * local_gated).astype(jnp.float32)
+    row_parts = lax.axis_size("row")
+    local_depth = in_weight.shape[0]
+    split = jnp.moveaxis(
+        normed_grid.reshape(frame_count, row_count, col_count, row_parts, local_depth), 3, 0
     )
-    conv_taps = conv_weight.reshape(9, 2 * local_gated).astype(jnp.float32)
-    frame_piece = lax.all_gather(normed_grid, "frame", axis=0, tiled=True)
-    piece_frames = frame_piece.shape[0]
-    piece_rows = frame_piece.shape[1]
-    projected = jnp.dot(
-        frame_piece.reshape(piece_frames * piece_rows * col_count, model_width),
-        in_full,
+    swapped = lax.all_to_all(split, "row", split_axis=0, concat_axis=0, tiled=True)
+    tokens = lax.all_gather(swapped, "frame", axis=1, tiled=True)
+    piece_frames = tokens.shape[1]
+    partial = jnp.dot(
+        tokens.reshape(-1, local_depth),
+        in_weight.reshape(local_depth, 2 * local_gated),
         preferred_element_type=jnp.float32,
+    ).astype(jnp.bfloat16)
+    summed = lax.psum_scatter(partial, "row", scatter_dimension=0, tiled=True).reshape(
+        piece_frames, row_count, col_count, 2 * local_gated
     )
-    expanded = (
-        jax.nn.silu(projected)
-        .astype(jnp.bfloat16)
-        .reshape(piece_frames, piece_rows, col_count, 2 * local_gated)
-    )
+    expanded = jax.nn.silu(summed.astype(jnp.float32)).astype(jnp.bfloat16)
     padded_expanded = padded_2(expanded, (("row", 1),), 1)
     hidden = depthwise(padded_expanded, conv_taps, row_count, col_count, local_gated)
     hidden_flat = hidden.reshape(-1, local_gated)

time: 295 us -> 272 us (0.922)
  blocking collectives: 85.9 us -> 24.1 us
  waiting for transfers between devices: 136 us -> 173 us
  other arithmetic: 7.42 us -> 14.7 us
  local copies, waits for them, and re-layouts: 29.5 us -> 26.5 us
    reduce_scatter x1 -> x2, waiting for transfers between devices: 7.2 us -> 91.8 us  [the longest x1 66.1 us: local(): lax.psum_scatter(partial, 'row', scatter_dimension=0, tiled=True)]
    all_gather x2 -> x1, waiting for transfers between devices: 84.7 us -> 11.8 us  [local(): tokens = lax.all_gather(swapped, 'frame', axis=1, tiled=True)]
    psum x0 -> x1, waiting for transfers between devices: none -> 38.1 us  [local(): stats = lax.psum(stats, 'row')]
    unnamed x2 -> x0, blocking collectives: 31.6 us -> none
    all_gather x1, blocking collectives: 39.5 us -> 9.82 us  [local(): stats = lax.all_gather(stats, 'frame', axis=1, tiled=True)]
    all_gather x1, local copies, waits for them, and re-layouts: 22.9 us -> 1.43 us  [local(): tokens = lax.all_gather(swapped, 'frame', axis=1, tiled=True)]
    psum x1 -> x0, blocking collectives: 14.8 us -> none  [local(): state_share, total_share = lax.psum((state_share, total_share), 'frame')]
    all_to_all x0 -> x1, blocking collectives: none -> 14.2 us  [local(): lax.all_to_all(split, 'row', split_axis=0, concat_axis=0, tiled=True)]
  transfers between devices with their start and end apart: 6 -> 7, of which waited for: 5 -> 7; matrix products, arithmetic and copies ran while one was open for 10% -> 7% of each run, Pallas kernels for 0% -> 0%
where the time goes in v1:
time: 272 us; the launch traced here: 268 us
  waiting for transfers between devices  173 us (64%)
  local copies, waits for them, and re-layouts  26.5 us (10%)
  blocking collectives  24.1 us (9%)
  other arithmetic  14.7 us (5%)
  between operations  14.2 us (5%)
  matrix products  9.26 us (3%)
  starting transfers between devices  6.96 us (3%)
    reduce_scatter x1, waiting for transfers between devices, local(): lax.psum_scatter(partial, 'row', scatter_dimension=0, tiled=True)  66.1 us
    psum x1, waiting for transfers between devices, local(): stats = lax.psum(stats, 'row')  38.1 us
    reduce_scatter x1, waiting for transfers between devices, local(): stats = lax.psum_scatter(stats, 'frame', scatter_dimension=1, tiled=True)  25.7 us
    reduce_scatter x1, waiting for transfers between devices, local(): lax.psum_scatter(jnp.dot(hidden_flat, out_weight, preferred_element_type=...  25.4 us
    all_to_all x1, blocking collectives, local(): lax.all_to_all(split, 'row', split_axis=0, concat_axis=0, tiled=True)  14.2 us
    mul x9, local copies, waits for them, and re-layouts, depthwise(): summed = summed + window * conv_taps[row_off * 3 + col_off]  12.3 us
    all_gather x1, waiting for transfers between devices, local(): tokens = lax.all_gather(swapped, 'frame', axis=1, tiled=True)  11.8 us
    all_gather x1, blocking collectives, local(): stats = lax.all_gather(stats, 'frame', axis=1, tiled=True)  9.82 us
  transfers between devices with their start and end apart: 7, of which 7 were waited for; matrix products, arithmetic and copies ran while one was open for 7% of the time, Pallas kernels for 0%

profile of v1, /device:TPU:2, one launch (start us, length us, event | category | flops | bytes accessed | tf_op | source)
XLA Modules:
  0.0 268.4 jit_solution(16932302883645566489)
XLA Ops:
  9.7 1.4 reshape.281
  12.1 1.4 pad_maximum_fusion
  13.6 25.7 %reduce-scatter.4.cloned.1.call-done = f32[113,560]{0,1:T(8,128)} async-done(((f32[113,2240]{0,1:T(8,128)}), f32[113,560]{0,1:T(8,128)}) %reduce-scatter.4.cloned.1.call-update) | async-done | bytes 253136 | tf_op jit(solution)/shard_map/reduce_scatter | solution.py:61
  40.5 38.1 %all-reduce.3.cloned.1.call-done = f32[113,560]{0,1:T(8,128)} async-done(((f32[113,560]{0,1:T(8,128)}), f32[113,560]{0,1:T(8,128)}) %all-reduce.3.cloned.1.call-update) | async-done | bytes 253136 | tf_op jit(solution)/shard_map/psum | solution.py:62
  78.6 9.8 %all_gather.6 = f32[113,2240]{0,1:T(8,128)S(1)} all-gather(f32[113,560]{0,1:T(8,128)} %all-reduce.3.cloned.1.call-done), channel_id=1, replica_groups=mesh['groups'=2,'frame'=4,'row'=4] {'frame'}, dimensions={1}, use_global_device_ids=true | all-gather | bytes 1265600 | tf_op jit(solution)/shard_map/all_gather | solution.py:63
  89.8 1.4 multiply_reduce_fusion
  93.8 14.2 %all_to_all.5 = bf16[4,1,1,64,560]{4,3,2,1,0:T(8,128)(2,1)} all-to-all(bf16[4,1,1,64,560]{4,3,2,1,0:T(8,128)(2,1)S(1)} %copy.44), channel_id=1, replica_groups=mesh['groups'=2,'frame'=4,'row'=4] {'row'}, dimensions={0} | all-to-all | bytes 573440 | tf_op jit(solution)/shard_map/all_to_all | solution.py:87
  108.1 4.3 %reshape.289 = bf16[560,1680]{1,0:T(8,128)(2,1)S(1)} reshape(bf16[560,2,840]{2,1,0:T(2,128)(2,1)} %param.15) | data formatting | bytes 3763200 | tf_op jit(solution)/shard_map/reshape | solution.py:92
  112.4 11.8 %all-gather.2.cloned.1.call-done = bf16[4,4,1,64,560]{4,3,2,0,1:T(8,128)(2,1)} async-done(((bf16[4,1,1,64,560]{4,3,2,0,1:T(8,128)(2,1)}), bf16[4,4,1,64,560]{4,3,2,0,1:T(8,128)(2,1)}) %all-gather.2.cloned.1.call-update) | async-done | bytes 1146896 | tf_op jit(solution)/shard_map/all_gather | solution.py:88
  124.2 1.4 copy.46
  125.7 4.4 %convolution_convert_fusion.1 = bf16[1024,1680]{0,1:T(8,128)(2,1)} fusion(bf16[1024,560]{1,0:T(8,128)(2,1)S(1)} %bitcast.46, bf16[560,1680]{1,0:T(8,128)(2,1)S(1)} %reshape.289), kind=kOutput, calls=%fused_computation.4 | convolution fusion | flops 1928478720 | bytes 6469120 | tf_op jit(solution)/shard_map/dot_general | solution.py:90
  130.2 66.1 %reduce-scatter.6.cloned.1.call-done = bf16[256,1680]{0,1:T(8,128)(2,1)} async-done(((bf16[1024,1680]{0,1:T(8,128)(2,1)}), bf16[256,1680]{0,1:T(8,128)(2,1)}) %reduce-scatter.6.cloned.1.call-update) | async-done | bytes 860176 | tf_op jit(solution)/shard_map/reduce_scatter | solution.py:95
  196.3 1.4 copy.47
  197.7 1.5 multiply_convert_fusion
  199.2 1.3 collective-permute-start.1
  200.5 5.5 %collective-permute-start = (bf16[4,1,64,1680]{3,2,0,1:T(8,128)(2,1)}, bf16[4,1,64,1680]{3,2,0,1:T(8,128)(2,1)}, u32[]{:S(2)}, u32[]{:S(2)}) collective-permute-start(bf16[4,1,64,1680]{3,2,0,1:T(8,128)(2,1)} %multiply_convert_fusion), channel_id=1, source_target_pairs={{0,1},{1,2},{2,3},{4,5},{5,6},{6,7},{8,9},{9,10},{10,11},{12,13},{... | collective-permute-start | bytes 2580488 | tf_op jit(solution)/shard_map/ppermute | solution.py:22
  206.6 1.4 mul.243
  208.0 1.4 mul.246
  209.3 1.4 mul.249
  210.7 1.4 mul.252
  212.1 1.4 mul.255
  213.4 1.4 mul.258
  214.8 1.4 mul.261
  216.2 1.4 mul.264
  217.5 1.4 mul.267
  219.0 4.3 %collective-permute-done.1 = bf16[4,1,64,1680]{3,2,0,1:T(8,128)(2,1)S(1)} collective-permute-done((bf16[4,1,64,1680]{3,2,0,1:T(8,128)(2,1)}, bf16[4,1,64,1680]{3,2,0,1:T(8,128)(2,1)S(1)}, u32[]{:S(2)}, u32[]{:S(2)}) %collective-permute-start.1) | collective-permute-done | bytes 860192 | tf_op jit(solution)/shard_map/ppermute | solution.py:24
  223.2 1.3 collective-permute-done
  224.5 2.2 fusion.5
  226.8 3.2 %multiply_add_fusion = f32[4,1,64,1680]{3,2,0,1:T(8,128)S(1)} fusion(bf16[4,1,64,1680]{3,2,0,1:T(8,128)(2,1)S(1)} %collective-permute-done.1, bf16[4,1,64,1680]{3,2,0,1:T(8,128)(2,1)} %collective-permute-done, bf16[4,3,66,1680]{3,2,0,1:T(8,128)(2,1)S(1)} %fusion.5, f32[1680]{0:T(1024)S(1)} %copy-done.13, f32[1680]{0:T(1024)S(1)} %copy-done.12, ...), kind=kLoop, calls=%fused_computation.10 | loop fusion | flops 13332480 | bytes 10382400 | tf_op jit(solution)/shard_map/add | solution.py:43
  230.5 2.4 convolution_convert_fusion
  234.7 25.4 %reduce-scatter.8.cloned.1.call-done = bf16[64,2240]{1,0:T(8,128)(2,1)} async-done(((bf16[256,2240]{1,0:T(8,128)(2,1)}), bf16[64,2240]{1,0:T(8,128)(2,1)}) %reduce-scatter.8.cloned.1.call-update) | async-done | bytes 286736 | tf_op jit(solution)/shard_map/reduce_scatter | solution.py:102
  260.1 1.7 fusion.14
  (72 shorter events, 11.6 us)
Async XLA Ops:
  7.2 32.1 %reduce-scatter.4.cloned.1.call-start = ((), (), s32[]{:S(2)}) async-start(), calls=%async_computation.4 | async-start | bytes 1433600 | tf_op jit(solution)/shard_map/reduce_scatter | solution.py:61
  12.1 27.3 %copy-start.3 = (bf16[1,1,64,2240]{3,2,1,0:T(8,128)(2,1)S(1)}, bf16[1,1,64,2240]{3,2,1,0:T(8,128)(2,1)}, u32[]{:S(2)}) copy-start(bf16[1,1,64,2240]{3,2,1,0:T(8,128)(2,1)} %param.9) | copy-start | bytes 860164
  13.5 25.9 %copy-start.14 = (bf16[2240]{0:T(1024)(128)(2,1)S(1)}, bf16[2240]{0:T(1024)(128)(2,1)}, u32[]{:S(2)}) copy-start(bf16[2240]{0:T(1024)(128)(2,1)} %param.13) | copy-start | bytes 13444
  13.5 26.0 %copy-start.15 = (bf16[2240]{0:T(1024)(128)(2,1)S(1)}, bf16[2240]{0:T(1024)(128)(2,1)}, u32[]{:S(2)}) copy-start(bf16[2240]{0:T(1024)(128)(2,1)} %param.14) | copy-start | bytes 13444
  13.5 26.5 %copy-start = (bf16[1,1,64,2240]{3,2,1,0:T(8,128)(2,1)S(1)}, bf16[1,1,64,2240]{3,2,1,0:T(8,128)(2,1)}, u32[]{:S(2)}) copy-start(bf16[1,1,64,2240]{3,2,1,0:T(8,128)(2,1)} %param.12) | copy-start | bytes 860164
  13.5 65.1 %all-reduce.3.cloned.1.call-start = ((), (), s32[]{:S(2)}) async-start(), calls=%async_computation.5 | async-start | bytes 573440 | tf_op jit(solution)/shard_map/psum | solution.py:62
  39.3 84.9 %all-gather.2.cloned.1.call-start = ((), (), s32[]{:S(2)}) async-start(), calls=%async_computation.6 | async-start | bytes 1638400 | tf_op jit(solution)/shard_map/all_gather | solution.py:88
  108.1 88.2 %reduce-scatter.6.cloned.1.call-start = ((), (), s32[]{:S(2)}) async-start(), calls=%async_computation.7 | async-start | bytes 4300800 | tf_op jit(solution)/shard_map/reduce_scatter | solution.py:95
  130.1 130.0 %reduce-scatter.8.cloned.1.call-start = ((), (), s32[]{:S(2)}) async-start(), calls=%async_computation.8 | async-start | bytes 1474560 | tf_op jit(solution)/shard_map/reduce_scatter | solution.py:102
  197.7 8.3 %copy-start.4 = (bf16[9,2,840]{2,1,0:T(2,128)(2,1)S(1)}, bf16[9,2,840]{2,1,0:T(2,128)(2,1)}, u32[]{:S(2)}) copy-start(bf16[9,2,840]{2,1,0:T(2,128)(2,1)} %param.16) | copy-start | bytes 90724
  199.2 24.0 %collective-permute-start.1 = (bf16[4,1,64,1680]{3,2,0,1:T(8,128)(2,1)}, bf16[4,1,64,1680]{3,2,0,1:T(8,128)(2,1)S(1)}, u32[]{:S(2)}, u32[]{:S(2)}) collective-permute-start(bf16[4,1,64,1680]{3,2,0,1:T(8,128)(2,1)} %multiply_convert_fusion), channel_id=1, source_target_pairs={{1,0},{2,1},{3,2},{5,4},{6,5},{7,6},{9,8},{10,9},{11,10},{13,12},{... | collective-permute-start | bytes 2580488 | tf_op jit(solution)/shard_map/ppermute | solution.py:24
  200.5 24.0 %collective-permute-start = (bf16[4,1,64,1680]{3,2,0,1:T(8,128)(2,1)}, bf16[4,1,64,1680]{3,2,0,1:T(8,128)(2,1)}, u32[]{:S(2)}, u32[]{:S(2)}) collective-permute-start(bf16[4,1,64,1680]{3,2,0,1:T(8,128)(2,1)} %multiply_convert_fusion), channel_id=1, source_target_pairs={{0,1},{1,2},{2,3},{4,5},{5,6},{6,7},{8,9},{9,10},{10,11},{12,13},{... | collective-permute-start | bytes 2580488 | tf_op jit(solution)/shard_map/ppermute | solution.py:22
  218.9 7.9 %copy-start.5 = (f32[1680]{0:T(1024)S(1)}, f32[1680]{0:T(1024)}, u32[]{:S(2)}) copy-start(f32[1680]{0:T(1024)} %mul.243) | copy-start | bytes 20164
  218.9 7.9 %copy-start.6 = (f32[1680]{0:T(1024)S(1)}, f32[1680]{0:T(1024)}, u32[]{:S(2)}) copy-start(f32[1680]{0:T(1024)} %mul.246) | copy-start | bytes 20164
  218.9 7.9 %copy-start.7 = (f32[1680]{0:T(1024)S(1)}, f32[1680]{0:T(1024)}, u32[]{:S(2)}) copy-start(f32[1680]{0:T(1024)} %mul.249) | copy-start | bytes 20164
  218.9 7.9 %copy-start.8 = (f32[1680]{0:T(1024)S(1)}, f32[1680]{0:T(1024)}, u32[]{:S(2)}) copy-start(f32[1680]{0:T(1024)} %mul.252) | copy-start | bytes 20164
  218.9 7.9 %copy-start.9 = (f32[1680]{0:T(1024)S(1)}, f32[1680]{0:T(1024)}, u32[]{:S(2)}) copy-start(f32[1680]{0:T(1024)} %mul.255) | copy-start | bytes 20164
  218.9 7.9 %copy-start.10 = (f32[1680]{0:T(1024)S(1)}, f32[1680]{0:T(1024)}, u32[]{:S(2)}) copy-start(f32[1680]{0:T(1024)} %mul.258) | copy-start | bytes 20164
  218.9 7.9 %copy-start.11 = (f32[1680]{0:T(1024)S(1)}, f32[1680]{0:T(1024)}, u32[]{:S(2)}) copy-start(f32[1680]{0:T(1024)} %mul.261) | copy-start | bytes 20164
  218.9 7.9 %copy-start.12 = (f32[1680]{0:T(1024)S(1)}, f32[1680]{0:T(1024)}, u32[]{:S(2)}) copy-start(f32[1680]{0:T(1024)} %mul.264) | copy-start | bytes 20164
  218.9 7.9 %copy-start.13 = (f32[1680]{0:T(1024)S(1)}, f32[1680]{0:T(1024)}, u32[]{:S(2)}) copy-start(f32[1680]{0:T(1024)} %mul.267) | copy-start | bytes 20164
  226.8 3.6 %copy-start.16 = (bf16[840,2240]{1,0:T(8,128)(2,1)S(1)}, bf16[840,2240]{1,0:T(8,128)(2,1)}, u32[]{:S(2)}) copy-start(bf16[840,2240]{1,0:T(8,128)(2,1)} %param.17) | copy-start | bytes 11289604
  232.9 1.0 copy-start.1
  232.9 27.2 %copy-start.2 = (bf16[64,2240]{1,0:T(8,128)(2,1)S(1)}, bf16[64,2240]{1,0:T(8,128)(2,1)}, u32[]{:S(2)}) copy-start(bf16[64,2240]{1,0:T(8,128)(2,1)} %get-tuple-element.3) | copy-start | bytes 860164
Sparse Core Ops, SparseCore 0:
  13.7 25.5 reduce-scatter.3
  41.8 36.8 all-reduce.2
  108.2 15.9 all-gather.1
  130.2 65.9 reduce-scatter.5
  233.1 26.9 reduce-scatter.7

commit v2 on v1

--- a/solution.py
+++ b/solution.py
@@ -26,6 +26,35 @@
             axis=dim,
         )
     return cells
+
+
+def exchange_steps(axes):
+    steps = []
+    for axis in axes:
+        count = lax.axis_size(axis)
+        bit = 1
+        while bit < count:
+            steps.append((axis, count, bit))
+            bit *= 2
+    return steps
+
+
+def halving_sum(block, axes):
+    steps = exchange_steps(axes)
+    for axis, count, bit in steps:
+        upper = (lax.axis_index(axis) & bit) != 0
+        half = block.shape[1] // 2
+        low, high = block[:, :half], block[:, half:]
+        sent = jnp.where(upper, low, high)
+        kept = jnp.where(upper, high, low)
+        block = kept + lax.ppermute(sent, axis, [(i, i ^ bit) for i in range(count)])
+    for axis, count, bit in reversed(steps):
+        upper = (lax.axis_index(axis) & bit) != 0
+        other = lax.ppermute(block, axis, [(i, i ^ bit) for i in range(count)])
+        block = jnp.where(
+            upper, jnp.concatenate([other, block], 1), jnp.concatenate([block, other], 1)
+        )
+    return block
 
 
 def rms_norm(features):
@@ -58,9 +87,12 @@
     ).reshape(HEAD_DIM, model_width)
     local_total = jnp.sum(key_pos.reshape(token_count, model_width), axis=0, dtype=jnp.float32)
     stats = jnp.concatenate([local_state, local_total[None, :]], axis=0)
-    stats = lax.psum_scatter(stats, "frame", scatter_dimension=1, tiled=True)
-    stats = lax.psum(stats, "row")
-    stats = lax.all_gather(stats, "frame", axis=1, tiled=True)
+    parts = 1
+    for axis, count, bit in exchange_steps(("frame", "row")):
+        parts *= 2
+    padded_width = -(-model_width // parts) * parts
+    stats = jnp.pad(stats, ((0, 0), (0, padded_width - model_width)))
+    stats = halving_sum(stats, ("frame", "row"))[:, :model_width]
     kv_state, key_total = stats[:HEAD_DIM], stats[HEAD_DIM]
     query_pos = jnp.maximum(query_in, 0).reshape(token_count, HEADS, HEAD_DIM).astype(jnp.float32)
     numerator = jnp.einsum(

time: 272 us -> 244 us (0.90)
  waiting for transfers between devices: 173 us -> 138 us
  starting transfers between devices: 6.96 us -> 18.3 us
  blocking collectives: 24.1 us -> 15.7 us
  local copies, waits for them, and re-layouts: 26.5 us -> 30 us
    psum x1 -> x0, waiting for transfers between devices: 38.1 us -> none  [local(): stats = lax.psum(stats, 'row')]
    ppermute x0 -> x8, waiting for transfers between devices: none -> 29 us  [the longest x4 17.2 us: halving_sum(): lax.ppermute(sent, axis, [(i, i ^ bit) for i in range(count)])]
    reduce_scatter x1 -> x0, waiting for transfers between devices: 25.7 us -> none  [local(): stats = lax.psum_scatter(stats, 'frame', scatter_dimension=1, tiled=True)]
    ppermute x0 -> x8, starting transfers between devices: none -> 11.2 us  [the longest x4 6.84 us: halving_sum(): other = lax.ppermute(block, axis, [(i, i ^ bit) for i in range(count)])]
    all_gather x1 -> x0, blocking collectives: 9.82 us -> none  [local(): stats = lax.all_gather(stats, 'frame', axis=1, tiled=True)]
  transfers between devices with their start and end apart: 7 -> 13, of which waited for: 7 -> 13; matrix products, arithmetic and copies ran while one was open for 7% -> 8% of each run, Pallas kernels for 0% -> 0%
where the time goes in v2:
time: 244 us; the launch traced here: 241 us
  waiting for transfers between devices  138 us (57%)
  local copies, waits for them, and re-layouts  30 us (12%)
  starting transfers between devices  18.3 us (8%)
  blocking collectives  15.7 us (6%)
  other arithmetic  15.4 us (6%)
  between operations  14.3 us (6%)
  matrix products  9.28 us (4%)
    reduce_scatter x1, waiting for transfers between devices, local(): lax.psum_scatter(partial, 'row', scatter_dimension=0, tiled=True)  65.9 us
    reduce_scatter x1, waiting for transfers between devices, local(): lax.psum_scatter(jnp.dot(hidden_flat, out_weight, preferred_element_type=...  25.4 us
    ppermute x4, waiting for transfers between devices, halving_sum(): lax.ppermute(sent, axis, [(i, i ^ bit) for i in range(count)])  17.2 us
    all_to_all x1, blocking collectives, local(): lax.all_to_all(split, 'row', split_axis=0, concat_axis=0, tiled=True)  15.7 us
    mul x9, local copies, waits for them, and re-layouts, depthwise(): summed = summed + window * conv_taps[row_off * 3 + col_off]  12.3 us
    all_gather x1, waiting for transfers between devices, local(): tokens = lax.all_gather(swapped, 'frame', axis=1, tiled=True)  11.9 us
    ppermute x4, waiting for transfers between devices, halving_sum(): other = lax.ppermute(block, axis, [(i, i ^ bit) for i in range(count)])  11.8 us
    ppermute x4, starting transfers between devices, halving_sum(): other = lax.ppermute(block, axis, [(i, i ^ bit) for i in range(count)])  6.84 us
  transfers between devices with their start and end apart: 13, of which 13 were waited for; matrix products, arithmetic and copies ran while one was open for 8% of the time, Pallas kernels for 0%

profile of v2, /device:TPU:2, one launch (start us, length us, event | category | flops | bytes accessed | tf_op | source)
XLA Modules:
  0.0 240.7 jit_solution(13183726941034829837)
XLA Ops:
  9.7 1.4 reshape.281
  13.6 2.2 collective-permute-done
  18.2 8.9 %collective-permute-done.1 = f32[113,560]{0,1:T(8,128)S(1)} collective-permute-done((f32[113,560]{0,1:T(8,128)S(1)}, f32[113,560]{0,1:T(8,128)S(1)}, u32[]{:S(2)}, u32[]{:S(2)}) %collective-permute-start.1) | collective-permute-done | bytes 253152 | tf_op jit(solution)/shard_map/ppermute | solution.py:50
  27.2 1.6 collective-permute-start.2
  28.8 3.5 %collective-permute-done.2 = f32[113,280]{0,1:T(8,128)S(1)} collective-permute-done((f32[113,280]{0,1:T(8,128)S(1)}, f32[113,280]{0,1:T(8,128)S(1)}, u32[]{:S(2)}, u32[]{:S(2)}) %collective-permute-start.2) | collective-permute-done | bytes 126592 | tf_op jit(solution)/shard_map/ppermute | solution.py:50
  32.4 2.7 %collective-permute-start.3 = (f32[113,140]{0,1:T(8,128)S(1)}, f32[113,140]{0,1:T(8,128)S(1)}, u32[]{:S(2)}, u32[]{:S(2)}) collective-permute-start(f32[113,140]{0,1:T(8,128)S(1)} %slice_select_fusion.2), channel_id=1, source_target_pairs={{0,2},{1,3},{2,0},{3,1},{4,6},{5,7},{6,4},{7,5},{8,10},{9,11},{10,... | collective-permute-start | bytes 189848 | tf_op jit(solution)/shard_map/ppermute | solution.py:50
  35.1 2.7 %collective-permute-done.3 = f32[113,140]{0,1:T(8,128)S(1)} collective-permute-done((f32[113,140]{0,1:T(8,128)S(1)}, f32[113,140]{0,1:T(8,128)S(1)}, u32[]{:S(2)}, u32[]{:S(2)}) %collective-permute-start.3) | collective-permute-done | bytes 63312 | tf_op jit(solution)/shard_map/ppermute | solution.py:50
  37.7 2.7 %collective-permute-start.4 = (f32[113,140]{0,1:T(8,128)S(1)}, f32[113,140]{0,1:T(8,128)S(1)}, u32[]{:S(2)}, u32[]{:S(2)}) collective-permute-start(f32[113,140]{0,1:T(8,128)S(1)} %select_add_fusion.3), channel_id=1, source_target_pairs={{0,2},{1,3},{2,0},{3,1},{4,6},{5,7},{6,4},{7,5},{8,10},{9,11},{10,... | collective-permute-start | bytes 189848 | tf_op jit(solution)/shard_map/ppermute | solution.py:53
  40.5 2.7 %collective-permute-done.4 = f32[113,140]{0,1:T(8,128)S(1)} collective-permute-done((f32[113,140]{0,1:T(8,128)S(1)}, f32[113,140]{0,1:T(8,128)S(1)}, u32[]{:S(2)}, u32[]{:S(2)}) %collective-permute-start.4) | collective-permute-done | bytes 63312 | tf_op jit(solution)/shard_map/ppermute | solution.py:53
  43.2 3.5 %collective-permute-start.5 = (f32[113,280]{0,1:T(8,128)S(1)}, f32[113,280]{0,1:T(8,128)S(1)}, u32[]{:S(2)}, u32[]{:S(2)}) collective-permute-start(f32[113,280]{0,1:T(8,128)S(1)} %maximum_select_fusion.3), channel_id=1, source_target_pairs={{0,1},{1,0},{2,3},{3,2},{4,5},{5,4},{6,7},{7,6},{8,9},{9,8},{10,11... | collective-permute-start | bytes 379688 | tf_op jit(solution)/shard_map/ppermute | solution.py:53
  46.6 3.1 %collective-permute-done.5 = f32[113,280]{0,1:T(8,128)S(1)} collective-permute-done((f32[113,280]{0,1:T(8,128)S(1)}, f32[113,280]{0,1:T(8,128)S(1)}, u32[]{:S(2)}, u32[]{:S(2)}) %collective-permute-start.5) | collective-permute-done | bytes 126592 | tf_op jit(solution)/shard_map/ppermute | solution.py:53
  50.6 5.9 %collective-permute-done.6 = f32[113,560]{0,1:T(8,128)S(1)} collective-permute-done((f32[113,560]{0,1:T(8,128)S(1)}, f32[113,560]{0,1:T(8,128)S(1)}, u32[]{:S(2)}, u32[]{:S(2)}) %collective-permute-start.6) | collective-permute-done | bytes 253152 | tf_op jit(solution)/shard_map/ppermute | solution.py:53
  60.6 1.4 multiply_reduce_fusion
  64.6 15.7 %all_to_all.5 = bf16[4,1,1,64,560]{4,3,2,1,0:T(8,128)(2,1)} all-to-all(bf16[4,1,1,64,560]{4,3,2,1,0:T(8,128)(2,1)S(1)} %copy.49), channel_id=1, replica_groups=mesh['groups'=2,'frame'=4,'row'=4] {'row'}, dimensions={0} | all-to-all | bytes 573440 | tf_op jit(solution)/shard_map/all_to_all | solution.py:119
  80.3 4.3 %reshape.289 = bf16[560,1680]{1,0:T(8,128)(2,1)S(1)} reshape(bf16[560,2,840]{2,1,0:T(2,128)(2,1)} %param.15) | data formatting | bytes 3763200 | tf_op jit(solution)/shard_map/reshape | solution.py:124
  84.6 11.9 %all-gather.2.cloned.1.call-done = bf16[4,4,1,64,560]{4,3,2,0,1:T(8,128)(2,1)} async-done(((bf16[4,1,1,64,560]{4,3,2,0,1:T(8,128)(2,1)}), bf16[4,4,1,64,560]{4,3,2,0,1:T(8,128)(2,1)}) %all-gather.2.cloned.1.call-update) | async-done | bytes 1146896 | tf_op jit(solution)/shard_map/all_gather | solution.py:120
  96.6 1.4 copy.51
  98.0 4.5 %convolution_convert_fusion.1 = bf16[1024,1680]{0,1:T(8,128)(2,1)} fusion(bf16[1024,560]{1,0:T(8,128)(2,1)S(1)} %bitcast.47, bf16[560,1680]{1,0:T(8,128)(2,1)S(1)} %reshape.289), kind=kOutput, calls=%fused_computation.4 | convolution fusion | flops 1928478720 | bytes 6469120 | tf_op jit(solution)/shard_map/dot_general | solution.py:122
  102.7 65.9 %reduce-scatter.3.cloned.1.call-done = bf16[256,1680]{0,1:T(8,128)(2,1)} async-done(((bf16[1024,1680]{0,1:T(8,128)(2,1)}), bf16[256,1680]{0,1:T(8,128)(2,1)}) %reduce-scatter.3.cloned.1.call-update) | async-done | bytes 860176 | tf_op jit(solution)/shard_map/reduce_scatter | solution.py:127
  168.6 1.4 copy.52
  170.1 1.5 multiply_convert_fusion
  172.8 5.5 %collective-permute-start.8 = (bf16[4,1,64,1680]{3,2,0,1:T(8,128)(2,1)}, bf16[4,1,64,1680]{3,2,0,1:T(8,128)(2,1)}, u32[]{:S(2)}, u32[]{:S(2)}) collective-permute-start(bf16[4,1,64,1680]{3,2,0,1:T(8,128)(2,1)} %multiply_convert_fusion), channel_id=1, source_target_pairs={{0,1},{1,2},{2,3},{4,5},{5,6},{6,7},{8,9},{9,10},{10,11},{12,13},{... | collective-permute-start | bytes 2580488 | tf_op jit(solution)/shard_map/ppermute | solution.py:22
  179.0 1.4 mul.243
  183.1 1.4 mul.252
  188.5 1.4 mul.264
  189.9 1.4 mul.267
  191.3 4.2 %collective-permute-done.9 = bf16[4,1,64,1680]{3,2,0,1:T(8,128)(2,1)S(1)} collective-permute-done((bf16[4,1,64,1680]{3,2,0,1:T(8,128)(2,1)}, bf16[4,1,64,1680]{3,2,0,1:T(8,128)(2,1)S(1)}, u32[]{:S(2)}, u32[]{:S(2)}) %collective-permute-start.9) | collective-permute-done | bytes 860192 | tf_op jit(solution)/shard_map/ppermute | solution.py:24
  196.9 2.2 fusion.5
  199.2 3.2 %multiply_add_fusion = f32[4,1,64,1680]{3,2,0,1:T(8,128)S(1)} fusion(bf16[4,1,64,1680]{3,2,0,1:T(8,128)(2,1)S(1)} %collective-permute-done.9, bf16[4,1,64,1680]{3,2,0,1:T(8,128)(2,1)} %collective-permute-done.8, bf16[4,3,66,1680]{3,2,0,1:T(8,128)(2,1)S(1)} %fusion.5, f32[1680]{0:T(1024)S(1)} %copy-done.14, f32[1680]{0:T(1024)S(1)} %copy-done.13, ...), kind=kLoop, calls=%fused_computation.10 | loop fusion | flops 13332480 | bytes 10382400 | tf_op jit(solution)/shard_map/add | solution.py:72
  202.8 2.4 %convolution_convert_fusion = bf16[256,2240]{1,0:T(8,128)(2,1)} fusion(bf16[256,840]{1,0:T(8,128)(2,1)S(1)} %bitcast.49, bf16[840,2240]{1,0:T(8,128)(2,1)S(1)} %copy-done.17), kind=kOutput, calls=%fused_computation.3 | convolution fusion | flops 963952640 | bytes 5340160 | tf_op jit(solution)/shard_map/dot_general | solution.py:135
  207.1 25.4 %reduce-scatter.5.cloned.1.call-done = bf16[64,2240]{1,0:T(8,128)(2,1)} async-done(((bf16[256,2240]{1,0:T(8,128)(2,1)}), bf16[64,2240]{1,0:T(8,128)(2,1)}) %reduce-scatter.5.cloned.1.call-update) | async-done | bytes 286736 | tf_op jit(solution)/shard_map/reduce_scatter | solution.py:134
  232.5 1.7 fusion.15
  (98 shorter events, 27.5 us)
Async XLA Ops:
  7.2 89.4 %all-gather.2.cloned.1.call-start = ((), (), s32[]{:S(2)}) async-start(), calls=%async_computation.3 | async-start | bytes 1638400 | tf_op jit(solution)/shard_map/all_gather | solution.py:120
  13.6 2.2 collective-permute-start
  18.1 32.3 %copy-start.15 = (bf16[2240]{0:T(1024)(128)(2,1)S(1)}, bf16[2240]{0:T(1024)(128)(2,1)}, u32[]{:S(2)}) copy-start(bf16[2240]{0:T(1024)(128)(2,1)} %param.13) | copy-start | bytes 13444
  18.1 32.3 %copy-start.16 = (bf16[2240]{0:T(1024)(128)(2,1)S(1)}, bf16[2240]{0:T(1024)(128)(2,1)}, u32[]{:S(2)}) copy-start(bf16[2240]{0:T(1024)(128)(2,1)} %param.14) | copy-start | bytes 13444
  18.1 8.9 %collective-permute-start.1 = (f32[113,560]{0,1:T(8,128)S(1)}, f32[113,560]{0,1:T(8,128)S(1)}, u32[]{:S(2)}, u32[]{:S(2)}) collective-permute-start(f32[113,560]{0,1:T(8,128)S(1)} %slice_select_fusion), channel_id=1, source_target_pairs={{0,8},{4,12},{8,0},{12,4},{1,9},{5,13},{9,1},{13,5},{2,10},{6,14},... | collective-permute-start | bytes 759368 | tf_op jit(solution)/shard_map/ppermute | solution.py:50
  27.2 5.2 %collective-permute-start.2 = (f32[113,280]{0,1:T(8,128)S(1)}, f32[113,280]{0,1:T(8,128)S(1)}, u32[]{:S(2)}, u32[]{:S(2)}) collective-permute-start(f32[113,280]{0,1:T(8,128)S(1)} %slice_select_fusion.1), channel_id=1, source_target_pairs={{0,1},{1,0},{2,3},{3,2},{4,5},{5,4},{6,7},{7,6},{8,9},{9,8},{10,11... | collective-permute-start | bytes 379688 | tf_op jit(solution)/shard_map/ppermute | solution.py:50
  32.4 24.5 %copy-start.4 = (bf16[1,1,64,2240]{3,2,1,0:T(8,128)(2,1)S(1)}, bf16[1,1,64,2240]{3,2,1,0:T(8,128)(2,1)}, u32[]{:S(2)}) copy-start(bf16[1,1,64,2240]{3,2,1,0:T(8,128)(2,1)} %param.9) | copy-start | bytes 860164
  32.4 5.3 %collective-permute-start.3 = (f32[113,140]{0,1:T(8,128)S(1)}, f32[113,140]{0,1:T(8,128)S(1)}, u32[]{:S(2)}, u32[]{:S(2)}) collective-permute-start(f32[113,140]{0,1:T(8,128)S(1)} %slice_select_fusion.2), channel_id=1, source_target_pairs={{0,2},{1,3},{2,0},{3,1},{4,6},{5,7},{6,4},{7,5},{8,10},{9,11},{10,... | collective-permute-start | bytes 189848 | tf_op jit(solution)/shard_map/ppermute | solution.py:50
  37.7 5.4 %collective-permute-start.4 = (f32[113,140]{0,1:T(8,128)S(1)}, f32[113,140]{0,1:T(8,128)S(1)}, u32[]{:S(2)}, u32[]{:S(2)}) collective-permute-start(f32[113,140]{0,1:T(8,128)S(1)} %select_add_fusion.3), channel_id=1, source_target_pairs={{0,2},{1,3},{2,0},{3,1},{4,6},{5,7},{6,4},{7,5},{8,10},{9,11},{10,... | collective-permute-start | bytes 189848 | tf_op jit(solution)/shard_map/ppermute | solution.py:53
  43.2 6.5 %collective-permute-start.5 = (f32[113,280]{0,1:T(8,128)S(1)}, f32[113,280]{0,1:T(8,128)S(1)}, u32[]{:S(2)}, u32[]{:S(2)}) collective-permute-start(f32[113,280]{0,1:T(8,128)S(1)} %maximum_select_fusion.3), channel_id=1, source_target_pairs={{0,1},{1,0},{2,3},{3,2},{4,5},{5,4},{6,7},{7,6},{8,9},{9,8},{10,11... | collective-permute-start | bytes 379688 | tf_op jit(solution)/shard_map/ppermute | solution.py:53
  49.8 7.6 %copy-start = (bf16[1,1,64,2240]{3,2,1,0:T(8,128)(2,1)S(1)}, bf16[1,1,64,2240]{3,2,1,0:T(8,128)(2,1)}, u32[]{:S(2)}) copy-start(bf16[1,1,64,2240]{3,2,1,0:T(8,128)(2,1)} %param.12) | copy-start | bytes 860164
  49.8 6.7 %collective-permute-start.6 = (f32[113,560]{0,1:T(8,128)S(1)}, f32[113,560]{0,1:T(8,128)S(1)}, u32[]{:S(2)}, u32[]{:S(2)}) collective-permute-start(f32[113,560]{0,1:T(8,128)S(1)} %maximum_select_fusion.2), channel_id=1, source_target_pairs={{0,8},{4,12},{8,0},{12,4},{1,9},{5,13},{9,1},{13,5},{2,10},{6,14},... | collective-permute-start | bytes 759368 | tf_op jit(solution)/shard_map/ppermute | solution.py:53
  56.8 2.0 collective-permute-start.7
  62.4 1.8 copy-start.2
  80.3 88.4 %reduce-scatter.3.cloned.1.call-start = ((), (), s32[]{:S(2)}) async-start(), calls=%async_computation.4 | async-start | bytes 4300800 | tf_op jit(solution)/shard_map/reduce_scatter | solution.py:127
  102.5 130.0 %reduce-scatter.5.cloned.1.call-start = ((), (), s32[]{:S(2)}) async-start(), calls=%async_computation.5 | async-start | bytes 1474560 | tf_op jit(solution)/shard_map/reduce_scatter | solution.py:134
  170.1 8.3 %copy-start.5 = (bf16[9,2,840]{2,1,0:T(2,128)(2,1)S(1)}, bf16[9,2,840]{2,1,0:T(2,128)(2,1)}, u32[]{:S(2)}) copy-start(bf16[9,2,840]{2,1,0:T(2,128)(2,1)} %param.16) | copy-start | bytes 90724
  171.6 24.0 %collective-permute-start.9 = (bf16[4,1,64,1680]{3,2,0,1:T(8,128)(2,1)}, bf16[4,1,64,1680]{3,2,0,1:T(8,128)(2,1)S(1)}, u32[]{:S(2)}, u32[]{:S(2)}) collective-permute-start(bf16[4,1,64,1680]{3,2,0,1:T(8,128)(2,1)} %multiply_convert_fusion), channel_id=1, source_target_pairs={{1,0},{2,1},{3,2},{5,4},{6,5},{7,6},{9,8},{10,9},{11,10},{13,12},{... | collective-permute-start | bytes 2580488 | tf_op jit(solution)/shard_map/ppermute | solution.py:24
  172.8 24.0 %collective-permute-start.8 = (bf16[4,1,64,1680]{3,2,0,1:T(8,128)(2,1)}, bf16[4,1,64,1680]{3,2,0,1:T(8,128)(2,1)}, u32[]{:S(2)}, u32[]{:S(2)}) collective-permute-start(bf16[4,1,64,1680]{3,2,0,1:T(8,128)(2,1)} %multiply_convert_fusion), channel_id=1, source_target_pairs={{0,1},{1,2},{2,3},{4,5},{5,6},{6,7},{8,9},{9,10},{10,11},{12,13},{... | collective-permute-start | bytes 2580488 | tf_op jit(solution)/shard_map/ppermute | solution.py:22
  191.3 7.8 %copy-start.6 = (f32[1680]{0:T(1024)S(1)}, f32[1680]{0:T(1024)}, u32[]{:S(2)}) copy-start(f32[1680]{0:T(1024)} %mul.243) | copy-start | bytes 20164
  191.3 7.8 %copy-start.7 = (f32[1680]{0:T(1024)S(1)}, f32[1680]{0:T(1024)}, u32[]{:S(2)}) copy-start(f32[1680]{0:T(1024)} %mul.246) | copy-start | bytes 20164
  191.3 7.8 %copy-start.8 = (f32[1680]{0:T(1024)S(1)}, f32[1680]{0:T(1024)}, u32[]{:S(2)}) copy-start(f32[1680]{0:T(1024)} %mul.249) | copy-start | bytes 20164
  191.3 7.8 %copy-start.9 = (f32[1680]{0:T(1024)S(1)}, f32[1680]{0:T(1024)}, u32[]{:S(2)}) copy-start(f32[1680]{0:T(1024)} %mul.252) | copy-start | bytes 20164
  191.3 7.9 %copy-start.10 = (f32[1680]{0:T(1024)S(1)}, f32[1680]{0:T(1024)}, u32[]{:S(2)}) copy-start(f32[1680]{0:T(1024)} %mul.255) | copy-start | bytes 20164
  191.3 7.9 %copy-start.11 = (f32[1680]{0:T(1024)S(1)}, f32[1680]{0:T(1024)}, u32[]{:S(2)}) copy-start(f32[1680]{0:T(1024)} %mul.258) | copy-start | bytes 20164
  191.3 7.9 %copy-start.12 = (f32[1680]{0:T(1024)S(1)}, f32[1680]{0:T(1024)}, u32[]{:S(2)}) copy-start(f32[1680]{0:T(1024)} %mul.261) | copy-start | bytes 20164
  191.3 7.9 %copy-start.13 = (f32[1680]{0:T(1024)S(1)}, f32[1680]{0:T(1024)}, u32[]{:S(2)}) copy-start(f32[1680]{0:T(1024)} %mul.264) | copy-start | bytes 20164
  191.3 7.9 %copy-start.14 = (f32[1680]{0:T(1024)S(1)}, f32[1680]{0:T(1024)}, u32[]{:S(2)}) copy-start(f32[1680]{0:T(1024)} %mul.267) | copy-start | bytes 20164
  199.2 3.6 %copy-start.17 = (bf16[840,2240]{1,0:T(8,128)(2,1)S(1)}, bf16[840,2240]{1,0:T(8,128)(2,1)}, u32[]{:S(2)}) copy-start(bf16[840,2240]{1,0:T(8,128)(2,1)} %param.17) | copy-start | bytes 11289604
  205.3 1.0 copy-start.1
  205.3 27.2 %copy-start.3 = (bf16[64,2240]{1,0:T(8,128)(2,1)S(1)}, bf16[64,2240]{1,0:T(8,128)(2,1)}, u32[]{:S(2)}) copy-start(bf16[64,2240]{1,0:T(8,128)(2,1)} %get-tuple-element.3) | copy-start | bytes 860164
Sparse Core Ops, SparseCore 0:
  80.4 16.1 all-gather.1
  102.6 65.9 reduce-scatter.2
  205.4 26.9 reduce-scatter.4

commit v3 on v2

--- a/solution.py
+++ b/solution.py
@@ -57,6 +57,21 @@
     return block
 
 
+def pick(blocks, index):
+    stacked = jnp.stack(blocks)
+    return lax.dynamic_index_in_dim(stacked, index, axis=0, keepdims=False)
+
+
+def swap_chunks(chunks, axis):
+    count = lax.axis_size(axis)
+    own = lax.axis_index(axis)
+    by_mask = [pick(chunks, own)]
+    for mask in range(1, count):
+        sent = pick(chunks, own ^ mask)
+        by_mask.append(lax.ppermute(sent, axis, [(i, i ^ mask) for i in range(count)]))
+    return [pick(by_mask, own ^ source) for source in range(count)]
+
+
 def rms_norm(features):
     return features * lax.rsqrt(jnp.mean(features * features, axis=-1, keepdims=True) + NORM_EPS)
 
@@ -113,12 +128,14 @@
     conv_taps = conv_weight.reshape(9, 2 * local_gated).astype(jnp.float32)
     row_parts = lax.axis_size("row")
     local_depth = in_weight.shape[0]
-    split = jnp.moveaxis(
-        normed_grid.reshape(frame_count, row_count, col_count, row_parts, local_depth), 3, 0
-    )
-    swapped = lax.all_to_all(split, "row", split_axis=0, concat_axis=0, tiled=True)
-    tokens = lax.all_gather(swapped, "frame", axis=1, tiled=True)
-    piece_frames = tokens.shape[1]
+    depth_chunks = [
+        normed_grid[..., part * local_depth : (part + 1) * local_depth] for part in range(row_parts)
+    ]
+    by_row = jnp.concatenate(swap_chunks(depth_chunks, "row"), axis=1)
+    frame_parts = lax.axis_size("frame")
+    by_frame = swap_chunks([by_row] * frame_parts, "frame")
+    tokens = jnp.stack([piece.transpose(1, 0, 2, 3) for piece in by_frame], axis=1)
+    piece_frames = tokens.shape[1] * tokens.shape[2]
     partial = jnp.dot(
         tokens.reshape(-1, local_depth),
         in_weight.reshape(local_depth, 2 * local_gated),
@@ -131,12 +148,13 @@
     padded_expanded = padded_2(expanded, (("row", 1),), 1)
     hidden = depthwise(padded_expanded, conv_taps, row_count, col_count, local_gated)
     hidden_flat = hidden.reshape(-1, local_gated)
-    ffn_rows = lax.psum_scatter(
-        jnp.dot(hidden_flat, out_weight, preferred_element_type=jnp.float32).astype(jnp.bfloat16),
-        "frame",
-        scatter_dimension=0,
-        tiled=True,
-    ).astype(jnp.float32)
+    projected = jnp.dot(hidden_flat, out_weight, preferred_element_type=jnp.float32).astype(
+        jnp.bfloat16
+    )
+    frame_blocks = jnp.split(projected, frame_parts, axis=0)
+    ffn_rows = sum(
+        piece.astype(jnp.float32) for piece in swap_chunks(frame_blocks, "frame")
+    ).reshape(token_count, model_width)
     block_out = (stream_out.astype(jnp.float32) + ffn_rows).astype(jnp.bfloat16)
     grid_shape = (frame_count, row_count, col_count, model_width)
     return (stream_out.reshape(grid_shape), block_out.reshape(grid_shape))

time: 244 us -> 240 us (0.984)
  blocking collectives: 15.7 us -> 0 us
  waiting for transfers between devices: 138 us -> 152 us
  local copies, waits for them, and re-layouts: 30 us -> 20.7 us
  starting transfers between devices: 18.3 us -> 24.1 us
    ppermute x0 -> x9, waiting for transfers between devices: none -> 34.1 us  [swap_chunks(): lax.ppermute(sent, axis, [(i, i ^ mask) for i in range(count)])]
    reduce_scatter x1 -> x0, waiting for transfers between devices: 25.4 us -> none  [local(): lax.psum_scatter(jnp.dot(hidden_flat, out_weight, preferred_element_type=...]
    ppermute x1, waiting for transfers between devices: 1.29 us -> 17.8 us  [padded_2(): lax.ppermute(tail, axis, [(i, (i + 1) % count) for i in range(ends)])]
    all_to_all x1 -> x0, blocking collectives: 15.7 us -> none  [local(): lax.all_to_all(split, 'row', split_axis=0, concat_axis=0, tiled=True)]
    all_gather x1 -> x0, waiting for transfers between devices: 11.9 us -> none  [local(): tokens = lax.all_gather(swapped, 'frame', axis=1, tiled=True)]
    mul x9, local copies, waits for them, and re-layouts: 12.3 us -> 0.71 us  [depthwise(): summed = summed + window * conv_taps[row_off * 3 + col_off]]
    ppermute x0 -> x9, starting transfers between devices: none -> 8.37 us  [swap_chunks(): lax.ppermute(sent, axis, [(i, i ^ mask) for i in range(count)])]
    another operation x0 -> x7, other arithmetic: none -> 3.9 us  [the longest x6 3.65 us: pick(): stacked = jnp.stack(blocks)]
  transfers between devices with their start and end apart: 13 -> 20, of which waited for: 13 -> 17; matrix products, arithmetic and copies ran while one was open for 8% -> 3% of each run, Pallas kernels for 0% -> 0%
where the time goes in v3:
time: 240 us; the launch traced here: 238 us
  waiting for transfers between devices  152 us (63%)
  starting transfers between devices  24.1 us (10%)
  local copies, waits for them, and re-layouts  20.7 us (9%)
  other arithmetic  17.6 us (7%)
  between operations  14.5 us (6%)
  matrix products  8.59 us (4%)
    reduce_scatter x1, waiting for transfers between devices, local(): lax.psum_scatter(partial, 'row', scatter_dimension=0, tiled=True)  65.8 us
    ppermute x9, waiting for transfers between devices, swap_chunks(): lax.ppermute(sent, axis, [(i, i ^ mask) for i in range(count)])  34.1 us
    ppermute x1, waiting for transfers between devices, padded_2(): lax.ppermute(tail, axis, [(i, (i + 1) % count) for i in range(ends)])  17.8 us
    ppermute x4, waiting for transfers between devices, halving_sum(): lax.ppermute(sent, axis, [(i, i ^ bit) for i in range(count)])  17.2 us
    ppermute x4, waiting for transfers between devices, halving_sum(): other = lax.ppermute(block, axis, [(i, i ^ bit) for i in range(count)])  13 us
    ppermute x9, starting transfers between devices, swap_chunks(): lax.ppermute(sent, axis, [(i, i ^ mask) for i in range(count)])  8.37 us
    ppermute x4, starting transfers between devices, halving_sum(): other = lax.ppermute(block, axis, [(i, i ^ bit) for i in range(count)])  6.84 us
  transfers between devices with their start and end apart: 20, of which 17 were waited for; matrix products, arithmetic and copies ran while one was open for 3% of the time, Pallas kernels for 0%

profile of v3, /device:TPU:2, one launch (start us, length us, event | category | flops | bytes accessed | tf_op | source)
XLA Modules:
  0.0 237.7 jit_solution(12524409836655923692)
XLA Ops:
  13.6 2.2 collective-permute-done
  18.2 8.9 %collective-permute-done.1 = f32[113,560]{0,1:T(8,128)S(1)} collective-permute-done((f32[113,560]{0,1:T(8,128)S(1)}, f32[113,560]{0,1:T(8,128)S(1)}, u32[]{:S(2)}, u32[]{:S(2)}) %collective-permute-start.1) | collective-permute-done | bytes 253152 | tf_op jit(solution)/shard_map/ppermute | solution.py:50
  27.2 1.6 collective-permute-start.2
  28.8 3.5 %collective-permute-done.2 = f32[113,280]{0,1:T(8,128)S(1)} collective-permute-done((f32[113,280]{0,1:T(8,128)S(1)}, f32[113,280]{0,1:T(8,128)S(1)}, u32[]{:S(2)}, u32[]{:S(2)}) %collective-permute-start.2) | collective-permute-done | bytes 126592 | tf_op jit(solution)/shard_map/ppermute | solution.py:50
  32.4 2.7 %collective-permute-start.3 = (f32[113,140]{0,1:T(8,128)S(1)}, f32[113,140]{0,1:T(8,128)S(1)}, u32[]{:S(2)}, u32[]{:S(2)}) collective-permute-start(f32[113,140]{0,1:T(8,128)S(1)} %slice_select_fusion.2), channel_id=1, source_target_pairs={{0,2},{1,3},{2,0},{3,1},{4,6},{5,7},{6,4},{7,5},{8,10},{9,11},{10,... | collective-permute-start | bytes 189848 | tf_op jit(solution)/shard_map/ppermute | solution.py:50
  35.1 2.7 %collective-permute-done.3 = f32[113,140]{0,1:T(8,128)S(1)} collective-permute-done((f32[113,140]{0,1:T(8,128)S(1)}, f32[113,140]{0,1:T(8,128)S(1)}, u32[]{:S(2)}, u32[]{:S(2)}) %collective-permute-start.3) | collective-permute-done | bytes 63312 | tf_op jit(solution)/shard_map/ppermute | solution.py:50
  37.7 2.7 %collective-permute-start.4 = (f32[113,140]{0,1:T(8,128)S(1)}, f32[113,140]{0,1:T(8,128)S(1)}, u32[]{:S(2)}, u32[]{:S(2)}) collective-permute-start(f32[113,140]{0,1:T(8,128)S(1)} %select_add_fusion.3), channel_id=1, source_target_pairs={{0,2},{1,3},{2,0},{3,1},{4,6},{5,7},{6,4},{7,5},{8,10},{9,11},{10,... | collective-permute-start | bytes 189848 | tf_op jit(solution)/shard_map/ppermute | solution.py:53
  40.5 2.7 %collective-permute-done.4 = f32[113,140]{0,1:T(8,128)S(1)} collective-permute-done((f32[113,140]{0,1:T(8,128)S(1)}, f32[113,140]{0,1:T(8,128)S(1)}, u32[]{:S(2)}, u32[]{:S(2)}) %collective-permute-start.4) | collective-permute-done | bytes 63312 | tf_op jit(solution)/shard_map/ppermute | solution.py:53
  43.2 3.5 %collective-permute-start.5 = (f32[113,280]{0,1:T(8,128)S(1)}, f32[113,280]{0,1:T(8,128)S(1)}, u32[]{:S(2)}, u32[]{:S(2)}) collective-permute-start(f32[113,280]{0,1:T(8,128)S(1)} %maximum_select_fusion.3), channel_id=1, source_target_pairs={{0,1},{1,0},{2,3},{3,2},{4,5},{5,4},{6,7},{7,6},{8,9},{9,8},{10,11... | collective-permute-start | bytes 379688 | tf_op jit(solution)/shard_map/ppermute | solution.py:53
  46.7 3.1 %collective-permute-done.5 = f32[113,280]{0,1:T(8,128)S(1)} collective-permute-done((f32[113,280]{0,1:T(8,128)S(1)}, f32[113,280]{0,1:T(8,128)S(1)}, u32[]{:S(2)}, u32[]{:S(2)}) %collective-permute-start.5) | collective-permute-done | bytes 126592 | tf_op jit(solution)/shard_map/ppermute | solution.py:53
  50.4 6.1 %collective-permute-done.6 = f32[113,560]{0,1:T(8,128)S(1)} collective-permute-done((f32[113,560]{0,1:T(8,128)S(1)}, f32[113,560]{0,1:T(8,128)S(1)}, u32[]{:S(2)}, u32[]{:S(2)}) %collective-permute-start.6) | collective-permute-done | bytes 253152 | tf_op jit(solution)/shard_map/ppermute | solution.py:53
  60.6 1.4 multiply_reduce_fusion.1
  62.8 1.5 fusion.11
  64.6 2.1 collective-permute-start.8
  66.7 2.3 collective-permute-start.9
  69.1 3.8 %collective-permute-done.8 = bf16[1,1,64,560]{2,3,1,0:T(8,128)(2,1)S(1)} collective-permute-done((bf16[1,1,64,560]{2,3,1,0:T(8,128)(2,1)S(1)}, bf16[1,1,64,560]{2,3,1,0:T(8,128)(2,1)S(1)}, u32[]{:S(2)}, u32[]{:S(2)}) %collective-permute-start.8) | collective-permute-done | bytes 71712 | tf_op jit(solution)/shard_map/ppermute | solution.py:71
  72.9 7.5 %collective-permute-done.9 = bf16[1,1,64,560]{2,3,1,0:T(8,128)(2,1)S(1)} collective-permute-done((bf16[1,1,64,560]{2,3,1,0:T(8,128)(2,1)S(1)}, bf16[1,1,64,560]{2,3,1,0:T(8,128)(2,1)S(1)}, u32[]{:S(2)}, u32[]{:S(2)}) %collective-permute-start.9) | collective-permute-done | bytes 71712 | tf_op jit(solution)/shard_map/ppermute | solution.py:71
  83.8 2.5 %reshape.324 = bf16[560,1680]{1,0:T(8,128)(2,1)} reshape(bf16[560,2,840]{2,1,0:T(2,128)(2,1)S(1)} %copy-done) | data formatting | bytes 3763200 | tf_op jit(solution)/shard_map/reshape | solution.py:141
  86.3 6.5 %collective-permute-done.12 = bf16[1,4,64,560]{3,2,1,0:T(8,128)(2,1)} collective-permute-done((bf16[1,4,64,560]{3,2,1,0:T(8,128)(2,1)}, bf16[1,4,64,560]{3,2,1,0:T(8,128)(2,1)}, u32[]{:S(2)}, u32[]{:S(2)}) %collective-permute-start.12) | collective-permute-done | bytes 286752 | tf_op jit(solution)/shard_map/ppermute | solution.py:71
  92.8 6.2 %collective-permute-done.13 = bf16[1,4,64,560]{3,2,1,0:T(8,128)(2,1)} collective-permute-done((bf16[1,4,64,560]{3,2,1,0:T(8,128)(2,1)}, bf16[1,4,64,560]{3,2,1,0:T(8,128)(2,1)}, u32[]{:S(2)}, u32[]{:S(2)}) %collective-permute-start.13) | collective-permute-done | bytes 286752 | tf_op jit(solution)/shard_map/ppermute | solution.py:71
  102.1 4.4 %convolution_convert_fusion.1 = bf16[1024,1680]{0,1:T(8,128)(2,1)} fusion(bf16[1024,560]{1,0:T(8,128)(2,1)S(1)} %bitcast.106, bf16[560,1680]{1,0:T(8,128)(2,1)S(1)} %copy-done.1), kind=kOutput, calls=%fused_computation.4 | convolution fusion | flops 1928478720 | bytes 6469120 | tf_op jit(solution)/shard_map/dot_general | solution.py:139
  106.5 65.8 %reduce-scatter.2.cloned.1.call-done = bf16[256,1680]{0,1:T(8,128)(2,1)} async-done(((bf16[1024,1680]{0,1:T(8,128)(2,1)}), bf16[256,1680]{0,1:T(8,128)(2,1)}) %reduce-scatter.2.cloned.1.call-update) | async-done | bytes 860176 | tf_op jit(solution)/shard_map/reduce_scatter | solution.py:144
  172.3 1.4 copy.94
  173.8 1.4 multiply_convert_fusion
  175.2 3.2 %collective-permute-start.14 = (bf16[4,1,64,1680]{3,2,0,1:T(8,128)(2,1)}, bf16[4,1,64,1680]{3,2,0,1:T(8,128)(2,1)S(1)}, u32[]{:S(2)}, u32[]{:S(2)}) collective-permute-start(bf16[4,1,64,1680]{3,2,0,1:T(8,128)(2,1)} %multiply_convert_fusion), channel_id=1, source_target_pairs={{0,1},{1,2},{2,3},{4,5},{5,6},{6,7},{8,9},{9,10},{10,11},{12,13},{... | collective-permute-start | bytes 2580488 | tf_op jit(solution)/shard_map/ppermute | solution.py:22
  180.4 17.8 %collective-permute-done.14 = bf16[4,1,64,1680]{3,2,0,1:T(8,128)(2,1)S(1)} collective-permute-done((bf16[4,1,64,1680]{3,2,0,1:T(8,128)(2,1)}, bf16[4,1,64,1680]{3,2,0,1:T(8,128)(2,1)S(1)}, u32[]{:S(2)}, u32[]{:S(2)}) %collective-permute-start.14) | collective-permute-done | bytes 860192 | tf_op jit(solution)/shard_map/ppermute | solution.py:22
  198.3 4.4 %collective-permute-done.15 = bf16[4,1,64,1680]{3,2,0,1:T(8,128)(2,1)} collective-permute-done((bf16[4,1,64,1680]{3,2,0,1:T(8,128)(2,1)}, bf16[4,1,64,1680]{3,2,0,1:T(8,128)(2,1)}, u32[]{:S(2)}, u32[]{:S(2)}) %collective-permute-start.15) | collective-permute-done | bytes 860192 | tf_op jit(solution)/shard_map/ppermute | solution.py:24
  202.7 2.2 fusion.5
  204.9 3.2 %multiply_add_fusion = f32[4,1,64,1680]{3,2,0,1:T(8,128)S(1)} fusion(bf16[4,1,64,1680]{3,2,0,1:T(8,128)(2,1)} %collective-permute-done.15, bf16[4,1,64,1680]{3,2,0,1:T(8,128)(2,1)S(1)} %collective-permute-done.14, bf16[4,3,66,1680]{3,2,0,1:T(8,128)(2,1)S(1)} %fusion.5, f32[1680]{0:T(1024)S(1)} %mul.224, f32[1680]{0:T(1024)S(1)} %mul.221, f32[1680]{0:T(1024)S(1)} %mul.218, ...), kind=kLoop, calls=%fused_computation.12 | loop fusion | flops 13332480 | bytes 10382400 | tf_op jit(solution)/shard_map/add | solution.py:87
  208.5 1.8 convolution_convert_fusion
  216.3 5.8 %collective-permute-done.17 = bf16[64,2240]{1,0:T(8,128)(2,1)} collective-permute-done((bf16[64,2240]{1,0:T(8,128)(2,1)S(1)}, bf16[64,2240]{1,0:T(8,128)(2,1)}, u32[]{:S(2)}, u32[]{:S(2)}) %collective-permute-start.17) | collective-permute-done | bytes 286752 | tf_op jit(solution)/shard_map/ppermute | solution.py:71
  223.4 4.2 %collective-permute-done.18 = bf16[64,2240]{1,0:T(8,128)(2,1)} collective-permute-done((bf16[64,2240]{1,0:T(8,128)(2,1)}, bf16[64,2240]{1,0:T(8,128)(2,1)}, u32[]{:S(2)}, u32[]{:S(2)}) %collective-permute-start.18) | collective-permute-done | bytes 286752 | tf_op jit(solution)/shard_map/ppermute | solution.py:71
  (107 shorter events, 34.1 us)
Async XLA Ops:
  7.2 165.2 %reduce-scatter.2.cloned.1.call-start = ((), (), s32[]{:S(2)}) async-start(), calls=%async_computation.1 | async-start | bytes 4300800 | tf_op jit(solution)/shard_map/reduce_scatter | solution.py:144
  13.6 2.2 collective-permute-start
  18.1 8.9 %collective-permute-start.1 = (f32[113,560]{0,1:T(8,128)S(1)}, f32[113,560]{0,1:T(8,128)S(1)}, u32[]{:S(2)}, u32[]{:S(2)}) collective-permute-start(f32[113,560]{0,1:T(8,128)S(1)} %slice_select_fusion), channel_id=1, source_target_pairs={{0,8},{4,12},{8,0},{12,4},{1,9},{5,13},{9,1},{13,5},{2,10},{6,14},... | collective-permute-start | bytes 759368 | tf_op jit(solution)/shard_map/ppermute | solution.py:50
  27.2 5.2 %collective-permute-start.2 = (f32[113,280]{0,1:T(8,128)S(1)}, f32[113,280]{0,1:T(8,128)S(1)}, u32[]{:S(2)}, u32[]{:S(2)}) collective-permute-start(f32[113,280]{0,1:T(8,128)S(1)} %slice_select_fusion.1), channel_id=1, source_target_pairs={{0,1},{1,0},{2,3},{3,2},{4,5},{5,4},{6,7},{7,6},{8,9},{9,8},{10,11... | collective-permute-start | bytes 379688 | tf_op jit(solution)/shard_map/ppermute | solution.py:50
  32.4 24.5 %copy-start.2 = (bf16[1,1,64,2240]{3,2,1,0:T(8,128)(2,1)S(1)}, bf16[1,1,64,2240]{3,2,1,0:T(8,128)(2,1)}, u32[]{:S(2)}) copy-start(bf16[1,1,64,2240]{3,2,1,0:T(8,128)(2,1)} %param.9) | copy-start | bytes 860164
  32.4 5.3 %collective-permute-start.3 = (f32[113,140]{0,1:T(8,128)S(1)}, f32[113,140]{0,1:T(8,128)S(1)}, u32[]{:S(2)}, u32[]{:S(2)}) collective-permute-start(f32[113,140]{0,1:T(8,128)S(1)} %slice_select_fusion.2), channel_id=1, source_target_pairs={{0,2},{1,3},{2,0},{3,1},{4,6},{5,7},{6,4},{7,5},{8,10},{9,11},{10,... | collective-permute-start | bytes 189848 | tf_op jit(solution)/shard_map/ppermute | solution.py:50
  37.7 5.4 %collective-permute-start.4 = (f32[113,140]{0,1:T(8,128)S(1)}, f32[113,140]{0,1:T(8,128)S(1)}, u32[]{:S(2)}, u32[]{:S(2)}) collective-permute-start(f32[113,140]{0,1:T(8,128)S(1)} %select_add_fusion.3), channel_id=1, source_target_pairs={{0,2},{1,3},{2,0},{3,1},{4,6},{5,7},{6,4},{7,5},{8,10},{9,11},{10,... | collective-permute-start | bytes 189848 | tf_op jit(solution)/shard_map/ppermute | solution.py:53
  43.2 6.5 %collective-permute-start.5 = (f32[113,280]{0,1:T(8,128)S(1)}, f32[113,280]{0,1:T(8,128)S(1)}, u32[]{:S(2)}, u32[]{:S(2)}) collective-permute-start(f32[113,280]{0,1:T(8,128)S(1)} %maximum_select_fusion.3), channel_id=1, source_target_pairs={{0,1},{1,0},{2,3},{3,2},{4,5},{5,4},{6,7},{7,6},{8,9},{9,8},{10,11... | collective-permute-start | bytes 379688 | tf_op jit(solution)/shard_map/ppermute | solution.py:53
  49.8 7.6 %copy-start.3 = (bf16[1,1,64,2240]{3,2,1,0:T(8,128)(2,1)S(1)}, bf16[1,1,64,2240]{3,2,1,0:T(8,128)(2,1)}, u32[]{:S(2)}) copy-start(bf16[1,1,64,2240]{3,2,1,0:T(8,128)(2,1)} %param.12) | copy-start | bytes 860164
  49.8 6.7 %collective-permute-start.6 = (f32[113,560]{0,1:T(8,128)S(1)}, f32[113,560]{0,1:T(8,128)S(1)}, u32[]{:S(2)}, u32[]{:S(2)}) collective-permute-start(f32[113,560]{0,1:T(8,128)S(1)} %maximum_select_fusion.2), channel_id=1, source_target_pairs={{0,8},{4,12},{8,0},{12,4},{1,9},{5,13},{9,1},{13,5},{2,10},{6,14},... | collective-permute-start | bytes 759368 | tf_op jit(solution)/shard_map/ppermute | solution.py:53
  56.6 1.1 copy-start.5
  56.6 1.1 copy-start.6
  56.8 2.0 collective-permute-start.7
  64.6 8.3 %collective-permute-start.8 = (bf16[1,1,64,560]{2,3,1,0:T(8,128)(2,1)S(1)}, bf16[1,1,64,560]{2,3,1,0:T(8,128)(2,1)S(1)}, u32[]{:S(2)}, u32[]{:S(2)}) collective-permute-start(bf16[1,1,64,560]{2,3,1,0:T(8,128)(2,1)S(1)} %get-tuple-element.35), channel_id=1, source_target_pairs={{0,1},{1,0},{2,3},{3,2},{4,5},{5,4},{6,7},{7,6},{8,9},{9,8},{10,11... | collective-permute-start | bytes 215048 | tf_op jit(solution)/shard_map/ppermute | solution.py:71
  66.7 13.7 %collective-permute-start.9 = (bf16[1,1,64,560]{2,3,1,0:T(8,128)(2,1)S(1)}, bf16[1,1,64,560]{2,3,1,0:T(8,128)(2,1)S(1)}, u32[]{:S(2)}, u32[]{:S(2)}) collective-permute-start(bf16[1,1,64,560]{2,3,1,0:T(8,128)(2,1)S(1)} %get-tuple-element.34), channel_id=1, source_target_pairs={{0,2},{1,3},{2,0},{3,1},{4,6},{5,7},{6,4},{7,5},{8,10},{9,11},{10,... | collective-permute-start | bytes 215048 | tf_op jit(solution)/shard_map/ppermute | solution.py:71
  69.0 11.4 %collective-permute-start.10 = (bf16[1,1,64,560]{2,3,1,0:T(8,128)(2,1)S(1)}, bf16[1,1,64,560]{2,3,1,0:T(8,128)(2,1)S(1)}, u32[]{:S(2)}, u32[]{:S(2)}) collective-permute-start(bf16[1,1,64,560]{2,3,1,0:T(8,128)(2,1)S(1)} %get-tuple-element.33), channel_id=1, source_target_pairs={{0,3},{1,2},{2,1},{3,0},{4,7},{5,6},{6,5},{7,4},{8,11},{9,10},{10,... | collective-permute-start | bytes 215048 | tf_op jit(solution)/shard_map/ppermute | solution.py:71
  80.4 3.5 %copy-start = (bf16[560,2,840]{2,1,0:T(2,128)(2,1)S(1)}, bf16[560,2,840]{2,1,0:T(2,128)(2,1)}, u32[]{:S(2)}) copy-start(bf16[560,2,840]{2,1,0:T(2,128)(2,1)} %param.15) | copy-start | bytes 5644804
  82.0 4.3 %collective-permute-start.11 = (bf16[1,4,64,560]{3,2,1,0:T(8,128)(2,1)}, bf16[1,4,64,560]{3,2,1,0:T(8,128)(2,1)S(1)}, u32[]{:S(2)}, u32[]{:S(2)}) collective-permute-start(bf16[1,4,64,560]{3,2,1,0:T(8,128)(2,1)} %get-tuple-element.41), channel_id=1, source_target_pairs={{0,4},{4,0},{8,12},{12,8},{1,5},{5,1},{9,13},{13,9},{2,6},{6,2},{1... | collective-permute-start | bytes 860168 | tf_op jit(solution)/shard_map/ppermute | solution.py:71
  82.0 10.8 %collective-permute-start.12 = (bf16[1,4,64,560]{3,2,1,0:T(8,128)(2,1)}, bf16[1,4,64,560]{3,2,1,0:T(8,128)(2,1)}, u32[]{:S(2)}, u32[]{:S(2)}) collective-permute-start(bf16[1,4,64,560]{3,2,1,0:T(8,128)(2,1)} %get-tuple-element.41), channel_id=1, source_target_pairs={{0,8},{4,12},{8,0},{12,4},{1,9},{5,13},{9,1},{13,5},{2,10},{6,14},... | collective-permute-start | bytes 860168 | tf_op jit(solution)/shard_map/ppermute | solution.py:71
  82.5 16.5 %collective-permute-start.13 = (bf16[1,4,64,560]{3,2,1,0:T(8,128)(2,1)}, bf16[1,4,64,560]{3,2,1,0:T(8,128)(2,1)}, u32[]{:S(2)}, u32[]{:S(2)}) collective-permute-start(bf16[1,4,64,560]{3,2,1,0:T(8,128)(2,1)} %get-tuple-element.41), channel_id=1, source_target_pairs={{0,12},{4,8},{8,4},{12,0},{1,13},{5,9},{9,5},{13,1},{2,14},{6,10},... | collective-permute-start | bytes 860168 | tf_op jit(solution)/shard_map/ppermute | solution.py:71
  100.5 1.6 copy-start.1
  173.8 5.9 %copy-start.4 = (bf16[9,2,840]{2,1,0:T(2,128)(2,1)S(1)}, bf16[9,2,840]{2,1,0:T(2,128)(2,1)}, u32[]{:S(2)}) copy-start(bf16[9,2,840]{2,1,0:T(2,128)(2,1)} %param.16) | copy-start | bytes 90724
  175.2 23.1 %collective-permute-start.14 = (bf16[4,1,64,1680]{3,2,0,1:T(8,128)(2,1)}, bf16[4,1,64,1680]{3,2,0,1:T(8,128)(2,1)S(1)}, u32[]{:S(2)}, u32[]{:S(2)}) collective-permute-start(bf16[4,1,64,1680]{3,2,0,1:T(8,128)(2,1)} %multiply_convert_fusion), channel_id=1, source_target_pairs={{0,1},{1,2},{2,3},{4,5},{5,6},{6,7},{8,9},{9,10},{10,11},{12,13},{... | collective-permute-start | bytes 2580488 | tf_op jit(solution)/shard_map/ppermute | solution.py:22
  178.4 24.3 %collective-permute-start.15 = (bf16[4,1,64,1680]{3,2,0,1:T(8,128)(2,1)}, bf16[4,1,64,1680]{3,2,0,1:T(8,128)(2,1)}, u32[]{:S(2)}, u32[]{:S(2)}) collective-permute-start(bf16[4,1,64,1680]{3,2,0,1:T(8,128)(2,1)} %multiply_convert_fusion), channel_id=1, source_target_pairs={{1,0},{2,1},{3,2},{5,4},{6,5},{7,6},{9,8},{10,9},{11,10},{13,12},{... | collective-permute-start | bytes 2580488 | tf_op jit(solution)/shard_map/ppermute | solution.py:24
  204.9 3.6 %copy-start.7 = (bf16[840,2240]{1,0:T(8,128)(2,1)S(1)}, bf16[840,2240]{1,0:T(8,128)(2,1)}, u32[]{:S(2)}) copy-start(bf16[840,2240]{1,0:T(8,128)(2,1)} %param.17) | copy-start | bytes 11289604
  211.9 4.1 %collective-permute-start.16 = (bf16[64,2240]{1,0:T(8,128)(2,1)S(1)}, bf16[64,2240]{1,0:T(8,128)(2,1)S(1)}, u32[]{:S(2)}, u32[]{:S(2)}) collective-permute-start(bf16[64,2240]{1,0:T(8,128)(2,1)S(1)} %bitcast.113), channel_id=1, source_target_pairs={{0,4},{4,0},{8,12},{12,8},{1,5},{5,1},{9,13},{13,9},{2,6},{6,2},{1... | collective-permute-start | bytes 860168 | tf_op jit(solution)/shard_map/ppermute | solution.py:71
  212.2 10.0 %collective-permute-start.17 = (bf16[64,2240]{1,0:T(8,128)(2,1)S(1)}, bf16[64,2240]{1,0:T(8,128)(2,1)}, u32[]{:S(2)}, u32[]{:S(2)}) collective-permute-start(bf16[64,2240]{1,0:T(8,128)(2,1)S(1)} %bitcast.114), channel_id=1, source_target_pairs={{0,8},{4,12},{8,0},{12,4},{1,9},{5,13},{9,1},{13,5},{2,10},{6,14},... | collective-permute-start | bytes 860168 | tf_op jit(solution)/shard_map/ppermute | solution.py:71
  213.7 13.9 %collective-permute-start.18 = (bf16[64,2240]{1,0:T(8,128)(2,1)}, bf16[64,2240]{1,0:T(8,128)(2,1)}, u32[]{:S(2)}, u32[]{:S(2)}) collective-permute-start(bf16[64,2240]{1,0:T(8,128)(2,1)} %bitcast.42), channel_id=1, source_target_pairs={{0,12},{4,8},{8,4},{12,0},{1,13},{5,9},{9,5},{13,1},{2,14},{6,10},... | collective-permute-start | bytes 860168 | tf_op jit(solution)/shard_map/ppermute | solution.py:71
Sparse Core Ops, SparseCore 0:
  106.7 65.6 reduce-scatter.1

commit v4 on v3

--- a/solution.py
+++ b/solution.py
@@ -136,21 +136,34 @@
     by_frame = swap_chunks([by_row] * frame_parts, "frame")
     tokens = jnp.stack([piece.transpose(1, 0, 2, 3) for piece in by_frame], axis=1)
     piece_frames = tokens.shape[1] * tokens.shape[2]
-    partial = jnp.dot(
-        tokens.reshape(-1, local_depth),
-        in_weight.reshape(local_depth, 2 * local_gated),
-        preferred_element_type=jnp.float32,
-    ).astype(jnp.bfloat16)
-    summed = lax.psum_scatter(partial, "row", scatter_dimension=0, tiled=True).reshape(
-        piece_frames, row_count, col_count, 2 * local_gated
-    )
-    expanded = jax.nn.silu(summed.astype(jnp.float32)).astype(jnp.bfloat16)
-    padded_expanded = padded_2(expanded, (("row", 1),), 1)
-    hidden = depthwise(padded_expanded, conv_taps, row_count, col_count, local_gated)
-    hidden_flat = hidden.reshape(-1, local_gated)
-    projected = jnp.dot(hidden_flat, out_weight, preferred_element_type=jnp.float32).astype(
-        jnp.bfloat16
-    )
+    weight_flat = in_weight.reshape(local_depth, 2 * local_gated)
+    halves = 2 if piece_frames % 2 == 0 else 1
+    half_frames = piece_frames // halves
+    chunks = [tokens[:, half * half_frames : (half + 1) * half_frames] for half in range(halves)]
+    sums = []
+    for half in range(halves):
+        chunk = chunks[half]
+        if sums:
+            sums[-1], chunk = lax.optimization_barrier((sums[-1], chunk))
+        partial = jnp.dot(
+            chunk.reshape(-1, local_depth), weight_flat, preferred_element_type=jnp.float32
+        ).astype(jnp.bfloat16)
+        sums.append(lax.psum_scatter(partial, "row", scatter_dimension=0, tiled=True))
+    projected_parts = []
+    for summed in sums:
+        expanded = (
+            jax.nn.silu(summed.astype(jnp.float32))
+            .astype(jnp.bfloat16)
+            .reshape(half_frames, row_count, col_count, 2 * local_gated)
+        )
+        padded_expanded = padded_2(expanded, (("row", 1),), 1)
+        hidden = depthwise(padded_expanded, conv_taps, row_count, col_count, local_gated)
+        projected_parts.append(
+            jnp.dot(
+                hidden.reshape(-1, local_gated), out_weight, preferred_element_type=jnp.float32
+            ).astype(jnp.bfloat16)
+        )
+    projected = jnp.concatenate(projected_parts, axis=0)
     frame_blocks = jnp.split(projected, frame_parts, axis=0)
     ffn_rows = sum(
         piece.astype(jnp.float32) for piece in swap_chunks(frame_blocks, "frame")

time: 240 us -> 254 us (1.058)
  waiting for transfers between devices: 152 us -> 144 us
  starting transfers between devices: 24.1 us -> 31.5 us
  local copies, waits for them, and re-layouts: 20.7 us -> 28 us
  matrix products: 8.59 us -> 15.4 us
    reduce_scatter x1, waiting for transfers between devices: 65.8 us -> 14.2 us  [local(): lax.psum_scatter(partial, 'row', scatter_dimension=0, tiled=True)]
    unnamed x1 -> x3, waiting for transfers between devices: 0.02 us -> 37.7 us
    ppermute x1 -> x2, waiting for transfers between devices: 4.4 us -> 27.3 us  [padded_2(): lax.ppermute(head, axis, [((i + 1) % count, i) for i in range(ends)])]
    ppermute x1 -> x2, waiting for transfers between devices: 17.8 us -> 1.18 us  [padded_2(): lax.ppermute(tail, axis, [(i, (i + 1) % count) for i in range(ends)])]
    unnamed x19 -> x27, local copies, waits for them, and re-layouts: 3.55 us -> 12 us
    ppermute x1 -> x2, starting transfers between devices: 3.15 us -> 9.37 us  [padded_2(): lax.ppermute(tail, axis, [(i, (i + 1) % count) for i in range(ends)])]
    dot_general x2 -> x4, matrix products: 6.22 us -> 12.1 us  [the longest x2 6.59 us: local(): jnp.dot(chunk.reshape(-1, local_depth), weight_flat, preferred_element_ty...]
  transfers between devices with their start and end apart: 20 -> 23, of which waited for: 17 -> 19; matrix products, arithmetic and copies ran while one was open for 3% -> 6% of each run, Pallas kernels for 0% -> 0%
where the time goes in v4:
time: 254 us; the launch traced here: 250 us
  waiting for transfers between devices  144 us (57%)
  starting transfers between devices  31.5 us (12%)
  local copies, waits for them, and re-layouts  28 us (11%)
  other arithmetic  16.3 us (6%)
  matrix products  15.4 us (6%)
  between operations  14.6 us (6%)
    unnamed x3, waiting for transfers between devices  37.7 us
    ppermute x9, waiting for transfers between devices, swap_chunks(): lax.ppermute(sent, axis, [(i, i ^ mask) for i in range(count)])  34.5 us
    ppermute x2, waiting for transfers between devices, padded_2(): lax.ppermute(head, axis, [((i + 1) % count, i) for i in range(ends)])  27.3 us
    ppermute x4, waiting for transfers between devices, halving_sum(): lax.ppermute(sent, axis, [(i, i ^ bit) for i in range(count)])  17.2 us
    reduce_scatter x1, waiting for transfers between devices, local(): lax.psum_scatter(partial, 'row', scatter_dimension=0, tiled=True)  14.2 us
    ppermute x4, waiting for transfers between devices, halving_sum(): other = lax.ppermute(block, axis, [(i, i ^ bit) for i in range(count)])  12.4 us
    unnamed x27, local copies, waits for them, and re-layouts  12 us
    ppermute x2, starting transfers between devices, padded_2(): lax.ppermute(tail, axis, [(i, (i + 1) % count) for i in range(ends)])  9.37 us
  transfers between devices with their start and end apart: 23, of which 19 were waited for; matrix products, arithmetic and copies ran while one was open for 6% of the time, Pallas kernels for 0%

profile of v4, /device:TPU:2, one launch (start us, length us, event | category | flops | bytes accessed | tf_op | source)
XLA Modules:
  0.0 250.3 jit_solution(16017154635400600700)
XLA Ops:
  12.7 2.2 collective-permute-done
  17.3 8.8 %collective-permute-done.1 = f32[113,560]{0,1:T(8,128)S(1)} collective-permute-done((f32[113,560]{0,1:T(8,128)S(1)}, f32[113,560]{0,1:T(8,128)S(1)}, u32[]{:S(2)}, u32[]{:S(2)}) %collective-permute-start.1) | collective-permute-done | bytes 253152 | tf_op jit(solution)/shard_map/ppermute | solution.py:50
  26.2 1.6 collective-permute-start.2
  27.9 3.5 %collective-permute-done.2 = f32[113,280]{0,1:T(8,128)S(1)} collective-permute-done((f32[113,280]{0,1:T(8,128)S(1)}, f32[113,280]{0,1:T(8,128)S(1)}, u32[]{:S(2)}, u32[]{:S(2)}) %collective-permute-start.2) | collective-permute-done | bytes 126592 | tf_op jit(solution)/shard_map/ppermute | solution.py:50
  31.4 2.7 %collective-permute-start.3 = (f32[113,140]{0,1:T(8,128)S(1)}, f32[113,140]{0,1:T(8,128)S(1)}, u32[]{:S(2)}, u32[]{:S(2)}) collective-permute-start(f32[113,140]{0,1:T(8,128)S(1)} %slice_select_fusion.2), channel_id=1, source_target_pairs={{0,2},{1,3},{2,0},{3,1},{4,6},{5,7},{6,4},{7,5},{8,10},{9,11},{10,... | collective-permute-start | bytes 189848 | tf_op jit(solution)/shard_map/ppermute | solution.py:50
  34.1 2.7 %collective-permute-done.3 = f32[113,140]{0,1:T(8,128)S(1)} collective-permute-done((f32[113,140]{0,1:T(8,128)S(1)}, f32[113,140]{0,1:T(8,128)S(1)}, u32[]{:S(2)}, u32[]{:S(2)}) %collective-permute-start.3) | collective-permute-done | bytes 63312 | tf_op jit(solution)/shard_map/ppermute | solution.py:50
  36.8 2.7 %collective-permute-start.4 = (f32[113,140]{0,1:T(8,128)S(1)}, f32[113,140]{0,1:T(8,128)S(1)}, u32[]{:S(2)}, u32[]{:S(2)}) collective-permute-start(f32[113,140]{0,1:T(8,128)S(1)} %select_add_fusion.3), channel_id=1, source_target_pairs={{0,2},{1,3},{2,0},{3,1},{4,6},{5,7},{6,4},{7,5},{8,10},{9,11},{10,... | collective-permute-start | bytes 189848 | tf_op jit(solution)/shard_map/ppermute | solution.py:53
  39.5 2.7 %collective-permute-done.4 = f32[113,140]{0,1:T(8,128)S(1)} collective-permute-done((f32[113,140]{0,1:T(8,128)S(1)}, f32[113,140]{0,1:T(8,128)S(1)}, u32[]{:S(2)}, u32[]{:S(2)}) %collective-permute-start.4) | collective-permute-done | bytes 63312 | tf_op jit(solution)/shard_map/ppermute | solution.py:53
  42.2 3.5 %collective-permute-start.5 = (f32[113,280]{0,1:T(8,128)S(1)}, f32[113,280]{0,1:T(8,128)S(1)}, u32[]{:S(2)}, u32[]{:S(2)}) collective-permute-start(f32[113,280]{0,1:T(8,128)S(1)} %maximum_select_fusion.3), channel_id=1, source_target_pairs={{0,1},{1,0},{2,3},{3,2},{4,5},{5,4},{6,7},{7,6},{8,9},{9,8},{10,11... | collective-permute-start | bytes 379688 | tf_op jit(solution)/shard_map/ppermute | solution.py:53
  45.7 3.1 %collective-permute-done.5 = f32[113,280]{0,1:T(8,128)S(1)} collective-permute-done((f32[113,280]{0,1:T(8,128)S(1)}, f32[113,280]{0,1:T(8,128)S(1)}, u32[]{:S(2)}, u32[]{:S(2)}) %collective-permute-start.5) | collective-permute-done | bytes 126592 | tf_op jit(solution)/shard_map/ppermute | solution.py:53
  50.0 5.5 %collective-permute-done.6 = f32[113,560]{0,1:T(8,128)S(1)} collective-permute-done((f32[113,560]{0,1:T(8,128)S(1)}, f32[113,560]{0,1:T(8,128)S(1)}, u32[]{:S(2)}, u32[]{:S(2)}) %collective-permute-start.6) | collective-permute-done | bytes 253152 | tf_op jit(solution)/shard_map/ppermute | solution.py:53
  59.7 2.4 multiply_reduce_fusion.1
  64.7 3.8 %collective-permute-start.10 = (bf16[1,1,64,560]{2,3,1,0:T(8,128)(2,1)S(1)}, bf16[1,1,64,560]{2,3,1,0:T(8,128)(2,1)S(1)}, u32[]{:S(2)}, u32[]{:S(2)}) collective-permute-start(bf16[1,1,64,560]{2,3,1,0:T(8,128)(2,1)S(1)} %get-tuple-element.37), channel_id=1, source_target_pairs={{0,3},{1,2},{2,1},{3,0},{4,7},{5,6},{6,5},{7,4},{8,11},{9,10},{10,... | collective-permute-start | bytes 215048 | tf_op jit(solution)/shard_map/ppermute | solution.py:71
  69.1 4.1 %collective-permute-done.10 = bf16[1,1,64,560]{2,3,1,0:T(8,128)(2,1)S(1)} collective-permute-done((bf16[1,1,64,560]{2,3,1,0:T(8,128)(2,1)S(1)}, bf16[1,1,64,560]{2,3,1,0:T(8,128)(2,1)S(1)}, u32[]{:S(2)}, u32[]{:S(2)}) %collective-permute-start.10) | collective-permute-done | bytes 71712 | tf_op jit(solution)/shard_map/ppermute | solution.py:71
  73.2 8.0 %collective-permute-done.9 = bf16[1,1,64,560]{2,3,1,0:T(8,128)(2,1)S(1)} collective-permute-done((bf16[1,1,64,560]{2,3,1,0:T(8,128)(2,1)S(1)}, bf16[1,1,64,560]{2,3,1,0:T(8,128)(2,1)S(1)}, u32[]{:S(2)}, u32[]{:S(2)}) %collective-permute-start.9) | collective-permute-done | bytes 71712 | tf_op jit(solution)/shard_map/ppermute | solution.py:71
  84.7 2.4 reshape.312
  87.1 5.9 %collective-permute-done.13 = bf16[1,4,64,560]{3,2,1,0:T(8,128)(2,1)S(1)} collective-permute-done((bf16[1,4,64,560]{3,2,1,0:T(8,128)(2,1)}, bf16[1,4,64,560]{3,2,1,0:T(8,128)(2,1)S(1)}, u32[]{:S(2)}, u32[]{:S(2)}) %collective-permute-start.13) | collective-permute-done | bytes 286752 | tf_op jit(solution)/shard_map/ppermute | solution.py:71
  93.0 6.5 %collective-permute-done.12 = bf16[1,4,64,560]{3,2,1,0:T(8,128)(2,1)} collective-permute-done((bf16[1,4,64,560]{3,2,1,0:T(8,128)(2,1)}, bf16[1,4,64,560]{3,2,1,0:T(8,128)(2,1)}, u32[]{:S(2)}, u32[]{:S(2)}) %collective-permute-start.12) | collective-permute-done | bytes 286752 | tf_op jit(solution)/shard_map/ppermute | solution.py:71
  102.4 2.8 %convolution_convert_fusion.3 = bf16[512,1680]{0,1:T(8,128)(2,1)} fusion(bf16[512,560]{1,0:T(8,128)(2,1)S(1)} %bitcast.124, bf16[560,1680]{1,0:T(8,128)(2,1)S(1)} %copy-done.2), kind=kOutput, calls=%fused_computation.6 | convolution fusion | flops 964239360 | bytes 4175360 | tf_op jit(solution)/shard_map/dot_general | solution.py:148
  105.2 3.7 %copy.112 = bf16[512,1680]{1,0:T(8,128)(2,1)} copy(bf16[512,1680]{0,1:T(8,128)(2,1)} %convolution_convert_fusion.3) | data formatting | bytes 3440640
  109.9 37.7 %reduce-scatter.7.cloned.1.call-done = bf16[128,1680]{1,0:T(8,128)(2,1)} async-done(((bf16[512,1680]{1,0:T(8,128)(2,1)}), bf16[128,1680]{1,0:T(8,128)(2,1)}) %reduce-scatter.7.cloned.1.call-update) | async-done | bytes 430096
  148.8 3.8 %convolution_convert_fusion.2 = bf16[512,1680]{0,1:T(8,128)(2,1)} fusion(bf16[512,560]{1,0:T(8,128)(2,1)} %bitcast.123, bf16[560,1680]{1,0:T(8,128)(2,1)S(1)} %copy-done.2), kind=kOutput, calls=%fused_computation.5 | convolution fusion | flops 964239360 | bytes 4175360 | tf_op jit(solution)/shard_map/dot_general | solution.py:148
  152.7 3.7 %copy.114 = bf16[512,1680]{1,0:T(8,128)(2,1)} copy(bf16[512,1680]{0,1:T(8,128)(2,1)} %convolution_convert_fusion.2) | data formatting | bytes 3440640
  158.2 4.6 %collective-permute-start.14 = (bf16[2,1,64,1680]{3,2,0,1:T(8,128)(2,1)S(1)}, bf16[2,1,64,1680]{3,2,0,1:T(8,128)(2,1)S(1)}, u32[]{:S(2)}, u32[]{:S(2)}) collective-permute-start(bf16[2,1,64,1680]{3,2,0,1:T(8,128)(2,1)S(1)} %bitcast.111), channel_id=1, source_target_pairs={{0,1},{1,2},{2,3},{4,5},{5,6},{6,7},{8,9},{9,10},{10,11},{12,13},{... | collective-permute-start | bytes 1290248 | tf_op jit(solution)/shard_map/ppermute | solution.py:22
  163.5 23.2 %collective-permute-done.15 = bf16[2,1,64,1680]{3,2,0,1:T(8,128)(2,1)S(1)} collective-permute-done((bf16[2,1,64,1680]{3,2,0,1:T(8,128)(2,1)S(1)}, bf16[2,1,64,1680]{3,2,0,1:T(8,128)(2,1)S(1)}, u32[]{:S(2)}, u32[]{:S(2)}) %collective-permute-start.15) | collective-permute-done | bytes 430112 | tf_op jit(solution)/shard_map/ppermute | solution.py:24
  188.0 14.2 %reduce-scatter.9.cloned.1.call-done = bf16[128,1680]{1,0:T(8,128)(2,1)} async-done(((bf16[512,1680]{1,0:T(8,128)(2,1)}), bf16[128,1680]{1,0:T(8,128)(2,1)}) %reduce-scatter.9.cloned.1.call-update) | async-done | bytes 430096 | tf_op jit(solution)/shard_map/reduce_scatter | solution.py:151
  204.7 4.8 %collective-permute-start.16 = (bf16[2,1,64,1680]{3,2,0,1:T(8,128)(2,1)S(1)}, bf16[2,1,64,1680]{3,2,0,1:T(8,128)(2,1)S(1)}, u32[]{:S(2)}, u32[]{:S(2)}) collective-permute-start(bf16[2,1,64,1680]{3,2,0,1:T(8,128)(2,1)S(1)} %bitcast.115), channel_id=1, source_target_pairs={{0,1},{1,2},{2,3},{4,5},{5,6},{6,7},{8,9},{9,10},{10,11},{12,13},{... | collective-permute-start | bytes 1290248 | tf_op jit(solution)/shard_map/ppermute | solution.py:22
  209.7 3.8 %convolution_convert_fusion.1 = bf16[128,2240]{0,1:T(8,128)(2,1)S(1)} fusion(bf16[128,840]{1,0:T(8,128)(2,1)S(1)} %bitcast.121, bf16[840,2240]{1,0:T(8,128)(2,1)} %param.17), kind=kOutput, calls=%fused_computation.3 | convolution fusion | flops 481976320 | bytes 4551680 | tf_op jit(solution)/shard_map/dot_general | solution.py:162
  213.5 4.2 %collective-permute-done.17 = bf16[2,1,64,1680]{3,2,0,1:T(8,128)(2,1)S(1)} collective-permute-done((bf16[2,1,64,1680]{3,2,0,1:T(8,128)(2,1)S(1)}, bf16[2,1,64,1680]{3,2,0,1:T(8,128)(2,1)S(1)}, u32[]{:S(2)}, u32[]{:S(2)}) %collective-permute-start.17) | collective-permute-done | bytes 430112 | tf_op jit(solution)/shard_map/ppermute | solution.py:24
  221.4 1.7 convolution_convert_fusion
  228.6 5.2 %collective-permute-done.20 = bf16[64,2240]{1,0:T(8,128)(2,1)S(1)} collective-permute-done((bf16[64,2240]{1,0:T(8,128)(2,1)S(1)}, bf16[64,2240]{1,0:T(8,128)(2,1)S(1)}, u32[]{:S(2)}, u32[]{:S(2)}) %collective-permute-start.20) | collective-permute-done | bytes 286752 | tf_op jit(solution)/shard_map/ppermute | solution.py:71
  234.2 4.8 %collective-permute-done.19 = bf16[64,2240]{1,0:T(8,128)(2,1)} collective-permute-done((bf16[64,2240]{1,0:T(8,128)(2,1)S(1)}, bf16[64,2240]{1,0:T(8,128)(2,1)}, u32[]{:S(2)}, u32[]{:S(2)}) %collective-permute-start.19) | collective-permute-done | bytes 286752 | tf_op jit(solution)/shard_map/ppermute | solution.py:71
  (130 shorter events, 45.7 us)
Async XLA Ops:
  7.2 2.5 copy-start.6
  7.2 140.4 %reduce-scatter.7.cloned.1.call-start = ((), (), s32[]{:S(2)}) async-start(), calls=%async_computation.2 | async-start | bytes 2293760
  12.7 2.2 collective-permute-start
  17.2 8.9 %collective-permute-start.1 = (f32[113,560]{0,1:T(8,128)S(1)}, f32[113,560]{0,1:T(8,128)S(1)}, u32[]{:S(2)}, u32[]{:S(2)}) collective-permute-start(f32[113,560]{0,1:T(8,128)S(1)} %slice_select_fusion), channel_id=1, source_target_pairs={{0,8},{4,12},{8,0},{12,4},{1,9},{5,13},{9,1},{13,5},{2,10},{6,14},... | collective-permute-start | bytes 759368 | tf_op jit(solution)/shard_map/ppermute | solution.py:50
  17.3 32.2 %copy-start.9 = (bf16[2240]{0:T(1024)(128)(2,1)S(1)}, bf16[2240]{0:T(1024)(128)(2,1)}, u32[]{:S(2)}) copy-start(bf16[2240]{0:T(1024)(128)(2,1)} %param.14) | copy-start | bytes 13444
  26.2 5.2 %collective-permute-start.2 = (f32[113,280]{0,1:T(8,128)S(1)}, f32[113,280]{0,1:T(8,128)S(1)}, u32[]{:S(2)}, u32[]{:S(2)}) collective-permute-start(f32[113,280]{0,1:T(8,128)S(1)} %slice_select_fusion.1), channel_id=1, source_target_pairs={{0,1},{1,0},{2,3},{3,2},{4,5},{5,4},{6,7},{7,6},{8,9},{9,8},{10,11... | collective-permute-start | bytes 379688 | tf_op jit(solution)/shard_map/ppermute | solution.py:50
  31.4 5.3 %collective-permute-start.3 = (f32[113,140]{0,1:T(8,128)S(1)}, f32[113,140]{0,1:T(8,128)S(1)}, u32[]{:S(2)}, u32[]{:S(2)}) collective-permute-start(f32[113,140]{0,1:T(8,128)S(1)} %slice_select_fusion.2), channel_id=1, source_target_pairs={{0,2},{1,3},{2,0},{3,1},{4,6},{5,7},{6,4},{7,5},{8,10},{9,11},{10,... | collective-permute-start | bytes 189848 | tf_op jit(solution)/shard_map/ppermute | solution.py:50
  36.8 19.2 %copy-start.4 = (bf16[1,1,64,2240]{3,2,1,0:T(8,128)(2,1)S(1)}, bf16[1,1,64,2240]{3,2,1,0:T(8,128)(2,1)}, u32[]{:S(2)}) copy-start(bf16[1,1,64,2240]{3,2,1,0:T(8,128)(2,1)} %param.9) | copy-start | bytes 860164
  36.8 5.4 %collective-permute-start.4 = (f32[113,140]{0,1:T(8,128)S(1)}, f32[113,140]{0,1:T(8,128)S(1)}, u32[]{:S(2)}, u32[]{:S(2)}) collective-permute-start(f32[113,140]{0,1:T(8,128)S(1)} %select_add_fusion.3), channel_id=1, source_target_pairs={{0,2},{1,3},{2,0},{3,1},{4,6},{5,7},{6,4},{7,5},{8,10},{9,11},{10,... | collective-permute-start | bytes 189848 | tf_op jit(solution)/shard_map/ppermute | solution.py:53
  42.2 6.5 %collective-permute-start.5 = (f32[113,280]{0,1:T(8,128)S(1)}, f32[113,280]{0,1:T(8,128)S(1)}, u32[]{:S(2)}, u32[]{:S(2)}) collective-permute-start(f32[113,280]{0,1:T(8,128)S(1)} %maximum_select_fusion.3), channel_id=1, source_target_pairs={{0,1},{1,0},{2,3},{3,2},{4,5},{5,4},{6,7},{7,6},{8,9},{9,8},{10,11... | collective-permute-start | bytes 379688 | tf_op jit(solution)/shard_map/ppermute | solution.py:53
  48.8 6.7 %collective-permute-start.6 = (f32[113,560]{0,1:T(8,128)S(1)}, f32[113,560]{0,1:T(8,128)S(1)}, u32[]{:S(2)}, u32[]{:S(2)}) collective-permute-start(f32[113,560]{0,1:T(8,128)S(1)} %maximum_select_fusion.2), channel_id=1, source_target_pairs={{0,8},{4,12},{8,0},{12,4},{1,9},{5,13},{9,1},{13,5},{2,10},{6,14},... | collective-permute-start | bytes 759368 | tf_op jit(solution)/shard_map/ppermute | solution.py:53
  50.0 6.4 %copy-start.5 = (bf16[1,1,64,2240]{3,2,1,0:T(8,128)(2,1)S(1)}, bf16[1,1,64,2240]{3,2,1,0:T(8,128)(2,1)}, u32[]{:S(2)}) copy-start(bf16[1,1,64,2240]{3,2,1,0:T(8,128)(2,1)} %param.12) | copy-start | bytes 860164
  55.9 2.0 collective-permute-start.7
  56.4 2.6 %copy-start.3 = (bf16[64,20,112]{2,1,0:T(8,128)(2,1)}, bf16[64,20,112]{2,1,0:T(8,128)(2,1)S(1)}, u32[]{:S(2)}) copy-start(bf16[64,20,112]{2,1,0:T(8,128)(2,1)S(1)} %reshape.308) | copy-start | bytes 860164
  64.7 8.5 %collective-permute-start.10 = (bf16[1,1,64,560]{2,3,1,0:T(8,128)(2,1)S(1)}, bf16[1,1,64,560]{2,3,1,0:T(8,128)(2,1)S(1)}, u32[]{:S(2)}, u32[]{:S(2)}) collective-permute-start(bf16[1,1,64,560]{2,3,1,0:T(8,128)(2,1)S(1)} %get-tuple-element.37), channel_id=1, source_target_pairs={{0,3},{1,2},{2,1},{3,0},{4,7},{5,6},{6,5},{7,4},{8,11},{9,10},{10,... | collective-permute-start | bytes 215048 | tf_op jit(solution)/shard_map/ppermute | solution.py:71
  68.4 12.7 %collective-permute-start.9 = (bf16[1,1,64,560]{2,3,1,0:T(8,128)(2,1)S(1)}, bf16[1,1,64,560]{2,3,1,0:T(8,128)(2,1)S(1)}, u32[]{:S(2)}, u32[]{:S(2)}) collective-permute-start(bf16[1,1,64,560]{2,3,1,0:T(8,128)(2,1)S(1)} %get-tuple-element.38), channel_id=1, source_target_pairs={{0,2},{1,3},{2,0},{3,1},{4,6},{5,7},{6,4},{7,5},{8,10},{9,11},{10,... | collective-permute-start | bytes 215048 | tf_op jit(solution)/shard_map/ppermute | solution.py:71
  68.5 12.7 %collective-permute-start.8 = (bf16[1,1,64,560]{2,3,1,0:T(8,128)(2,1)S(1)}, bf16[1,1,64,560]{2,3,1,0:T(8,128)(2,1)S(1)}, u32[]{:S(2)}, u32[]{:S(2)}) collective-permute-start(bf16[1,1,64,560]{2,3,1,0:T(8,128)(2,1)S(1)} %get-tuple-element.39), channel_id=1, source_target_pairs={{0,1},{1,0},{2,3},{3,2},{4,5},{5,4},{6,7},{7,6},{8,9},{9,8},{10,11... | collective-permute-start | bytes 215048 | tf_op jit(solution)/shard_map/ppermute | solution.py:71
  81.4 3.3 %copy-start.1 = (bf16[560,2,840]{2,1,0:T(2,128)(2,1)S(1)}, bf16[560,2,840]{2,1,0:T(2,128)(2,1)}, u32[]{:S(2)}) copy-start(bf16[560,2,840]{2,1,0:T(2,128)(2,1)} %param.15) | copy-start | bytes 5644804
  82.8 10.2 %collective-permute-start.13 = (bf16[1,4,64,560]{3,2,1,0:T(8,128)(2,1)}, bf16[1,4,64,560]{3,2,1,0:T(8,128)(2,1)S(1)}, u32[]{:S(2)}, u32[]{:S(2)}) collective-permute-start(bf16[1,4,64,560]{3,2,1,0:T(8,128)(2,1)} %get-tuple-element.45), channel_id=1, source_target_pairs={{0,12},{4,8},{8,4},{12,0},{1,13},{5,9},{9,5},{13,1},{2,14},{6,10},... | collective-permute-start | bytes 860168 | tf_op jit(solution)/shard_map/ppermute | solution.py:71
  82.8 16.7 %collective-permute-start.12 = (bf16[1,4,64,560]{3,2,1,0:T(8,128)(2,1)}, bf16[1,4,64,560]{3,2,1,0:T(8,128)(2,1)}, u32[]{:S(2)}, u32[]{:S(2)}) collective-permute-start(bf16[1,4,64,560]{3,2,1,0:T(8,128)(2,1)} %get-tuple-element.45), channel_id=1, source_target_pairs={{0,8},{4,12},{8,0},{12,4},{1,9},{5,13},{9,1},{13,5},{2,10},{6,14},... | collective-permute-start | bytes 860168 | tf_op jit(solution)/shard_map/ppermute | solution.py:71
  84.0 15.6 %collective-permute-start.11 = (bf16[1,4,64,560]{3,2,1,0:T(8,128)(2,1)}, bf16[1,4,64,560]{3,2,1,0:T(8,128)(2,1)}, u32[]{:S(2)}, u32[]{:S(2)}) collective-permute-start(bf16[1,4,64,560]{3,2,1,0:T(8,128)(2,1)} %get-tuple-element.45), channel_id=1, source_target_pairs={{0,4},{4,0},{8,12},{12,8},{1,5},{5,1},{9,13},{13,9},{2,6},{6,2},{1... | collective-permute-start | bytes 860168 | tf_op jit(solution)/shard_map/ppermute | solution.py:71
  100.9 1.6 copy-start.2
  108.9 93.2 %reduce-scatter.9.cloned.1.call-start = ((), (), s32[]{:S(2)}) async-start(), calls=%async_computation.3 | async-start | bytes 2293760 | tf_op jit(solution)/shard_map/reduce_scatter | solution.py:151
  156.4 6.4 %copy-start.7 = (bf16[9,2,840]{2,1,0:T(2,128)(2,1)S(1)}, bf16[9,2,840]{2,1,0:T(2,128)(2,1)}, u32[]{:S(2)}) copy-start(bf16[9,2,840]{2,1,0:T(2,128)(2,1)} %param.16) | copy-start | bytes 90724
  156.9 29.8 %collective-permute-start.15 = (bf16[2,1,64,1680]{3,2,0,1:T(8,128)(2,1)S(1)}, bf16[2,1,64,1680]{3,2,0,1:T(8,128)(2,1)S(1)}, u32[]{:S(2)}, u32[]{:S(2)}) collective-permute-start(bf16[2,1,64,1680]{3,2,0,1:T(8,128)(2,1)S(1)} %bitcast.110), channel_id=1, source_target_pairs={{1,0},{2,1},{3,2},{5,4},{6,5},{7,6},{9,8},{10,9},{11,10},{13,12},{... | collective-permute-start | bytes 1290248 | tf_op jit(solution)/shard_map/ppermute | solution.py:24
  158.2 28.5 %collective-permute-start.14 = (bf16[2,1,64,1680]{3,2,0,1:T(8,128)(2,1)S(1)}, bf16[2,1,64,1680]{3,2,0,1:T(8,128)(2,1)S(1)}, u32[]{:S(2)}, u32[]{:S(2)}) collective-permute-start(bf16[2,1,64,1680]{3,2,0,1:T(8,128)(2,1)S(1)} %bitcast.111), channel_id=1, source_target_pairs={{0,1},{1,2},{2,3},{4,5},{5,6},{6,7},{8,9},{9,10},{10,11},{12,13},{... | collective-permute-start | bytes 1290248 | tf_op jit(solution)/shard_map/ppermute | solution.py:22
  203.4 14.3 %collective-permute-start.17 = (bf16[2,1,64,1680]{3,2,0,1:T(8,128)(2,1)S(1)}, bf16[2,1,64,1680]{3,2,0,1:T(8,128)(2,1)S(1)}, u32[]{:S(2)}, u32[]{:S(2)}) collective-permute-start(bf16[2,1,64,1680]{3,2,0,1:T(8,128)(2,1)S(1)} %bitcast.114), channel_id=1, source_target_pairs={{1,0},{2,1},{3,2},{5,4},{6,5},{7,6},{9,8},{10,9},{11,10},{13,12},{... | collective-permute-start | bytes 1290248 | tf_op jit(solution)/shard_map/ppermute | solution.py:24
  204.7 14.1 %collective-permute-start.16 = (bf16[2,1,64,1680]{3,2,0,1:T(8,128)(2,1)S(1)}, bf16[2,1,64,1680]{3,2,0,1:T(8,128)(2,1)S(1)}, u32[]{:S(2)}, u32[]{:S(2)}) collective-permute-start(bf16[2,1,64,1680]{3,2,0,1:T(8,128)(2,1)S(1)} %bitcast.115), channel_id=1, source_target_pairs={{0,1},{1,2},{2,3},{4,5},{5,6},{6,7},{8,9},{9,10},{10,11},{12,13},{... | collective-permute-start | bytes 1290248 | tf_op jit(solution)/shard_map/ppermute | solution.py:22
  219.3 2.1 copy-start
  224.5 9.3 %collective-permute-start.20 = (bf16[64,2240]{1,0:T(8,128)(2,1)S(1)}, bf16[64,2240]{1,0:T(8,128)(2,1)S(1)}, u32[]{:S(2)}, u32[]{:S(2)}) collective-permute-start(bf16[64,2240]{1,0:T(8,128)(2,1)S(1)} %bitcast.130), channel_id=1, source_target_pairs={{0,12},{4,8},{8,4},{12,0},{1,13},{5,9},{9,5},{13,1},{2,14},{6,10},... | collective-permute-start | bytes 860168 | tf_op jit(solution)/shard_map/ppermute | solution.py:71
  224.8 14.2 %collective-permute-start.19 = (bf16[64,2240]{1,0:T(8,128)(2,1)S(1)}, bf16[64,2240]{1,0:T(8,128)(2,1)}, u32[]{:S(2)}, u32[]{:S(2)}) collective-permute-start(bf16[64,2240]{1,0:T(8,128)(2,1)S(1)} %bitcast.131), channel_id=1, source_target_pairs={{0,8},{4,12},{8,0},{12,4},{1,9},{5,13},{9,1},{13,5},{2,10},{6,14},... | collective-permute-start | bytes 860168 | tf_op jit(solution)/shard_map/ppermute | solution.py:71
  226.6 13.7 %collective-permute-start.18 = (bf16[64,2240]{1,0:T(8,128)(2,1)}, bf16[64,2240]{1,0:T(8,128)(2,1)}, u32[]{:S(2)}, u32[]{:S(2)}) collective-permute-start(bf16[64,2240]{1,0:T(8,128)(2,1)} %bitcast.41), channel_id=1, source_target_pairs={{0,4},{4,0},{8,12},{12,8},{1,5},{5,1},{9,13},{13,9},{2,6},{6,2},{1... | collective-permute-start | bytes 860168 | tf_op jit(solution)/shard_map/ppermute | solution.py:71
  (2 other events, 1.9 us)
Sparse Core Ops, SparseCore 0:
  109.0 38.4 reduce-scatter.6
  156.5 45.5 reduce-scatter.8

commit v5 on v3

--- a/solution.py
+++ b/solution.py
@@ -70,6 +70,34 @@
         sent = pick(chunks, own ^ mask)
         by_mask.append(lax.ppermute(sent, axis, [(i, i ^ mask) for i in range(count)]))
     return [pick(by_mask, own ^ source) for source in range(count)]
+
+
+def gather_depth_chunks(chunks, frame_parts):
+    row_parts = len(chunks)
+    frame_at = lax.axis_index("frame")
+    row_at = lax.axis_index("row")
+    pairs_of = lambda fm, rm: [
+        (f * row_parts + r, (f ^ fm) * row_parts + (r ^ rm))
+        for f in range(frame_parts)
+        for r in range(row_parts)
+    ]
+    by_mask = []
+    for frame_mask in range(frame_parts):
+        for row_mask in range(row_parts):
+            sent = pick(chunks, row_at ^ row_mask)
+            if frame_mask == 0 and row_mask == 0:
+                by_mask.append(sent)
+            else:
+                by_mask.append(
+                    lax.ppermute(sent, ("frame", "row"), pairs_of(frame_mask, row_mask))
+                )
+    return [
+        [
+            pick(by_mask, (frame_at ^ source_frame) * row_parts + (row_at ^ source_row))
+            for source_frame in range(frame_parts)
+        ]
+        for source_row in range(row_parts)
+    ]
 
 
 def rms_norm(features):
@@ -131,10 +159,14 @@
     depth_chunks = [
         normed_grid[..., part * local_depth : (part + 1) * local_depth] for part in range(row_parts)
     ]
-    by_row = jnp.concatenate(swap_chunks(depth_chunks, "row"), axis=1)
     frame_parts = lax.axis_size("frame")
-    by_frame = swap_chunks([by_row] * frame_parts, "frame")
-    tokens = jnp.stack([piece.transpose(1, 0, 2, 3) for piece in by_frame], axis=1)
+    if frame_parts * row_parts <= 16 and frame_count == 1 and row_count == 1:
+        grid = gather_depth_chunks(depth_chunks, frame_parts)
+        tokens = jnp.stack([jnp.concatenate(per_row, axis=0) for per_row in grid])
+    else:
+        by_row = jnp.concatenate(swap_chunks(depth_chunks, "row"), axis=1)
+        by_frame = swap_chunks([by_row] * frame_parts, "frame")
+        tokens = jnp.stack([piece.transpose(1, 0, 2, 3) for piece in by_frame], axis=1)
     piece_frames = tokens.shape[1] * tokens.shape[2]
     partial = jnp.dot(
         tokens.reshape(-1, local_depth),

time: 240 us -> 279 us (1.16)
  starting transfers between devices: 24.1 us -> 45.6 us
  local copies, waits for them, and re-layouts: 20.7 us -> 34.7 us
  waiting for transfers between devices: 152 us -> 157 us
    ppermute x0 -> x15, starting transfers between devices: none -> 27.9 us  [gather_depth_chunks(): lax.ppermute(sent, ('frame', 'row'), pairs_of(frame_mask, row_mask))]
    ppermute x0 -> x15, waiting for transfers between devices: none -> 24.8 us  [gather_depth_chunks(): lax.ppermute(sent, ('frame', 'row'), pairs_of(frame_mask, row_mask))]
    ppermute x9 -> x3, waiting for transfers between devices: 34.1 us -> 10.1 us  [swap_chunks(): lax.ppermute(sent, axis, [(i, i ^ mask) for i in range(count)])]
    ppermute x9 -> x3, starting transfers between devices: 8.37 us -> 1.98 us  [swap_chunks(): lax.ppermute(sent, axis, [(i, i ^ mask) for i in range(count)])]
    squeeze x0 -> x13, local copies, waits for them, and re-layouts: none -> 5.39 us  [pick(): return lax.dynamic_index_in_dim(stacked, index, axis=0, keepdims=False)]
    dynamic_slice x10 -> x9, local copies, waits for them, and re-layouts: 2.25 us -> 7.2 us  [pick(): return lax.dynamic_index_in_dim(stacked, index, axis=0, keepdims=False)]
    reduce_scatter x1, waiting for transfers between devices: 65.8 us -> 70 us  [local(): lax.psum_scatter(partial, 'row', scatter_dimension=0, tiled=True)]
  transfers between devices with their start and end apart: 20 -> 29, of which waited for: 17 -> 18; matrix products, arithmetic and copies ran while one was open for 3% -> 4% of each run, Pallas kernels for 0% -> 0%
where the time goes in v5:
time: 279 us; the launch traced here: 277 us
  waiting for transfers between devices  157 us (56%)
  starting transfers between devices  45.6 us (16%)
  local copies, waits for them, and re-layouts  34.7 us (12%)
  other arithmetic  15.5 us (6%)
  between operations  14.8 us (5%)
  matrix products  8.59 us (3%)
    reduce_scatter x1, waiting for transfers between devices, local(): lax.psum_scatter(partial, 'row', scatter_dimension=0, tiled=True)  70 us
    ppermute x15, starting transfers between devices, gather_depth_chunks(): lax.ppermute(sent, ('frame', 'row'), pairs_of(frame_mask, row_mask))  27.9 us
    ppermute x15, waiting for transfers between devices, gather_depth_chunks(): lax.ppermute(sent, ('frame', 'row'), pairs_of(frame_mask, row_mask))  24.8 us
    ppermute x1, waiting for transfers between devices, padded_2(): lax.ppermute(tail, axis, [(i, (i + 1) % count) for i in range(ends)])  17.8 us
    ppermute x4, waiting for transfers between devices, halving_sum(): lax.ppermute(sent, axis, [(i, i ^ bit) for i in range(count)])  17.2 us
    ppermute x4, waiting for transfers between devices, halving_sum(): other = lax.ppermute(block, axis, [(i, i ^ bit) for i in range(count)])  13 us
    ppermute x3, waiting for transfers between devices, swap_chunks(): lax.ppermute(sent, axis, [(i, i ^ mask) for i in range(count)])  10.1 us
    dynamic_slice x9, local copies, waits for them, and re-layouts, pick(): return lax.dynamic_index_in_dim(stacked, index, axis=0, keepdims=False)  7.2 us
  transfers between devices with their start and end apart: 29, of which 18 were waited for; matrix products, arithmetic and copies ran while one was open for 4% of the time, Pallas kernels for 0%

profile of v5, /device:TPU:2, one launch (start us, length us, event | category | flops | bytes accessed | tf_op | source)
XLA Modules:
  0.0 276.6 jit_solution(12796947488533760522)
XLA Ops:
  13.6 2.2 collective-permute-done
  18.2 8.9 %collective-permute-done.1 = f32[113,560]{0,1:T(8,128)S(1)} collective-permute-done((f32[113,560]{0,1:T(8,128)S(1)}, f32[113,560]{0,1:T(8,128)S(1)}, u32[]{:S(2)}, u32[]{:S(2)}) %collective-permute-start.1) | collective-permute-done | bytes 253152 | tf_op jit(solution)/shard_map/ppermute | solution.py:50
  28.8 3.5 %collective-permute-done.2 = f32[113,280]{0,1:T(8,128)S(1)} collective-permute-done((f32[113,280]{0,1:T(8,128)S(1)}, f32[113,280]{0,1:T(8,128)S(1)}, u32[]{:S(2)}, u32[]{:S(2)}) %collective-permute-start.2) | collective-permute-done | bytes 126592 | tf_op jit(solution)/shard_map/ppermute | solution.py:50
  32.4 2.7 collective-permute-start.3
  35.0 2.7 collective-permute-done.3
  37.7 2.7 collective-permute-start.4
  40.4 2.7 collective-permute-done.4
  43.1 3.5 %collective-permute-start.5 = (f32[113,280]{0,1:T(8,128)S(1)}, f32[113,280]{0,1:T(8,128)S(1)}, u32[]{:S(2)}, u32[]{:S(2)}) collective-permute-start(f32[113,280]{0,1:T(8,128)S(1)} %maximum_select_fusion.3), channel_id=1, source_target_pairs={{0,1},{1,0},{2,3},{3,2},{4,5},{5,4},{6,7},{7,6},{8,9},{9,8},{10,11... | collective-permute-start | bytes 379688 | tf_op jit(solution)/shard_map/ppermute | solution.py:53
  46.6 3.1 %collective-permute-done.5 = f32[113,280]{0,1:T(8,128)S(1)} collective-permute-done((f32[113,280]{0,1:T(8,128)S(1)}, f32[113,280]{0,1:T(8,128)S(1)}, u32[]{:S(2)}, u32[]{:S(2)}) %collective-permute-start.5) | collective-permute-done | bytes 126592 | tf_op jit(solution)/shard_map/ppermute | solution.py:53
  50.3 6.1 %collective-permute-done.6 = f32[113,560]{0,1:T(8,128)S(1)} collective-permute-done((f32[113,560]{0,1:T(8,128)S(1)}, f32[113,560]{0,1:T(8,128)S(1)}, u32[]{:S(2)}, u32[]{:S(2)}) %collective-permute-start.6) | collective-permute-done | bytes 253152 | tf_op jit(solution)/shard_map/ppermute | solution.py:53
  64.6 2.1 collective-permute-start.8
  66.7 5.2 %reshape.311 = bf16[560,1680]{1,0:T(8,128)(2,1)} reshape(bf16[560,2,840]{2,1,0:T(2,128)(2,1)} %param.15) | data formatting | bytes 3763200 | tf_op jit(solution)/shard_map/reshape | solution.py:173
  71.9 2.3 collective-permute-start.9
  74.4 3.6 %collective-permute-start.10 = (bf16[1,1,64,560]{2,3,1,0:T(8,128)(2,1)S(1)}, bf16[1,1,64,560]{2,3,1,0:T(8,128)(2,1)S(1)}, u32[]{:S(2)}, u32[]{:S(2)}) collective-permute-start(bf16[1,1,64,560]{2,3,1,0:T(8,128)(2,1)S(1)} %get-tuple-element.42), channel_id=1, source_target_pairs={{0,3},{1,2},{2,1},{3,0},{4,7},{5,6},{6,5},{7,4},{8,11},{9,10},{10,... | collective-permute-start | bytes 215048 | tf_op jit(solution)/shard_map/ppermute | solution.py:92
  79.4 9.6 %collective-permute-done.10 = bf16[1,1,64,560]{2,3,1,0:T(8,128)(2,1)S(1)} collective-permute-done((bf16[1,1,64,560]{2,3,1,0:T(8,128)(2,1)S(1)}, bf16[1,1,64,560]{2,3,1,0:T(8,128)(2,1)S(1)}, u32[]{:S(2)}, u32[]{:S(2)}) %collective-permute-start.10) | collective-permute-done | bytes 71712 | tf_op jit(solution)/shard_map/ppermute | solution.py:92
  89.6 10.3 %collective-permute-start.16 = (bf16[1,1,64,560]{2,3,1,0:T(8,128)(2,1)S(1)}, bf16[1,1,64,560]{2,3,1,0:T(8,128)(2,1)S(1)}, u32[]{:S(2)}, u32[]{:S(2)}) collective-permute-start(bf16[1,1,64,560]{2,3,1,0:T(8,128)(2,1)S(1)} %get-tuple-element.44), channel_id=1, source_target_pairs={{0,9},{1,8},{2,11},{3,10},{4,13},{5,12},{6,15},{7,14},{8,1},{9,0},... | collective-permute-start | bytes 215048 | tf_op jit(solution)/shard_map/ppermute | solution.py:92
  99.9 1.9 collective-permute-start.17
  103.5 2.4 collective-permute-start.20
  105.9 1.9 collective-permute-start.21
  107.8 6.3 %collective-permute-done.17 = bf16[1,1,64,560]{2,3,1,0:T(8,128)(2,1)S(1)} collective-permute-done((bf16[1,1,64,560]{2,3,1,0:T(8,128)(2,1)S(1)}, bf16[1,1,64,560]{2,3,1,0:T(8,128)(2,1)S(1)}, u32[]{:S(2)}, u32[]{:S(2)}) %collective-permute-start.17) | collective-permute-done | bytes 71712 | tf_op jit(solution)/shard_map/ppermute | solution.py:92
  115.3 2.2 collective-permute-done.19
  117.6 6.3 %collective-permute-done.21 = bf16[1,1,64,560]{2,3,1,0:T(8,128)(2,1)S(1)} collective-permute-done((bf16[1,1,64,560]{2,3,1,0:T(8,128)(2,1)S(1)}, bf16[1,1,64,560]{2,3,1,0:T(8,128)(2,1)S(1)}, u32[]{:S(2)}, u32[]{:S(2)}) %collective-permute-start.21) | collective-permute-done | bytes 71712 | tf_op jit(solution)/shard_map/ppermute | solution.py:92
  136.6 4.4 %convolution_convert_fusion.1 = bf16[1024,1680]{0,1:T(8,128)(2,1)} fusion(bf16[1024,560]{1,0:T(8,128)(2,1)S(1)} %bitcast.154, bf16[560,1680]{1,0:T(8,128)(2,1)S(1)} %copy-done), kind=kOutput, calls=%fused_computation.4 | convolution fusion | flops 1928478720 | bytes 6469120 | tf_op jit(solution)/shard_map/dot_general | solution.py:171
  141.1 70.0 %reduce-scatter.2.cloned.1.call-done = bf16[256,1680]{0,1:T(8,128)(2,1)} async-done(((bf16[1024,1680]{0,1:T(8,128)(2,1)}), bf16[256,1680]{0,1:T(8,128)(2,1)}) %reduce-scatter.2.cloned.1.call-update) | async-done | bytes 860176 | tf_op jit(solution)/shard_map/reduce_scatter | solution.py:176
  214.0 3.2 %collective-permute-start.23 = (bf16[4,1,64,1680]{3,2,0,1:T(8,128)(2,1)}, bf16[4,1,64,1680]{3,2,0,1:T(8,128)(2,1)S(1)}, u32[]{:S(2)}, u32[]{:S(2)}) collective-permute-start(bf16[4,1,64,1680]{3,2,0,1:T(8,128)(2,1)} %multiply_convert_fusion), channel_id=1, source_target_pairs={{0,1},{1,2},{2,3},{4,5},{5,6},{6,7},{8,9},{9,10},{10,11},{12,13},{... | collective-permute-start | bytes 2580488 | tf_op jit(solution)/shard_map/ppermute | solution.py:22
  219.3 17.8 %collective-permute-done.23 = bf16[4,1,64,1680]{3,2,0,1:T(8,128)(2,1)S(1)} collective-permute-done((bf16[4,1,64,1680]{3,2,0,1:T(8,128)(2,1)}, bf16[4,1,64,1680]{3,2,0,1:T(8,128)(2,1)S(1)}, u32[]{:S(2)}, u32[]{:S(2)}) %collective-permute-start.23) | collective-permute-done | bytes 860192 | tf_op jit(solution)/shard_map/ppermute | solution.py:22
  237.1 4.4 %collective-permute-done.24 = bf16[4,1,64,1680]{3,2,0,1:T(8,128)(2,1)} collective-permute-done((bf16[4,1,64,1680]{3,2,0,1:T(8,128)(2,1)}, bf16[4,1,64,1680]{3,2,0,1:T(8,128)(2,1)}, u32[]{:S(2)}, u32[]{:S(2)}) %collective-permute-start.24) | collective-permute-done | bytes 860192 | tf_op jit(solution)/shard_map/ppermute | solution.py:24
  241.5 2.2 fusion.5
  243.8 3.2 %multiply_add_fusion = f32[4,1,64,1680]{3,2,0,1:T(8,128)S(1)} fusion(bf16[4,1,64,1680]{3,2,0,1:T(8,128)(2,1)} %collective-permute-done.24, bf16[4,1,64,1680]{3,2,0,1:T(8,128)(2,1)S(1)} %collective-permute-done.23, bf16[4,3,66,1680]{3,2,0,1:T(8,128)(2,1)S(1)} %fusion.5, f32[1680]{0:T(1024)S(1)} %mul.252, f32[1680]{0:T(1024)S(1)} %mul.249, f32[1680]{0:T(1024)S(1)} %mul.246, ...), kind=kLoop, calls=%fused_computation.12 | loop fusion | flops 13332480 | bytes 10382400 | tf_op jit(solution)/shard_map/add | solution.py:115
  247.4 1.8 convolution_convert_fusion
  255.1 5.8 %collective-permute-done.26 = bf16[64,2240]{1,0:T(8,128)(2,1)} collective-permute-done((bf16[64,2240]{1,0:T(8,128)(2,1)S(1)}, bf16[64,2240]{1,0:T(8,128)(2,1)}, u32[]{:S(2)}, u32[]{:S(2)}) %collective-permute-start.26) | collective-permute-done | bytes 286752 | tf_op jit(solution)/shard_map/ppermute | solution.py:71
  262.3 4.2 %collective-permute-done.27 = bf16[64,2240]{1,0:T(8,128)(2,1)} collective-permute-done((bf16[64,2240]{1,0:T(8,128)(2,1)}, bf16[64,2240]{1,0:T(8,128)(2,1)}, u32[]{:S(2)}, u32[]{:S(2)}) %collective-permute-start.27) | collective-permute-done | bytes 286752 | tf_op jit(solution)/shard_map/ppermute | solution.py:71
  (157 shorter events, 52.6 us)
Async XLA Ops:
  7.2 204.0 %reduce-scatter.2.cloned.1.call-start = ((), (), s32[]{:S(2)}) async-start(), calls=%async_computation.1 | async-start | bytes 4300800 | tf_op jit(solution)/shard_map/reduce_scatter | solution.py:176
  13.6 2.2 collective-permute-start
  18.1 8.9 %collective-permute-start.1 = (f32[113,560]{0,1:T(8,128)S(1)}, f32[113,560]{0,1:T(8,128)S(1)}, u32[]{:S(2)}, u32[]{:S(2)}) collective-permute-start(f32[113,560]{0,1:T(8,128)S(1)} %slice_select_fusion), channel_id=1, source_target_pairs={{0,8},{4,12},{8,0},{12,4},{1,9},{5,13},{9,1},{13,5},{2,10},{6,14},... | collective-permute-start | bytes 759368 | tf_op jit(solution)/shard_map/ppermute | solution.py:50
  27.1 5.2 %collective-permute-start.2 = (f32[113,280]{0,1:T(8,128)S(1)}, f32[113,280]{0,1:T(8,128)S(1)}, u32[]{:S(2)}, u32[]{:S(2)}) collective-permute-start(f32[113,280]{0,1:T(8,128)S(1)} %slice_select_fusion.1), channel_id=1, source_target_pairs={{0,1},{1,0},{2,3},{3,2},{4,5},{5,4},{6,7},{7,6},{8,9},{9,8},{10,11... | collective-permute-start | bytes 379688 | tf_op jit(solution)/shard_map/ppermute | solution.py:50
  32.3 24.6 %copy-start.5 = (bf16[1,1,64,2240]{3,2,1,0:T(8,128)(2,1)S(1)}, bf16[1,1,64,2240]{3,2,1,0:T(8,128)(2,1)}, u32[]{:S(2)}) copy-start(bf16[1,1,64,2240]{3,2,1,0:T(8,128)(2,1)} %param.9) | copy-start | bytes 860164
  32.4 5.3 %collective-permute-start.3 = (f32[113,140]{0,1:T(8,128)S(1)}, f32[113,140]{0,1:T(8,128)S(1)}, u32[]{:S(2)}, u32[]{:S(2)}) collective-permute-start(f32[113,140]{0,1:T(8,128)S(1)} %slice_select_fusion.2), channel_id=1, source_target_pairs={{0,2},{1,3},{2,0},{3,1},{4,6},{5,7},{6,4},{7,5},{8,10},{9,11},{10,... | collective-permute-start | bytes 189848 | tf_op jit(solution)/shard_map/ppermute | solution.py:50
  37.7 5.4 %collective-permute-start.4 = (f32[113,140]{0,1:T(8,128)S(1)}, f32[113,140]{0,1:T(8,128)S(1)}, u32[]{:S(2)}, u32[]{:S(2)}) collective-permute-start(f32[113,140]{0,1:T(8,128)S(1)} %select_add_fusion.3), channel_id=1, source_target_pairs={{0,2},{1,3},{2,0},{3,1},{4,6},{5,7},{6,4},{7,5},{8,10},{9,11},{10,... | collective-permute-start | bytes 189848 | tf_op jit(solution)/shard_map/ppermute | solution.py:53
  43.1 6.5 %collective-permute-start.5 = (f32[113,280]{0,1:T(8,128)S(1)}, f32[113,280]{0,1:T(8,128)S(1)}, u32[]{:S(2)}, u32[]{:S(2)}) collective-permute-start(f32[113,280]{0,1:T(8,128)S(1)} %maximum_select_fusion.3), channel_id=1, source_target_pairs={{0,1},{1,0},{2,3},{3,2},{4,5},{5,4},{6,7},{7,6},{8,9},{9,8},{10,11... | collective-permute-start | bytes 379688 | tf_op jit(solution)/shard_map/ppermute | solution.py:53
  49.7 6.7 %collective-permute-start.6 = (f32[113,560]{0,1:T(8,128)S(1)}, f32[113,560]{0,1:T(8,128)S(1)}, u32[]{:S(2)}, u32[]{:S(2)}) collective-permute-start(f32[113,560]{0,1:T(8,128)S(1)} %maximum_select_fusion.2), channel_id=1, source_target_pairs={{0,8},{4,12},{8,0},{12,4},{1,9},{5,13},{9,1},{13,5},{2,10},{6,14},... | collective-permute-start | bytes 759368 | tf_op jit(solution)/shard_map/ppermute | solution.py:53
  56.8 2.0 collective-permute-start.7
  64.6 13.4 %collective-permute-start.8 = (bf16[1,1,64,560]{2,3,1,0:T(8,128)(2,1)S(1)}, bf16[1,1,64,560]{2,3,1,0:T(8,128)(2,1)}, u32[]{:S(2)}, u32[]{:S(2)}) collective-permute-start(bf16[1,1,64,560]{2,3,1,0:T(8,128)(2,1)S(1)} %get-tuple-element.44), channel_id=1, source_target_pairs={{0,1},{1,0},{2,3},{3,2},{4,5},{5,4},{6,7},{7,6},{8,9},{9,8},{10,11... | collective-permute-start | bytes 215048 | tf_op jit(solution)/shard_map/ppermute | solution.py:92
  71.9 28.0 %collective-permute-start.12 = (bf16[1,1,64,560]{2,3,1,0:T(8,128)(2,1)S(1)}, bf16[1,1,64,560]{2,3,1,0:T(8,128)(2,1)S(1)}, u32[]{:S(2)}, u32[]{:S(2)}) collective-permute-start(bf16[1,1,64,560]{2,3,1,0:T(8,128)(2,1)S(1)} %get-tuple-element.44), channel_id=1, source_target_pairs={{0,5},{1,4},{2,7},{3,6},{4,1},{5,0},{6,3},{7,2},{8,13},{9,12},{10,... | collective-permute-start | bytes 215048 | tf_op jit(solution)/shard_map/ppermute | solution.py:92
  71.9 7.5 %collective-permute-start.9 = (bf16[1,1,64,560]{2,3,1,0:T(8,128)(2,1)S(1)}, bf16[1,1,64,560]{2,3,1,0:T(8,128)(2,1)S(1)}, u32[]{:S(2)}, u32[]{:S(2)}) collective-permute-start(bf16[1,1,64,560]{2,3,1,0:T(8,128)(2,1)S(1)} %get-tuple-element.43), channel_id=1, source_target_pairs={{0,2},{1,3},{2,0},{3,1},{4,6},{5,7},{6,4},{7,5},{8,10},{9,11},{10,... | collective-permute-start | bytes 215048 | tf_op jit(solution)/shard_map/ppermute | solution.py:92
  74.2 27.6 %collective-permute-start.13 = (bf16[1,1,64,560]{2,3,1,0:T(8,128)(2,1)S(1)}, bf16[1,1,64,560]{2,3,1,0:T(8,128)(2,1)S(1)}, u32[]{:S(2)}, u32[]{:S(2)}) collective-permute-start(bf16[1,1,64,560]{2,3,1,0:T(8,128)(2,1)S(1)} %get-tuple-element.43), channel_id=1, source_target_pairs={{0,6},{1,7},{2,4},{3,5},{4,2},{5,3},{6,0},{7,1},{8,14},{9,15},{10,... | collective-permute-start | bytes 215048 | tf_op jit(solution)/shard_map/ppermute | solution.py:92
  74.4 14.6 %collective-permute-start.10 = (bf16[1,1,64,560]{2,3,1,0:T(8,128)(2,1)S(1)}, bf16[1,1,64,560]{2,3,1,0:T(8,128)(2,1)S(1)}, u32[]{:S(2)}, u32[]{:S(2)}) collective-permute-start(bf16[1,1,64,560]{2,3,1,0:T(8,128)(2,1)S(1)} %get-tuple-element.42), channel_id=1, source_target_pairs={{0,3},{1,2},{2,1},{3,0},{4,7},{5,6},{6,5},{7,4},{8,11},{9,10},{10,... | collective-permute-start | bytes 215048 | tf_op jit(solution)/shard_map/ppermute | solution.py:92
  78.0 25.3 %collective-permute-start.14 = (bf16[1,1,64,560]{2,3,1,0:T(8,128)(2,1)S(1)}, bf16[1,1,64,560]{2,3,1,0:T(8,128)(2,1)S(1)}, u32[]{:S(2)}, u32[]{:S(2)}) collective-permute-start(bf16[1,1,64,560]{2,3,1,0:T(8,128)(2,1)S(1)} %get-tuple-element.42), channel_id=1, source_target_pairs={{0,7},{1,6},{2,5},{3,4},{4,3},{5,2},{6,1},{7,0},{8,15},{9,14},{10,... | collective-permute-start | bytes 215048 | tf_op jit(solution)/shard_map/ppermute | solution.py:92
  79.4 10.2 %collective-permute-start.11 = (bf16[1,1,64,560]{2,3,1,0:T(8,128)(2,1)S(1)}, bf16[1,1,64,560]{2,3,1,0:T(8,128)(2,1)S(1)}, u32[]{:S(2)}, u32[]{:S(2)}) collective-permute-start(bf16[1,1,64,560]{2,3,1,0:T(8,128)(2,1)S(1)} %get-tuple-element.40), channel_id=1, source_target_pairs={{0,4},{1,5},{2,6},{3,7},{4,0},{5,1},{6,2},{7,3},{8,12},{9,13},{10,... | collective-permute-start | bytes 215048 | tf_op jit(solution)/shard_map/ppermute | solution.py:92
  89.0 14.5 %collective-permute-start.15 = (bf16[1,1,64,560]{2,3,1,0:T(8,128)(2,1)S(1)}, bf16[1,1,64,560]{2,3,1,0:T(8,128)(2,1)S(1)}, u32[]{:S(2)}, u32[]{:S(2)}) collective-permute-start(bf16[1,1,64,560]{2,3,1,0:T(8,128)(2,1)S(1)} %get-tuple-element.40), channel_id=1, source_target_pairs={{0,8},{1,9},{2,10},{3,11},{4,12},{5,13},{6,14},{7,15},{8,0},{9,1},... | collective-permute-start | bytes 215048 | tf_op jit(solution)/shard_map/ppermute | solution.py:92
  89.6 16.3 %collective-permute-start.16 = (bf16[1,1,64,560]{2,3,1,0:T(8,128)(2,1)S(1)}, bf16[1,1,64,560]{2,3,1,0:T(8,128)(2,1)S(1)}, u32[]{:S(2)}, u32[]{:S(2)}) collective-permute-start(bf16[1,1,64,560]{2,3,1,0:T(8,128)(2,1)S(1)} %get-tuple-element.44), channel_id=1, source_target_pairs={{0,9},{1,8},{2,11},{3,10},{4,13},{5,12},{6,15},{7,14},{8,1},{9,0},... | collective-permute-start | bytes 215048 | tf_op jit(solution)/shard_map/ppermute | solution.py:92
  99.9 14.1 %collective-permute-start.17 = (bf16[1,1,64,560]{2,3,1,0:T(8,128)(2,1)S(1)}, bf16[1,1,64,560]{2,3,1,0:T(8,128)(2,1)S(1)}, u32[]{:S(2)}, u32[]{:S(2)}) collective-permute-start(bf16[1,1,64,560]{2,3,1,0:T(8,128)(2,1)S(1)} %get-tuple-element.43), channel_id=1, source_target_pairs={{0,10},{1,11},{2,8},{3,9},{4,14},{5,15},{6,12},{7,13},{8,2},{9,3},... | collective-permute-start | bytes 215048 | tf_op jit(solution)/shard_map/ppermute | solution.py:92
  101.8 13.4 %collective-permute-start.18 = (bf16[1,1,64,560]{2,3,1,0:T(8,128)(2,1)S(1)}, bf16[1,1,64,560]{2,3,1,0:T(8,128)(2,1)S(1)}, u32[]{:S(2)}, u32[]{:S(2)}) collective-permute-start(bf16[1,1,64,560]{2,3,1,0:T(8,128)(2,1)S(1)} %get-tuple-element.42), channel_id=1, source_target_pairs={{0,11},{1,10},{2,9},{3,8},{4,15},{5,14},{6,13},{7,12},{8,3},{9,2},... | collective-permute-start | bytes 215048 | tf_op jit(solution)/shard_map/ppermute | solution.py:92
  103.4 14.1 %collective-permute-start.19 = (bf16[1,1,64,560]{2,3,1,0:T(8,128)(2,1)S(1)}, bf16[1,1,64,560]{2,3,1,0:T(8,128)(2,1)S(1)}, u32[]{:S(2)}, u32[]{:S(2)}) collective-permute-start(bf16[1,1,64,560]{2,3,1,0:T(8,128)(2,1)S(1)} %get-tuple-element.40), channel_id=1, source_target_pairs={{0,12},{1,13},{2,14},{3,15},{4,8},{5,9},{6,10},{7,11},{8,4},{9,5},... | collective-permute-start | bytes 215048 | tf_op jit(solution)/shard_map/ppermute | solution.py:92
  103.5 14.0 %collective-permute-start.20 = (bf16[1,1,64,560]{2,3,1,0:T(8,128)(2,1)S(1)}, bf16[1,1,64,560]{2,3,1,0:T(8,128)(2,1)S(1)}, u32[]{:S(2)}, u32[]{:S(2)}) collective-permute-start(bf16[1,1,64,560]{2,3,1,0:T(8,128)(2,1)S(1)} %get-tuple-element.44), channel_id=1, source_target_pairs={{0,13},{1,12},{2,15},{3,14},{4,9},{5,8},{6,11},{7,10},{8,5},{9,4},... | collective-permute-start | bytes 215048 | tf_op jit(solution)/shard_map/ppermute | solution.py:92
  105.9 18.0 %collective-permute-start.21 = (bf16[1,1,64,560]{2,3,1,0:T(8,128)(2,1)S(1)}, bf16[1,1,64,560]{2,3,1,0:T(8,128)(2,1)S(1)}, u32[]{:S(2)}, u32[]{:S(2)}) collective-permute-start(bf16[1,1,64,560]{2,3,1,0:T(8,128)(2,1)S(1)} %get-tuple-element.43), channel_id=1, source_target_pairs={{0,14},{1,15},{2,12},{3,13},{4,10},{5,11},{6,8},{7,9},{8,6},{9,7},... | collective-permute-start | bytes 215048 | tf_op jit(solution)/shard_map/ppermute | solution.py:92
  114.1 9.8 %collective-permute-start.22 = (bf16[1,1,64,560]{2,3,1,0:T(8,128)(2,1)S(1)}, bf16[1,1,64,560]{2,3,1,0:T(8,128)(2,1)S(1)}, u32[]{:S(2)}, u32[]{:S(2)}) collective-permute-start(bf16[1,1,64,560]{2,3,1,0:T(8,128)(2,1)S(1)} %get-tuple-element.42), channel_id=1, source_target_pairs={{0,15},{1,14},{2,13},{3,12},{4,11},{5,10},{6,9},{7,8},{8,7},{9,6},... | collective-permute-start | bytes 215048 | tf_op jit(solution)/shard_map/ppermute | solution.py:92
  125.4 8.7 %copy-start.2 = (bf16[1,1,64,560]{2,3,1,0:T(8,128)(2,1)S(1)}, bf16[1,1,64,560]{2,3,1,0:T(8,128)(2,1)}, u32[]{:S(2)}) copy-start(bf16[1,1,64,560]{2,3,1,0:T(8,128)(2,1)} %get-tuple-element.26) | copy-start | bytes 215044
  125.4 8.8 %copy-start.1 = (bf16[1,1,64,560]{2,3,1,0:T(8,128)(2,1)S(1)}, bf16[1,1,64,560]{2,3,1,0:T(8,128)(2,1)}, u32[]{:S(2)}) copy-start(bf16[1,1,64,560]{2,3,1,0:T(8,128)(2,1)} %get-tuple-element.25) | copy-start | bytes 215044
  214.0 23.1 %collective-permute-start.23 = (bf16[4,1,64,1680]{3,2,0,1:T(8,128)(2,1)}, bf16[4,1,64,1680]{3,2,0,1:T(8,128)(2,1)S(1)}, u32[]{:S(2)}, u32[]{:S(2)}) collective-permute-start(bf16[4,1,64,1680]{3,2,0,1:T(8,128)(2,1)} %multiply_convert_fusion), channel_id=1, source_target_pairs={{0,1},{1,2},{2,3},{4,5},{5,6},{6,7},{8,9},{9,10},{10,11},{12,13},{... | collective-permute-start | bytes 2580488 | tf_op jit(solution)/shard_map/ppermute | solution.py:22
  217.2 24.3 %collective-permute-start.24 = (bf16[4,1,64,1680]{3,2,0,1:T(8,128)(2,1)}, bf16[4,1,64,1680]{3,2,0,1:T(8,128)(2,1)}, u32[]{:S(2)}, u32[]{:S(2)}) collective-permute-start(bf16[4,1,64,1680]{3,2,0,1:T(8,128)(2,1)} %multiply_convert_fusion), channel_id=1, source_target_pairs={{1,0},{2,1},{3,2},{5,4},{6,5},{7,6},{9,8},{10,9},{11,10},{13,12},{... | collective-permute-start | bytes 2580488 | tf_op jit(solution)/shard_map/ppermute | solution.py:24
  250.7 4.1 %collective-permute-start.25 = (bf16[64,2240]{1,0:T(8,128)(2,1)S(1)}, bf16[64,2240]{1,0:T(8,128)(2,1)S(1)}, u32[]{:S(2)}, u32[]{:S(2)}) collective-permute-start(bf16[64,2240]{1,0:T(8,128)(2,1)S(1)} %bitcast.160), channel_id=1, source_target_pairs={{0,4},{4,0},{8,12},{12,8},{1,5},{5,1},{9,13},{13,9},{2,6},{6,2},{1... | collective-permute-start | bytes 860168 | tf_op jit(solution)/shard_map/ppermute | solution.py:71
  251.0 10.0 %collective-permute-start.26 = (bf16[64,2240]{1,0:T(8,128)(2,1)S(1)}, bf16[64,2240]{1,0:T(8,128)(2,1)}, u32[]{:S(2)}, u32[]{:S(2)}) collective-permute-start(bf16[64,2240]{1,0:T(8,128)(2,1)S(1)} %bitcast.161), channel_id=1, source_target_pairs={{0,8},{4,12},{8,0},{12,4},{1,9},{5,13},{9,1},{13,5},{2,10},{6,14},... | collective-permute-start | bytes 860168 | tf_op jit(solution)/shard_map/ppermute | solution.py:71
  252.6 13.9 %collective-permute-start.27 = (bf16[64,2240]{1,0:T(8,128)(2,1)}, bf16[64,2240]{1,0:T(8,128)(2,1)}, u32[]{:S(2)}, u32[]{:S(2)}) collective-permute-start(bf16[64,2240]{1,0:T(8,128)(2,1)} %bitcast.63), channel_id=1, source_target_pairs={{0,12},{4,8},{8,4},{12,0},{1,13},{5,9},{9,5},{13,1},{2,14},{6,10},... | collective-permute-start | bytes 860168 | tf_op jit(solution)/shard_map/ppermute | solution.py:71
  (8 other events, 38.0 us)
Sparse Core Ops, SparseCore 0:
  141.2 69.8 reduce-scatter.1

commit v6 on v3

--- a/solution.py
+++ b/solution.py
@@ -134,12 +134,39 @@
     by_row = jnp.concatenate(swap_chunks(depth_chunks, "row"), axis=1)
     frame_parts = lax.axis_size("frame")
     by_frame = swap_chunks([by_row] * frame_parts, "frame")
+    whole_frames = frame_parts == row_parts and frame_count == 1 and row_count == 1
+    weight_flat = in_weight.reshape(local_depth, 2 * local_gated)
+    if whole_frames:
+        tokens = jnp.stack([piece[0] for piece in by_frame])
+        partial = jnp.dot(
+            tokens.reshape(-1, local_depth), weight_flat, preferred_element_type=jnp.float32
+        ).astype(jnp.bfloat16)
+        summed = lax.psum_scatter(partial, "row", scatter_dimension=0, tiled=True)
+        frame_rows = tokens.shape[1]
+        expanded = (
+            jax.nn.silu(summed.astype(jnp.float32))
+            .astype(jnp.bfloat16)
+            .reshape(1, frame_rows, col_count, 2 * local_gated)
+        )
+        padded_expanded = jnp.pad(expanded, ((0, 0), (1, 1), (0, 0), (0, 0)))
+        hidden = depthwise(padded_expanded, conv_taps, frame_rows, col_count, local_gated)
+        projected = jnp.dot(
+            hidden.reshape(-1, local_gated), out_weight, preferred_element_type=jnp.float32
+        ).astype(jnp.bfloat16)
+        row_blocks = jnp.split(projected, frame_parts, axis=0)
+        crossed = sum(piece.astype(jnp.float32) for piece in swap_chunks(row_blocks, "frame"))
+        ffn_rows = lax.ppermute(
+            crossed,
+            ("frame", "row"),
+            [(f * row_parts + r, r * row_parts + f) for f in range(frame_parts) for r in range(row_parts)],
+        ).reshape(token_count, model_width)
+        block_out = (stream_out.astype(jnp.float32) + ffn_rows).astype(jnp.bfloat16)
+        grid_shape = (frame_count, row_count, col_count, model_width)
+        return (stream_out.reshape(grid_shape), block_out.reshape(grid_shape))
     tokens = jnp.stack([piece.transpose(1, 0, 2, 3) for piece in by_frame], axis=1)
     piece_frames = tokens.shape[1] * tokens.shape[2]
     partial = jnp.dot(
-        tokens.reshape(-1, local_depth),
-        in_weight.reshape(local_depth, 2 * local_gated),
-        preferred_element_type=jnp.float32,
+        tokens.reshape(-1, local_depth), weight_flat, preferred_element_type=jnp.float32
     ).astype(jnp.bfloat16)
     summed = lax.psum_scatter(partial, "row", scatter_dimension=0, tiled=True).reshape(
         piece_frames, row_count, col_count, 2 * local_gated

time: 240 us -> 231 us (0.963)
  local copies, waits for them, and re-layouts: 20.7 us -> 16.2 us
  other arithmetic: 17.6 us -> 14.8 us
    ppermute x2 -> x1, waiting for transfers between devices: 22.2 us -> 27.2 us  [local(): lax.ppermute(crossed, ('frame', 'row'), [(f * row_parts + r, r * row_part...]
    reduce_scatter x1, waiting for transfers between devices: 65.8 us -> 62.9 us  [local(): summed = lax.psum_scatter(partial, 'row', scatter_dimension=0, tiled=True)]
    ppermute x9, waiting for transfers between devices: 34.1 us -> 31.7 us  [swap_chunks(): lax.ppermute(sent, axis, [(i, i ^ mask) for i in range(count)])]
    ppermute x2 -> x1, starting transfers between devices: 4.44 us -> 4.81 us  [local(): lax.ppermute(crossed, ('frame', 'row'), [(f * row_parts + r, r * row_part...]
  transfers between devices with their start and end apart: 20 -> 19, of which waited for: 17 -> 16; matrix products, arithmetic and copies ran while one was open for 3% -> 2% of each run, Pallas kernels for 0% -> 0%
where the time goes in v6:
time: 231 us
  waiting for transfers between devices  152 us (66%)
  starting transfers between devices  24.4 us (11%)
  local copies, waits for them, and re-layouts  16.2 us (7%)
  other arithmetic  14.8 us (6%)
  between operations  14.6 us (6%)
  matrix products  8.59 us (4%)
    reduce_scatter x1, waiting for transfers between devices, local(): summed = lax.psum_scatter(partial, 'row', scatter_dimension=0, tiled=True)  62.9 us
    ppermute x9, waiting for transfers between devices, swap_chunks(): lax.ppermute(sent, axis, [(i, i ^ mask) for i in range(count)])  31.7 us
    ppermute x1, waiting for transfers between devices, local(): lax.ppermute(crossed, ('frame', 'row'), [(f * row_parts + r, r * row_part...  27.2 us
    ppermute x4, waiting for transfers between devices, halving_sum(): lax.ppermute(sent, axis, [(i, i ^ bit) for i in range(count)])  17.2 us
    ppermute x4, waiting for transfers between devices, halving_sum(): other = lax.ppermute(block, axis, [(i, i ^ bit) for i in range(count)])  13.3 us
    ppermute x9, starting transfers between devices, swap_chunks(): lax.ppermute(sent, axis, [(i, i ^ mask) for i in range(count)])  8.36 us
    ppermute x4, starting transfers between devices, halving_sum(): other = lax.ppermute(block, axis, [(i, i ^ bit) for i in range(count)])  6.84 us
    ppermute x1, starting transfers between devices, local(): lax.ppermute(crossed, ('frame', 'row'), [(f * row_parts + r, r * row_part...  4.81 us
  transfers between devices with their start and end apart: 19, of which 16 were waited for; matrix products, arithmetic and copies ran while one was open for 2% of the time, Pallas kernels for 0%

profile of v6, /device:TPU:2, one launch (start us, length us, event | category | flops | bytes accessed | tf_op | source)
XLA Modules:
  0.0 230.9 jit_solution(9517577705213046447)
XLA Ops:
  12.7 2.2 collective-permute-done
  15.9 1.3 select_add_fusion
  17.3 8.9 %collective-permute-done.1 = f32[113,560]{0,1:T(8,128)S(1)} collective-permute-done((f32[113,560]{0,1:T(8,128)S(1)}, f32[113,560]{0,1:T(8,128)S(1)}, u32[]{:S(2)}, u32[]{:S(2)}) %collective-permute-start.1) | collective-permute-done | bytes 253152 | tf_op jit(solution)/shard_map/ppermute | solution.py:50
  26.3 1.6 collective-permute-start.2
  27.9 3.5 %collective-permute-done.2 = f32[113,280]{0,1:T(8,128)S(1)} collective-permute-done((f32[113,280]{0,1:T(8,128)S(1)}, f32[113,280]{0,1:T(8,128)S(1)}, u32[]{:S(2)}, u32[]{:S(2)}) %collective-permute-start.2) | collective-permute-done | bytes 126592 | tf_op jit(solution)/shard_map/ppermute | solution.py:50
  31.5 2.7 %collective-permute-start.3 = (f32[113,140]{0,1:T(8,128)S(1)}, f32[113,140]{0,1:T(8,128)S(1)}, u32[]{:S(2)}, u32[]{:S(2)}) collective-permute-start(f32[113,140]{0,1:T(8,128)S(1)} %slice_select_fusion.2), channel_id=1, source_target_pairs={{0,2},{1,3},{2,0},{3,1},{4,6},{5,7},{6,4},{7,5},{8,10},{9,11},{10,... | collective-permute-start | bytes 189848 | tf_op jit(solution)/shard_map/ppermute | solution.py:50
  34.2 2.7 %collective-permute-done.3 = f32[113,140]{0,1:T(8,128)S(1)} collective-permute-done((f32[113,140]{0,1:T(8,128)S(1)}, f32[113,140]{0,1:T(8,128)S(1)}, u32[]{:S(2)}, u32[]{:S(2)}) %collective-permute-start.3) | collective-permute-done | bytes 63312 | tf_op jit(solution)/shard_map/ppermute | solution.py:50
  36.9 2.7 %collective-permute-start.4 = (f32[113,140]{0,1:T(8,128)S(1)}, f32[113,140]{0,1:T(8,128)S(1)}, u32[]{:S(2)}, u32[]{:S(2)}) collective-permute-start(f32[113,140]{0,1:T(8,128)S(1)} %select_add_fusion.3), channel_id=1, source_target_pairs={{0,2},{1,3},{2,0},{3,1},{4,6},{5,7},{6,4},{7,5},{8,10},{9,11},{10,... | collective-permute-start | bytes 189848 | tf_op jit(solution)/shard_map/ppermute | solution.py:53
  39.6 2.7 %collective-permute-done.4 = f32[113,140]{0,1:T(8,128)S(1)} collective-permute-done((f32[113,140]{0,1:T(8,128)S(1)}, f32[113,140]{0,1:T(8,128)S(1)}, u32[]{:S(2)}, u32[]{:S(2)}) %collective-permute-start.4) | collective-permute-done | bytes 63312 | tf_op jit(solution)/shard_map/ppermute | solution.py:53
  42.3 3.5 %collective-permute-start.5 = (f32[113,280]{0,1:T(8,128)S(1)}, f32[113,280]{0,1:T(8,128)S(1)}, u32[]{:S(2)}, u32[]{:S(2)}) collective-permute-start(f32[113,280]{0,1:T(8,128)S(1)} %maximum_select_fusion.3), channel_id=1, source_target_pairs={{0,1},{1,0},{2,3},{3,2},{4,5},{5,4},{6,7},{7,6},{8,9},{9,8},{10,11... | collective-permute-start | bytes 379688 | tf_op jit(solution)/shard_map/ppermute | solution.py:53
  45.8 3.1 %collective-permute-done.5 = f32[113,280]{0,1:T(8,128)S(1)} collective-permute-done((f32[113,280]{0,1:T(8,128)S(1)}, f32[113,280]{0,1:T(8,128)S(1)}, u32[]{:S(2)}, u32[]{:S(2)}) %collective-permute-start.5) | collective-permute-done | bytes 126592 | tf_op jit(solution)/shard_map/ppermute | solution.py:53
  49.5 6.1 %collective-permute-done.6 = f32[113,560]{0,1:T(8,128)S(1)} collective-permute-done((f32[113,560]{0,1:T(8,128)S(1)}, f32[113,560]{0,1:T(8,128)S(1)}, u32[]{:S(2)}, u32[]{:S(2)}) %collective-permute-start.6) | collective-permute-done | bytes 253152 | tf_op jit(solution)/shard_map/ppermute | solution.py:53
  56.5 1.4 collective-permute-done.7
  59.7 1.4 multiply_reduce_fusion
  63.6 3.8 %collective-permute-start.10 = (bf16[1,1,64,560]{3,2,1,0:T(8,128)(2,1)S(1)}, bf16[1,1,64,560]{3,2,1,0:T(8,128)(2,1)S(1)}, u32[]{:S(2)}, u32[]{:S(2)}) collective-permute-start(bf16[1,1,64,560]{3,2,1,0:T(8,128)(2,1)S(1)} %get-tuple-element.33), channel_id=1, source_target_pairs={{0,3},{1,2},{2,1},{3,0},{4,7},{5,6},{6,5},{7,4},{8,11},{9,10},{10,... | collective-permute-start | bytes 215048 | tf_op jit(solution)/shard_map/ppermute | solution.py:71
  68.1 2.8 %collective-permute-done.10 = bf16[1,1,64,560]{3,2,1,0:T(8,128)(2,1)S(1)} collective-permute-done((bf16[1,1,64,560]{3,2,1,0:T(8,128)(2,1)S(1)}, bf16[1,1,64,560]{3,2,1,0:T(8,128)(2,1)S(1)}, u32[]{:S(2)}, u32[]{:S(2)}) %collective-permute-start.10) | collective-permute-done | bytes 71712 | tf_op jit(solution)/shard_map/ppermute | solution.py:71
  70.8 4.0 %collective-permute-done.9 = bf16[1,1,64,560]{3,2,1,0:T(8,128)(2,1)S(1)} collective-permute-done((bf16[1,1,64,560]{3,2,1,0:T(8,128)(2,1)S(1)}, bf16[1,1,64,560]{3,2,1,0:T(8,128)(2,1)S(1)}, u32[]{:S(2)}, u32[]{:S(2)}) %collective-permute-start.9) | collective-permute-done | bytes 71712 | tf_op jit(solution)/shard_map/ppermute | solution.py:71
  77.7 2.5 %reshape.227 = bf16[560,1680]{1,0:T(8,128)(2,1)} reshape(bf16[560,2,840]{2,1,0:T(2,128)(2,1)S(1)} %copy-done) | data formatting | bytes 3763200 | tf_op jit(solution)/shard_map/reshape | solution.py:138
  80.1 5.9 %collective-permute-done.13 = bf16[1,4,64,560]{3,2,1,0:T(8,128)(2,1)S(1)} collective-permute-done((bf16[1,4,64,560]{3,2,1,0:T(8,128)(2,1)}, bf16[1,4,64,560]{3,2,1,0:T(8,128)(2,1)S(1)}, u32[]{:S(2)}, u32[]{:S(2)}) %collective-permute-start.13) | collective-permute-done | bytes 286752 | tf_op jit(solution)/shard_map/ppermute | solution.py:71
  86.0 6.4 %collective-permute-done.12 = bf16[1,4,64,560]{3,2,1,0:T(8,128)(2,1)S(1)} collective-permute-done((bf16[1,4,64,560]{3,2,1,0:T(8,128)(2,1)}, bf16[1,4,64,560]{3,2,1,0:T(8,128)(2,1)S(1)}, u32[]{:S(2)}, u32[]{:S(2)}) %collective-permute-start.12) | collective-permute-done | bytes 286752 | tf_op jit(solution)/shard_map/ppermute | solution.py:71
  94.1 1.3 copy-done.1
  95.4 4.4 %convolution_convert_fusion.1 = bf16[1024,1680]{0,1:T(8,128)(2,1)} fusion(bf16[1024,560]{1,0:T(8,128)(2,1)S(1)} %bitcast.101, bf16[560,1680]{1,0:T(8,128)(2,1)S(1)} %copy-done.1), kind=kOutput, calls=%fused_computation.1 | convolution fusion | flops 1928478720 | bytes 6469120 | tf_op jit(solution)/shard_map/dot_general | solution.py:141
  101.3 62.9 %reduce-scatter.2.cloned.1.call-done = bf16[256,1680]{0,1:T(8,128)(2,1)} async-done(((bf16[1024,1680]{0,1:T(8,128)(2,1)}), bf16[256,1680]{0,1:T(8,128)(2,1)}) %reduce-scatter.2.cloned.1.call-update) | async-done | bytes 860176 | tf_op jit(solution)/shard_map/reduce_scatter | solution.py:144
  164.2 1.6 fusion.3
  166.6 2.7 %multiply_add_fusion = f32[1,4,64,1680]{3,2,1,0:T(8,128)S(1)} fusion(bf16[1,4,64,1680]{3,2,1,0:T(8,128)(2,1)S(1)} %bitcast.96, bf16[1,6,64,1680]{3,2,1,0:T(8,128)(2,1)S(1)} %pad.8, f32[1680]{0:T(1024)S(1)} %mul.211, f32[1680]{0:T(1024)S(1)} %mul.208, f32[1680]{0:T(1024)S(1)} %mul.205, f32[1680]{0:T(1024)S(1)} %mul.202, f32[1680]{0:T(1024)S(1)} %mul.199, ...), kind=kLoop, calls=%fused_computation.6 | loop fusion | flops 11182080 | bytes 5922816 | tf_op jit(solution)/shard_map/add | solution.py:87
  169.7 1.8 convolution_convert_fusion
  173.3 1.4 collective-permute-start.15
  175.5 6.8 %collective-permute-done.16 = bf16[64,2240]{1,0:T(8,128)(2,1)S(1)} collective-permute-done((bf16[64,2240]{1,0:T(8,128)(2,1)S(1)}, bf16[64,2240]{1,0:T(8,128)(2,1)S(1)}, u32[]{:S(2)}, u32[]{:S(2)}) %collective-permute-start.16) | collective-permute-done | bytes 286752 | tf_op jit(solution)/shard_map/ppermute | solution.py:71
  182.7 5.7 %collective-permute-done.15 = bf16[64,2240]{1,0:T(8,128)(2,1)S(1)} collective-permute-done((bf16[64,2240]{1,0:T(8,128)(2,1)S(1)}, bf16[64,2240]{1,0:T(8,128)(2,1)S(1)}, u32[]{:S(2)}, u32[]{:S(2)}) %collective-permute-start.15) | collective-permute-done | bytes 286752 | tf_op jit(solution)/shard_map/ppermute | solution.py:71
  188.7 1.3 copy.85
  191.3 4.8 %collective-permute-start.17 = (f32[64,2240]{1,0:T(8,128)S(1)}, f32[64,2240]{1,0:T(8,128)S(1)}, u32[]{:S(2)}, u32[]{:S(2)}) collective-permute-start(f32[64,2240]{1,0:T(8,128)S(1)} %copy.90), channel_id=1, source_target_pairs={{0,0},{1,4},{2,8},{3,12},{4,1},{5,5},{6,9},{7,13},{8,2},{9,6},{10,... | collective-permute-start | bytes 1720328 | tf_op jit(solution)/shard_map/ppermute | solution.py:158
  196.1 27.2 %collective-permute-done.17 = f32[64,2240]{1,0:T(8,128)S(1)} collective-permute-done((f32[64,2240]{1,0:T(8,128)S(1)}, f32[64,2240]{1,0:T(8,128)S(1)}, u32[]{:S(2)}, u32[]{:S(2)}) %collective-permute-start.17) | collective-permute-done | bytes 573472 | tf_op jit(solution)/shard_map/ppermute | solution.py:158
  (104 shorter events, 25.3 us)
Async XLA Ops:
  7.2 2.5 %copy-start.4 = (bf16[1,1,64,2240]{3,2,1,0:T(8,128)(2,1)S(1)}, bf16[1,1,64,2240]{3,2,1,0:T(8,128)(2,1)}, u32[]{:S(2)}) copy-start(bf16[1,1,64,2240]{3,2,1,0:T(8,128)(2,1)} %param.11) | copy-start | bytes 860164
  7.2 157.0 %reduce-scatter.2.cloned.1.call-start = ((), (), s32[]{:S(2)}) async-start(), calls=%async_computation.1 | async-start | bytes 4300800 | tf_op jit(solution)/shard_map/reduce_scatter | solution.py:144
  12.7 2.2 collective-permute-start
  17.2 32.2 %copy-start.6 = (bf16[2240]{0:T(1024)(128)(2,1)S(1)}, bf16[2240]{0:T(1024)(128)(2,1)}, u32[]{:S(2)}) copy-start(bf16[2240]{0:T(1024)(128)(2,1)} %param.14) | copy-start | bytes 13444
  17.3 8.9 %collective-permute-start.1 = (f32[113,560]{0,1:T(8,128)S(1)}, f32[113,560]{0,1:T(8,128)S(1)}, u32[]{:S(2)}, u32[]{:S(2)}) collective-permute-start(f32[113,560]{0,1:T(8,128)S(1)} %slice_select_fusion), channel_id=1, source_target_pairs={{0,8},{4,12},{8,0},{12,4},{1,9},{5,13},{9,1},{13,5},{2,10},{6,14},... | collective-permute-start | bytes 759368 | tf_op jit(solution)/shard_map/ppermute | solution.py:50
  26.3 5.2 %collective-permute-start.2 = (f32[113,280]{0,1:T(8,128)S(1)}, f32[113,280]{0,1:T(8,128)S(1)}, u32[]{:S(2)}, u32[]{:S(2)}) collective-permute-start(f32[113,280]{0,1:T(8,128)S(1)} %slice_select_fusion.1), channel_id=1, source_target_pairs={{0,1},{1,0},{2,3},{3,2},{4,5},{5,4},{6,7},{7,6},{8,9},{9,8},{10,11... | collective-permute-start | bytes 379688 | tf_op jit(solution)/shard_map/ppermute | solution.py:50
  31.5 24.5 %copy-start.3 = (bf16[1,1,64,2240]{3,2,1,0:T(8,128)(2,1)S(1)}, bf16[1,1,64,2240]{3,2,1,0:T(8,128)(2,1)}, u32[]{:S(2)}) copy-start(bf16[1,1,64,2240]{3,2,1,0:T(8,128)(2,1)} %param.9) | copy-start | bytes 860164
  31.5 5.3 %collective-permute-start.3 = (f32[113,140]{0,1:T(8,128)S(1)}, f32[113,140]{0,1:T(8,128)S(1)}, u32[]{:S(2)}, u32[]{:S(2)}) collective-permute-start(f32[113,140]{0,1:T(8,128)S(1)} %slice_select_fusion.2), channel_id=1, source_target_pairs={{0,2},{1,3},{2,0},{3,1},{4,6},{5,7},{6,4},{7,5},{8,10},{9,11},{10,... | collective-permute-start | bytes 189848 | tf_op jit(solution)/shard_map/ppermute | solution.py:50
  36.9 5.4 %collective-permute-start.4 = (f32[113,140]{0,1:T(8,128)S(1)}, f32[113,140]{0,1:T(8,128)S(1)}, u32[]{:S(2)}, u32[]{:S(2)}) collective-permute-start(f32[113,140]{0,1:T(8,128)S(1)} %select_add_fusion.3), channel_id=1, source_target_pairs={{0,2},{1,3},{2,0},{3,1},{4,6},{5,7},{6,4},{7,5},{8,10},{9,11},{10,... | collective-permute-start | bytes 189848 | tf_op jit(solution)/shard_map/ppermute | solution.py:53
  42.3 6.5 %collective-permute-start.5 = (f32[113,280]{0,1:T(8,128)S(1)}, f32[113,280]{0,1:T(8,128)S(1)}, u32[]{:S(2)}, u32[]{:S(2)}) collective-permute-start(f32[113,280]{0,1:T(8,128)S(1)} %maximum_select_fusion.3), channel_id=1, source_target_pairs={{0,1},{1,0},{2,3},{3,2},{4,5},{5,4},{6,7},{7,6},{8,9},{9,8},{10,11... | collective-permute-start | bytes 379688 | tf_op jit(solution)/shard_map/ppermute | solution.py:53
  48.9 7.6 %copy-start.7 = (bf16[2240]{0:T(1024)(128)(2,1)S(1)}, bf16[2240]{0:T(1024)(128)(2,1)}, u32[]{:S(2)}) copy-start(bf16[2240]{0:T(1024)(128)(2,1)} %param.13) | copy-start | bytes 13444
  48.9 6.7 %collective-permute-start.6 = (f32[113,560]{0,1:T(8,128)S(1)}, f32[113,560]{0,1:T(8,128)S(1)}, u32[]{:S(2)}, u32[]{:S(2)}) collective-permute-start(f32[113,560]{0,1:T(8,128)S(1)} %maximum_select_fusion.2), channel_id=1, source_target_pairs={{0,8},{4,12},{8,0},{12,4},{1,9},{5,13},{9,1},{13,5},{2,10},{6,14},... | collective-permute-start | bytes 759368 | tf_op jit(solution)/shard_map/ppermute | solution.py:53
  55.9 2.0 collective-permute-start.7
  61.1 1.0 copy-start.2
  63.5 14.2 %copy-start = (bf16[560,2,840]{2,1,0:T(2,128)(2,1)S(1)}, bf16[560,2,840]{2,1,0:T(2,128)(2,1)}, u32[]{:S(2)}) copy-start(bf16[560,2,840]{2,1,0:T(2,128)(2,1)} %param.15) | copy-start | bytes 5644804
  63.6 7.2 %collective-permute-start.10 = (bf16[1,1,64,560]{3,2,1,0:T(8,128)(2,1)S(1)}, bf16[1,1,64,560]{3,2,1,0:T(8,128)(2,1)S(1)}, u32[]{:S(2)}, u32[]{:S(2)}) collective-permute-start(bf16[1,1,64,560]{3,2,1,0:T(8,128)(2,1)S(1)} %get-tuple-element.33), channel_id=1, source_target_pairs={{0,3},{1,2},{2,1},{3,0},{4,7},{5,6},{6,5},{7,4},{8,11},{9,10},{10,... | collective-permute-start | bytes 215048 | tf_op jit(solution)/shard_map/ppermute | solution.py:71
  67.4 7.5 %collective-permute-start.9 = (bf16[1,1,64,560]{3,2,1,0:T(8,128)(2,1)S(1)}, bf16[1,1,64,560]{3,2,1,0:T(8,128)(2,1)S(1)}, u32[]{:S(2)}, u32[]{:S(2)}) collective-permute-start(bf16[1,1,64,560]{3,2,1,0:T(8,128)(2,1)S(1)} %get-tuple-element.34), channel_id=1, source_target_pairs={{0,2},{1,3},{2,0},{3,1},{4,6},{5,7},{6,4},{7,5},{8,10},{9,11},{10,... | collective-permute-start | bytes 215048 | tf_op jit(solution)/shard_map/ppermute | solution.py:71
  67.4 7.5 %collective-permute-start.8 = (bf16[1,1,64,560]{3,2,1,0:T(8,128)(2,1)S(1)}, bf16[1,1,64,560]{3,2,1,0:T(8,128)(2,1)S(1)}, u32[]{:S(2)}, u32[]{:S(2)}) collective-permute-start(bf16[1,1,64,560]{3,2,1,0:T(8,128)(2,1)S(1)} %get-tuple-element.35), channel_id=1, source_target_pairs={{0,1},{1,0},{2,3},{3,2},{4,5},{5,4},{6,7},{7,6},{8,9},{9,8},{10,11... | collective-permute-start | bytes 215048 | tf_op jit(solution)/shard_map/ppermute | solution.py:71
  75.8 10.2 %collective-permute-start.13 = (bf16[1,4,64,560]{3,2,1,0:T(8,128)(2,1)}, bf16[1,4,64,560]{3,2,1,0:T(8,128)(2,1)S(1)}, u32[]{:S(2)}, u32[]{:S(2)}) collective-permute-start(bf16[1,4,64,560]{3,2,1,0:T(8,128)(2,1)} %get-tuple-element.27), channel_id=1, source_target_pairs={{0,12},{4,8},{8,4},{12,0},{1,13},{5,9},{9,5},{13,1},{2,14},{6,10},... | collective-permute-start | bytes 860168 | tf_op jit(solution)/shard_map/ppermute | solution.py:71
  75.8 16.6 %collective-permute-start.12 = (bf16[1,4,64,560]{3,2,1,0:T(8,128)(2,1)}, bf16[1,4,64,560]{3,2,1,0:T(8,128)(2,1)S(1)}, u32[]{:S(2)}, u32[]{:S(2)}) collective-permute-start(bf16[1,4,64,560]{3,2,1,0:T(8,128)(2,1)} %get-tuple-element.27), channel_id=1, source_target_pairs={{0,8},{4,12},{8,0},{12,4},{1,9},{5,13},{9,1},{13,5},{2,10},{6,14},... | collective-permute-start | bytes 860168 | tf_op jit(solution)/shard_map/ppermute | solution.py:71
  76.9 15.5 %collective-permute-start.11 = (bf16[1,4,64,560]{3,2,1,0:T(8,128)(2,1)}, bf16[1,4,64,560]{3,2,1,0:T(8,128)(2,1)}, u32[]{:S(2)}, u32[]{:S(2)}) collective-permute-start(bf16[1,4,64,560]{3,2,1,0:T(8,128)(2,1)} %get-tuple-element.27), channel_id=1, source_target_pairs={{0,4},{4,0},{8,12},{12,8},{1,5},{5,1},{9,13},{13,9},{2,6},{6,2},{1... | collective-permute-start | bytes 860168 | tf_op jit(solution)/shard_map/ppermute | solution.py:71
  93.8 1.6 copy-start.1
  99.8 0.8 copy-start.5
  166.5 3.1 %copy-start.8 = (bf16[840,2240]{1,0:T(8,128)(2,1)S(1)}, bf16[840,2240]{1,0:T(8,128)(2,1)}, u32[]{:S(2)}) copy-start(bf16[840,2240]{1,0:T(8,128)(2,1)} %param.17) | copy-start | bytes 11289604
  173.0 9.4 %collective-permute-start.16 = (bf16[64,2240]{1,0:T(8,128)(2,1)S(1)}, bf16[64,2240]{1,0:T(8,128)(2,1)S(1)}, u32[]{:S(2)}, u32[]{:S(2)}) collective-permute-start(bf16[64,2240]{1,0:T(8,128)(2,1)S(1)} %bitcast.105), channel_id=1, source_target_pairs={{0,12},{4,8},{8,4},{12,0},{1,13},{5,9},{9,5},{13,1},{2,14},{6,10},... | collective-permute-start | bytes 860168 | tf_op jit(solution)/shard_map/ppermute | solution.py:71
  173.3 15.1 %collective-permute-start.15 = (bf16[64,2240]{1,0:T(8,128)(2,1)S(1)}, bf16[64,2240]{1,0:T(8,128)(2,1)S(1)}, u32[]{:S(2)}, u32[]{:S(2)}) collective-permute-start(bf16[64,2240]{1,0:T(8,128)(2,1)S(1)} %bitcast.106), channel_id=1, source_target_pairs={{0,8},{4,12},{8,0},{12,4},{1,9},{5,13},{9,1},{13,5},{2,10},{6,14},... | collective-permute-start | bytes 860168 | tf_op jit(solution)/shard_map/ppermute | solution.py:71
  174.9 13.8 %collective-permute-start.14 = (bf16[64,2240]{1,0:T(8,128)(2,1)S(1)}, bf16[64,2240]{1,0:T(8,128)(2,1)}, u32[]{:S(2)}, u32[]{:S(2)}) collective-permute-start(bf16[64,2240]{1,0:T(8,128)(2,1)S(1)} %bitcast.107), channel_id=1, source_target_pairs={{0,4},{4,0},{8,12},{12,8},{1,5},{5,1},{9,13},{13,9},{2,6},{6,2},{1... | collective-permute-start | bytes 860168 | tf_op jit(solution)/shard_map/ppermute | solution.py:71
  191.3 32.0 %collective-permute-start.17 = (f32[64,2240]{1,0:T(8,128)S(1)}, f32[64,2240]{1,0:T(8,128)S(1)}, u32[]{:S(2)}, u32[]{:S(2)}) collective-permute-start(f32[64,2240]{1,0:T(8,128)S(1)} %copy.90), channel_id=1, source_target_pairs={{0,0},{1,4},{2,8},{3,12},{4,1},{5,5},{6,9},{7,13},{8,2},{9,6},{10,... | collective-permute-start | bytes 1720328 | tf_op jit(solution)/shard_map/ppermute | solution.py:158
Sparse Core Ops, SparseCore 0:
  99.9 64.1 reduce-scatter.1

commit v7 on v6

--- a/solution.py
+++ b/solution.py
@@ -154,12 +154,21 @@
             hidden.reshape(-1, local_gated), out_weight, preferred_element_type=jnp.float32
         ).astype(jnp.bfloat16)
         row_blocks = jnp.split(projected, frame_parts, axis=0)
-        crossed = sum(piece.astype(jnp.float32) for piece in swap_chunks(row_blocks, "frame"))
-        ffn_rows = lax.ppermute(
-            crossed,
-            ("frame", "row"),
-            [(f * row_parts + r, r * row_parts + f) for f in range(frame_parts) for r in range(row_parts)],
-        ).reshape(token_count, model_width)
+        frame_at = lax.axis_index("frame")
+        arrived = []
+        for mask in range(row_parts):
+            arrived.append(
+                lax.ppermute(
+                    pick(row_blocks, frame_at ^ mask),
+                    ("frame", "row"),
+                    [
+                        (f * row_parts + r, r * row_parts + (f ^ mask))
+                        for f in range(frame_parts)
+                        for r in range(row_parts)
+                    ],
+                ).astype(jnp.float32)
+            )
+        ffn_rows = sum(arrived).reshape(token_count, model_width)
         block_out = (stream_out.astype(jnp.float32) + ffn_rows).astype(jnp.bfloat16)
         grid_shape = (frame_count, row_count, col_count, model_width)
         return (stream_out.reshape(grid_shape), block_out.reshape(grid_shape))

time: 231 us -> 215 us (0.931)
  waiting for transfers between devices: 152 us -> 137 us
    ppermute x9 -> x6, waiting for transfers between devices: 31.7 us -> 19.1 us  [swap_chunks(): lax.ppermute(sent, axis, [(i, i ^ mask) for i in range(count)])]
    ppermute x1 -> x4, starting transfers between devices: 4.81 us -> 8.83 us  [local(): lax.ppermute(pick(row_blocks, frame_at ^ mask), ('frame', 'row'), [(f * r...]
    ppermute x1 -> x4, waiting for transfers between devices: 27.2 us -> 24 us  [local(): lax.ppermute(pick(row_blocks, frame_at ^ mask), ('frame', 'row'), [(f * r...]
    ppermute x9 -> x6, starting transfers between devices: 8.36 us -> 6.31 us  [swap_chunks(): lax.ppermute(sent, axis, [(i, i ^ mask) for i in range(count)])]
where the time goes in v7:
time: 215 us; the launch traced here: 214 us
  waiting for transfers between devices  137 us (64%)
  starting transfers between devices  26.4 us (12%)
  between operations  14.5 us (7%)
  local copies, waits for them, and re-layouts  14.2 us (7%)
  other arithmetic  14.1 us (7%)
  matrix products  8.59 us (4%)
    reduce_scatter x1, waiting for transfers between devices, local(): summed = lax.psum_scatter(partial, 'row', scatter_dimension=0, tiled=True)  62.9 us
    ppermute x4, waiting for transfers between devices, local(): lax.ppermute(pick(row_blocks, frame_at ^ mask), ('frame', 'row'), [(f * r...  24 us
    ppermute x6, waiting for transfers between devices, swap_chunks(): lax.ppermute(sent, axis, [(i, i ^ mask) for i in range(count)])  19.1 us
    ppermute x4, waiting for transfers between devices, halving_sum(): lax.ppermute(sent, axis, [(i, i ^ bit) for i in range(count)])  17.2 us
    ppermute x4, waiting for transfers between devices, halving_sum(): other = lax.ppermute(block, axis, [(i, i ^ bit) for i in range(count)])  13.3 us
    ppermute x4, starting transfers between devices, local(): lax.ppermute(pick(row_blocks, frame_at ^ mask), ('frame', 'row'), [(f * r...  8.83 us
    ppermute x4, starting transfers between devices, halving_sum(): other = lax.ppermute(block, axis, [(i, i ^ bit) for i in range(count)])  6.84 us
    ppermute x6, starting transfers between devices, swap_chunks(): lax.ppermute(sent, axis, [(i, i ^ mask) for i in range(count)])  6.31 us
  transfers between devices with their start and end apart: 19, of which 16 were waited for; matrix products, arithmetic and copies ran while one was open for 2% of the time, Pallas kernels for 0%

profile of v7, /device:TPU:2, one launch (start us, length us, event | category | flops | bytes accessed | tf_op | source)
XLA Modules:
  0.0 214.3 jit_solution(15594945979255814606)
XLA Ops:
  12.7 2.2 %collective-permute-done = f32[113,1120]{1,0:T(8,128)S(1)} collective-permute-done((f32[113,1120]{1,0:T(8,128)}, f32[113,1120]{1,0:T(8,128)S(1)}, u32[]{:S(2)}, u32[]{:S(2)}) %collective-permute-start) | collective-permute-done | bytes 506272 | tf_op jit(solution)/shard_map/ppermute | solution.py:50
  15.9 1.3 select_add_fusion
  17.3 8.9 %collective-permute-done.1 = f32[113,560]{0,1:T(8,128)S(1)} collective-permute-done((f32[113,560]{0,1:T(8,128)S(1)}, f32[113,560]{0,1:T(8,128)S(1)}, u32[]{:S(2)}, u32[]{:S(2)}) %collective-permute-start.1) | collective-permute-done | bytes 253152 | tf_op jit(solution)/shard_map/ppermute | solution.py:50
  26.3 1.6 collective-permute-start.2
  27.9 3.5 %collective-permute-done.2 = f32[113,280]{0,1:T(8,128)S(1)} collective-permute-done((f32[113,280]{0,1:T(8,128)S(1)}, f32[113,280]{0,1:T(8,128)S(1)}, u32[]{:S(2)}, u32[]{:S(2)}) %collective-permute-start.2) | collective-permute-done | bytes 126592 | tf_op jit(solution)/shard_map/ppermute | solution.py:50
  31.5 2.7 %collective-permute-start.3 = (f32[113,140]{0,1:T(8,128)S(1)}, f32[113,140]{0,1:T(8,128)S(1)}, u32[]{:S(2)}, u32[]{:S(2)}) collective-permute-start(f32[113,140]{0,1:T(8,128)S(1)} %slice_select_fusion.2), channel_id=1, source_target_pairs={{0,2},{1,3},{2,0},{3,1},{4,6},{5,7},{6,4},{7,5},{8,10},{9,11},{10,... | collective-permute-start | bytes 189848 | tf_op jit(solution)/shard_map/ppermute | solution.py:50
  34.2 2.7 %collective-permute-done.3 = f32[113,140]{0,1:T(8,128)S(1)} collective-permute-done((f32[113,140]{0,1:T(8,128)S(1)}, f32[113,140]{0,1:T(8,128)S(1)}, u32[]{:S(2)}, u32[]{:S(2)}) %collective-permute-start.3) | collective-permute-done | bytes 63312 | tf_op jit(solution)/shard_map/ppermute | solution.py:50
  36.9 2.7 %collective-permute-start.4 = (f32[113,140]{0,1:T(8,128)S(1)}, f32[113,140]{0,1:T(8,128)S(1)}, u32[]{:S(2)}, u32[]{:S(2)}) collective-permute-start(f32[113,140]{0,1:T(8,128)S(1)} %select_add_fusion.3), channel_id=1, source_target_pairs={{0,2},{1,3},{2,0},{3,1},{4,6},{5,7},{6,4},{7,5},{8,10},{9,11},{10,... | collective-permute-start | bytes 189848 | tf_op jit(solution)/shard_map/ppermute | solution.py:53
  39.6 2.7 %collective-permute-done.4 = f32[113,140]{0,1:T(8,128)S(1)} collective-permute-done((f32[113,140]{0,1:T(8,128)S(1)}, f32[113,140]{0,1:T(8,128)S(1)}, u32[]{:S(2)}, u32[]{:S(2)}) %collective-permute-start.4) | collective-permute-done | bytes 63312 | tf_op jit(solution)/shard_map/ppermute | solution.py:53
  42.3 3.5 %collective-permute-start.5 = (f32[113,280]{0,1:T(8,128)S(1)}, f32[113,280]{0,1:T(8,128)S(1)}, u32[]{:S(2)}, u32[]{:S(2)}) collective-permute-start(f32[113,280]{0,1:T(8,128)S(1)} %maximum_select_fusion.3), channel_id=1, source_target_pairs={{0,1},{1,0},{2,3},{3,2},{4,5},{5,4},{6,7},{7,6},{8,9},{9,8},{10,11... | collective-permute-start | bytes 379688 | tf_op jit(solution)/shard_map/ppermute | solution.py:53
  45.8 3.1 %collective-permute-done.5 = f32[113,280]{0,1:T(8,128)S(1)} collective-permute-done((f32[113,280]{0,1:T(8,128)S(1)}, f32[113,280]{0,1:T(8,128)S(1)}, u32[]{:S(2)}, u32[]{:S(2)}) %collective-permute-start.5) | collective-permute-done | bytes 126592 | tf_op jit(solution)/shard_map/ppermute | solution.py:53
  49.5 6.1 %collective-permute-done.6 = f32[113,560]{0,1:T(8,128)S(1)} collective-permute-done((f32[113,560]{0,1:T(8,128)S(1)}, f32[113,560]{0,1:T(8,128)S(1)}, u32[]{:S(2)}, u32[]{:S(2)}) %collective-permute-start.6) | collective-permute-done | bytes 253152 | tf_op jit(solution)/shard_map/ppermute | solution.py:53
  56.5 1.4 collective-permute-done.7
  59.7 1.4 multiply_reduce_fusion
  63.6 3.8 %collective-permute-start.10 = (bf16[1,1,64,560]{3,2,1,0:T(8,128)(2,1)S(1)}, bf16[1,1,64,560]{3,2,1,0:T(8,128)(2,1)S(1)}, u32[]{:S(2)}, u32[]{:S(2)}) collective-permute-start(bf16[1,1,64,560]{3,2,1,0:T(8,128)(2,1)S(1)} %get-tuple-element.27), channel_id=1, source_target_pairs={{0,3},{1,2},{2,1},{3,0},{4,7},{5,6},{6,5},{7,4},{8,11},{9,10},{10,... | collective-permute-start | bytes 215048 | tf_op jit(solution)/shard_map/ppermute | solution.py:71
  68.1 2.8 %collective-permute-done.10 = bf16[1,1,64,560]{3,2,1,0:T(8,128)(2,1)S(1)} collective-permute-done((bf16[1,1,64,560]{3,2,1,0:T(8,128)(2,1)S(1)}, bf16[1,1,64,560]{3,2,1,0:T(8,128)(2,1)S(1)}, u32[]{:S(2)}, u32[]{:S(2)}) %collective-permute-start.10) | collective-permute-done | bytes 71712 | tf_op jit(solution)/shard_map/ppermute | solution.py:71
  70.8 4.0 %collective-permute-done.9 = bf16[1,1,64,560]{3,2,1,0:T(8,128)(2,1)S(1)} collective-permute-done((bf16[1,1,64,560]{3,2,1,0:T(8,128)(2,1)S(1)}, bf16[1,1,64,560]{3,2,1,0:T(8,128)(2,1)S(1)}, u32[]{:S(2)}, u32[]{:S(2)}) %collective-permute-start.9) | collective-permute-done | bytes 71712 | tf_op jit(solution)/shard_map/ppermute | solution.py:71
  77.7 2.5 %reshape.220 = bf16[560,1680]{1,0:T(8,128)(2,1)} reshape(bf16[560,2,840]{2,1,0:T(2,128)(2,1)S(1)} %copy-done) | data formatting | bytes 3763200 | tf_op jit(solution)/shard_map/reshape | solution.py:138
  80.1 5.9 %collective-permute-done.13 = bf16[1,4,64,560]{3,2,1,0:T(8,128)(2,1)S(1)} collective-permute-done((bf16[1,4,64,560]{3,2,1,0:T(8,128)(2,1)}, bf16[1,4,64,560]{3,2,1,0:T(8,128)(2,1)S(1)}, u32[]{:S(2)}, u32[]{:S(2)}) %collective-permute-start.13) | collective-permute-done | bytes 286752 | tf_op jit(solution)/shard_map/ppermute | solution.py:71
  86.0 6.4 %collective-permute-done.12 = bf16[1,4,64,560]{3,2,1,0:T(8,128)(2,1)S(1)} collective-permute-done((bf16[1,4,64,560]{3,2,1,0:T(8,128)(2,1)}, bf16[1,4,64,560]{3,2,1,0:T(8,128)(2,1)S(1)}, u32[]{:S(2)}, u32[]{:S(2)}) %collective-permute-start.12) | collective-permute-done | bytes 286752 | tf_op jit(solution)/shard_map/ppermute | solution.py:71
  94.1 1.3 copy-done.1
  95.4 4.4 %convolution_convert_fusion.1 = bf16[1024,1680]{0,1:T(8,128)(2,1)} fusion(bf16[1024,560]{1,0:T(8,128)(2,1)S(1)} %bitcast.94, bf16[560,1680]{1,0:T(8,128)(2,1)S(1)} %copy-done.1), kind=kOutput, calls=%fused_computation.1 | convolution fusion | flops 1928478720 | bytes 6469120 | tf_op jit(solution)/shard_map/dot_general | solution.py:141
  101.3 62.9 %reduce-scatter.2.cloned.1.call-done = bf16[256,1680]{0,1:T(8,128)(2,1)} async-done(((bf16[1024,1680]{0,1:T(8,128)(2,1)}), bf16[256,1680]{0,1:T(8,128)(2,1)}) %reduce-scatter.2.cloned.1.call-update) | async-done | bytes 860176 | tf_op jit(solution)/shard_map/reduce_scatter | solution.py:144
  164.2 1.6 fusion.3
  166.6 2.7 %multiply_add_fusion = f32[1,4,64,1680]{3,2,1,0:T(8,128)S(1)} fusion(bf16[1,4,64,1680]{3,2,1,0:T(8,128)(2,1)S(1)} %bitcast.92, bf16[1,6,64,1680]{3,2,1,0:T(8,128)(2,1)S(1)} %pad.8, f32[1680]{0:T(1024)S(1)} %mul.211, f32[1680]{0:T(1024)S(1)} %mul.208, f32[1680]{0:T(1024)S(1)} %mul.205, f32[1680]{0:T(1024)S(1)} %mul.202, f32[1680]{0:T(1024)S(1)} %mul.199, ...), kind=kLoop, calls=%fused_computation.5 | loop fusion | flops 11182080 | bytes 5922816 | tf_op jit(solution)/shard_map/add | solution.py:87
  169.7 1.8 convolution_convert_fusion
  174.5 1.7 collective-permute-start.16
  176.4 2.2 %collective-permute-start.15 = (bf16[64,2240]{1,0:T(8,128)(2,1)S(1)}, bf16[64,2240]{1,0:T(8,128)(2,1)S(1)}, u32[]{:S(2)}, u32[]{:S(2)}) collective-permute-start(bf16[64,2240]{1,0:T(8,128)(2,1)S(1)} %bitcast.100), channel_id=1, source_target_pairs={{0,1},{1,5},{2,9},{3,13},{4,0},{5,4},{6,8},{7,12},{8,3},{9,7},{10,... | collective-permute-start | bytes 860168 | tf_op jit(solution)/shard_map/ppermute | solution.py:161
  178.9 3.6 %collective-permute-start.14 = (bf16[64,2240]{1,0:T(8,128)(2,1)S(1)}, bf16[64,2240]{1,0:T(8,128)(2,1)S(1)}, u32[]{:S(2)}, u32[]{:S(2)}) collective-permute-start(bf16[64,2240]{1,0:T(8,128)(2,1)S(1)} %bitcast.101), channel_id=1, source_target_pairs={{0,0},{1,4},{2,8},{3,12},{4,1},{5,5},{6,9},{7,13},{8,2},{9,6},{10,... | collective-permute-start | bytes 860168 | tf_op jit(solution)/shard_map/ppermute | solution.py:161
  182.5 13.1 %collective-permute-done.17 = bf16[64,2240]{1,0:T(8,128)(2,1)S(1)} collective-permute-done((bf16[64,2240]{1,0:T(8,128)(2,1)S(1)}, bf16[64,2240]{1,0:T(8,128)(2,1)S(1)}, u32[]{:S(2)}, u32[]{:S(2)}) %collective-permute-start.17) | collective-permute-done | bytes 286752 | tf_op jit(solution)/shard_map/ppermute | solution.py:161
  195.6 6.6 %collective-permute-done.16 = bf16[64,2240]{1,0:T(8,128)(2,1)S(1)} collective-permute-done((bf16[64,2240]{1,0:T(8,128)(2,1)S(1)}, bf16[64,2240]{1,0:T(8,128)(2,1)S(1)}, u32[]{:S(2)}, u32[]{:S(2)}) %collective-permute-start.16) | collective-permute-done | bytes 286752 | tf_op jit(solution)/shard_map/ppermute | solution.py:161
  202.2 4.3 %collective-permute-done.14 = bf16[64,2240]{1,0:T(8,128)(2,1)S(1)} collective-permute-done((bf16[64,2240]{1,0:T(8,128)(2,1)S(1)}, bf16[64,2240]{1,0:T(8,128)(2,1)S(1)}, u32[]{:S(2)}, u32[]{:S(2)}) %collective-permute-start.14) | collective-permute-done | bytes 286752 | tf_op jit(solution)/shard_map/ppermute | solution.py:161
  (99 shorter events, 24.4 us)
Async XLA Ops:
  7.2 2.5 %copy-start.4 = (bf16[1,1,64,2240]{3,2,1,0:T(8,128)(2,1)S(1)}, bf16[1,1,64,2240]{3,2,1,0:T(8,128)(2,1)}, u32[]{:S(2)}) copy-start(bf16[1,1,64,2240]{3,2,1,0:T(8,128)(2,1)} %param.11) | copy-start | bytes 860164
  7.2 157.0 %reduce-scatter.2.cloned.1.call-start = ((), (), s32[]{:S(2)}) async-start(), calls=%async_computation.1 | async-start | bytes 4300800 | tf_op jit(solution)/shard_map/reduce_scatter | solution.py:144
  12.7 2.2 %collective-permute-start = (f32[113,1120]{1,0:T(8,128)}, f32[113,1120]{1,0:T(8,128)S(1)}, u32[]{:S(2)}, u32[]{:S(2)}) collective-permute-start(f32[113,1120]{1,0:T(8,128)} %copy.43), channel_id=1, source_target_pairs={{0,4},{4,0},{8,12},{12,8},{1,5},{5,1},{9,13},{13,9},{2,6},{6,2},{1... | collective-permute-start | bytes 1518728 | tf_op jit(solution)/shard_map/ppermute | solution.py:50
  17.2 32.2 %copy-start.6 = (bf16[2240]{0:T(1024)(128)(2,1)S(1)}, bf16[2240]{0:T(1024)(128)(2,1)}, u32[]{:S(2)}) copy-start(bf16[2240]{0:T(1024)(128)(2,1)} %param.14) | copy-start | bytes 13444
  17.3 8.9 %collective-permute-start.1 = (f32[113,560]{0,1:T(8,128)S(1)}, f32[113,560]{0,1:T(8,128)S(1)}, u32[]{:S(2)}, u32[]{:S(2)}) collective-permute-start(f32[113,560]{0,1:T(8,128)S(1)} %slice_select_fusion), channel_id=1, source_target_pairs={{0,8},{4,12},{8,0},{12,4},{1,9},{5,13},{9,1},{13,5},{2,10},{6,14},... | collective-permute-start | bytes 759368 | tf_op jit(solution)/shard_map/ppermute | solution.py:50
  26.3 5.2 %collective-permute-start.2 = (f32[113,280]{0,1:T(8,128)S(1)}, f32[113,280]{0,1:T(8,128)S(1)}, u32[]{:S(2)}, u32[]{:S(2)}) collective-permute-start(f32[113,280]{0,1:T(8,128)S(1)} %slice_select_fusion.1), channel_id=1, source_target_pairs={{0,1},{1,0},{2,3},{3,2},{4,5},{5,4},{6,7},{7,6},{8,9},{9,8},{10,11... | collective-permute-start | bytes 379688 | tf_op jit(solution)/shard_map/ppermute | solution.py:50
  31.5 24.5 %copy-start.3 = (bf16[1,1,64,2240]{3,2,1,0:T(8,128)(2,1)S(1)}, bf16[1,1,64,2240]{3,2,1,0:T(8,128)(2,1)}, u32[]{:S(2)}) copy-start(bf16[1,1,64,2240]{3,2,1,0:T(8,128)(2,1)} %param.9) | copy-start | bytes 860164
  31.5 5.3 %collective-permute-start.3 = (f32[113,140]{0,1:T(8,128)S(1)}, f32[113,140]{0,1:T(8,128)S(1)}, u32[]{:S(2)}, u32[]{:S(2)}) collective-permute-start(f32[113,140]{0,1:T(8,128)S(1)} %slice_select_fusion.2), channel_id=1, source_target_pairs={{0,2},{1,3},{2,0},{3,1},{4,6},{5,7},{6,4},{7,5},{8,10},{9,11},{10,... | collective-permute-start | bytes 189848 | tf_op jit(solution)/shard_map/ppermute | solution.py:50
  36.9 5.4 %collective-permute-start.4 = (f32[113,140]{0,1:T(8,128)S(1)}, f32[113,140]{0,1:T(8,128)S(1)}, u32[]{:S(2)}, u32[]{:S(2)}) collective-permute-start(f32[113,140]{0,1:T(8,128)S(1)} %select_add_fusion.3), channel_id=1, source_target_pairs={{0,2},{1,3},{2,0},{3,1},{4,6},{5,7},{6,4},{7,5},{8,10},{9,11},{10,... | collective-permute-start | bytes 189848 | tf_op jit(solution)/shard_map/ppermute | solution.py:53
  42.3 6.5 %collective-permute-start.5 = (f32[113,280]{0,1:T(8,128)S(1)}, f32[113,280]{0,1:T(8,128)S(1)}, u32[]{:S(2)}, u32[]{:S(2)}) collective-permute-start(f32[113,280]{0,1:T(8,128)S(1)} %maximum_select_fusion.3), channel_id=1, source_target_pairs={{0,1},{1,0},{2,3},{3,2},{4,5},{5,4},{6,7},{7,6},{8,9},{9,8},{10,11... | collective-permute-start | bytes 379688 | tf_op jit(solution)/shard_map/ppermute | solution.py:53
  48.9 7.6 %copy-start.7 = (bf16[2240]{0:T(1024)(128)(2,1)S(1)}, bf16[2240]{0:T(1024)(128)(2,1)}, u32[]{:S(2)}) copy-start(bf16[2240]{0:T(1024)(128)(2,1)} %param.13) | copy-start | bytes 13444
  48.9 6.7 %collective-permute-start.6 = (f32[113,560]{0,1:T(8,128)S(1)}, f32[113,560]{0,1:T(8,128)S(1)}, u32[]{:S(2)}, u32[]{:S(2)}) collective-permute-start(f32[113,560]{0,1:T(8,128)S(1)} %maximum_select_fusion.2), channel_id=1, source_target_pairs={{0,8},{4,12},{8,0},{12,4},{1,9},{5,13},{9,1},{13,5},{2,10},{6,14},... | collective-permute-start | bytes 759368 | tf_op jit(solution)/shard_map/ppermute | solution.py:53
  55.9 2.0 collective-permute-start.7
  61.1 1.0 copy-start.2
  63.5 14.2 %copy-start = (bf16[560,2,840]{2,1,0:T(2,128)(2,1)S(1)}, bf16[560,2,840]{2,1,0:T(2,128)(2,1)}, u32[]{:S(2)}) copy-start(bf16[560,2,840]{2,1,0:T(2,128)(2,1)} %param.15) | copy-start | bytes 5644804
  63.6 7.2 %collective-permute-start.10 = (bf16[1,1,64,560]{3,2,1,0:T(8,128)(2,1)S(1)}, bf16[1,1,64,560]{3,2,1,0:T(8,128)(2,1)S(1)}, u32[]{:S(2)}, u32[]{:S(2)}) collective-permute-start(bf16[1,1,64,560]{3,2,1,0:T(8,128)(2,1)S(1)} %get-tuple-element.27), channel_id=1, source_target_pairs={{0,3},{1,2},{2,1},{3,0},{4,7},{5,6},{6,5},{7,4},{8,11},{9,10},{10,... | collective-permute-start | bytes 215048 | tf_op jit(solution)/shard_map/ppermute | solution.py:71
  67.4 7.5 %collective-permute-start.9 = (bf16[1,1,64,560]{3,2,1,0:T(8,128)(2,1)S(1)}, bf16[1,1,64,560]{3,2,1,0:T(8,128)(2,1)S(1)}, u32[]{:S(2)}, u32[]{:S(2)}) collective-permute-start(bf16[1,1,64,560]{3,2,1,0:T(8,128)(2,1)S(1)} %get-tuple-element.28), channel_id=1, source_target_pairs={{0,2},{1,3},{2,0},{3,1},{4,6},{5,7},{6,4},{7,5},{8,10},{9,11},{10,... | collective-permute-start | bytes 215048 | tf_op jit(solution)/shard_map/ppermute | solution.py:71
  67.4 7.5 %collective-permute-start.8 = (bf16[1,1,64,560]{3,2,1,0:T(8,128)(2,1)S(1)}, bf16[1,1,64,560]{3,2,1,0:T(8,128)(2,1)S(1)}, u32[]{:S(2)}, u32[]{:S(2)}) collective-permute-start(bf16[1,1,64,560]{3,2,1,0:T(8,128)(2,1)S(1)} %get-tuple-element.29), channel_id=1, source_target_pairs={{0,1},{1,0},{2,3},{3,2},{4,5},{5,4},{6,7},{7,6},{8,9},{9,8},{10,11... | collective-permute-start | bytes 215048 | tf_op jit(solution)/shard_map/ppermute | solution.py:71
  75.8 10.2 %collective-permute-start.13 = (bf16[1,4,64,560]{3,2,1,0:T(8,128)(2,1)}, bf16[1,4,64,560]{3,2,1,0:T(8,128)(2,1)S(1)}, u32[]{:S(2)}, u32[]{:S(2)}) collective-permute-start(bf16[1,4,64,560]{3,2,1,0:T(8,128)(2,1)} %get-tuple-element.21), channel_id=1, source_target_pairs={{0,12},{4,8},{8,4},{12,0},{1,13},{5,9},{9,5},{13,1},{2,14},{6,10},... | collective-permute-start | bytes 860168 | tf_op jit(solution)/shard_map/ppermute | solution.py:71
  75.8 16.6 %collective-permute-start.12 = (bf16[1,4,64,560]{3,2,1,0:T(8,128)(2,1)}, bf16[1,4,64,560]{3,2,1,0:T(8,128)(2,1)S(1)}, u32[]{:S(2)}, u32[]{:S(2)}) collective-permute-start(bf16[1,4,64,560]{3,2,1,0:T(8,128)(2,1)} %get-tuple-element.21), channel_id=1, source_target_pairs={{0,8},{4,12},{8,0},{12,4},{1,9},{5,13},{9,1},{13,5},{2,10},{6,14},... | collective-permute-start | bytes 860168 | tf_op jit(solution)/shard_map/ppermute | solution.py:71
  76.9 15.5 %collective-permute-start.11 = (bf16[1,4,64,560]{3,2,1,0:T(8,128)(2,1)}, bf16[1,4,64,560]{3,2,1,0:T(8,128)(2,1)}, u32[]{:S(2)}, u32[]{:S(2)}) collective-permute-start(bf16[1,4,64,560]{3,2,1,0:T(8,128)(2,1)} %get-tuple-element.21), channel_id=1, source_target_pairs={{0,4},{4,0},{8,12},{12,8},{1,5},{5,1},{9,13},{13,9},{2,6},{6,2},{1... | collective-permute-start | bytes 860168 | tf_op jit(solution)/shard_map/ppermute | solution.py:71
  93.8 1.6 copy-start.1
  99.8 0.8 copy-start.5
  166.5 3.1 %copy-start.8 = (bf16[840,2240]{1,0:T(8,128)(2,1)S(1)}, bf16[840,2240]{1,0:T(8,128)(2,1)}, u32[]{:S(2)}) copy-start(bf16[840,2240]{1,0:T(8,128)(2,1)} %param.17) | copy-start | bytes 11289604
  173.0 22.6 %collective-permute-start.17 = (bf16[64,2240]{1,0:T(8,128)(2,1)S(1)}, bf16[64,2240]{1,0:T(8,128)(2,1)S(1)}, u32[]{:S(2)}, u32[]{:S(2)}) collective-permute-start(bf16[64,2240]{1,0:T(8,128)(2,1)S(1)} %bitcast.98), channel_id=1, source_target_pairs={{0,3},{1,7},{2,11},{3,15},{4,2},{5,6},{6,10},{7,14},{8,1},{9,5},{1... | collective-permute-start | bytes 860168 | tf_op jit(solution)/shard_map/ppermute | solution.py:161
  174.5 27.7 %collective-permute-start.16 = (bf16[64,2240]{1,0:T(8,128)(2,1)S(1)}, bf16[64,2240]{1,0:T(8,128)(2,1)S(1)}, u32[]{:S(2)}, u32[]{:S(2)}) collective-permute-start(bf16[64,2240]{1,0:T(8,128)(2,1)S(1)} %bitcast.99), channel_id=1, source_target_pairs={{0,2},{1,6},{2,10},{3,14},{4,3},{5,7},{6,11},{7,15},{8,0},{9,4},{1... | collective-permute-start | bytes 860168 | tf_op jit(solution)/shard_map/ppermute | solution.py:161
  176.4 25.8 %collective-permute-start.15 = (bf16[64,2240]{1,0:T(8,128)(2,1)S(1)}, bf16[64,2240]{1,0:T(8,128)(2,1)S(1)}, u32[]{:S(2)}, u32[]{:S(2)}) collective-permute-start(bf16[64,2240]{1,0:T(8,128)(2,1)S(1)} %bitcast.100), channel_id=1, source_target_pairs={{0,1},{1,5},{2,9},{3,13},{4,0},{5,4},{6,8},{7,12},{8,3},{9,7},{10,... | collective-permute-start | bytes 860168 | tf_op jit(solution)/shard_map/ppermute | solution.py:161
  178.9 27.7 %collective-permute-start.14 = (bf16[64,2240]{1,0:T(8,128)(2,1)S(1)}, bf16[64,2240]{1,0:T(8,128)(2,1)S(1)}, u32[]{:S(2)}, u32[]{:S(2)}) collective-permute-start(bf16[64,2240]{1,0:T(8,128)(2,1)S(1)} %bitcast.101), channel_id=1, source_target_pairs={{0,0},{1,4},{2,8},{3,12},{4,1},{5,5},{6,9},{7,13},{8,2},{9,6},{10,... | collective-permute-start | bytes 860168 | tf_op jit(solution)/shard_map/ppermute | solution.py:161
Sparse Core Ops, SparseCore 0:
  99.9 64.1 reduce-scatter.1

commit v8 on v7

--- a/solution.py
+++ b/solution.py
@@ -39,7 +39,7 @@
     return steps
 
 
-def halving_sum(block, axes):
+def halving_sum(block, axes, inner_axis):
     steps = exchange_steps(axes)
     for axis, count, bit in steps:
         upper = (lax.axis_index(axis) & bit) != 0
@@ -48,6 +48,10 @@
         sent = jnp.where(upper, low, high)
         kept = jnp.where(upper, high, low)
         block = kept + lax.ppermute(sent, axis, [(i, i ^ bit) for i in range(count)])
+    inner_count = lax.axis_size(inner_axis)
+    pieces = jnp.split(block, inner_count, axis=1)
+    mine = sum(swap_chunks(pieces, inner_axis))
+    block = jnp.concatenate(swap_chunks([mine] * inner_count, inner_axis), axis=1)
     for axis, count, bit in reversed(steps):
         upper = (lax.axis_index(axis) & bit) != 0
         other = lax.ppermute(block, axis, [(i, i ^ bit) for i in range(count)])
@@ -70,6 +74,23 @@
         sent = pick(chunks, own ^ mask)
         by_mask.append(lax.ppermute(sent, axis, [(i, i ^ mask) for i in range(count)]))
     return [pick(by_mask, own ^ source) for source in range(count)]
+
+
+def doubling_gather(block, axis):
+    count = lax.axis_size(axis)
+    own = lax.axis_index(axis)
+    by_mask = {0: block}
+    bit = count // 2
+    while bit >= 1:
+        keys = sorted(by_mask)
+        received = lax.ppermute(
+            jnp.stack([by_mask[key] for key in keys]), axis, [(i, i ^ bit) for i in range(count)]
+        )
+        for at, key in enumerate(keys):
+            by_mask[key ^ bit] = received[at]
+        bit //= 2
+    ordered = [by_mask[mask] for mask in range(count)]
+    return [pick(ordered, own ^ source) for source in range(count)]
 
 
 def rms_norm(features):
@@ -107,7 +128,7 @@
         parts *= 2
     padded_width = -(-model_width // parts) * parts
     stats = jnp.pad(stats, ((0, 0), (0, padded_width - model_width)))
-    stats = halving_sum(stats, ("frame", "row"))[:, :model_width]
+    stats = halving_sum(stats, ("frame",), inner_axis="row")[:, :model_width]
     kv_state, key_total = stats[:HEAD_DIM], stats[HEAD_DIM]
     query_pos = jnp.maximum(query_in, 0).reshape(token_count, HEADS, HEAD_DIM).astype(jnp.float32)
     numerator = jnp.einsum(
@@ -133,7 +154,7 @@
     ]
     by_row = jnp.concatenate(swap_chunks(depth_chunks, "row"), axis=1)
     frame_parts = lax.axis_size("frame")
-    by_frame = swap_chunks([by_row] * frame_parts, "frame")
+    by_frame = doubling_gather(by_row, "frame")
     whole_frames = frame_parts == row_parts and frame_count == 1 and row_count == 1
     weight_flat = in_weight.reshape(local_depth, 2 * local_gated)
     if whole_frames:

time: 215 us -> 207 us (0.963)
  waiting for transfers between devices: 137 us -> 129 us
  local copies, waits for them, and re-layouts: 14.2 us -> 17.2 us
  starting transfers between devices: 26.4 us -> 23.5 us
    ppermute x0 -> x2, waiting for transfers between devices: none -> 9.2 us  [doubling_gather(): lax.ppermute(jnp.stack([by_mask[key] for key in keys]), axis, [(i, i ^ bi...]
    ppermute x6 -> x9, starting transfers between devices: 6.31 us -> 13.4 us  [swap_chunks(): lax.ppermute(sent, axis, [(i, i ^ mask) for i in range(count)])]
    ppermute x4 -> x2, waiting for transfers between devices: 17.2 us -> 11 us  [halving_sum(): lax.ppermute(sent, axis, [(i, i ^ bit) for i in range(count)])]
    ppermute x4 -> x2, starting transfers between devices: 6.84 us -> 0.66 us  [halving_sum(): other = lax.ppermute(block, axis, [(i, i ^ bit) for i in range(count)])]
    ppermute x4 -> x2, waiting for transfers between devices: 13.3 us -> 7.56 us  [halving_sum(): other = lax.ppermute(block, axis, [(i, i ^ bit) for i in range(count)])]
    ppermute x6 -> x9, waiting for transfers between devices: 19.1 us -> 14.8 us  [swap_chunks(): lax.ppermute(sent, axis, [(i, i ^ mask) for i in range(count)])]
    ppermute x4 -> x2, starting transfers between devices: 4.37 us -> 0.07 us  [halving_sum(): lax.ppermute(sent, axis, [(i, i ^ bit) for i in range(count)])]
  transfers between devices with their start and end apart: 19 -> 20, of which waited for: 16 -> 16; matrix products, arithmetic and copies ran while one was open for 2% -> 2% of each run, Pallas kernels for 0% -> 0%
where the time goes in v8:
time: 207 us
  waiting for transfers between devices  129 us (62%)
  starting transfers between devices  23.5 us (11%)
  local copies, waits for them, and re-layouts  17.2 us (8%)
  between operations  14.6 us (7%)
  other arithmetic  13.5 us (7%)
  matrix products  8.62 us (4%)
    reduce_scatter x1, waiting for transfers between devices, local(): summed = lax.psum_scatter(partial, 'row', scatter_dimension=0, tiled=True)  63.2 us
    ppermute x4, waiting for transfers between devices, local(): lax.ppermute(pick(row_blocks, frame_at ^ mask), ('frame', 'row'), [(f * r...  23.3 us
    ppermute x9, waiting for transfers between devices, swap_chunks(): lax.ppermute(sent, axis, [(i, i ^ mask) for i in range(count)])  14.8 us
    ppermute x9, starting transfers between devices, swap_chunks(): lax.ppermute(sent, axis, [(i, i ^ mask) for i in range(count)])  13.4 us
    ppermute x2, waiting for transfers between devices, halving_sum(): lax.ppermute(sent, axis, [(i, i ^ bit) for i in range(count)])  11 us
    ppermute x2, waiting for transfers between devices, doubling_gather(): lax.ppermute(jnp.stack([by_mask[key] for key in keys]), axis, [(i, i ^ bi...  9.2 us
    ppermute x4, starting transfers between devices, local(): lax.ppermute(pick(row_blocks, frame_at ^ mask), ('frame', 'row'), [(f * r...  8.81 us
    ppermute x2, waiting for transfers between devices, halving_sum(): other = lax.ppermute(block, axis, [(i, i ^ bit) for i in range(count)])  7.56 us
  transfers between devices with their start and end apart: 20, of which 16 were waited for; matrix products, arithmetic and copies ran while one was open for 2% of the time, Pallas kernels for 0%

profile of v8, /device:TPU:2, one launch (start us, length us, event | category | flops | bytes accessed | tf_op | source)
XLA Modules:
  0.0 206.6 jit_solution(207137703550913443)
XLA Ops:
  12.7 2.2 %collective-permute-done = f32[113,1120]{1,0:T(8,128)S(1)} collective-permute-done((f32[113,1120]{1,0:T(8,128)}, f32[113,1120]{1,0:T(8,128)S(1)}, u32[]{:S(2)}, u32[]{:S(2)}) %collective-permute-start) | collective-permute-done | bytes 506272 | tf_op jit(solution)/shard_map/ppermute | solution.py:50
  15.9 1.3 select_add_fusion
  17.3 8.8 %collective-permute-done.1 = f32[113,560]{0,1:T(8,128)S(1)} collective-permute-done((f32[113,560]{0,1:T(8,128)S(1)}, f32[113,560]{0,1:T(8,128)S(1)}, u32[]{:S(2)}, u32[]{:S(2)}) %collective-permute-start.1) | collective-permute-done | bytes 253152 | tf_op jit(solution)/shard_map/ppermute | solution.py:50
  26.3 3.7 %collective-permute-start.4 = (f32[113,140]{0,1:T(8,128)S(1)}, f32[113,140]{0,1:T(8,128)S(1)}, u32[]{:S(2)}, u32[]{:S(2)}) collective-permute-start(f32[113,140]{0,1:T(8,128)S(1)} %get-tuple-element.39), channel_id=1, source_target_pairs={{0,3},{1,2},{2,1},{3,0},{4,7},{5,6},{6,5},{7,4},{8,11},{9,10},{10,... | collective-permute-start | bytes 189848 | tf_op jit(solution)/shard_map/ppermute | solution.py:75
  30.8 2.4 %collective-permute-done.4 = f32[113,140]{0,1:T(8,128)S(1)} collective-permute-done((f32[113,140]{0,1:T(8,128)S(1)}, f32[113,140]{0,1:T(8,128)S(1)}, u32[]{:S(2)}, u32[]{:S(2)}) %collective-permute-start.4) | collective-permute-done | bytes 63312 | tf_op jit(solution)/shard_map/ppermute | solution.py:75
  33.2 2.6 %collective-permute-done.3 = f32[113,140]{0,1:T(8,128)S(1)} collective-permute-done((f32[113,140]{0,1:T(8,128)S(1)}, f32[113,140]{0,1:T(8,128)S(1)}, u32[]{:S(2)}, u32[]{:S(2)}) %collective-permute-start.3) | collective-permute-done | bytes 63312 | tf_op jit(solution)/shard_map/ppermute | solution.py:75
  35.9 2.7 %collective-permute-start.7 = (f32[113,140]{0,1:T(8,128)S(1)}, f32[113,140]{0,1:T(8,128)S(1)}, u32[]{:S(2)}, u32[]{:S(2)}) collective-permute-start(f32[113,140]{0,1:T(8,128)S(1)} %fusion.29), channel_id=1, source_target_pairs={{0,3},{1,2},{2,1},{3,0},{4,7},{5,6},{6,5},{7,4},{8,11},{9,10},{10,... | collective-permute-start | bytes 189848 | tf_op jit(solution)/shard_map/ppermute | solution.py:75
  38.5 1.8 collective-permute-start.5
  40.3 2.6 %collective-permute-done.7 = f32[113,140]{0,1:T(8,128)S(1)} collective-permute-done((f32[113,140]{0,1:T(8,128)S(1)}, f32[113,140]{0,1:T(8,128)S(1)}, u32[]{:S(2)}, u32[]{:S(2)}) %collective-permute-start.7) | collective-permute-done | bytes 63312 | tf_op jit(solution)/shard_map/ppermute | solution.py:75
  42.9 1.7 collective-permute-done.6
  45.3 6.1 %collective-permute-done.8 = f32[113,560]{0,1:T(8,128)S(1)} collective-permute-done((f32[113,560]{0,1:T(8,128)S(1)}, f32[113,560]{0,1:T(8,128)S(1)}, u32[]{:S(2)}, u32[]{:S(2)}) %collective-permute-start.8) | collective-permute-done | bytes 253152 | tf_op jit(solution)/shard_map/ppermute | solution.py:57
  53.5 1.5 collective-permute-done.9
  56.7 1.4 multiply_reduce_fusion
  60.6 1.9 collective-permute-start.12
  62.9 2.2 %collective-permute-start.10 = (bf16[1,1,64,560]{3,2,1,0:T(8,128)(2,1)S(1)}, bf16[1,1,64,560]{3,2,1,0:T(8,128)(2,1)S(1)}, u32[]{:S(2)}, u32[]{:S(2)}) collective-permute-start(bf16[1,1,64,560]{3,2,1,0:T(8,128)(2,1)S(1)} %get-tuple-element.29), channel_id=1, source_target_pairs={{0,1},{1,0},{2,3},{3,2},{4,5},{5,4},{6,7},{7,6},{8,9},{9,8},{10,11... | collective-permute-start | bytes 215048 | tf_op jit(solution)/shard_map/ppermute | solution.py:75
  65.1 2.8 %collective-permute-done.12 = bf16[1,1,64,560]{3,2,1,0:T(8,128)(2,1)S(1)} collective-permute-done((bf16[1,1,64,560]{3,2,1,0:T(8,128)(2,1)S(1)}, bf16[1,1,64,560]{3,2,1,0:T(8,128)(2,1)S(1)}, u32[]{:S(2)}, u32[]{:S(2)}) %collective-permute-start.12) | collective-permute-done | bytes 71712 | tf_op jit(solution)/shard_map/ppermute | solution.py:75
  67.9 2.7 %collective-permute-done.11 = bf16[1,1,64,560]{3,2,1,0:T(8,128)(2,1)S(1)} collective-permute-done((bf16[1,1,64,560]{3,2,1,0:T(8,128)(2,1)S(1)}, bf16[1,1,64,560]{3,2,1,0:T(8,128)(2,1)S(1)}, u32[]{:S(2)}, u32[]{:S(2)}) %collective-permute-start.11) | collective-permute-done | bytes 71712 | tf_op jit(solution)/shard_map/ppermute | solution.py:75
  71.3 9.2 %collective-permute-done.13 = bf16[1,1,4,64,560]{4,3,2,1,0:T(8,128)(2,1)S(1)} collective-permute-done((bf16[1,1,4,64,560]{4,3,2,1,0:T(8,128)(2,1)S(1)}, bf16[1,1,4,64,560]{4,3,2,1,0:T(8,128)(2,1)S(1)}, u32[]{:S(2)}, u32[]{:S(2)}) %collective-permute-start.13) | collective-permute-done | bytes 286752 | tf_op jit(solution)/shard_map/ppermute | solution.py:86
  81.5 2.5 %reshape.221 = bf16[560,1680]{1,0:T(8,128)(2,1)} reshape(bf16[560,2,840]{2,1,0:T(2,128)(2,1)S(1)} %copy-done) | data formatting | bytes 3763200 | tf_op jit(solution)/shard_map/reshape | solution.py:159
  85.8 1.3 copy-done.1
  87.0 4.5 %convolution_convert_fusion.1 = bf16[1024,1680]{0,1:T(8,128)(2,1)} fusion(bf16[1024,560]{1,0:T(8,128)(2,1)S(1)} %bitcast.121, bf16[560,1680]{1,0:T(8,128)(2,1)S(1)} %copy-done.1), kind=kOutput, calls=%fused_computation.1 | convolution fusion | flops 1928478720 | bytes 6469120 | tf_op jit(solution)/shard_map/dot_general | solution.py:162
  93.0 63.2 %reduce-scatter.2.cloned.1.call-done = bf16[256,1680]{0,1:T(8,128)(2,1)} async-done(((bf16[1024,1680]{0,1:T(8,128)(2,1)}), bf16[256,1680]{0,1:T(8,128)(2,1)}) %reduce-scatter.2.cloned.1.call-update) | async-done | bytes 860176 | tf_op jit(solution)/shard_map/reduce_scatter | solution.py:165
  156.2 1.6 fusion.3
  158.6 3.0 %multiply_add_fusion = f32[1,4,64,1680]{3,2,1,0:T(8,128)S(1)} fusion(bf16[1,4,64,1680]{3,2,1,0:T(8,128)(2,1)S(1)} %bitcast.119, bf16[1,6,64,1680]{3,2,1,0:T(8,128)(2,1)S(1)} %pad.8, f32[1680]{0:T(1024)S(1)} %mul.211, f32[1680]{0:T(1024)S(1)} %mul.208, f32[1680]{0:T(1024)S(1)} %mul.205, f32[1680]{0:T(1024)S(1)} %mul.202, f32[1680]{0:T(1024)S(1)} %mul.199, ...), kind=kLoop, calls=%fused_computation.5 | loop fusion | flops 11182080 | bytes 5922816 | tf_op jit(solution)/shard_map/add | solution.py:108
  161.9 1.8 convolution_convert_fusion
  165.3 1.2 collective-permute-start.18
  166.7 1.7 collective-permute-start.17
  168.7 2.2 %collective-permute-start.16 = (bf16[64,2240]{1,0:T(8,128)(2,1)S(1)}, bf16[64,2240]{1,0:T(8,128)(2,1)S(1)}, u32[]{:S(2)}, u32[]{:S(2)}) collective-permute-start(bf16[64,2240]{1,0:T(8,128)(2,1)S(1)} %bitcast.125), channel_id=1, source_target_pairs={{0,1},{1,5},{2,9},{3,13},{4,0},{5,4},{6,8},{7,12},{8,3},{9,7},{10,... | collective-permute-start | bytes 860168 | tf_op jit(solution)/shard_map/ppermute | solution.py:182
  171.9 3.6 %collective-permute-start.15 = (bf16[64,2240]{1,0:T(8,128)(2,1)}, bf16[64,2240]{1,0:T(8,128)(2,1)S(1)}, u32[]{:S(2)}, u32[]{:S(2)}) collective-permute-start(bf16[64,2240]{1,0:T(8,128)(2,1)} %bitcast.126), channel_id=1, source_target_pairs={{0,0},{1,4},{2,8},{3,12},{4,1},{5,5},{6,9},{7,13},{8,2},{9,6},{10,... | collective-permute-start | bytes 860168 | tf_op jit(solution)/shard_map/ppermute | solution.py:182
  175.5 12.4 %collective-permute-done.18 = bf16[64,2240]{1,0:T(8,128)(2,1)S(1)} collective-permute-done((bf16[64,2240]{1,0:T(8,128)(2,1)S(1)}, bf16[64,2240]{1,0:T(8,128)(2,1)S(1)}, u32[]{:S(2)}, u32[]{:S(2)}) %collective-permute-start.18) | collective-permute-done | bytes 286752 | tf_op jit(solution)/shard_map/ppermute | solution.py:182
  187.9 6.6 %collective-permute-done.17 = bf16[64,2240]{1,0:T(8,128)(2,1)S(1)} collective-permute-done((bf16[64,2240]{1,0:T(8,128)(2,1)S(1)}, bf16[64,2240]{1,0:T(8,128)(2,1)S(1)}, u32[]{:S(2)}, u32[]{:S(2)}) %collective-permute-start.17) | collective-permute-done | bytes 286752 | tf_op jit(solution)/shard_map/ppermute | solution.py:182
  194.5 4.3 %collective-permute-done.15 = bf16[64,2240]{1,0:T(8,128)(2,1)S(1)} collective-permute-done((bf16[64,2240]{1,0:T(8,128)(2,1)}, bf16[64,2240]{1,0:T(8,128)(2,1)S(1)}, u32[]{:S(2)}, u32[]{:S(2)}) %collective-permute-start.15) | collective-permute-done | bytes 286752 | tf_op jit(solution)/shard_map/ppermute | solution.py:182
  (108 shorter events, 24.7 us)
Async XLA Ops:
  7.2 2.5 %copy-start.4 = (bf16[1,1,64,2240]{3,2,1,0:T(8,128)(2,1)S(1)}, bf16[1,1,64,2240]{3,2,1,0:T(8,128)(2,1)}, u32[]{:S(2)}) copy-start(bf16[1,1,64,2240]{3,2,1,0:T(8,128)(2,1)} %param.11) | copy-start | bytes 860164
  7.2 149.1 %reduce-scatter.2.cloned.1.call-start = ((), (), s32[]{:S(2)}) async-start(), calls=%async_computation.1 | async-start | bytes 4300800 | tf_op jit(solution)/shard_map/reduce_scatter | solution.py:165
  12.7 2.2 %collective-permute-start = (f32[113,1120]{1,0:T(8,128)}, f32[113,1120]{1,0:T(8,128)S(1)}, u32[]{:S(2)}, u32[]{:S(2)}) collective-permute-start(f32[113,1120]{1,0:T(8,128)} %copy.43), channel_id=1, source_target_pairs={{0,4},{4,0},{8,12},{12,8},{1,5},{5,1},{9,13},{13,9},{2,6},{6,2},{1... | collective-permute-start | bytes 1518728 | tf_op jit(solution)/shard_map/ppermute | solution.py:50
  17.2 8.9 %collective-permute-start.1 = (f32[113,560]{0,1:T(8,128)S(1)}, f32[113,560]{0,1:T(8,128)S(1)}, u32[]{:S(2)}, u32[]{:S(2)}) collective-permute-start(f32[113,560]{0,1:T(8,128)S(1)} %slice_select_fusion), channel_id=1, source_target_pairs={{0,8},{4,12},{8,0},{12,4},{1,9},{5,13},{9,1},{13,5},{2,10},{6,14},... | collective-permute-start | bytes 759368 | tf_op jit(solution)/shard_map/ppermute | solution.py:50
  26.3 19.1 %copy-start.6 = (bf16[2240]{0:T(1024)(128)(2,1)S(1)}, bf16[2240]{0:T(1024)(128)(2,1)}, u32[]{:S(2)}) copy-start(bf16[2240]{0:T(1024)(128)(2,1)} %param.14) | copy-start | bytes 13444
  26.3 6.9 %collective-permute-start.4 = (f32[113,140]{0,1:T(8,128)S(1)}, f32[113,140]{0,1:T(8,128)S(1)}, u32[]{:S(2)}, u32[]{:S(2)}) collective-permute-start(f32[113,140]{0,1:T(8,128)S(1)} %get-tuple-element.39), channel_id=1, source_target_pairs={{0,3},{1,2},{2,1},{3,0},{4,7},{5,6},{6,5},{7,4},{8,11},{9,10},{10,... | collective-permute-start | bytes 189848 | tf_op jit(solution)/shard_map/ppermute | solution.py:75
  30.0 5.8 %collective-permute-start.3 = (f32[113,140]{0,1:T(8,128)S(1)}, f32[113,140]{0,1:T(8,128)S(1)}, u32[]{:S(2)}, u32[]{:S(2)}) collective-permute-start(f32[113,140]{0,1:T(8,128)S(1)} %get-tuple-element.40), channel_id=1, source_target_pairs={{0,2},{1,3},{2,0},{3,1},{4,6},{5,7},{6,4},{7,5},{8,10},{9,11},{10,... | collective-permute-start | bytes 189848 | tf_op jit(solution)/shard_map/ppermute | solution.py:75
  30.0 5.8 %collective-permute-start.2 = (f32[113,140]{0,1:T(8,128)S(1)}, f32[113,140]{0,1:T(8,128)S(1)}, u32[]{:S(2)}, u32[]{:S(2)}) collective-permute-start(f32[113,140]{0,1:T(8,128)S(1)} %get-tuple-element.41), channel_id=1, source_target_pairs={{0,1},{1,0},{2,3},{3,2},{4,5},{5,4},{6,7},{7,6},{8,9},{9,8},{10,11... | collective-permute-start | bytes 189848 | tf_op jit(solution)/shard_map/ppermute | solution.py:75
  35.9 7.1 %collective-permute-start.7 = (f32[113,140]{0,1:T(8,128)S(1)}, f32[113,140]{0,1:T(8,128)S(1)}, u32[]{:S(2)}, u32[]{:S(2)}) collective-permute-start(f32[113,140]{0,1:T(8,128)S(1)} %fusion.29), channel_id=1, source_target_pairs={{0,3},{1,2},{2,1},{3,0},{4,7},{5,6},{6,5},{7,4},{8,11},{9,10},{10,... | collective-permute-start | bytes 189848 | tf_op jit(solution)/shard_map/ppermute | solution.py:75
  38.5 6.1 %collective-permute-start.6 = (f32[113,140]{0,1:T(8,128)S(1)}, f32[113,140]{0,1:T(8,128)S(1)}, u32[]{:S(2)}, u32[]{:S(2)}) collective-permute-start(f32[113,140]{0,1:T(8,128)S(1)} %fusion.29), channel_id=1, source_target_pairs={{0,2},{1,3},{2,0},{3,1},{4,6},{5,7},{6,4},{7,5},{8,10},{9,11},{10,... | collective-permute-start | bytes 189848 | tf_op jit(solution)/shard_map/ppermute | solution.py:75
  38.5 6.1 %collective-permute-start.5 = (f32[113,140]{0,1:T(8,128)S(1)}, f32[113,140]{0,1:T(8,128)S(1)}, u32[]{:S(2)}, u32[]{:S(2)}) collective-permute-start(f32[113,140]{0,1:T(8,128)S(1)} %fusion.29), channel_id=1, source_target_pairs={{0,1},{1,0},{2,3},{3,2},{4,5},{5,4},{6,7},{7,6},{8,9},{9,8},{10,11... | collective-permute-start | bytes 189848 | tf_op jit(solution)/shard_map/ppermute | solution.py:75
  44.7 6.7 %collective-permute-start.8 = (f32[113,560]{0,1:T(8,128)S(1)}, f32[113,560]{0,1:T(8,128)S(1)}, u32[]{:S(2)}, u32[]{:S(2)}) collective-permute-start(f32[113,560]{0,1:T(8,128)S(1)} %pad_maximum_fusion.10), channel_id=1, source_target_pairs={{0,8},{4,12},{8,0},{12,4},{1,9},{5,13},{9,1},{13,5},{2,10},{6,14},... | collective-permute-start | bytes 759368 | tf_op jit(solution)/shard_map/ppermute | solution.py:57
  52.0 1.0 copy-start.3
  52.6 0.9 copy-start.7
  52.9 2.0 collective-permute-start.9
  58.1 1.0 copy-start.2
  60.5 20.9 %copy-start = (bf16[560,2,840]{2,1,0:T(2,128)(2,1)S(1)}, bf16[560,2,840]{2,1,0:T(2,128)(2,1)}, u32[]{:S(2)}) copy-start(bf16[560,2,840]{2,1,0:T(2,128)(2,1)} %param.15) | copy-start | bytes 5644804
  60.6 7.3 %collective-permute-start.12 = (bf16[1,1,64,560]{3,2,1,0:T(8,128)(2,1)S(1)}, bf16[1,1,64,560]{3,2,1,0:T(8,128)(2,1)S(1)}, u32[]{:S(2)}, u32[]{:S(2)}) collective-permute-start(bf16[1,1,64,560]{3,2,1,0:T(8,128)(2,1)S(1)} %get-tuple-element.27), channel_id=1, source_target_pairs={{0,3},{1,2},{2,1},{3,0},{4,7},{5,6},{6,5},{7,4},{8,11},{9,10},{10,... | collective-permute-start | bytes 215048 | tf_op jit(solution)/shard_map/ppermute | solution.py:75
  62.5 8.0 %collective-permute-start.11 = (bf16[1,1,64,560]{3,2,1,0:T(8,128)(2,1)S(1)}, bf16[1,1,64,560]{3,2,1,0:T(8,128)(2,1)S(1)}, u32[]{:S(2)}, u32[]{:S(2)}) collective-permute-start(bf16[1,1,64,560]{3,2,1,0:T(8,128)(2,1)S(1)} %get-tuple-element.28), channel_id=1, source_target_pairs={{0,2},{1,3},{2,0},{3,1},{4,6},{5,7},{6,4},{7,5},{8,10},{9,11},{10,... | collective-permute-start | bytes 215048 | tf_op jit(solution)/shard_map/ppermute | solution.py:75
  62.9 7.7 %collective-permute-start.10 = (bf16[1,1,64,560]{3,2,1,0:T(8,128)(2,1)S(1)}, bf16[1,1,64,560]{3,2,1,0:T(8,128)(2,1)S(1)}, u32[]{:S(2)}, u32[]{:S(2)}) collective-permute-start(bf16[1,1,64,560]{3,2,1,0:T(8,128)(2,1)S(1)} %get-tuple-element.29), channel_id=1, source_target_pairs={{0,1},{1,0},{2,3},{3,2},{4,5},{5,4},{6,7},{7,6},{8,9},{9,8},{10,11... | collective-permute-start | bytes 215048 | tf_op jit(solution)/shard_map/ppermute | solution.py:75
  70.7 9.8 %collective-permute-start.13 = (bf16[1,1,4,64,560]{4,3,2,1,0:T(8,128)(2,1)S(1)}, bf16[1,1,4,64,560]{4,3,2,1,0:T(8,128)(2,1)S(1)}, u32[]{:S(2)}, u32[]{:S(2)}) collective-permute-start(bf16[1,1,4,64,560]{4,3,2,1,0:T(8,128)(2,1)S(1)} %maximum_bitcast_fusion), channel_id=1, source_target_pairs={{0,8},{4,12},{8,0},{12,4},{1,9},{5,13},{9,1},{13,5},{2,10},{6,14},... | collective-permute-start | bytes 860168 | tf_op jit(solution)/shard_map/ppermute | solution.py:86
  81.5 2.5 %collective-permute-start.14 = (bf16[2,1,4,64,560]{4,3,2,1,0:T(8,128)(2,1)}, bf16[2,1,4,64,560]{4,3,2,1,0:T(8,128)(2,1)}, u32[]{:S(2)}, u32[]{:S(2)}) collective-permute-start(bf16[2,1,4,64,560]{4,3,2,1,0:T(8,128)(2,1)} %pad_maximum_fusion.3), channel_id=1, source_target_pairs={{0,4},{4,0},{8,12},{12,8},{1,5},{5,1},{9,13},{13,9},{2,6},{6,2},{1... | collective-permute-start | bytes 1720328 | tf_op jit(solution)/shard_map/ppermute | solution.py:86
  85.5 1.6 copy-start.1
  91.5 0.8 copy-start.5
  158.6 3.3 %copy-start.8 = (bf16[840,2240]{1,0:T(8,128)(2,1)S(1)}, bf16[840,2240]{1,0:T(8,128)(2,1)}, u32[]{:S(2)}) copy-start(bf16[840,2240]{1,0:T(8,128)(2,1)} %param.17) | copy-start | bytes 11289604
  165.3 22.6 %collective-permute-start.18 = (bf16[64,2240]{1,0:T(8,128)(2,1)S(1)}, bf16[64,2240]{1,0:T(8,128)(2,1)S(1)}, u32[]{:S(2)}, u32[]{:S(2)}) collective-permute-start(bf16[64,2240]{1,0:T(8,128)(2,1)S(1)} %bitcast.123), channel_id=1, source_target_pairs={{0,3},{1,7},{2,11},{3,15},{4,2},{5,6},{6,10},{7,14},{8,1},{9,5},{1... | collective-permute-start | bytes 860168 | tf_op jit(solution)/shard_map/ppermute | solution.py:182
  166.7 27.8 %collective-permute-start.17 = (bf16[64,2240]{1,0:T(8,128)(2,1)S(1)}, bf16[64,2240]{1,0:T(8,128)(2,1)S(1)}, u32[]{:S(2)}, u32[]{:S(2)}) collective-permute-start(bf16[64,2240]{1,0:T(8,128)(2,1)S(1)} %bitcast.124), channel_id=1, source_target_pairs={{0,2},{1,6},{2,10},{3,14},{4,3},{5,7},{6,11},{7,15},{8,0},{9,4},{1... | collective-permute-start | bytes 860168 | tf_op jit(solution)/shard_map/ppermute | solution.py:182
  168.7 25.8 %collective-permute-start.16 = (bf16[64,2240]{1,0:T(8,128)(2,1)S(1)}, bf16[64,2240]{1,0:T(8,128)(2,1)S(1)}, u32[]{:S(2)}, u32[]{:S(2)}) collective-permute-start(bf16[64,2240]{1,0:T(8,128)(2,1)S(1)} %bitcast.125), channel_id=1, source_target_pairs={{0,1},{1,5},{2,9},{3,13},{4,0},{5,4},{6,8},{7,12},{8,3},{9,7},{10,... | collective-permute-start | bytes 860168 | tf_op jit(solution)/shard_map/ppermute | solution.py:182
  171.9 27.0 %collective-permute-start.15 = (bf16[64,2240]{1,0:T(8,128)(2,1)}, bf16[64,2240]{1,0:T(8,128)(2,1)S(1)}, u32[]{:S(2)}, u32[]{:S(2)}) collective-permute-start(bf16[64,2240]{1,0:T(8,128)(2,1)} %bitcast.126), channel_id=1, source_target_pairs={{0,0},{1,4},{2,8},{3,12},{4,1},{5,5},{6,9},{7,13},{8,2},{9,6},{10,... | collective-permute-start | bytes 860168 | tf_op jit(solution)/shard_map/ppermute | solution.py:182
Sparse Core Ops, SparseCore 0:
  91.7 64.5 reduce-scatter.1

commit v9 on v8

--- a/solution.py
+++ b/solution.py
@@ -47,10 +47,13 @@
         low, high = block[:, :half], block[:, half:]
         sent = jnp.where(upper, low, high)
         kept = jnp.where(upper, high, low)
-        block = kept + lax.ppermute(sent, axis, [(i, i ^ bit) for i in range(count)])
+        sent = sent.astype(jnp.bfloat16)
+        block = kept + lax.ppermute(sent, axis, [(i, i ^ bit) for i in range(count)]).astype(
+            jnp.float32
+        )
     inner_count = lax.axis_size(inner_axis)
-    pieces = jnp.split(block, inner_count, axis=1)
-    mine = sum(swap_chunks(pieces, inner_axis))
+    pieces = [piece.astype(jnp.bfloat16) for piece in jnp.split(block, inner_count, axis=1)]
+    mine = sum(piece.astype(jnp.float32) for piece in swap_chunks(pieces, inner_axis))
     block = jnp.concatenate(swap_chunks([mine] * inner_count, inner_axis), axis=1)
     for axis, count, bit in reversed(steps):
         upper = (lax.axis_index(axis) & bit) != 0

time: 207 us -> 200 us (0.966)
  waiting for transfers between devices: 129 us -> 124 us
  local copies, waits for them, and re-layouts: 17.2 us -> 15.1 us
    ppermute x2, waiting for transfers between devices: 11 us -> 7.45 us  [halving_sum(): lax.ppermute(sent, axis, [(i, i ^ bit) for i in range(count)])]
  transfers between devices with their start and end apart: 20 -> 20, of which waited for: 16 -> 15; matrix products, arithmetic and copies ran while one was open for 2% -> 3% of each run, Pallas kernels for 0% -> 0%
where the time goes in v9:
time: 200 us; the launch traced here: 199 us
  waiting for transfers between devices  124 us (62%)
  starting transfers between devices  23.6 us (12%)
  local copies, waits for them, and re-layouts  15.1 us (8%)
  between operations  14.6 us (7%)
  other arithmetic  13.4 us (7%)
  matrix products  8.62 us (4%)
    reduce_scatter x1, waiting for transfers between devices, local(): summed = lax.psum_scatter(partial, 'row', scatter_dimension=0, tiled=True)  63.3 us
    ppermute x4, waiting for transfers between devices, local(): lax.ppermute(pick(row_blocks, frame_at ^ mask), ('frame', 'row'), [(f * r...  23.3 us
    ppermute x9, starting transfers between devices, swap_chunks(): lax.ppermute(sent, axis, [(i, i ^ mask) for i in range(count)])  13.4 us
    ppermute x9, waiting for transfers between devices, swap_chunks(): lax.ppermute(sent, axis, [(i, i ^ mask) for i in range(count)])  13.2 us
    ppermute x2, waiting for transfers between devices, doubling_gather(): lax.ppermute(jnp.stack([by_mask[key] for key in keys]), axis, [(i, i ^ bi...  9.03 us
    ppermute x4, starting transfers between devices, local(): lax.ppermute(pick(row_blocks, frame_at ^ mask), ('frame', 'row'), [(f * r...  8.8 us
    ppermute x2, waiting for transfers between devices, halving_sum(): other = lax.ppermute(block, axis, [(i, i ^ bit) for i in range(count)])  7.56 us
    ppermute x2, waiting for transfers between devices, halving_sum(): lax.ppermute(sent, axis, [(i, i ^ bit) for i in range(count)])  7.45 us
  transfers between devices with their start and end apart: 20, of which 15 were waited for; matrix products, arithmetic and copies ran while one was open for 3% of the time, Pallas kernels for 0%

profile of v9, /device:TPU:2, one launch (start us, length us, event | category | flops | bytes accessed | tf_op | source)
XLA Modules:
  0.0 199.2 jit_solution(5853056951102509159)
XLA Ops:
  11.6 1.7 collective-permute-done
  13.3 1.2 convert_add_fusion.2
  14.6 5.8 %collective-permute-done.1 = bf16[113,560]{0,1:T(8,128)(2,1)S(1)} collective-permute-done((bf16[113,560]{0,1:T(8,128)(2,1)S(1)}, bf16[113,560]{0,1:T(8,128)(2,1)S(1)}, u32[]{:S(2)}, u32[]{:S(2)}) %collective-permute-start.1) | collective-permute-done | bytes 126592 | tf_op jit(solution)/shard_map/ppermute | solution.py:51
  20.6 3.7 %collective-permute-start.4 = (bf16[113,140]{0,1:T(8,128)(2,1)S(1)}, bf16[113,140]{0,1:T(8,128)(2,1)S(1)}, u32[]{:S(2)}, u32[]{:S(2)}) collective-permute-start(bf16[113,140]{0,1:T(8,128)(2,1)S(1)} %get-tuple-element.39), channel_id=1, source_target_pairs={{0,3},{1,2},{2,1},{3,0},{4,7},{5,6},{6,5},{7,4},{8,11},{9,10},{10,... | collective-permute-start | bytes 94928 | tf_op jit(solution)/shard_map/ppermute | solution.py:78
  25.0 1.6 collective-permute-done.4
  26.6 2.5 %collective-permute-done.3 = bf16[113,140]{0,1:T(8,128)(2,1)S(1)} collective-permute-done((bf16[113,140]{0,1:T(8,128)(2,1)S(1)}, bf16[113,140]{0,1:T(8,128)(2,1)S(1)}, u32[]{:S(2)}, u32[]{:S(2)}) %collective-permute-start.3) | collective-permute-done | bytes 31672 | tf_op jit(solution)/shard_map/ppermute | solution.py:78
  29.2 1.5 collective-permute-start.7
  31.3 2.3 %collective-permute-start.5 = (f32[113,140]{0,1:T(8,128)S(1)}, f32[113,140]{0,1:T(8,128)S(1)}, u32[]{:S(2)}, u32[]{:S(2)}) collective-permute-start(f32[113,140]{0,1:T(8,128)S(1)} %fusion.29), channel_id=1, source_target_pairs={{0,1},{1,0},{2,3},{3,2},{4,5},{5,4},{6,7},{7,6},{8,9},{9,8},{10,11... | collective-permute-start | bytes 189848 | tf_op jit(solution)/shard_map/ppermute | solution.py:78
  33.6 1.9 collective-permute-done.7
  35.5 1.5 collective-permute-done.6
  37.8 6.1 %collective-permute-done.8 = f32[113,560]{0,1:T(8,128)S(1)} collective-permute-done((f32[113,560]{0,1:T(8,128)S(1)}, f32[113,560]{0,1:T(8,128)S(1)}, u32[]{:S(2)}, u32[]{:S(2)}) %collective-permute-start.8) | collective-permute-done | bytes 253152 | tf_op jit(solution)/shard_map/ppermute | solution.py:60
  45.9 1.5 collective-permute-done.9
  49.1 1.4 multiply_reduce_fusion
  53.0 2.4 %collective-permute-start.12 = (bf16[1,1,64,560]{3,2,1,0:T(8,128)(2,1)S(1)}, bf16[1,1,64,560]{3,2,1,0:T(8,128)(2,1)S(1)}, u32[]{:S(2)}, u32[]{:S(2)}) collective-permute-start(bf16[1,1,64,560]{3,2,1,0:T(8,128)(2,1)S(1)} %get-tuple-element.27), channel_id=1, source_target_pairs={{0,3},{1,2},{2,1},{3,0},{4,7},{5,6},{6,5},{7,4},{8,11},{9,10},{10,... | collective-permute-start | bytes 215048 | tf_op jit(solution)/shard_map/ppermute | solution.py:78
  55.5 2.0 collective-permute-start.10
  57.5 2.8 %collective-permute-done.12 = bf16[1,1,64,560]{3,2,1,0:T(8,128)(2,1)S(1)} collective-permute-done((bf16[1,1,64,560]{3,2,1,0:T(8,128)(2,1)S(1)}, bf16[1,1,64,560]{3,2,1,0:T(8,128)(2,1)S(1)}, u32[]{:S(2)}, u32[]{:S(2)}) %collective-permute-start.12) | collective-permute-done | bytes 71712 | tf_op jit(solution)/shard_map/ppermute | solution.py:78
  60.3 2.9 %collective-permute-done.11 = bf16[1,1,64,560]{3,2,1,0:T(8,128)(2,1)S(1)} collective-permute-done((bf16[1,1,64,560]{3,2,1,0:T(8,128)(2,1)S(1)}, bf16[1,1,64,560]{3,2,1,0:T(8,128)(2,1)S(1)}, u32[]{:S(2)}, u32[]{:S(2)}) %collective-permute-start.11) | collective-permute-done | bytes 71712 | tf_op jit(solution)/shard_map/ppermute | solution.py:78
  64.0 9.0 %collective-permute-done.13 = bf16[1,1,4,64,560]{4,3,2,1,0:T(8,128)(2,1)S(1)} collective-permute-done((bf16[1,1,4,64,560]{4,3,2,1,0:T(8,128)(2,1)S(1)}, bf16[1,1,4,64,560]{4,3,2,1,0:T(8,128)(2,1)S(1)}, u32[]{:S(2)}, u32[]{:S(2)}) %collective-permute-start.13) | collective-permute-done | bytes 286752 | tf_op jit(solution)/shard_map/ppermute | solution.py:89
  74.0 2.5 %reshape.225 = bf16[560,1680]{1,0:T(8,128)(2,1)} reshape(bf16[560,2,840]{2,1,0:T(2,128)(2,1)S(1)} %copy-done) | data formatting | bytes 3763200 | tf_op jit(solution)/shard_map/reshape | solution.py:162
  78.3 1.3 copy-done.1
  79.6 4.5 %convolution_convert_fusion.1 = bf16[1024,1680]{0,1:T(8,128)(2,1)} fusion(bf16[1024,560]{1,0:T(8,128)(2,1)S(1)} %bitcast.121, bf16[560,1680]{1,0:T(8,128)(2,1)S(1)} %copy-done.1), kind=kOutput, calls=%fused_computation.1 | convolution fusion | flops 1928478720 | bytes 6469120 | tf_op jit(solution)/shard_map/dot_general | solution.py:165
  85.5 63.3 %reduce-scatter.2.cloned.1.call-done = bf16[256,1680]{0,1:T(8,128)(2,1)} async-done(((bf16[1024,1680]{0,1:T(8,128)(2,1)}), bf16[256,1680]{0,1:T(8,128)(2,1)}) %reduce-scatter.2.cloned.1.call-update) | async-done | bytes 860176 | tf_op jit(solution)/shard_map/reduce_scatter | solution.py:168
  148.9 1.6 fusion.3
  151.2 3.0 %multiply_add_fusion = f32[1,4,64,1680]{3,2,1,0:T(8,128)S(1)} fusion(bf16[1,4,64,1680]{3,2,1,0:T(8,128)(2,1)S(1)} %bitcast.119, bf16[1,6,64,1680]{3,2,1,0:T(8,128)(2,1)S(1)} %pad.8, f32[1680]{0:T(1024)S(1)} %mul.211, f32[1680]{0:T(1024)S(1)} %mul.208, f32[1680]{0:T(1024)S(1)} %mul.205, f32[1680]{0:T(1024)S(1)} %mul.202, f32[1680]{0:T(1024)S(1)} %mul.199, ...), kind=kLoop, calls=%fused_computation.5 | loop fusion | flops 11182080 | bytes 5922816 | tf_op jit(solution)/shard_map/add | solution.py:111
  154.6 1.8 convolution_convert_fusion
  157.9 1.2 collective-permute-start.18
  159.4 1.7 collective-permute-start.17
  161.3 2.2 %collective-permute-start.16 = (bf16[64,2240]{1,0:T(8,128)(2,1)S(1)}, bf16[64,2240]{1,0:T(8,128)(2,1)S(1)}, u32[]{:S(2)}, u32[]{:S(2)}) collective-permute-start(bf16[64,2240]{1,0:T(8,128)(2,1)S(1)} %bitcast.125), channel_id=1, source_target_pairs={{0,1},{1,5},{2,9},{3,13},{4,0},{5,4},{6,8},{7,12},{8,3},{9,7},{10,... | collective-permute-start | bytes 860168 | tf_op jit(solution)/shard_map/ppermute | solution.py:185
  164.5 3.6 %collective-permute-start.15 = (bf16[64,2240]{1,0:T(8,128)(2,1)}, bf16[64,2240]{1,0:T(8,128)(2,1)S(1)}, u32[]{:S(2)}, u32[]{:S(2)}) collective-permute-start(bf16[64,2240]{1,0:T(8,128)(2,1)} %bitcast.126), channel_id=1, source_target_pairs={{0,0},{1,4},{2,8},{3,12},{4,1},{5,5},{6,9},{7,13},{8,2},{9,6},{10,... | collective-permute-start | bytes 860168 | tf_op jit(solution)/shard_map/ppermute | solution.py:185
  168.1 12.4 %collective-permute-done.18 = bf16[64,2240]{1,0:T(8,128)(2,1)S(1)} collective-permute-done((bf16[64,2240]{1,0:T(8,128)(2,1)S(1)}, bf16[64,2240]{1,0:T(8,128)(2,1)S(1)}, u32[]{:S(2)}, u32[]{:S(2)}) %collective-permute-start.18) | collective-permute-done | bytes 286752 | tf_op jit(solution)/shard_map/ppermute | solution.py:185
  180.5 6.6 %collective-permute-done.17 = bf16[64,2240]{1,0:T(8,128)(2,1)S(1)} collective-permute-done((bf16[64,2240]{1,0:T(8,128)(2,1)S(1)}, bf16[64,2240]{1,0:T(8,128)(2,1)S(1)}, u32[]{:S(2)}, u32[]{:S(2)}) %collective-permute-start.17) | collective-permute-done | bytes 286752 | tf_op jit(solution)/shard_map/ppermute | solution.py:185
  187.1 4.3 %collective-permute-done.15 = bf16[64,2240]{1,0:T(8,128)(2,1)S(1)} collective-permute-done((bf16[64,2240]{1,0:T(8,128)(2,1)}, bf16[64,2240]{1,0:T(8,128)(2,1)S(1)}, u32[]{:S(2)}, u32[]{:S(2)}) %collective-permute-start.15) | collective-permute-done | bytes 286752 | tf_op jit(solution)/shard_map/ppermute | solution.py:185
  (106 shorter events, 23.0 us)
Async XLA Ops:
  7.2 2.5 %copy-start.4 = (bf16[1,1,64,2240]{3,2,1,0:T(8,128)(2,1)S(1)}, bf16[1,1,64,2240]{3,2,1,0:T(8,128)(2,1)}, u32[]{:S(2)}) copy-start(bf16[1,1,64,2240]{3,2,1,0:T(8,128)(2,1)} %param.11) | copy-start | bytes 860164
  7.2 141.7 %reduce-scatter.2.cloned.1.call-start = ((), (), s32[]{:S(2)}) async-start(), calls=%async_computation.1 | async-start | bytes 4300800 | tf_op jit(solution)/shard_map/reduce_scatter | solution.py:168
  11.5 1.8 collective-permute-start
  14.5 5.9 %collective-permute-start.1 = (bf16[113,560]{0,1:T(8,128)(2,1)S(1)}, bf16[113,560]{0,1:T(8,128)(2,1)S(1)}, u32[]{:S(2)}, u32[]{:S(2)}) collective-permute-start(bf16[113,560]{0,1:T(8,128)(2,1)S(1)} %select_convert_fusion.1), channel_id=1, source_target_pairs={{0,8},{4,12},{8,0},{12,4},{1,9},{5,13},{9,1},{13,5},{2,10},{6,14},... | collective-permute-start | bytes 379688 | tf_op jit(solution)/shard_map/ppermute | solution.py:51
  20.4 17.3 %copy-start.6 = (bf16[2240]{0:T(1024)(128)(2,1)S(1)}, bf16[2240]{0:T(1024)(128)(2,1)}, u32[]{:S(2)}) copy-start(bf16[2240]{0:T(1024)(128)(2,1)} %param.14) | copy-start | bytes 13444
  20.6 6.1 %collective-permute-start.4 = (bf16[113,140]{0,1:T(8,128)(2,1)S(1)}, bf16[113,140]{0,1:T(8,128)(2,1)S(1)}, u32[]{:S(2)}, u32[]{:S(2)}) collective-permute-start(bf16[113,140]{0,1:T(8,128)(2,1)S(1)} %get-tuple-element.39), channel_id=1, source_target_pairs={{0,3},{1,2},{2,1},{3,0},{4,7},{5,6},{6,5},{7,4},{8,11},{9,10},{10,... | collective-permute-start | bytes 94928 | tf_op jit(solution)/shard_map/ppermute | solution.py:78
  24.2 4.9 %collective-permute-start.3 = (bf16[113,140]{0,1:T(8,128)(2,1)S(1)}, bf16[113,140]{0,1:T(8,128)(2,1)S(1)}, u32[]{:S(2)}, u32[]{:S(2)}) collective-permute-start(bf16[113,140]{0,1:T(8,128)(2,1)S(1)} %get-tuple-element.40), channel_id=1, source_target_pairs={{0,2},{1,3},{2,0},{3,1},{4,6},{5,7},{6,4},{7,5},{8,10},{9,11},{10,... | collective-permute-start | bytes 94928 | tf_op jit(solution)/shard_map/ppermute | solution.py:78
  24.2 4.9 %collective-permute-start.2 = (bf16[113,140]{0,1:T(8,128)(2,1)S(1)}, bf16[113,140]{0,1:T(8,128)(2,1)S(1)}, u32[]{:S(2)}, u32[]{:S(2)}) collective-permute-start(bf16[113,140]{0,1:T(8,128)(2,1)S(1)} %get-tuple-element.41), channel_id=1, source_target_pairs={{0,1},{1,0},{2,3},{3,2},{4,5},{5,4},{6,7},{7,6},{8,9},{9,8},{10,11... | collective-permute-start | bytes 94928 | tf_op jit(solution)/shard_map/ppermute | solution.py:78
  29.2 6.4 %collective-permute-start.7 = (f32[113,140]{0,1:T(8,128)S(1)}, f32[113,140]{0,1:T(8,128)S(1)}, u32[]{:S(2)}, u32[]{:S(2)}) collective-permute-start(f32[113,140]{0,1:T(8,128)S(1)} %fusion.29), channel_id=1, source_target_pairs={{0,3},{1,2},{2,1},{3,0},{4,7},{5,6},{6,5},{7,4},{8,11},{9,10},{10,... | collective-permute-start | bytes 189848 | tf_op jit(solution)/shard_map/ppermute | solution.py:78
  30.7 6.3 %collective-permute-start.6 = (f32[113,140]{0,1:T(8,128)S(1)}, f32[113,140]{0,1:T(8,128)S(1)}, u32[]{:S(2)}, u32[]{:S(2)}) collective-permute-start(f32[113,140]{0,1:T(8,128)S(1)} %fusion.29), channel_id=1, source_target_pairs={{0,2},{1,3},{2,0},{3,1},{4,6},{5,7},{6,4},{7,5},{8,10},{9,11},{10,... | collective-permute-start | bytes 189848 | tf_op jit(solution)/shard_map/ppermute | solution.py:78
  31.3 5.7 %collective-permute-start.5 = (f32[113,140]{0,1:T(8,128)S(1)}, f32[113,140]{0,1:T(8,128)S(1)}, u32[]{:S(2)}, u32[]{:S(2)}) collective-permute-start(f32[113,140]{0,1:T(8,128)S(1)} %fusion.29), channel_id=1, source_target_pairs={{0,1},{1,0},{2,3},{3,2},{4,5},{5,4},{6,7},{7,6},{8,9},{9,8},{10,11... | collective-permute-start | bytes 189848 | tf_op jit(solution)/shard_map/ppermute | solution.py:78
  37.1 6.7 %collective-permute-start.8 = (f32[113,560]{0,1:T(8,128)S(1)}, f32[113,560]{0,1:T(8,128)S(1)}, u32[]{:S(2)}, u32[]{:S(2)}) collective-permute-start(f32[113,560]{0,1:T(8,128)S(1)} %pad_maximum_fusion.8), channel_id=1, source_target_pairs={{0,8},{4,12},{8,0},{12,4},{1,9},{5,13},{9,1},{13,5},{2,10},{6,14},... | collective-permute-start | bytes 759368 | tf_op jit(solution)/shard_map/ppermute | solution.py:60
  44.5 1.0 copy-start.3
  45.0 0.9 copy-start.7
  45.4 2.0 %collective-permute-start.9 = (f32[113,1120]{1,0:T(8,128)S(1)}, f32[113,1120]{1,0:T(8,128)S(1)}, u32[]{:S(2)}, u32[]{:S(2)}) collective-permute-start(f32[113,1120]{1,0:T(8,128)S(1)} %copy.43), channel_id=1, source_target_pairs={{0,4},{4,0},{8,12},{12,8},{1,5},{5,1},{9,13},{13,9},{2,6},{6,2},{1... | collective-permute-start | bytes 1518728 | tf_op jit(solution)/shard_map/ppermute | solution.py:60
  50.6 1.0 copy-start.2
  53.0 21.0 %copy-start = (bf16[560,2,840]{2,1,0:T(2,128)(2,1)S(1)}, bf16[560,2,840]{2,1,0:T(2,128)(2,1)}, u32[]{:S(2)}) copy-start(bf16[560,2,840]{2,1,0:T(2,128)(2,1)} %param.15) | copy-start | bytes 5644804
  53.0 7.3 %collective-permute-start.12 = (bf16[1,1,64,560]{3,2,1,0:T(8,128)(2,1)S(1)}, bf16[1,1,64,560]{3,2,1,0:T(8,128)(2,1)S(1)}, u32[]{:S(2)}, u32[]{:S(2)}) collective-permute-start(bf16[1,1,64,560]{3,2,1,0:T(8,128)(2,1)S(1)} %get-tuple-element.27), channel_id=1, source_target_pairs={{0,3},{1,2},{2,1},{3,0},{4,7},{5,6},{6,5},{7,4},{8,11},{9,10},{10,... | collective-permute-start | bytes 215048 | tf_op jit(solution)/shard_map/ppermute | solution.py:78
  55.4 7.8 %collective-permute-start.11 = (bf16[1,1,64,560]{3,2,1,0:T(8,128)(2,1)S(1)}, bf16[1,1,64,560]{3,2,1,0:T(8,128)(2,1)S(1)}, u32[]{:S(2)}, u32[]{:S(2)}) collective-permute-start(bf16[1,1,64,560]{3,2,1,0:T(8,128)(2,1)S(1)} %get-tuple-element.28), channel_id=1, source_target_pairs={{0,2},{1,3},{2,0},{3,1},{4,6},{5,7},{6,4},{7,5},{8,10},{9,11},{10,... | collective-permute-start | bytes 215048 | tf_op jit(solution)/shard_map/ppermute | solution.py:78
  55.5 7.7 %collective-permute-start.10 = (bf16[1,1,64,560]{3,2,1,0:T(8,128)(2,1)S(1)}, bf16[1,1,64,560]{3,2,1,0:T(8,128)(2,1)S(1)}, u32[]{:S(2)}, u32[]{:S(2)}) collective-permute-start(bf16[1,1,64,560]{3,2,1,0:T(8,128)(2,1)S(1)} %get-tuple-element.29), channel_id=1, source_target_pairs={{0,1},{1,0},{2,3},{3,2},{4,5},{5,4},{6,7},{7,6},{8,9},{9,8},{10,11... | collective-permute-start | bytes 215048 | tf_op jit(solution)/shard_map/ppermute | solution.py:78
  63.4 9.6 %collective-permute-start.13 = (bf16[1,1,4,64,560]{4,3,2,1,0:T(8,128)(2,1)S(1)}, bf16[1,1,4,64,560]{4,3,2,1,0:T(8,128)(2,1)S(1)}, u32[]{:S(2)}, u32[]{:S(2)}) collective-permute-start(bf16[1,1,4,64,560]{4,3,2,1,0:T(8,128)(2,1)S(1)} %maximum_bitcast_fusion), channel_id=1, source_target_pairs={{0,8},{4,12},{8,0},{12,4},{1,9},{5,13},{9,1},{13,5},{2,10},{6,14},... | collective-permute-start | bytes 860168 | tf_op jit(solution)/shard_map/ppermute | solution.py:89
  74.0 2.5 %collective-permute-start.14 = (bf16[2,1,4,64,560]{4,3,2,1,0:T(8,128)(2,1)}, bf16[2,1,4,64,560]{4,3,2,1,0:T(8,128)(2,1)}, u32[]{:S(2)}, u32[]{:S(2)}) collective-permute-start(bf16[2,1,4,64,560]{4,3,2,1,0:T(8,128)(2,1)} %pad_maximum_fusion.3), channel_id=1, source_target_pairs={{0,4},{4,0},{8,12},{12,8},{1,5},{5,1},{9,13},{13,9},{2,6},{6,2},{1... | collective-permute-start | bytes 1720328 | tf_op jit(solution)/shard_map/ppermute | solution.py:89
  78.0 1.6 copy-start.1
  84.0 0.8 copy-start.5
  151.2 3.3 %copy-start.8 = (bf16[840,2240]{1,0:T(8,128)(2,1)S(1)}, bf16[840,2240]{1,0:T(8,128)(2,1)}, u32[]{:S(2)}) copy-start(bf16[840,2240]{1,0:T(8,128)(2,1)} %param.17) | copy-start | bytes 11289604
  157.9 22.6 %collective-permute-start.18 = (bf16[64,2240]{1,0:T(8,128)(2,1)S(1)}, bf16[64,2240]{1,0:T(8,128)(2,1)S(1)}, u32[]{:S(2)}, u32[]{:S(2)}) collective-permute-start(bf16[64,2240]{1,0:T(8,128)(2,1)S(1)} %bitcast.123), channel_id=1, source_target_pairs={{0,3},{1,7},{2,11},{3,15},{4,2},{5,6},{6,10},{7,14},{8,1},{9,5},{1... | collective-permute-start | bytes 860168 | tf_op jit(solution)/shard_map/ppermute | solution.py:185
  159.4 27.8 %collective-permute-start.17 = (bf16[64,2240]{1,0:T(8,128)(2,1)S(1)}, bf16[64,2240]{1,0:T(8,128)(2,1)S(1)}, u32[]{:S(2)}, u32[]{:S(2)}) collective-permute-start(bf16[64,2240]{1,0:T(8,128)(2,1)S(1)} %bitcast.124), channel_id=1, source_target_pairs={{0,2},{1,6},{2,10},{3,14},{4,3},{5,7},{6,11},{7,15},{8,0},{9,4},{1... | collective-permute-start | bytes 860168 | tf_op jit(solution)/shard_map/ppermute | solution.py:185
  161.3 25.8 %collective-permute-start.16 = (bf16[64,2240]{1,0:T(8,128)(2,1)S(1)}, bf16[64,2240]{1,0:T(8,128)(2,1)S(1)}, u32[]{:S(2)}, u32[]{:S(2)}) collective-permute-start(bf16[64,2240]{1,0:T(8,128)(2,1)S(1)} %bitcast.125), channel_id=1, source_target_pairs={{0,1},{1,5},{2,9},{3,13},{4,0},{5,4},{6,8},{7,12},{8,3},{9,7},{10,... | collective-permute-start | bytes 860168 | tf_op jit(solution)/shard_map/ppermute | solution.py:185
  164.5 27.0 %collective-permute-start.15 = (bf16[64,2240]{1,0:T(8,128)(2,1)}, bf16[64,2240]{1,0:T(8,128)(2,1)S(1)}, u32[]{:S(2)}, u32[]{:S(2)}) collective-permute-start(bf16[64,2240]{1,0:T(8,128)(2,1)} %bitcast.126), channel_id=1, source_target_pairs={{0,0},{1,4},{2,8},{3,12},{4,1},{5,5},{6,9},{7,13},{8,2},{9,6},{10,... | collective-permute-start | bytes 860168 | tf_op jit(solution)/shard_map/ppermute | solution.py:185
Sparse Core Ops, SparseCore 0:
  84.2 64.6 reduce-scatter.1

commit v10 on v9

--- a/solution.py
+++ b/solution.py
@@ -39,9 +39,9 @@
     return steps
 
 
-def halving_sum(block, axes, inner_axis):
+def halving_sum(block, axes, inner_axis, rider):
     steps = exchange_steps(axes)
-    for axis, count, bit in steps:
+    for at, (axis, count, bit) in enumerate(steps):
         upper = (lax.axis_index(axis) & bit) != 0
         half = block.shape[1] // 2
         low, high = block[:, :half], block[:, half:]
@@ -51,6 +51,8 @@
         block = kept + lax.ppermute(sent, axis, [(i, i ^ bit) for i in range(count)]).astype(
             jnp.float32
         )
+        if at == 0:
+            block, rider = lax.optimization_barrier((block, rider))
     inner_count = lax.axis_size(inner_axis)
     pieces = [piece.astype(jnp.bfloat16) for piece in jnp.split(block, inner_count, axis=1)]
     mine = sum(piece.astype(jnp.float32) for piece in swap_chunks(pieces, inner_axis))
@@ -61,7 +63,7 @@
         block = jnp.where(
             upper, jnp.concatenate([other, block], 1), jnp.concatenate([block, other], 1)
         )
-    return block
+    return block, rider
 
 
 def pick(blocks, index):
@@ -79,7 +81,7 @@
     return [pick(by_mask, own ^ source) for source in range(count)]
 
 
-def doubling_gather(block, axis):
+def doubling_gather(block, axis, by_source=True):
     count = lax.axis_size(axis)
     own = lax.axis_index(axis)
     by_mask = {0: block}
@@ -93,6 +95,8 @@
             by_mask[key ^ bit] = received[at]
         bit //= 2
     ordered = [by_mask[mask] for mask in range(count)]
+    if not by_source:
+        return ordered
     return [pick(ordered, own ^ source) for source in range(count)]
 
 
@@ -131,7 +135,9 @@
         parts *= 2
     padded_width = -(-model_width // parts) * parts
     stats = jnp.pad(stats, ((0, 0), (0, padded_width - model_width)))
-    stats = halving_sum(stats, ("frame",), inner_axis="row")[:, :model_width]
+    weight_flat = in_weight.reshape(in_weight.shape[0], 2 * local_gated)
+    stats, weight_flat = halving_sum(stats, ("frame",), "row", weight_flat)
+    stats = stats[:, :model_width]
     kv_state, key_total = stats[:HEAD_DIM], stats[HEAD_DIM]
     query_pos = jnp.maximum(query_in, 0).reshape(token_count, HEADS, HEAD_DIM).astype(jnp.float32)
     numerator = jnp.einsum(
@@ -157,9 +163,8 @@
     ]
     by_row = jnp.concatenate(swap_chunks(depth_chunks, "row"), axis=1)
     frame_parts = lax.axis_size("frame")
-    by_frame = doubling_gather(by_row, "frame")
     whole_frames = frame_parts == row_parts and frame_count == 1 and row_count == 1
-    weight_flat = in_weight.reshape(local_depth, 2 * local_gated)
+    by_frame = doubling_gather(by_row, "frame", by_source=not whole_frames)
     if whole_frames:
         tokens = jnp.stack([piece[0] for piece in by_frame])
         partial = jnp.dot(
@@ -186,7 +191,7 @@
                     pick(row_blocks, frame_at ^ mask),
                     ("frame", "row"),
                     [
-                        (f * row_parts + r, r * row_parts + (f ^ mask))
+                        (f * row_parts + r, (f ^ r) * row_parts + (f ^ mask))
                         for f in range(frame_parts)
                         for r in range(row_parts)
                     ],

time: 200 us -> 204 us (1.020)
  starting transfers between devices: 23.6 us -> 28.2 us
    ppermute x4, starting transfers between devices: 8.8 us -> 13.3 us  [local(): lax.ppermute(pick(row_blocks, frame_at ^ mask), ('frame', 'row'), [(f * r...]
    reshape x1, local copies, waits for them, and re-layouts: 2.45 us -> 5.24 us  [local(): weight_flat = in_weight.reshape(in_weight.shape[0], 2 * local_gated)]
    ppermute x2, waiting for transfers between devices: 9.03 us -> 11.2 us  [doubling_gather(): lax.ppermute(jnp.stack([by_mask[key] for key in keys]), axis, [(i, i ^ bi...]
  transfers between devices with their start and end apart: 20 -> 20, of which waited for: 15 -> 15; matrix products, arithmetic and copies ran while one was open for 3% -> 4% of each run, Pallas kernels for 0% -> 0%
where the time goes in v10:
time: 204 us; the launch traced here: 203 us
  waiting for transfers between devices  124 us (61%)
  starting transfers between devices  28.2 us (14%)
  local copies, waits for them, and re-layouts  15.4 us (8%)
  between operations  14.6 us (7%)
  other arithmetic  12.3 us (6%)
  matrix products  8.62 us (4%)
    reduce_scatter x1, waiting for transfers between devices, local(): summed = lax.psum_scatter(partial, 'row', scatter_dimension=0, tiled=True)  62.9 us
    ppermute x4, waiting for transfers between devices, local(): lax.ppermute(pick(row_blocks, frame_at ^ mask), ('frame', 'row'), [(f * r...  21.9 us
    ppermute x9, starting transfers between devices, swap_chunks(): lax.ppermute(sent, axis, [(i, i ^ mask) for i in range(count)])  13.4 us
    ppermute x4, starting transfers between devices, local(): lax.ppermute(pick(row_blocks, frame_at ^ mask), ('frame', 'row'), [(f * r...  13.3 us
    ppermute x9, waiting for transfers between devices, swap_chunks(): lax.ppermute(sent, axis, [(i, i ^ mask) for i in range(count)])  13.3 us
    ppermute x2, waiting for transfers between devices, doubling_gather(): lax.ppermute(jnp.stack([by_mask[key] for key in keys]), axis, [(i, i ^ bi...  11.2 us
    ppermute x2, waiting for transfers between devices, halving_sum(): other = lax.ppermute(block, axis, [(i, i ^ bit) for i in range(count)])  8.62 us
    ppermute x2, waiting for transfers between devices, halving_sum(): lax.ppermute(sent, axis, [(i, i ^ bit) for i in range(count)])  6.12 us
  transfers between devices with their start and end apart: 20, of which 15 were waited for; matrix products, arithmetic and copies ran while one was open for 4% of the time, Pallas kernels for 0%

profile of v10, /device:TPU:2, one launch (start us, length us, event | category | flops | bytes accessed | tf_op | source)
XLA Modules:
  0.0 203.1 jit_solution(8279094623793545286)
XLA Ops:
  7.2 1.1 convert_reduce_fusion
  8.3 1.0 broadcast_maximum_fusion.1
  11.6 5.2 %reshape.220 = bf16[560,1680]{1,0:T(8,128)(2,1)} reshape(bf16[560,2,840]{2,1,0:T(2,128)(2,1)} %param.15) | data formatting | bytes 3763200 | tf_op jit(solution)/shard_map/reshape | solution.py:138
  16.8 1.2 convert_add_fusion.2
  18.2 6.1 %collective-permute-done.1 = bf16[113,560]{0,1:T(8,128)(2,1)S(1)} collective-permute-done((bf16[113,560]{0,1:T(8,128)(2,1)S(1)}, bf16[113,560]{0,1:T(8,128)(2,1)S(1)}, u32[]{:S(2)}, u32[]{:S(2)}) %collective-permute-start.1) | collective-permute-done | bytes 126592 | tf_op jit(solution)/shard_map/ppermute | solution.py:51
  24.5 3.7 %collective-permute-start.4 = (bf16[113,140]{0,1:T(8,128)(2,1)S(1)}, bf16[113,140]{0,1:T(8,128)(2,1)S(1)}, u32[]{:S(2)}, u32[]{:S(2)}) collective-permute-start(bf16[113,140]{0,1:T(8,128)(2,1)S(1)} %get-tuple-element.39), channel_id=1, source_target_pairs={{0,3},{1,2},{2,1},{3,0},{4,7},{5,6},{6,5},{7,4},{8,11},{9,10},{10,... | collective-permute-start | bytes 94928 | tf_op jit(solution)/shard_map/ppermute | solution.py:80
  28.9 1.6 collective-permute-done.4
  30.5 2.5 %collective-permute-done.3 = bf16[113,140]{0,1:T(8,128)(2,1)S(1)} collective-permute-done((bf16[113,140]{0,1:T(8,128)(2,1)S(1)}, bf16[113,140]{0,1:T(8,128)(2,1)S(1)}, u32[]{:S(2)}, u32[]{:S(2)}) %collective-permute-start.3) | collective-permute-done | bytes 31672 | tf_op jit(solution)/shard_map/ppermute | solution.py:80
  33.1 1.5 collective-permute-start.7
  35.2 2.3 %collective-permute-start.5 = (f32[113,140]{0,1:T(8,128)S(1)}, f32[113,140]{0,1:T(8,128)S(1)}, u32[]{:S(2)}, u32[]{:S(2)}) collective-permute-start(f32[113,140]{0,1:T(8,128)S(1)} %fusion.28), channel_id=1, source_target_pairs={{0,1},{1,0},{2,3},{3,2},{4,5},{5,4},{6,7},{7,6},{8,9},{9,8},{10,11... | collective-permute-start | bytes 189848 | tf_op jit(solution)/shard_map/ppermute | solution.py:80
  37.6 1.9 collective-permute-done.7
  39.4 1.9 collective-permute-done.6
  42.1 7.2 %collective-permute-done.8 = f32[113,560]{0,1:T(8,128)S(1)} collective-permute-done((f32[113,560]{0,1:T(8,128)S(1)}, f32[113,560]{0,1:T(8,128)S(1)}, u32[]{:S(2)}, u32[]{:S(2)}) %collective-permute-start.8) | collective-permute-done | bytes 253152 | tf_op jit(solution)/shard_map/ppermute | solution.py:62
  51.3 1.5 collective-permute-done.9
  54.5 1.4 multiply_reduce_fusion
  58.4 1.8 collective-permute-start.12
  60.2 2.7 %collective-permute-start.10 = (bf16[1,1,64,560]{3,2,1,0:T(8,128)(2,1)S(1)}, bf16[1,1,64,560]{3,2,1,0:T(8,128)(2,1)S(1)}, u32[]{:S(2)}, u32[]{:S(2)}) collective-permute-start(bf16[1,1,64,560]{3,2,1,0:T(8,128)(2,1)S(1)} %get-tuple-element.29), channel_id=1, source_target_pairs={{0,1},{1,0},{2,3},{3,2},{4,5},{5,4},{6,7},{7,6},{8,9},{9,8},{10,11... | collective-permute-start | bytes 215048 | tf_op jit(solution)/shard_map/ppermute | solution.py:80
  62.9 2.8 %collective-permute-done.12 = bf16[1,1,64,560]{3,2,1,0:T(8,128)(2,1)S(1)} collective-permute-done((bf16[1,1,64,560]{3,2,1,0:T(8,128)(2,1)S(1)}, bf16[1,1,64,560]{3,2,1,0:T(8,128)(2,1)S(1)}, u32[]{:S(2)}, u32[]{:S(2)}) %collective-permute-start.12) | collective-permute-done | bytes 71712 | tf_op jit(solution)/shard_map/ppermute | solution.py:80
  65.7 2.6 %collective-permute-done.11 = bf16[1,1,64,560]{3,2,1,0:T(8,128)(2,1)S(1)} collective-permute-done((bf16[1,1,64,560]{3,2,1,0:T(8,128)(2,1)S(1)}, bf16[1,1,64,560]{3,2,1,0:T(8,128)(2,1)S(1)}, u32[]{:S(2)}, u32[]{:S(2)}) %collective-permute-start.11) | collective-permute-done | bytes 71712 | tf_op jit(solution)/shard_map/ppermute | solution.py:80
  69.1 9.1 %collective-permute-done.13 = bf16[1,1,4,64,560]{4,3,2,1,0:T(8,128)(2,1)S(1)} collective-permute-done((bf16[1,1,4,64,560]{4,3,2,1,0:T(8,128)(2,1)S(1)}, bf16[1,1,4,64,560]{4,3,2,1,0:T(8,128)(2,1)S(1)}, u32[]{:S(2)}, u32[]{:S(2)}) %collective-permute-start.13) | collective-permute-done | bytes 286752 | tf_op jit(solution)/shard_map/ppermute | solution.py:91
  78.3 2.1 %collective-permute-done.14 = bf16[2,1,4,64,560]{4,3,2,1,0:T(8,128)(2,1)S(1)} collective-permute-done((bf16[2,1,4,64,560]{4,3,2,1,0:T(8,128)(2,1)S(1)}, bf16[2,1,4,64,560]{4,3,2,1,0:T(8,128)(2,1)S(1)}, u32[]{:S(2)}, u32[]{:S(2)}) %collective-permute-start.14) | collective-permute-done | bytes 573472 | tf_op jit(solution)/shard_map/ppermute | solution.py:91
  80.8 4.5 %convolution_convert_fusion.1 = bf16[1024,1680]{0,1:T(8,128)(2,1)} fusion(bf16[1024,560]{1,0:T(8,128)(2,1)S(1)} %bitcast.119, bf16[560,1680]{1,0:T(8,128)(2,1)S(1)} %copy-done), kind=kOutput, calls=%fused_computation.1 | convolution fusion | flops 1928478720 | bytes 6469120 | tf_op jit(solution)/shard_map/dot_general | solution.py:170
  86.8 62.9 %reduce-scatter.2.cloned.1.call-done = bf16[256,1680]{0,1:T(8,128)(2,1)} async-done(((bf16[1024,1680]{0,1:T(8,128)(2,1)}), bf16[256,1680]{0,1:T(8,128)(2,1)}) %reduce-scatter.2.cloned.1.call-update) | async-done | bytes 860176 | tf_op jit(solution)/shard_map/reduce_scatter | solution.py:173
  149.7 1.6 fusion.3
  152.0 2.9 %multiply_add_fusion = f32[1,4,64,1680]{3,2,1,0:T(8,128)S(1)} fusion(bf16[1,4,64,1680]{3,2,1,0:T(8,128)(2,1)S(1)} %bitcast.116, bf16[1,6,64,1680]{3,2,1,0:T(8,128)(2,1)S(1)} %pad.8, f32[1680]{0:T(1024)S(1)} %mul.211, f32[1680]{0:T(1024)S(1)} %mul.208, f32[1680]{0:T(1024)S(1)} %mul.205, f32[1680]{0:T(1024)S(1)} %mul.202, f32[1680]{0:T(1024)S(1)} %mul.199, ...), kind=kLoop, calls=%fused_computation.5 | loop fusion | flops 11182080 | bytes 5922816 | tf_op jit(solution)/shard_map/add | solution.py:115
  155.3 1.8 convolution_convert_fusion
  158.7 3.1 %collective-permute-start.18 = (bf16[64,2240]{1,0:T(8,128)(2,1)S(1)}, bf16[64,2240]{1,0:T(8,128)(2,1)S(1)}, u32[]{:S(2)}, u32[]{:S(2)}) collective-permute-start(bf16[64,2240]{1,0:T(8,128)(2,1)S(1)} %bitcast.121), channel_id=1, source_target_pairs={{0,3},{1,7},{2,11},{3,15},{4,6},{5,2},{6,14},{7,10},{8,9},{9,13},{... | collective-permute-start | bytes 860168 | tf_op jit(solution)/shard_map/ppermute | solution.py:190
  162.9 7.6 %collective-permute-start.16 = (bf16[64,2240]{1,0:T(8,128)(2,1)S(1)}, bf16[64,2240]{1,0:T(8,128)(2,1)S(1)}, u32[]{:S(2)}, u32[]{:S(2)}) collective-permute-start(bf16[64,2240]{1,0:T(8,128)(2,1)S(1)} %bitcast.123), channel_id=1, source_target_pairs={{0,1},{1,5},{2,9},{3,13},{4,4},{5,0},{6,12},{7,8},{8,11},{9,15},{1... | collective-permute-start | bytes 860168 | tf_op jit(solution)/shard_map/ppermute | solution.py:190
  171.5 1.9 collective-permute-start.15
  173.4 1.5 collective-permute-done.18
  174.9 3.0 %collective-permute-done.16 = bf16[64,2240]{1,0:T(8,128)(2,1)S(1)} collective-permute-done((bf16[64,2240]{1,0:T(8,128)(2,1)S(1)}, bf16[64,2240]{1,0:T(8,128)(2,1)S(1)}, u32[]{:S(2)}, u32[]{:S(2)}) %collective-permute-start.16) | collective-permute-done | bytes 286752 | tf_op jit(solution)/shard_map/ppermute | solution.py:190
  177.9 17.4 %collective-permute-done.15 = bf16[64,2240]{1,0:T(8,128)(2,1)S(1)} collective-permute-done((bf16[64,2240]{1,0:T(8,128)(2,1)}, bf16[64,2240]{1,0:T(8,128)(2,1)S(1)}, u32[]{:S(2)}, u32[]{:S(2)}) %collective-permute-start.15) | collective-permute-done | bytes 286752 | tf_op jit(solution)/shard_map/ppermute | solution.py:190
  (102 shorter events, 19.2 us)
Async XLA Ops:
  7.2 2.5 %copy-start.3 = (bf16[1,1,64,2240]{3,2,1,0:T(8,128)(2,1)S(1)}, bf16[1,1,64,2240]{3,2,1,0:T(8,128)(2,1)}, u32[]{:S(2)}) copy-start(bf16[1,1,64,2240]{3,2,1,0:T(8,128)(2,1)} %param.11) | copy-start | bytes 860164
  7.2 142.5 %reduce-scatter.2.cloned.1.call-start = ((), (), s32[]{:S(2)}) async-start(), calls=%async_computation.1 | async-start | bytes 4300800 | tf_op jit(solution)/shard_map/reduce_scatter | solution.py:173
  11.5 5.3 %collective-permute-start = (bf16[113,1120]{0,1:T(8,128)(2,1)S(1)}, bf16[113,1120]{0,1:T(8,128)(2,1)}, u32[]{:S(2)}, u32[]{:S(2)}) collective-permute-start(bf16[113,1120]{0,1:T(8,128)(2,1)S(1)} %get-tuple-element.10), channel_id=1, source_target_pairs={{0,4},{4,0},{8,12},{12,8},{1,5},{5,1},{9,13},{13,9},{2,6},{6,2},{1... | collective-permute-start | bytes 759368 | tf_op jit(solution)/shard_map/ppermute | solution.py:51
  18.1 6.2 %collective-permute-start.1 = (bf16[113,560]{0,1:T(8,128)(2,1)S(1)}, bf16[113,560]{0,1:T(8,128)(2,1)S(1)}, u32[]{:S(2)}, u32[]{:S(2)}) collective-permute-start(bf16[113,560]{0,1:T(8,128)(2,1)S(1)} %select_convert_fusion.1), channel_id=1, source_target_pairs={{0,8},{4,12},{8,0},{12,4},{1,9},{5,13},{9,1},{13,5},{2,10},{6,14},... | collective-permute-start | bytes 379688 | tf_op jit(solution)/shard_map/ppermute | solution.py:51
  24.3 17.7 %copy-start.5 = (bf16[2240]{0:T(1024)(128)(2,1)S(1)}, bf16[2240]{0:T(1024)(128)(2,1)}, u32[]{:S(2)}) copy-start(bf16[2240]{0:T(1024)(128)(2,1)} %param.14) | copy-start | bytes 13444
  24.5 6.1 %collective-permute-start.4 = (bf16[113,140]{0,1:T(8,128)(2,1)S(1)}, bf16[113,140]{0,1:T(8,128)(2,1)S(1)}, u32[]{:S(2)}, u32[]{:S(2)}) collective-permute-start(bf16[113,140]{0,1:T(8,128)(2,1)S(1)} %get-tuple-element.39), channel_id=1, source_target_pairs={{0,3},{1,2},{2,1},{3,0},{4,7},{5,6},{6,5},{7,4},{8,11},{9,10},{10,... | collective-permute-start | bytes 94928 | tf_op jit(solution)/shard_map/ppermute | solution.py:80
  28.1 4.9 %collective-permute-start.3 = (bf16[113,140]{0,1:T(8,128)(2,1)S(1)}, bf16[113,140]{0,1:T(8,128)(2,1)S(1)}, u32[]{:S(2)}, u32[]{:S(2)}) collective-permute-start(bf16[113,140]{0,1:T(8,128)(2,1)S(1)} %get-tuple-element.40), channel_id=1, source_target_pairs={{0,2},{1,3},{2,0},{3,1},{4,6},{5,7},{6,4},{7,5},{8,10},{9,11},{10,... | collective-permute-start | bytes 94928 | tf_op jit(solution)/shard_map/ppermute | solution.py:80
  28.1 4.9 %collective-permute-start.2 = (bf16[113,140]{0,1:T(8,128)(2,1)S(1)}, bf16[113,140]{0,1:T(8,128)(2,1)S(1)}, u32[]{:S(2)}, u32[]{:S(2)}) collective-permute-start(bf16[113,140]{0,1:T(8,128)(2,1)S(1)} %get-tuple-element.41), channel_id=1, source_target_pairs={{0,1},{1,0},{2,3},{3,2},{4,5},{5,4},{6,7},{7,6},{8,9},{9,8},{10,11... | collective-permute-start | bytes 94928 | tf_op jit(solution)/shard_map/ppermute | solution.py:80
  33.1 6.4 %collective-permute-start.7 = (f32[113,140]{0,1:T(8,128)S(1)}, f32[113,140]{0,1:T(8,128)S(1)}, u32[]{:S(2)}, u32[]{:S(2)}) collective-permute-start(f32[113,140]{0,1:T(8,128)S(1)} %fusion.28), channel_id=1, source_target_pairs={{0,3},{1,2},{2,1},{3,0},{4,7},{5,6},{6,5},{7,4},{8,11},{9,10},{10,... | collective-permute-start | bytes 189848 | tf_op jit(solution)/shard_map/ppermute | solution.py:80
  34.6 6.7 %collective-permute-start.6 = (f32[113,140]{0,1:T(8,128)S(1)}, f32[113,140]{0,1:T(8,128)S(1)}, u32[]{:S(2)}, u32[]{:S(2)}) collective-permute-start(f32[113,140]{0,1:T(8,128)S(1)} %fusion.28), channel_id=1, source_target_pairs={{0,2},{1,3},{2,0},{3,1},{4,6},{5,7},{6,4},{7,5},{8,10},{9,11},{10,... | collective-permute-start | bytes 189848 | tf_op jit(solution)/shard_map/ppermute | solution.py:80
  35.2 6.1 %collective-permute-start.5 = (f32[113,140]{0,1:T(8,128)S(1)}, f32[113,140]{0,1:T(8,128)S(1)}, u32[]{:S(2)}, u32[]{:S(2)}) collective-permute-start(f32[113,140]{0,1:T(8,128)S(1)} %fusion.28), channel_id=1, source_target_pairs={{0,1},{1,0},{2,3},{3,2},{4,5},{5,4},{6,7},{7,6},{8,9},{9,8},{10,11... | collective-permute-start | bytes 189848 | tf_op jit(solution)/shard_map/ppermute | solution.py:80
  41.5 7.8 %collective-permute-start.8 = (f32[113,560]{0,1:T(8,128)S(1)}, f32[113,560]{0,1:T(8,128)S(1)}, u32[]{:S(2)}, u32[]{:S(2)}) collective-permute-start(f32[113,560]{0,1:T(8,128)S(1)} %pad_maximum_fusion.7), channel_id=1, source_target_pairs={{0,8},{4,12},{8,0},{12,4},{1,9},{5,13},{9,1},{13,5},{2,10},{6,14},... | collective-permute-start | bytes 759368 | tf_op jit(solution)/shard_map/ppermute | solution.py:62
  49.8 1.0 copy-start.2
  50.4 0.9 copy-start.6
  50.7 2.0 collective-permute-start.9
  55.9 1.0 copy-start.1
  58.4 7.3 %collective-permute-start.12 = (bf16[1,1,64,560]{3,2,1,0:T(8,128)(2,1)S(1)}, bf16[1,1,64,560]{3,2,1,0:T(8,128)(2,1)S(1)}, u32[]{:S(2)}, u32[]{:S(2)}) collective-permute-start(bf16[1,1,64,560]{3,2,1,0:T(8,128)(2,1)S(1)} %get-tuple-element.27), channel_id=1, source_target_pairs={{0,3},{1,2},{2,1},{3,0},{4,7},{5,6},{6,5},{7,4},{8,11},{9,10},{10,... | collective-permute-start | bytes 215048 | tf_op jit(solution)/shard_map/ppermute | solution.py:80
  60.2 8.1 %collective-permute-start.11 = (bf16[1,1,64,560]{3,2,1,0:T(8,128)(2,1)S(1)}, bf16[1,1,64,560]{3,2,1,0:T(8,128)(2,1)S(1)}, u32[]{:S(2)}, u32[]{:S(2)}) collective-permute-start(bf16[1,1,64,560]{3,2,1,0:T(8,128)(2,1)S(1)} %get-tuple-element.28), channel_id=1, source_target_pairs={{0,2},{1,3},{2,0},{3,1},{4,6},{5,7},{6,4},{7,5},{8,10},{9,11},{10,... | collective-permute-start | bytes 215048 | tf_op jit(solution)/shard_map/ppermute | solution.py:80
  60.2 8.1 %collective-permute-start.10 = (bf16[1,1,64,560]{3,2,1,0:T(8,128)(2,1)S(1)}, bf16[1,1,64,560]{3,2,1,0:T(8,128)(2,1)S(1)}, u32[]{:S(2)}, u32[]{:S(2)}) collective-permute-start(bf16[1,1,64,560]{3,2,1,0:T(8,128)(2,1)S(1)} %get-tuple-element.29), channel_id=1, source_target_pairs={{0,1},{1,0},{2,3},{3,2},{4,5},{5,4},{6,7},{7,6},{8,9},{9,8},{10,11... | collective-permute-start | bytes 215048 | tf_op jit(solution)/shard_map/ppermute | solution.py:80
  68.5 9.7 %collective-permute-start.13 = (bf16[1,1,4,64,560]{4,3,2,1,0:T(8,128)(2,1)S(1)}, bf16[1,1,4,64,560]{4,3,2,1,0:T(8,128)(2,1)S(1)}, u32[]{:S(2)}, u32[]{:S(2)}) collective-permute-start(bf16[1,1,4,64,560]{4,3,2,1,0:T(8,128)(2,1)S(1)} %maximum_bitcast_fusion), channel_id=1, source_target_pairs={{0,8},{4,12},{8,0},{12,4},{1,9},{5,13},{9,1},{13,5},{2,10},{6,14},... | collective-permute-start | bytes 860168 | tf_op jit(solution)/shard_map/ppermute | solution.py:91
  78.3 2.5 %copy-start = (bf16[560,1680]{1,0:T(8,128)(2,1)S(1)}, bf16[560,1680]{1,0:T(8,128)(2,1)}, u32[]{:S(2)}) copy-start(bf16[560,1680]{1,0:T(8,128)(2,1)} %reshape.220) | copy-start | bytes 5644804
  78.3 2.2 %collective-permute-start.14 = (bf16[2,1,4,64,560]{4,3,2,1,0:T(8,128)(2,1)S(1)}, bf16[2,1,4,64,560]{4,3,2,1,0:T(8,128)(2,1)S(1)}, u32[]{:S(2)}, u32[]{:S(2)}) collective-permute-start(bf16[2,1,4,64,560]{4,3,2,1,0:T(8,128)(2,1)S(1)} %pad_maximum_fusion.2), channel_id=1, source_target_pairs={{0,4},{4,0},{8,12},{12,8},{1,5},{5,1},{9,13},{13,9},{2,6},{6,2},{1... | collective-permute-start | bytes 1720328 | tf_op jit(solution)/shard_map/ppermute | solution.py:91
  85.3 0.8 copy-start.4
  152.0 3.3 %copy-start.7 = (bf16[840,2240]{1,0:T(8,128)(2,1)S(1)}, bf16[840,2240]{1,0:T(8,128)(2,1)}, u32[]{:S(2)}) copy-start(bf16[840,2240]{1,0:T(8,128)(2,1)} %param.17) | copy-start | bytes 11289604
  158.7 16.3 %collective-permute-start.18 = (bf16[64,2240]{1,0:T(8,128)(2,1)S(1)}, bf16[64,2240]{1,0:T(8,128)(2,1)S(1)}, u32[]{:S(2)}, u32[]{:S(2)}) collective-permute-start(bf16[64,2240]{1,0:T(8,128)(2,1)S(1)} %bitcast.121), channel_id=1, source_target_pairs={{0,3},{1,7},{2,11},{3,15},{4,6},{5,2},{6,14},{7,10},{8,9},{9,13},{... | collective-permute-start | bytes 860168 | tf_op jit(solution)/shard_map/ppermute | solution.py:190
  162.0 12.9 %collective-permute-start.17 = (bf16[64,2240]{1,0:T(8,128)(2,1)S(1)}, bf16[64,2240]{1,0:T(8,128)(2,1)S(1)}, u32[]{:S(2)}, u32[]{:S(2)}) collective-permute-start(bf16[64,2240]{1,0:T(8,128)(2,1)S(1)} %bitcast.122), channel_id=1, source_target_pairs={{0,2},{1,6},{2,10},{3,14},{4,7},{5,3},{6,15},{7,11},{8,8},{9,12},{... | collective-permute-start | bytes 860168 | tf_op jit(solution)/shard_map/ppermute | solution.py:190
  162.9 15.0 %collective-permute-start.16 = (bf16[64,2240]{1,0:T(8,128)(2,1)S(1)}, bf16[64,2240]{1,0:T(8,128)(2,1)S(1)}, u32[]{:S(2)}, u32[]{:S(2)}) collective-permute-start(bf16[64,2240]{1,0:T(8,128)(2,1)S(1)} %bitcast.123), channel_id=1, source_target_pairs={{0,1},{1,5},{2,9},{3,13},{4,4},{5,0},{6,12},{7,8},{8,11},{9,15},{1... | collective-permute-start | bytes 860168 | tf_op jit(solution)/shard_map/ppermute | solution.py:190
  171.5 23.9 %collective-permute-start.15 = (bf16[64,2240]{1,0:T(8,128)(2,1)}, bf16[64,2240]{1,0:T(8,128)(2,1)S(1)}, u32[]{:S(2)}, u32[]{:S(2)}) collective-permute-start(bf16[64,2240]{1,0:T(8,128)(2,1)} %bitcast.124), channel_id=1, source_target_pairs={{0,0},{1,4},{2,8},{3,12},{4,5},{5,1},{6,13},{7,9},{8,10},{9,14},{1... | collective-permute-start | bytes 860168 | tf_op jit(solution)/shard_map/ppermute | solution.py:190
Sparse Core Ops, SparseCore 0:
  85.4 64.2 reduce-scatter.1

commit v11 on v9

--- a/solution.py
+++ b/solution.py
@@ -54,10 +54,13 @@
     inner_count = lax.axis_size(inner_axis)
     pieces = [piece.astype(jnp.bfloat16) for piece in jnp.split(block, inner_count, axis=1)]
     mine = sum(piece.astype(jnp.float32) for piece in swap_chunks(pieces, inner_axis))
-    block = jnp.concatenate(swap_chunks([mine] * inner_count, inner_axis), axis=1)
+    shared = swap_chunks([mine.astype(jnp.bfloat16)] * inner_count, inner_axis)
+    block = jnp.concatenate([piece.astype(jnp.float32) for piece in shared], axis=1)
     for axis, count, bit in reversed(steps):
         upper = (lax.axis_index(axis) & bit) != 0
-        other = lax.ppermute(block, axis, [(i, i ^ bit) for i in range(count)])
+        other = lax.ppermute(
+            block.astype(jnp.bfloat16), axis, [(i, i ^ bit) for i in range(count)]
+        ).astype(jnp.float32)
         block = jnp.where(
             upper, jnp.concatenate([other, block], 1), jnp.concatenate([block, other], 1)
         )

time: 200 us -> 197 us (0.985)
  waiting for transfers between devices: 124 us -> 121 us
  transfers between devices with their start and end apart: 20 -> 20, of which waited for: 15 -> 16; matrix products, arithmetic and copies ran while one was open for 3% -> 3% of each run, Pallas kernels for 0% -> 0%
where the time goes in v11:
time: 197 us; the launch traced here: 196 us
  waiting for transfers between devices  121 us (61%)
  starting transfers between devices  23.6 us (12%)
  local copies, waits for them, and re-layouts  14.6 us (7%)
  between operations  14.6 us (7%)
  other arithmetic  13.5 us (7%)
  matrix products  8.6 us (4%)
    reduce_scatter x1, waiting for transfers between devices, local(): summed = lax.psum_scatter(partial, 'row', scatter_dimension=0, tiled=True)  63.6 us
    ppermute x4, waiting for transfers between devices, local(): lax.ppermute(pick(row_blocks, frame_at ^ mask), ('frame', 'row'), [(f * r...  23.3 us
    ppermute x9, starting transfers between devices, swap_chunks(): lax.ppermute(sent, axis, [(i, i ^ mask) for i in range(count)])  13.4 us
    ppermute x9, waiting for transfers between devices, swap_chunks(): lax.ppermute(sent, axis, [(i, i ^ mask) for i in range(count)])  12.8 us
    ppermute x4, starting transfers between devices, local(): lax.ppermute(pick(row_blocks, frame_at ^ mask), ('frame', 'row'), [(f * r...  8.8 us
    ppermute x2, waiting for transfers between devices, doubling_gather(): lax.ppermute(jnp.stack([by_mask[key] for key in keys]), axis, [(i, i ^ bi...  8.4 us
    ppermute x2, waiting for transfers between devices, halving_sum(): lax.ppermute(sent, axis, [(i, i ^ bit) for i in range(count)])  7.45 us
    ppermute x2, waiting for transfers between devices, halving_sum(): lax.ppermute(block.astype(jnp.bfloat16), axis, [(i, i ^ bit) for i in ran...  5.6 us
  transfers between devices with their start and end apart: 20, of which 16 were waited for; matrix products, arithmetic and copies ran while one was open for 3% of the time, Pallas kernels for 0%

profile of v11, /device:TPU:2, one launch (start us, length us, event | category | flops | bytes accessed | tf_op | source)
XLA Modules:
  0.0 196.1 jit_solution(4599575845676003786)
XLA Ops:
  7.2 1.1 convert_reduce_fusion
  11.6 1.7 collective-permute-done
  13.3 1.2 convert_add_fusion.2
  14.6 5.8 %collective-permute-done.1 = bf16[113,560]{0,1:T(8,128)(2,1)S(1)} collective-permute-done((bf16[113,560]{0,1:T(8,128)(2,1)S(1)}, bf16[113,560]{0,1:T(8,128)(2,1)S(1)}, u32[]{:S(2)}, u32[]{:S(2)}) %collective-permute-start.1) | collective-permute-done | bytes 126592 | tf_op jit(solution)/shard_map/ppermute | solution.py:51
  20.5 3.7 %collective-permute-start.4 = (bf16[113,140]{0,1:T(8,128)(2,1)S(1)}, bf16[113,140]{0,1:T(8,128)(2,1)S(1)}, u32[]{:S(2)}, u32[]{:S(2)}) collective-permute-start(bf16[113,140]{0,1:T(8,128)(2,1)S(1)} %get-tuple-element.41), channel_id=1, source_target_pairs={{0,3},{1,2},{2,1},{3,0},{4,7},{5,6},{6,5},{7,4},{8,11},{9,10},{10,... | collective-permute-start | bytes 94928 | tf_op jit(solution)/shard_map/ppermute | solution.py:81
  25.0 1.6 collective-permute-done.4
  26.6 2.5 %collective-permute-done.3 = bf16[113,140]{0,1:T(8,128)(2,1)S(1)} collective-permute-done((bf16[113,140]{0,1:T(8,128)(2,1)S(1)}, bf16[113,140]{0,1:T(8,128)(2,1)S(1)}, u32[]{:S(2)}, u32[]{:S(2)}) %collective-permute-start.3) | collective-permute-done | bytes 31672 | tf_op jit(solution)/shard_map/ppermute | solution.py:81
  29.2 1.5 collective-permute-start.7
  31.3 2.3 %collective-permute-start.5 = (bf16[113,140]{0,1:T(8,128)(2,1)S(1)}, bf16[113,140]{0,1:T(8,128)(2,1)S(1)}, u32[]{:S(2)}, u32[]{:S(2)}) collective-permute-start(bf16[113,140]{0,1:T(8,128)(2,1)S(1)} %fusion.30), channel_id=1, source_target_pairs={{0,1},{1,0},{2,3},{3,2},{4,5},{5,4},{6,7},{7,6},{8,9},{9,8},{10,11... | collective-permute-start | bytes 94928 | tf_op jit(solution)/shard_map/ppermute | solution.py:81
  33.6 1.3 collective-permute-done.7
  36.7 4.6 %collective-permute-done.8 = bf16[113,560]{0,1:T(8,128)(2,1)S(1)} collective-permute-done((bf16[113,560]{0,1:T(8,128)(2,1)S(1)}, bf16[113,560]{0,1:T(8,128)(2,1)S(1)}, u32[]{:S(2)}, u32[]{:S(2)}) %collective-permute-start.8) | collective-permute-done | bytes 126592 | tf_op jit(solution)/shard_map/ppermute | solution.py:61
  45.8 1.4 multiply_reduce_fusion
  49.7 2.4 %collective-permute-start.12 = (bf16[1,1,64,560]{3,2,1,0:T(8,128)(2,1)S(1)}, bf16[1,1,64,560]{3,2,1,0:T(8,128)(2,1)S(1)}, u32[]{:S(2)}, u32[]{:S(2)}) collective-permute-start(bf16[1,1,64,560]{3,2,1,0:T(8,128)(2,1)S(1)} %get-tuple-element.29), channel_id=1, source_target_pairs={{0,3},{1,2},{2,1},{3,0},{4,7},{5,6},{6,5},{7,4},{8,11},{9,10},{10,... | collective-permute-start | bytes 215048 | tf_op jit(solution)/shard_map/ppermute | solution.py:81
  52.9 1.3 collective-permute-start.10
  54.1 2.8 %collective-permute-done.12 = bf16[1,1,64,560]{3,2,1,0:T(8,128)(2,1)S(1)} collective-permute-done((bf16[1,1,64,560]{3,2,1,0:T(8,128)(2,1)S(1)}, bf16[1,1,64,560]{3,2,1,0:T(8,128)(2,1)S(1)}, u32[]{:S(2)}, u32[]{:S(2)}) %collective-permute-start.12) | collective-permute-done | bytes 71712 | tf_op jit(solution)/shard_map/ppermute | solution.py:81
  56.9 3.6 %collective-permute-done.11 = bf16[1,1,64,560]{3,2,1,0:T(8,128)(2,1)S(1)} collective-permute-done((bf16[1,1,64,560]{3,2,1,0:T(8,128)(2,1)S(1)}, bf16[1,1,64,560]{3,2,1,0:T(8,128)(2,1)S(1)}, u32[]{:S(2)}, u32[]{:S(2)}) %collective-permute-start.11) | collective-permute-done | bytes 71712 | tf_op jit(solution)/shard_map/ppermute | solution.py:81
  61.4 8.4 %collective-permute-done.13 = bf16[1,1,4,64,560]{4,3,2,1,0:T(8,128)(2,1)S(1)} collective-permute-done((bf16[1,1,4,64,560]{4,3,2,1,0:T(8,128)(2,1)S(1)}, bf16[1,1,4,64,560]{4,3,2,1,0:T(8,128)(2,1)S(1)}, u32[]{:S(2)}, u32[]{:S(2)}) %collective-permute-start.13) | collective-permute-done | bytes 286752 | tf_op jit(solution)/shard_map/ppermute | solution.py:92
  70.7 2.4 %reshape.234 = bf16[560,1680]{1,0:T(8,128)(2,1)} reshape(bf16[560,2,840]{2,1,0:T(2,128)(2,1)S(1)} %copy-done) | data formatting | bytes 3763200 | tf_op jit(solution)/shard_map/reshape | solution.py:165
  73.2 1.1 fusion.22
  75.0 1.3 copy-done.1
  76.3 4.5 %convolution_convert_fusion.1 = bf16[1024,1680]{0,1:T(8,128)(2,1)} fusion(bf16[1024,560]{1,0:T(8,128)(2,1)S(1)} %bitcast.121, bf16[560,1680]{1,0:T(8,128)(2,1)S(1)} %copy-done.1), kind=kOutput, calls=%fused_computation.1 | convolution fusion | flops 1928478720 | bytes 6469120 | tf_op jit(solution)/shard_map/dot_general | solution.py:168
  82.2 63.6 %reduce-scatter.2.cloned.1.call-done = bf16[256,1680]{0,1:T(8,128)(2,1)} async-done(((bf16[1024,1680]{0,1:T(8,128)(2,1)}), bf16[256,1680]{0,1:T(8,128)(2,1)}) %reduce-scatter.2.cloned.1.call-update) | async-done | bytes 860176 | tf_op jit(solution)/shard_map/reduce_scatter | solution.py:171
  145.8 1.6 fusion.3
  148.2 3.0 %multiply_add_fusion = f32[1,4,64,1680]{3,2,1,0:T(8,128)S(1)} fusion(bf16[1,4,64,1680]{3,2,1,0:T(8,128)(2,1)S(1)} %bitcast.119, bf16[1,6,64,1680]{3,2,1,0:T(8,128)(2,1)S(1)} %pad.8, f32[1680]{0:T(1024)S(1)} %mul.211, f32[1680]{0:T(1024)S(1)} %mul.208, f32[1680]{0:T(1024)S(1)} %mul.205, f32[1680]{0:T(1024)S(1)} %mul.202, f32[1680]{0:T(1024)S(1)} %mul.199, ...), kind=kLoop, calls=%fused_computation.5 | loop fusion | flops 11182080 | bytes 5922816 | tf_op jit(solution)/shard_map/add | solution.py:114
  151.5 1.8 convolution_convert_fusion
  154.8 1.2 collective-permute-start.18
  156.3 1.7 collective-permute-start.17
  158.2 2.2 %collective-permute-start.16 = (bf16[64,2240]{1,0:T(8,128)(2,1)S(1)}, bf16[64,2240]{1,0:T(8,128)(2,1)S(1)}, u32[]{:S(2)}, u32[]{:S(2)}) collective-permute-start(bf16[64,2240]{1,0:T(8,128)(2,1)S(1)} %bitcast.125), channel_id=1, source_target_pairs={{0,1},{1,5},{2,9},{3,13},{4,0},{5,4},{6,8},{7,12},{8,3},{9,7},{10,... | collective-permute-start | bytes 860168 | tf_op jit(solution)/shard_map/ppermute | solution.py:188
  161.4 3.6 %collective-permute-start.15 = (bf16[64,2240]{1,0:T(8,128)(2,1)}, bf16[64,2240]{1,0:T(8,128)(2,1)S(1)}, u32[]{:S(2)}, u32[]{:S(2)}) collective-permute-start(bf16[64,2240]{1,0:T(8,128)(2,1)} %bitcast.126), channel_id=1, source_target_pairs={{0,0},{1,4},{2,8},{3,12},{4,1},{5,5},{6,9},{7,13},{8,2},{9,6},{10,... | collective-permute-start | bytes 860168 | tf_op jit(solution)/shard_map/ppermute | solution.py:188
  165.1 12.4 %collective-permute-done.18 = bf16[64,2240]{1,0:T(8,128)(2,1)S(1)} collective-permute-done((bf16[64,2240]{1,0:T(8,128)(2,1)S(1)}, bf16[64,2240]{1,0:T(8,128)(2,1)S(1)}, u32[]{:S(2)}, u32[]{:S(2)}) %collective-permute-start.18) | collective-permute-done | bytes 286752 | tf_op jit(solution)/shard_map/ppermute | solution.py:188
  177.5 6.6 %collective-permute-done.17 = bf16[64,2240]{1,0:T(8,128)(2,1)S(1)} collective-permute-done((bf16[64,2240]{1,0:T(8,128)(2,1)S(1)}, bf16[64,2240]{1,0:T(8,128)(2,1)S(1)}, u32[]{:S(2)}, u32[]{:S(2)}) %collective-permute-start.17) | collective-permute-done | bytes 286752 | tf_op jit(solution)/shard_map/ppermute | solution.py:188
  184.1 4.3 %collective-permute-done.15 = bf16[64,2240]{1,0:T(8,128)(2,1)S(1)} collective-permute-done((bf16[64,2240]{1,0:T(8,128)(2,1)}, bf16[64,2240]{1,0:T(8,128)(2,1)S(1)}, u32[]{:S(2)}, u32[]{:S(2)}) %collective-permute-start.15) | collective-permute-done | bytes 286752 | tf_op jit(solution)/shard_map/ppermute | solution.py:188
  (105 shorter events, 23.1 us)
Async XLA Ops:
  7.2 2.5 %copy-start.4 = (bf16[1,1,64,2240]{3,2,1,0:T(8,128)(2,1)S(1)}, bf16[1,1,64,2240]{3,2,1,0:T(8,128)(2,1)}, u32[]{:S(2)}) copy-start(bf16[1,1,64,2240]{3,2,1,0:T(8,128)(2,1)} %param.11) | copy-start | bytes 860164
  7.2 138.6 %reduce-scatter.2.cloned.1.call-start = ((), (), s32[]{:S(2)}) async-start(), calls=%async_computation.1 | async-start | bytes 4300800 | tf_op jit(solution)/shard_map/reduce_scatter | solution.py:171
  11.5 1.8 collective-permute-start
  14.5 5.9 %collective-permute-start.1 = (bf16[113,560]{0,1:T(8,128)(2,1)S(1)}, bf16[113,560]{0,1:T(8,128)(2,1)S(1)}, u32[]{:S(2)}, u32[]{:S(2)}) collective-permute-start(bf16[113,560]{0,1:T(8,128)(2,1)S(1)} %select_convert_fusion.1), channel_id=1, source_target_pairs={{0,8},{4,12},{8,0},{12,4},{1,9},{5,13},{9,1},{13,5},{2,10},{6,14},... | collective-permute-start | bytes 379688 | tf_op jit(solution)/shard_map/ppermute | solution.py:51
  20.5 6.1 %collective-permute-start.4 = (bf16[113,140]{0,1:T(8,128)(2,1)S(1)}, bf16[113,140]{0,1:T(8,128)(2,1)S(1)}, u32[]{:S(2)}, u32[]{:S(2)}) collective-permute-start(bf16[113,140]{0,1:T(8,128)(2,1)S(1)} %get-tuple-element.41), channel_id=1, source_target_pairs={{0,3},{1,2},{2,1},{3,0},{4,7},{5,6},{6,5},{7,4},{8,11},{9,10},{10,... | collective-permute-start | bytes 94928 | tf_op jit(solution)/shard_map/ppermute | solution.py:81
  24.2 4.9 %collective-permute-start.3 = (bf16[113,140]{0,1:T(8,128)(2,1)S(1)}, bf16[113,140]{0,1:T(8,128)(2,1)S(1)}, u32[]{:S(2)}, u32[]{:S(2)}) collective-permute-start(bf16[113,140]{0,1:T(8,128)(2,1)S(1)} %get-tuple-element.42), channel_id=1, source_target_pairs={{0,2},{1,3},{2,0},{3,1},{4,6},{5,7},{6,4},{7,5},{8,10},{9,11},{10,... | collective-permute-start | bytes 94928 | tf_op jit(solution)/shard_map/ppermute | solution.py:81
  24.2 4.9 %collective-permute-start.2 = (bf16[113,140]{0,1:T(8,128)(2,1)S(1)}, bf16[113,140]{0,1:T(8,128)(2,1)S(1)}, u32[]{:S(2)}, u32[]{:S(2)}) collective-permute-start(bf16[113,140]{0,1:T(8,128)(2,1)S(1)} %get-tuple-element.43), channel_id=1, source_target_pairs={{0,1},{1,0},{2,3},{3,2},{4,5},{5,4},{6,7},{7,6},{8,9},{9,8},{10,11... | collective-permute-start | bytes 94928 | tf_op jit(solution)/shard_map/ppermute | solution.py:81
  29.2 5.8 %collective-permute-start.7 = (bf16[113,140]{0,1:T(8,128)(2,1)S(1)}, bf16[113,140]{0,1:T(8,128)(2,1)S(1)}, u32[]{:S(2)}, u32[]{:S(2)}) collective-permute-start(bf16[113,140]{0,1:T(8,128)(2,1)S(1)} %fusion.30), channel_id=1, source_target_pairs={{0,3},{1,2},{2,1},{3,0},{4,7},{5,6},{6,5},{7,4},{8,11},{9,10},{10,... | collective-permute-start | bytes 94928 | tf_op jit(solution)/shard_map/ppermute | solution.py:81
  30.7 4.9 %collective-permute-start.6 = (bf16[113,140]{0,1:T(8,128)(2,1)S(1)}, bf16[113,140]{0,1:T(8,128)(2,1)S(1)}, u32[]{:S(2)}, u32[]{:S(2)}) collective-permute-start(bf16[113,140]{0,1:T(8,128)(2,1)S(1)} %fusion.30), channel_id=1, source_target_pairs={{0,2},{1,3},{2,0},{3,1},{4,6},{5,7},{6,4},{7,5},{8,10},{9,11},{10,... | collective-permute-start | bytes 94928 | tf_op jit(solution)/shard_map/ppermute | solution.py:81
  31.3 4.6 %collective-permute-start.5 = (bf16[113,140]{0,1:T(8,128)(2,1)S(1)}, bf16[113,140]{0,1:T(8,128)(2,1)S(1)}, u32[]{:S(2)}, u32[]{:S(2)}) collective-permute-start(bf16[113,140]{0,1:T(8,128)(2,1)S(1)} %fusion.30), channel_id=1, source_target_pairs={{0,1},{1,0},{2,3},{3,2},{4,5},{5,4},{6,7},{7,6},{8,9},{9,8},{10,11... | collective-permute-start | bytes 94928 | tf_op jit(solution)/shard_map/ppermute | solution.py:81
  36.1 6.5 %copy-start.3 = (bf16[1,1,64,2240]{3,2,1,0:T(8,128)(2,1)S(1)}, bf16[1,1,64,2240]{3,2,1,0:T(8,128)(2,1)}, u32[]{:S(2)}) copy-start(bf16[1,1,64,2240]{3,2,1,0:T(8,128)(2,1)} %param.9) | copy-start | bytes 860164
  36.1 5.2 %collective-permute-start.8 = (bf16[113,560]{0,1:T(8,128)(2,1)S(1)}, bf16[113,560]{0,1:T(8,128)(2,1)S(1)}, u32[]{:S(2)}, u32[]{:S(2)}) collective-permute-start(bf16[113,560]{0,1:T(8,128)(2,1)S(1)} %pad_maximum_fusion.10), channel_id=1, source_target_pairs={{0,8},{4,12},{8,0},{12,4},{1,9},{5,13},{9,1},{13,5},{2,10},{6,14},... | collective-permute-start | bytes 379688 | tf_op jit(solution)/shard_map/ppermute | solution.py:61
  41.9 0.8 copy-start.6
  42.4 0.7 copy-start.7
  42.5 1.6 collective-permute-start.9
  47.2 1.0 copy-start.2
  49.6 21.1 %copy-start = (bf16[560,2,840]{2,1,0:T(2,128)(2,1)S(1)}, bf16[560,2,840]{2,1,0:T(2,128)(2,1)}, u32[]{:S(2)}) copy-start(bf16[560,2,840]{2,1,0:T(2,128)(2,1)} %param.15) | copy-start | bytes 5644804
  49.7 7.3 %collective-permute-start.12 = (bf16[1,1,64,560]{3,2,1,0:T(8,128)(2,1)S(1)}, bf16[1,1,64,560]{3,2,1,0:T(8,128)(2,1)S(1)}, u32[]{:S(2)}, u32[]{:S(2)}) collective-permute-start(bf16[1,1,64,560]{3,2,1,0:T(8,128)(2,1)S(1)} %get-tuple-element.29), channel_id=1, source_target_pairs={{0,3},{1,2},{2,1},{3,0},{4,7},{5,6},{6,5},{7,4},{8,11},{9,10},{10,... | collective-permute-start | bytes 215048 | tf_op jit(solution)/shard_map/ppermute | solution.py:81
  52.1 8.5 %collective-permute-start.11 = (bf16[1,1,64,560]{3,2,1,0:T(8,128)(2,1)S(1)}, bf16[1,1,64,560]{3,2,1,0:T(8,128)(2,1)S(1)}, u32[]{:S(2)}, u32[]{:S(2)}) collective-permute-start(bf16[1,1,64,560]{3,2,1,0:T(8,128)(2,1)S(1)} %get-tuple-element.30), channel_id=1, source_target_pairs={{0,2},{1,3},{2,0},{3,1},{4,6},{5,7},{6,4},{7,5},{8,10},{9,11},{10,... | collective-permute-start | bytes 215048 | tf_op jit(solution)/shard_map/ppermute | solution.py:81
  52.9 7.7 %collective-permute-start.10 = (bf16[1,1,64,560]{3,2,1,0:T(8,128)(2,1)S(1)}, bf16[1,1,64,560]{3,2,1,0:T(8,128)(2,1)S(1)}, u32[]{:S(2)}, u32[]{:S(2)}) collective-permute-start(bf16[1,1,64,560]{3,2,1,0:T(8,128)(2,1)S(1)} %get-tuple-element.31), channel_id=1, source_target_pairs={{0,1},{1,0},{2,3},{3,2},{4,5},{5,4},{6,7},{7,6},{8,9},{9,8},{10,11... | collective-permute-start | bytes 215048 | tf_op jit(solution)/shard_map/ppermute | solution.py:81
  60.8 9.0 %collective-permute-start.13 = (bf16[1,1,4,64,560]{4,3,2,1,0:T(8,128)(2,1)S(1)}, bf16[1,1,4,64,560]{4,3,2,1,0:T(8,128)(2,1)S(1)}, u32[]{:S(2)}, u32[]{:S(2)}) collective-permute-start(bf16[1,1,4,64,560]{4,3,2,1,0:T(8,128)(2,1)S(1)} %maximum_bitcast_fusion), channel_id=1, source_target_pairs={{0,8},{4,12},{8,0},{12,4},{1,9},{5,13},{9,1},{13,5},{2,10},{6,14},... | collective-permute-start | bytes 860168 | tf_op jit(solution)/shard_map/ppermute | solution.py:92
  70.7 2.5 %collective-permute-start.14 = (bf16[2,1,4,64,560]{4,3,2,1,0:T(8,128)(2,1)}, bf16[2,1,4,64,560]{4,3,2,1,0:T(8,128)(2,1)}, u32[]{:S(2)}, u32[]{:S(2)}) collective-permute-start(bf16[2,1,4,64,560]{4,3,2,1,0:T(8,128)(2,1)} %pad_maximum_fusion.3), channel_id=1, source_target_pairs={{0,4},{4,0},{8,12},{12,8},{1,5},{5,1},{9,13},{13,9},{2,6},{6,2},{1... | collective-permute-start | bytes 1720328 | tf_op jit(solution)/shard_map/ppermute | solution.py:92
  74.7 1.6 copy-start.1
  80.7 0.8 copy-start.5
  148.2 3.3 %copy-start.8 = (bf16[840,2240]{1,0:T(8,128)(2,1)S(1)}, bf16[840,2240]{1,0:T(8,128)(2,1)}, u32[]{:S(2)}) copy-start(bf16[840,2240]{1,0:T(8,128)(2,1)} %param.17) | copy-start | bytes 11289604
  154.8 22.6 %collective-permute-start.18 = (bf16[64,2240]{1,0:T(8,128)(2,1)S(1)}, bf16[64,2240]{1,0:T(8,128)(2,1)S(1)}, u32[]{:S(2)}, u32[]{:S(2)}) collective-permute-start(bf16[64,2240]{1,0:T(8,128)(2,1)S(1)} %bitcast.123), channel_id=1, source_target_pairs={{0,3},{1,7},{2,11},{3,15},{4,2},{5,6},{6,10},{7,14},{8,1},{9,5},{1... | collective-permute-start | bytes 860168 | tf_op jit(solution)/shard_map/ppermute | solution.py:188
  156.3 27.8 %collective-permute-start.17 = (bf16[64,2240]{1,0:T(8,128)(2,1)S(1)}, bf16[64,2240]{1,0:T(8,128)(2,1)S(1)}, u32[]{:S(2)}, u32[]{:S(2)}) collective-permute-start(bf16[64,2240]{1,0:T(8,128)(2,1)S(1)} %bitcast.124), channel_id=1, source_target_pairs={{0,2},{1,6},{2,10},{3,14},{4,3},{5,7},{6,11},{7,15},{8,0},{9,4},{1... | collective-permute-start | bytes 860168 | tf_op jit(solution)/shard_map/ppermute | solution.py:188
  158.2 25.8 %collective-permute-start.16 = (bf16[64,2240]{1,0:T(8,128)(2,1)S(1)}, bf16[64,2240]{1,0:T(8,128)(2,1)S(1)}, u32[]{:S(2)}, u32[]{:S(2)}) collective-permute-start(bf16[64,2240]{1,0:T(8,128)(2,1)S(1)} %bitcast.125), channel_id=1, source_target_pairs={{0,1},{1,5},{2,9},{3,13},{4,0},{5,4},{6,8},{7,12},{8,3},{9,7},{10,... | collective-permute-start | bytes 860168 | tf_op jit(solution)/shard_map/ppermute | solution.py:188
  161.4 26.9 %collective-permute-start.15 = (bf16[64,2240]{1,0:T(8,128)(2,1)}, bf16[64,2240]{1,0:T(8,128)(2,1)S(1)}, u32[]{:S(2)}, u32[]{:S(2)}) collective-permute-start(bf16[64,2240]{1,0:T(8,128)(2,1)} %bitcast.126), channel_id=1, source_target_pairs={{0,0},{1,4},{2,8},{3,12},{4,1},{5,5},{6,9},{7,13},{8,2},{9,6},{10,... | collective-permute-start | bytes 860168 | tf_op jit(solution)/shard_map/ppermute | solution.py:188
Sparse Core Ops, SparseCore 0:
  80.9 64.8 reduce-scatter.1

commit v12 on v11

--- a/solution.py
+++ b/solution.py
@@ -97,6 +97,29 @@
         bit //= 2
     ordered = [by_mask[mask] for mask in range(count)]
     return [pick(ordered, own ^ source) for source in range(count)]
+
+
+def line_reduce_scatter(blocks, axis):
+    count = lax.axis_size(axis)
+    own = lax.axis_index(axis)
+    from_left = None
+    from_right = None
+    for step in range(1, count):
+        rightward = pick(blocks, jnp.minimum(count - step + own, count - 1)).astype(jnp.float32)
+        leftward = pick(blocks, jnp.maximum(own + step - count, 0)).astype(jnp.float32)
+        if from_left is not None:
+            rightward = rightward + from_left.astype(jnp.float32)
+            leftward = leftward + from_right.astype(jnp.float32)
+        from_left = lax.ppermute(
+            rightward.astype(jnp.bfloat16), axis, [(p, p + 1) for p in range(step)]
+        )
+        from_right = lax.ppermute(
+            leftward.astype(jnp.bfloat16), axis, [(p, p - 1) for p in range(count - step, count)]
+        )
+    mine = pick(blocks, own).astype(jnp.float32)
+    if from_left is None:
+        return mine
+    return mine + from_left.astype(jnp.float32) + from_right.astype(jnp.float32)
 
 
 def rms_norm(features):
@@ -168,7 +191,7 @@
         partial = jnp.dot(
             tokens.reshape(-1, local_depth), weight_flat, preferred_element_type=jnp.float32
         ).astype(jnp.bfloat16)
-        summed = lax.psum_scatter(partial, "row", scatter_dimension=0, tiled=True)
+        summed = line_reduce_scatter(jnp.split(partial, row_parts, axis=0), "row")
         frame_rows = tokens.shape[1]
         expanded = (
             jax.nn.silu(summed.astype(jnp.float32))

time: 197 us -> 217 us (1.10)
  starting transfers between devices: 23.6 us -> 40.5 us
  between operations: 14.6 us -> 1.25 us
  other arithmetic: 13.5 us -> 23.5 us
  waiting for transfers between devices: 121 us -> 128 us
    ppermute x0 -> x6, waiting for transfers between devices: none -> 70.7 us  [the longest x3 47.6 us: line_reduce_scatter(): lax.ppermute(rightward.astype(jnp.bfloat16), axis, [(p, p + 1) for p in r...]
    reduce_scatter x1 -> x0, waiting for transfers between devices: 63.6 us -> none  [local(): summed = lax.psum_scatter(partial, 'row', scatter_dimension=0, tiled=True)]
    ppermute x0 -> x6, starting transfers between devices: none -> 17.3 us  [the longest x3 12.7 us: line_reduce_scatter(): lax.ppermute(rightward.astype(jnp.bfloat16), axis, [(p, p + 1) for p in r...]
    convert_element_type x0 -> x3, other arithmetic: none -> 7.65 us  [the longest x2 5.36 us: line_reduce_scatter(): rightward.astype(jnp.bfloat16)]
  transfers between devices with their start and end apart: 20 -> 25, of which waited for: 16 -> 19; matrix products, arithmetic and copies ran while one was open for 3% -> 4% of each run, Pallas kernels for 0% -> 0%
where the time goes in v12:
time: 217 us; the launch traced here: 216 us
  waiting for transfers between devices  128 us (59%)
  starting transfers between devices  40.5 us (19%)
  other arithmetic  23.5 us (11%)
  local copies, waits for them, and re-layouts  16 us (7%)
  matrix products  7.28 us (3%)
    ppermute x3, waiting for transfers between devices, line_reduce_scatter(): lax.ppermute(rightward.astype(jnp.bfloat16), axis, [(p, p + 1) for p in r...  47.6 us
    ppermute x3, waiting for transfers between devices, line_reduce_scatter(): lax.ppermute(leftward.astype(jnp.bfloat16), axis, [(p, p - 1) for p in ra...  23.1 us
    ppermute x4, waiting for transfers between devices, local(): lax.ppermute(pick(row_blocks, frame_at ^ mask), ('frame', 'row'), [(f * r...  22.7 us
    ppermute x9, starting transfers between devices, swap_chunks(): lax.ppermute(sent, axis, [(i, i ^ mask) for i in range(count)])  13.4 us
    ppermute x9, waiting for transfers between devices, swap_chunks(): lax.ppermute(sent, axis, [(i, i ^ mask) for i in range(count)])  12.8 us
    ppermute x3, starting transfers between devices, line_reduce_scatter(): lax.ppermute(rightward.astype(jnp.bfloat16), axis, [(p, p + 1) for p in r...  12.7 us
    ppermute x4, starting transfers between devices, local(): lax.ppermute(pick(row_blocks, frame_at ^ mask), ('frame', 'row'), [(f * r...  8.41 us
    ppermute x2, waiting for transfers between devices, doubling_gather(): lax.ppermute(jnp.stack([by_mask[key] for key in keys]), axis, [(i, i ^ bi...  8.4 us
  transfers between devices with their start and end apart: 25, of which 19 were waited for; matrix products, arithmetic and copies ran while one was open for 4% of the time, Pallas kernels for 0%

profile of v12, /device:TPU:2, one launch (start us, length us, event | category | flops | bytes accessed | tf_op | source)
XLA Modules:
  0.0 216.0 jit_solution(4149905210454687132)
XLA Ops:
  8.6 5.8 %collective-permute-done.1 = bf16[113,560]{0,1:T(8,128)(2,1)S(1)} collective-permute-done((bf16[113,560]{0,1:T(8,128)(2,1)S(1)}, bf16[113,560]{0,1:T(8,128)(2,1)S(1)}, u32[]{:S(2)}, u32[]{:S(2)}) %collective-permute-start.1) | collective-permute-done | bytes 126592 | tf_op jit(solution)/shard_map/ppermute | solution.py:51
  14.6 3.7 %collective-permute-start.4 = (bf16[113,140]{0,1:T(8,128)(2,1)S(1)}, bf16[113,140]{0,1:T(8,128)(2,1)S(1)}, u32[]{:S(2)}, u32[]{:S(2)}) collective-permute-start(bf16[113,140]{0,1:T(8,128)(2,1)S(1)} %get-tuple-element.49), channel_id=1, source_target_pairs={{0,3},{1,2},{2,1},{3,0},{4,7},{5,6},{6,5},{7,4},{8,11},{9,10},{10,... | collective-permute-start | bytes 94928 | tf_op jit(solution)/shard_map/ppermute | solution.py:81
  19.0 1.6 collective-permute-done.4
  20.6 2.5 %collective-permute-done.3 = bf16[113,140]{0,1:T(8,128)(2,1)S(1)} collective-permute-done((bf16[113,140]{0,1:T(8,128)(2,1)S(1)}, bf16[113,140]{0,1:T(8,128)(2,1)S(1)}, u32[]{:S(2)}, u32[]{:S(2)}) %collective-permute-start.3) | collective-permute-done | bytes 31672 | tf_op jit(solution)/shard_map/ppermute | solution.py:81
  25.3 2.3 %collective-permute-start.5 = (bf16[113,140]{0,1:T(8,128)(2,1)S(1)}, bf16[113,140]{0,1:T(8,128)(2,1)S(1)}, u32[]{:S(2)}, u32[]{:S(2)}) collective-permute-start(bf16[113,140]{0,1:T(8,128)(2,1)S(1)} %fusion.31), channel_id=1, source_target_pairs={{0,1},{1,0},{2,3},{3,2},{4,5},{5,4},{6,7},{7,6},{8,9},{9,8},{10,11... | collective-permute-start | bytes 94928 | tf_op jit(solution)/shard_map/ppermute | solution.py:81
  30.7 4.6 %collective-permute-done.8 = bf16[113,560]{0,1:T(8,128)(2,1)S(1)} collective-permute-done((bf16[113,560]{0,1:T(8,128)(2,1)S(1)}, bf16[113,560]{0,1:T(8,128)(2,1)S(1)}, u32[]{:S(2)}, u32[]{:S(2)}) %collective-permute-start.8) | collective-permute-done | bytes 126592 | tf_op jit(solution)/shard_map/ppermute | solution.py:61
  44.4 2.4 %collective-permute-start.12 = (bf16[1,1,64,560]{3,2,1,0:T(8,128)(2,1)S(1)}, bf16[1,1,64,560]{3,2,1,0:T(8,128)(2,1)S(1)}, u32[]{:S(2)}, u32[]{:S(2)}) collective-permute-start(bf16[1,1,64,560]{3,2,1,0:T(8,128)(2,1)S(1)} %get-tuple-element.37), channel_id=1, source_target_pairs={{0,3},{1,2},{2,1},{3,0},{4,7},{5,6},{6,5},{7,4},{8,11},{9,10},{10,... | collective-permute-start | bytes 215048 | tf_op jit(solution)/shard_map/ppermute | solution.py:81
  48.9 2.8 %collective-permute-done.12 = bf16[1,1,64,560]{3,2,1,0:T(8,128)(2,1)S(1)} collective-permute-done((bf16[1,1,64,560]{3,2,1,0:T(8,128)(2,1)S(1)}, bf16[1,1,64,560]{3,2,1,0:T(8,128)(2,1)S(1)}, u32[]{:S(2)}, u32[]{:S(2)}) %collective-permute-start.12) | collective-permute-done | bytes 71712 | tf_op jit(solution)/shard_map/ppermute | solution.py:81
  51.7 3.6 %collective-permute-done.11 = bf16[1,1,64,560]{3,2,1,0:T(8,128)(2,1)S(1)} collective-permute-done((bf16[1,1,64,560]{3,2,1,0:T(8,128)(2,1)S(1)}, bf16[1,1,64,560]{3,2,1,0:T(8,128)(2,1)S(1)}, u32[]{:S(2)}, u32[]{:S(2)}) %collective-permute-start.11) | collective-permute-done | bytes 71712 | tf_op jit(solution)/shard_map/ppermute | solution.py:81
  56.1 8.4 %collective-permute-done.13 = bf16[1,1,4,64,560]{4,3,2,1,0:T(8,128)(2,1)S(1)} collective-permute-done((bf16[1,1,4,64,560]{4,3,2,1,0:T(8,128)(2,1)S(1)}, bf16[1,1,4,64,560]{4,3,2,1,0:T(8,128)(2,1)S(1)}, u32[]{:S(2)}, u32[]{:S(2)}) %collective-permute-start.13) | collective-permute-done | bytes 286752 | tf_op jit(solution)/shard_map/ppermute | solution.py:92
  65.4 2.5 %reshape.244 = bf16[560,1680]{1,0:T(8,128)(2,1)} reshape(bf16[560,2,840]{2,1,0:T(2,128)(2,1)S(1)} %copy-done) | data formatting | bytes 3763200 | tf_op jit(solution)/shard_map/reshape | solution.py:188
  70.0 3.1 %convolution_convert_fusion.1 = bf16[1024,1680]{0,1:T(8,128)(2,1)S(1)} fusion(bf16[1024,560]{1,0:T(8,128)(2,1)S(1)} %bitcast.148, bf16[560,1680]{1,0:T(8,128)(2,1)S(1)} %copy-done.1), kind=kOutput, calls=%fused_computation.1 | convolution fusion | flops 1928478720 | bytes 6469120 | tf_op jit(solution)/shard_map/dot_general | solution.py:191
  75.1 2.4 %collective-permute-start.15 = (bf16[256,1680]{0,1:T(8,128)(2,1)}, bf16[256,1680]{0,1:T(8,128)(2,1)}, u32[]{:S(2)}, u32[]{:S(2)}) collective-permute-start(bf16[256,1680]{0,1:T(8,128)(2,1)} %get-tuple-element.12), channel_id=1, source_target_pairs={{0,1},{4,5},{8,9},{12,13},{16,17},{20,21},{24,25},{28,29}} | collective-permute-start | bytes 2580488 | tf_op jit(solution)/shard_map/ppermute | solution.py:113
  79.1 17.1 %collective-permute-done.15 = bf16[256,1680]{0,1:T(8,128)(2,1)} collective-permute-done((bf16[256,1680]{0,1:T(8,128)(2,1)}, bf16[256,1680]{0,1:T(8,128)(2,1)}, u32[]{:S(2)}, u32[]{:S(2)}) %collective-permute-start.15) | collective-permute-done | bytes 860192 | tf_op jit(solution)/shard_map/ppermute | solution.py:113
  96.2 2.3 %fusion.2 = bf16[256,1680]{0,1:T(8,128)(2,1)} fusion(bf16[256,1680]{0,1:T(8,128)(2,1)} %collective-permute-done.15, bf16[4,256,1680]{1,2,0:T(8,128)(2,1)S(1)} %pad_maximum_fusion, s32[]{:T(128)S(6)} %select_n.123), kind=kLoop, calls=%fused_computation.10 | loop fusion | flops 1720320 | bytes 2580484 | tf_op jit(solution)/shard_map/convert_element_type | solution.py:114
  98.5 5.4 %collective-permute-start.16 = (bf16[256,1680]{0,1:T(8,128)(2,1)}, bf16[256,1680]{0,1:T(8,128)(2,1)}, u32[]{:S(2)}, u32[]{:S(2)}) collective-permute-start(bf16[256,1680]{0,1:T(8,128)(2,1)} %fusion.2), channel_id=1, source_target_pairs={{0,1},{1,2},{4,5},{5,6},{8,9},{9,10},{12,13},{13,14},{16,17},{17,1... | collective-permute-start | bytes 2580488 | tf_op jit(solution)/shard_map/ppermute | solution.py:113
  103.9 17.8 %collective-permute-done.16 = bf16[256,1680]{0,1:T(8,128)(2,1)} collective-permute-done((bf16[256,1680]{0,1:T(8,128)(2,1)}, bf16[256,1680]{0,1:T(8,128)(2,1)}, u32[]{:S(2)}, u32[]{:S(2)}) %collective-permute-start.16) | collective-permute-done | bytes 860192 | tf_op jit(solution)/shard_map/ppermute | solution.py:113
  121.7 3.1 %fusion.3 = (bf16[256,1680]{0,1:T(8,128)(2,1)}, bf16[256,1680]{0,1:T(8,128)(2,1)}) fusion(bf16[256,1680]{0,1:T(8,128)(2,1)} %collective-permute-done.16, bf16[4,256,1680]{1,2,0:T(8,128)(2,1)S(1)} %pad_maximum_fusion, s32[]{:T(128)S(6)} %select_n.122, bf16[256,1680]{0,1:T(8,128)(2,1)} %collective-permute-done.18, s32[]{:T(128)S(6)} %max.18), kind=kLoop, calls=%fused_computation.12 | loop fusion | flops 3440640 | bytes 5160968 | tf_op jit(solution)/shard_map/convert_element_type | solution.py:114
  124.8 1.7 collective-permute-start.19
  126.5 5.0 %collective-permute-start.17 = (bf16[256,1680]{0,1:T(8,128)(2,1)}, bf16[256,1680]{0,1:T(8,128)(2,1)}, u32[]{:S(2)}, u32[]{:S(2)}) collective-permute-start(bf16[256,1680]{0,1:T(8,128)(2,1)} %get-tuple-element.10), channel_id=1, source_target_pairs={{0,1},{1,2},{2,3},{4,5},{5,6},{6,7},{8,9},{9,10},{10,11},{12,13},{... | collective-permute-start | bytes 2580488 | tf_op jit(solution)/shard_map/ppermute | solution.py:113
  131.5 2.3 %fusion.1 = bf16[256,1680]{0,1:T(8,128)(2,1)} fusion(bf16[256,1680]{0,1:T(8,128)(2,1)} %collective-permute-done.19, bf16[4,256,1680]{1,2,0:T(8,128)(2,1)S(1)} %pad_maximum_fusion, s32[]{:T(128)S(6)} %max.17), kind=kLoop, calls=%fused_computation.8 | loop fusion | flops 1720320 | bytes 2580484 | tf_op jit(solution)/shard_map/convert_element_type | solution.py:117
  135.8 12.6 %collective-permute-done.17 = bf16[256,1680]{0,1:T(8,128)(2,1)} collective-permute-done((bf16[256,1680]{0,1:T(8,128)(2,1)}, bf16[256,1680]{0,1:T(8,128)(2,1)}, u32[]{:S(2)}, u32[]{:S(2)}) %collective-permute-start.17) | collective-permute-done | bytes 860192 | tf_op jit(solution)/shard_map/ppermute | solution.py:113
  148.5 23.1 %collective-permute-done.20 = bf16[256,1680]{0,1:T(8,128)(2,1)} collective-permute-done((bf16[256,1680]{0,1:T(8,128)(2,1)}, bf16[256,1680]{0,1:T(8,128)(2,1)}, u32[]{:S(2)}, u32[]{:S(2)}) %collective-permute-start.20) | collective-permute-done | bytes 860192 | tf_op jit(solution)/shard_map/ppermute | solution.py:116
  171.6 2.9 %multiply_convert_fusion = bf16[256,1680]{0,1:T(8,128)(2,1)} fusion(bf16[256,1680]{0,1:T(8,128)(2,1)} %collective-permute-done.20, bf16[256,1680]{0,1:T(8,128)(2,1)} %collective-permute-done.17, bf16[4,256,1680]{1,2,0:T(8,128)(2,1)S(1)} %pad_maximum_fusion, s32[]{:T(128)S(6)} %select_n.112), kind=kLoop, calls=%fused_computation.15 | loop fusion | flops 4300800 | bytes 3440644 | tf_op jit(solution)/shard_map/convert_element_type | solution.py:198
  176.1 2.7 %multiply_add_fusion = f32[1,4,64,1680]{3,2,1,0:T(8,128)S(1)} fusion(bf16[1,4,64,1680]{3,2,1,0:T(8,128)(2,1)S(1)} %bitcast.146, bf16[1,6,64,1680]{3,2,1,0:T(8,128)(2,1)S(1)} %pad.8, f32[1680]{0:T(1024)S(1)} %mul.211, f32[1680]{0:T(1024)S(1)} %mul.208, f32[1680]{0:T(1024)S(1)} %mul.205, f32[1680]{0:T(1024)S(1)} %mul.202, f32[1680]{0:T(1024)S(1)} %mul.199, ...), kind=kLoop, calls=%fused_computation.4 | loop fusion | flops 11182080 | bytes 5922816 | tf_op jit(solution)/shard_map/add | solution.py:137
  179.2 1.8 convolution_convert_fusion
  182.5 1.8 collective-permute-start.24
  184.9 3.3 %collective-permute-start.22 = (bf16[64,2240]{1,0:T(8,128)(2,1)S(1)}, bf16[64,2240]{1,0:T(8,128)(2,1)S(1)}, u32[]{:S(2)}, u32[]{:S(2)}) collective-permute-start(bf16[64,2240]{1,0:T(8,128)(2,1)S(1)} %bitcast.152), channel_id=1, source_target_pairs={{0,1},{1,5},{2,9},{3,13},{4,0},{5,4},{6,8},{7,12},{8,3},{9,7},{10,... | collective-permute-start | bytes 860168 | tf_op jit(solution)/shard_map/ppermute | solution.py:211
  189.1 3.2 %collective-permute-start.21 = (bf16[64,2240]{1,0:T(8,128)(2,1)}, bf16[64,2240]{1,0:T(8,128)(2,1)S(1)}, u32[]{:S(2)}, u32[]{:S(2)}) collective-permute-start(bf16[64,2240]{1,0:T(8,128)(2,1)} %bitcast.153), channel_id=1, source_target_pairs={{0,0},{1,4},{2,8},{3,12},{4,1},{5,5},{6,9},{7,13},{8,2},{9,6},{10,... | collective-permute-start | bytes 860168 | tf_op jit(solution)/shard_map/ppermute | solution.py:211
  192.4 11.0 %collective-permute-done.24 = bf16[64,2240]{1,0:T(8,128)(2,1)S(1)} collective-permute-done((bf16[64,2240]{1,0:T(8,128)(2,1)S(1)}, bf16[64,2240]{1,0:T(8,128)(2,1)S(1)}, u32[]{:S(2)}, u32[]{:S(2)}) %collective-permute-start.24) | collective-permute-done | bytes 286752 | tf_op jit(solution)/shard_map/ppermute | solution.py:211
  203.4 6.4 %collective-permute-done.23 = bf16[64,2240]{1,0:T(8,128)(2,1)S(1)} collective-permute-done((bf16[64,2240]{1,0:T(8,128)(2,1)S(1)}, bf16[64,2240]{1,0:T(8,128)(2,1)S(1)}, u32[]{:S(2)}, u32[]{:S(2)}) %collective-permute-start.23) | collective-permute-done | bytes 286752 | tf_op jit(solution)/shard_map/ppermute | solution.py:211
  209.8 5.3 %collective-permute-done.21 = bf16[64,2240]{1,0:T(8,128)(2,1)S(1)} collective-permute-done((bf16[64,2240]{1,0:T(8,128)(2,1)}, bf16[64,2240]{1,0:T(8,128)(2,1)S(1)}, u32[]{:S(2)}, u32[]{:S(2)}) %collective-permute-start.21) | collective-permute-done | bytes 286752 | tf_op jit(solution)/shard_map/ppermute | solution.py:211
  (124 shorter events, 40.2 us)
Async XLA Ops:
  0.6 2.5 %copy-start.5 = (bf16[1,1,64,2240]{3,2,1,0:T(8,128)(2,1)S(1)}, bf16[1,1,64,2240]{3,2,1,0:T(8,128)(2,1)}, u32[]{:S(2)}) copy-start(bf16[1,1,64,2240]{3,2,1,0:T(8,128)(2,1)} %param.11) | copy-start | bytes 860164
  5.0 1.6 collective-permute-start
  8.5 5.9 %collective-permute-start.1 = (bf16[113,560]{0,1:T(8,128)(2,1)S(1)}, bf16[113,560]{0,1:T(8,128)(2,1)S(1)}, u32[]{:S(2)}, u32[]{:S(2)}) collective-permute-start(bf16[113,560]{0,1:T(8,128)(2,1)S(1)} %select_convert_fusion.1), channel_id=1, source_target_pairs={{0,8},{4,12},{8,0},{12,4},{1,9},{5,13},{9,1},{13,5},{2,10},{6,14},... | collective-permute-start | bytes 379688 | tf_op jit(solution)/shard_map/ppermute | solution.py:51
  14.6 6.1 %collective-permute-start.4 = (bf16[113,140]{0,1:T(8,128)(2,1)S(1)}, bf16[113,140]{0,1:T(8,128)(2,1)S(1)}, u32[]{:S(2)}, u32[]{:S(2)}) collective-permute-start(bf16[113,140]{0,1:T(8,128)(2,1)S(1)} %get-tuple-element.49), channel_id=1, source_target_pairs={{0,3},{1,2},{2,1},{3,0},{4,7},{5,6},{6,5},{7,4},{8,11},{9,10},{10,... | collective-permute-start | bytes 94928 | tf_op jit(solution)/shard_map/ppermute | solution.py:81
  18.2 4.9 %collective-permute-start.3 = (bf16[113,140]{0,1:T(8,128)(2,1)S(1)}, bf16[113,140]{0,1:T(8,128)(2,1)S(1)}, u32[]{:S(2)}, u32[]{:S(2)}) collective-permute-start(bf16[113,140]{0,1:T(8,128)(2,1)S(1)} %get-tuple-element.50), channel_id=1, source_target_pairs={{0,2},{1,3},{2,0},{3,1},{4,6},{5,7},{6,4},{7,5},{8,10},{9,11},{10,... | collective-permute-start | bytes 94928 | tf_op jit(solution)/shard_map/ppermute | solution.py:81
  18.2 4.9 %collective-permute-start.2 = (bf16[113,140]{0,1:T(8,128)(2,1)S(1)}, bf16[113,140]{0,1:T(8,128)(2,1)S(1)}, u32[]{:S(2)}, u32[]{:S(2)}) collective-permute-start(bf16[113,140]{0,1:T(8,128)(2,1)S(1)} %get-tuple-element.51), channel_id=1, source_target_pairs={{0,1},{1,0},{2,3},{3,2},{4,5},{5,4},{6,7},{7,6},{8,9},{9,8},{10,11... | collective-permute-start | bytes 94928 | tf_op jit(solution)/shard_map/ppermute | solution.py:81
  23.2 5.8 %collective-permute-start.7 = (bf16[113,140]{0,1:T(8,128)(2,1)S(1)}, bf16[113,140]{0,1:T(8,128)(2,1)S(1)}, u32[]{:S(2)}, u32[]{:S(2)}) collective-permute-start(bf16[113,140]{0,1:T(8,128)(2,1)S(1)} %fusion.31), channel_id=1, source_target_pairs={{0,3},{1,2},{2,1},{3,0},{4,7},{5,6},{6,5},{7,4},{8,11},{9,10},{10,... | collective-permute-start | bytes 94928 | tf_op jit(solution)/shard_map/ppermute | solution.py:81
  24.7 4.9 %collective-permute-start.6 = (bf16[113,140]{0,1:T(8,128)(2,1)S(1)}, bf16[113,140]{0,1:T(8,128)(2,1)S(1)}, u32[]{:S(2)}, u32[]{:S(2)}) collective-permute-start(bf16[113,140]{0,1:T(8,128)(2,1)S(1)} %fusion.31), channel_id=1, source_target_pairs={{0,2},{1,3},{2,0},{3,1},{4,6},{5,7},{6,4},{7,5},{8,10},{9,11},{10,... | collective-permute-start | bytes 94928 | tf_op jit(solution)/shard_map/ppermute | solution.py:81
  25.3 4.6 %collective-permute-start.5 = (bf16[113,140]{0,1:T(8,128)(2,1)S(1)}, bf16[113,140]{0,1:T(8,128)(2,1)S(1)}, u32[]{:S(2)}, u32[]{:S(2)}) collective-permute-start(bf16[113,140]{0,1:T(8,128)(2,1)S(1)} %fusion.31), channel_id=1, source_target_pairs={{0,1},{1,0},{2,3},{3,2},{4,5},{5,4},{6,7},{7,6},{8,9},{9,8},{10,11... | collective-permute-start | bytes 94928 | tf_op jit(solution)/shard_map/ppermute | solution.py:81
  30.1 6.5 %copy-start.4 = (bf16[1,1,64,2240]{3,2,1,0:T(8,128)(2,1)S(1)}, bf16[1,1,64,2240]{3,2,1,0:T(8,128)(2,1)}, u32[]{:S(2)}) copy-start(bf16[1,1,64,2240]{3,2,1,0:T(8,128)(2,1)} %param.9) | copy-start | bytes 860164
  30.1 5.2 %collective-permute-start.8 = (bf16[113,560]{0,1:T(8,128)(2,1)S(1)}, bf16[113,560]{0,1:T(8,128)(2,1)S(1)}, u32[]{:S(2)}, u32[]{:S(2)}) collective-permute-start(bf16[113,560]{0,1:T(8,128)(2,1)S(1)} %pad_maximum_fusion.11), channel_id=1, source_target_pairs={{0,8},{4,12},{8,0},{12,4},{1,9},{5,13},{9,1},{13,5},{2,10},{6,14},... | collective-permute-start | bytes 379688 | tf_op jit(solution)/shard_map/ppermute | solution.py:61
  36.5 1.6 collective-permute-start.9
  44.4 21.1 %copy-start = (bf16[560,2,840]{2,1,0:T(2,128)(2,1)S(1)}, bf16[560,2,840]{2,1,0:T(2,128)(2,1)}, u32[]{:S(2)}) copy-start(bf16[560,2,840]{2,1,0:T(2,128)(2,1)} %param.15) | copy-start | bytes 5644804
  44.4 7.3 %collective-permute-start.12 = (bf16[1,1,64,560]{3,2,1,0:T(8,128)(2,1)S(1)}, bf16[1,1,64,560]{3,2,1,0:T(8,128)(2,1)S(1)}, u32[]{:S(2)}, u32[]{:S(2)}) collective-permute-start(bf16[1,1,64,560]{3,2,1,0:T(8,128)(2,1)S(1)} %get-tuple-element.37), channel_id=1, source_target_pairs={{0,3},{1,2},{2,1},{3,0},{4,7},{5,6},{6,5},{7,4},{8,11},{9,10},{10,... | collective-permute-start | bytes 215048 | tf_op jit(solution)/shard_map/ppermute | solution.py:81
  46.9 8.5 %collective-permute-start.11 = (bf16[1,1,64,560]{3,2,1,0:T(8,128)(2,1)S(1)}, bf16[1,1,64,560]{3,2,1,0:T(8,128)(2,1)S(1)}, u32[]{:S(2)}, u32[]{:S(2)}) collective-permute-start(bf16[1,1,64,560]{3,2,1,0:T(8,128)(2,1)S(1)} %get-tuple-element.38), channel_id=1, source_target_pairs={{0,2},{1,3},{2,0},{3,1},{4,6},{5,7},{6,4},{7,5},{8,10},{9,11},{10,... | collective-permute-start | bytes 215048 | tf_op jit(solution)/shard_map/ppermute | solution.py:81
  47.6 7.7 %collective-permute-start.10 = (bf16[1,1,64,560]{3,2,1,0:T(8,128)(2,1)S(1)}, bf16[1,1,64,560]{3,2,1,0:T(8,128)(2,1)S(1)}, u32[]{:S(2)}, u32[]{:S(2)}) collective-permute-start(bf16[1,1,64,560]{3,2,1,0:T(8,128)(2,1)S(1)} %get-tuple-element.39), channel_id=1, source_target_pairs={{0,1},{1,0},{2,3},{3,2},{4,5},{5,4},{6,7},{7,6},{8,9},{9,8},{10,11... | collective-permute-start | bytes 215048 | tf_op jit(solution)/shard_map/ppermute | solution.py:81
  55.5 9.0 %collective-permute-start.13 = (bf16[1,1,4,64,560]{4,3,2,1,0:T(8,128)(2,1)S(1)}, bf16[1,1,4,64,560]{4,3,2,1,0:T(8,128)(2,1)S(1)}, u32[]{:S(2)}, u32[]{:S(2)}) collective-permute-start(bf16[1,1,4,64,560]{4,3,2,1,0:T(8,128)(2,1)S(1)} %maximum_bitcast_fusion), channel_id=1, source_target_pairs={{0,8},{4,12},{8,0},{12,4},{1,9},{5,13},{9,1},{13,5},{2,10},{6,14},... | collective-permute-start | bytes 860168 | tf_op jit(solution)/shard_map/ppermute | solution.py:92
  65.4 2.5 %collective-permute-start.14 = (bf16[2,1,4,64,560]{4,3,2,1,0:T(8,128)(2,1)}, bf16[2,1,4,64,560]{4,3,2,1,0:T(8,128)(2,1)S(1)}, u32[]{:S(2)}, u32[]{:S(2)}) collective-permute-start(bf16[2,1,4,64,560]{4,3,2,1,0:T(8,128)(2,1)} %pad_maximum_fusion.4), channel_id=1, source_target_pairs={{0,4},{4,0},{8,12},{12,8},{1,5},{5,1},{9,13},{13,9},{2,6},{6,2},{1... | collective-permute-start | bytes 1720328 | tf_op jit(solution)/shard_map/ppermute | solution.py:92
  68.4 1.6 copy-start.1
  75.1 21.1 %collective-permute-start.15 = (bf16[256,1680]{0,1:T(8,128)(2,1)}, bf16[256,1680]{0,1:T(8,128)(2,1)}, u32[]{:S(2)}, u32[]{:S(2)}) collective-permute-start(bf16[256,1680]{0,1:T(8,128)(2,1)} %get-tuple-element.12), channel_id=1, source_target_pairs={{0,1},{4,5},{8,9},{12,13},{16,17},{20,21},{24,25},{28,29}} | collective-permute-start | bytes 2580488 | tf_op jit(solution)/shard_map/ppermute | solution.py:113
  77.5 26.4 %collective-permute-start.18 = (bf16[256,1680]{0,1:T(8,128)(2,1)}, bf16[256,1680]{0,1:T(8,128)(2,1)}, u32[]{:S(2)}, u32[]{:S(2)}) collective-permute-start(bf16[256,1680]{0,1:T(8,128)(2,1)} %get-tuple-element.13), channel_id=1, source_target_pairs={{3,2},{7,6},{11,10},{15,14},{19,18},{23,22},{27,26},{31,30}} | collective-permute-start | bytes 2580488 | tf_op jit(solution)/shard_map/ppermute | solution.py:116
  98.5 23.2 %collective-permute-start.16 = (bf16[256,1680]{0,1:T(8,128)(2,1)}, bf16[256,1680]{0,1:T(8,128)(2,1)}, u32[]{:S(2)}, u32[]{:S(2)}) collective-permute-start(bf16[256,1680]{0,1:T(8,128)(2,1)} %fusion.2), channel_id=1, source_target_pairs={{0,1},{1,2},{4,5},{5,6},{8,9},{9,10},{12,13},{13,14},{16,17},{17,1... | collective-permute-start | bytes 2580488 | tf_op jit(solution)/shard_map/ppermute | solution.py:113
  124.8 10.3 %copy-start.7 = (bf16[9,2,840]{2,1,0:T(2,128)(2,1)S(1)}, bf16[9,2,840]{2,1,0:T(2,128)(2,1)}, u32[]{:S(2)}) copy-start(bf16[9,2,840]{2,1,0:T(2,128)(2,1)} %param.16) | copy-start | bytes 90724
  124.8 6.7 %collective-permute-start.19 = (bf16[256,1680]{0,1:T(8,128)(2,1)}, bf16[256,1680]{0,1:T(8,128)(2,1)}, u32[]{:S(2)}, u32[]{:S(2)}) collective-permute-start(bf16[256,1680]{0,1:T(8,128)(2,1)} %get-tuple-element.11), channel_id=1, source_target_pairs={{2,1},{3,2},{6,5},{7,6},{10,9},{11,10},{14,13},{15,14},{18,17},{19... | collective-permute-start | bytes 2580488 | tf_op jit(solution)/shard_map/ppermute | solution.py:116
  126.5 22.0 %collective-permute-start.17 = (bf16[256,1680]{0,1:T(8,128)(2,1)}, bf16[256,1680]{0,1:T(8,128)(2,1)}, u32[]{:S(2)}, u32[]{:S(2)}) collective-permute-start(bf16[256,1680]{0,1:T(8,128)(2,1)} %get-tuple-element.10), channel_id=1, source_target_pairs={{0,1},{1,2},{2,3},{4,5},{5,6},{6,7},{8,9},{9,10},{10,11},{12,13},{... | collective-permute-start | bytes 2580488 | tf_op jit(solution)/shard_map/ppermute | solution.py:113
  133.8 37.8 %collective-permute-start.20 = (bf16[256,1680]{0,1:T(8,128)(2,1)}, bf16[256,1680]{0,1:T(8,128)(2,1)}, u32[]{:S(2)}, u32[]{:S(2)}) collective-permute-start(bf16[256,1680]{0,1:T(8,128)(2,1)} %fusion.1), channel_id=1, source_target_pairs={{1,0},{2,1},{3,2},{5,4},{6,5},{7,6},{9,8},{10,9},{11,10},{13,12},{... | collective-permute-start | bytes 2580488 | tf_op jit(solution)/shard_map/ppermute | solution.py:116
  176.1 3.1 %copy-start.10 = (bf16[840,2240]{1,0:T(8,128)(2,1)S(1)}, bf16[840,2240]{1,0:T(8,128)(2,1)}, u32[]{:S(2)}) copy-start(bf16[840,2240]{1,0:T(8,128)(2,1)} %param.17) | copy-start | bytes 11289604
  182.3 32.8 %copy-start.3 = (bf16[64,2240]{1,0:T(8,128)(2,1)S(1)}, bf16[64,2240]{1,0:T(8,128)(2,1)}, u32[]{:S(2)}) copy-start(bf16[64,2240]{1,0:T(8,128)(2,1)} %get-tuple-element.5) | copy-start | bytes 860164
  182.5 20.8 %collective-permute-start.24 = (bf16[64,2240]{1,0:T(8,128)(2,1)S(1)}, bf16[64,2240]{1,0:T(8,128)(2,1)S(1)}, u32[]{:S(2)}, u32[]{:S(2)}) collective-permute-start(bf16[64,2240]{1,0:T(8,128)(2,1)S(1)} %bitcast.150), channel_id=1, source_target_pairs={{0,3},{1,7},{2,11},{3,15},{4,2},{5,6},{6,10},{7,14},{8,1},{9,5},{1... | collective-permute-start | bytes 860168 | tf_op jit(solution)/shard_map/ppermute | solution.py:211
  184.6 25.2 %collective-permute-start.23 = (bf16[64,2240]{1,0:T(8,128)(2,1)S(1)}, bf16[64,2240]{1,0:T(8,128)(2,1)S(1)}, u32[]{:S(2)}, u32[]{:S(2)}) collective-permute-start(bf16[64,2240]{1,0:T(8,128)(2,1)S(1)} %bitcast.151), channel_id=1, source_target_pairs={{0,2},{1,6},{2,10},{3,14},{4,3},{5,7},{6,11},{7,15},{8,0},{9,4},{1... | collective-permute-start | bytes 860168 | tf_op jit(solution)/shard_map/ppermute | solution.py:211
  184.9 24.9 %collective-permute-start.22 = (bf16[64,2240]{1,0:T(8,128)(2,1)S(1)}, bf16[64,2240]{1,0:T(8,128)(2,1)S(1)}, u32[]{:S(2)}, u32[]{:S(2)}) collective-permute-start(bf16[64,2240]{1,0:T(8,128)(2,1)S(1)} %bitcast.152), channel_id=1, source_target_pairs={{0,1},{1,5},{2,9},{3,13},{4,0},{5,4},{6,8},{7,12},{8,3},{9,7},{10,... | collective-permute-start | bytes 860168 | tf_op jit(solution)/shard_map/ppermute | solution.py:211
  189.1 25.9 %collective-permute-start.21 = (bf16[64,2240]{1,0:T(8,128)(2,1)}, bf16[64,2240]{1,0:T(8,128)(2,1)S(1)}, u32[]{:S(2)}, u32[]{:S(2)}) collective-permute-start(bf16[64,2240]{1,0:T(8,128)(2,1)} %bitcast.153), channel_id=1, source_target_pairs={{0,0},{1,4},{2,8},{3,12},{4,1},{5,5},{6,9},{7,13},{8,2},{9,6},{10,... | collective-permute-start | bytes 860168 | tf_op jit(solution)/shard_map/ppermute | solution.py:211
  (4 other events, 3.2 us)

commit v13 on v11

--- a/solution.py
+++ b/solution.py
@@ -97,6 +97,18 @@
         bit //= 2
     ordered = [by_mask[mask] for mask in range(count)]
     return [pick(ordered, own ^ source) for source in range(count)]
+
+
+def exchange_sum(block, axes):
+    for axis in axes:
+        count = lax.axis_size(axis)
+        pieces = [piece.astype(jnp.bfloat16) for piece in jnp.split(block, count, axis=1)]
+        block = sum(piece.astype(jnp.float32) for piece in swap_chunks(pieces, axis))
+    block = block.astype(jnp.bfloat16)
+    for axis in reversed(axes):
+        count = lax.axis_size(axis)
+        block = jnp.concatenate(swap_chunks([block] * count, axis), axis=1)
+    return block.astype(jnp.float32)
 
 
 def rms_norm(features):
@@ -129,12 +141,10 @@
     ).reshape(HEAD_DIM, model_width)
     local_total = jnp.sum(key_pos.reshape(token_count, model_width), axis=0, dtype=jnp.float32)
     stats = jnp.concatenate([local_state, local_total[None, :]], axis=0)
-    parts = 1
-    for axis, count, bit in exchange_steps(("frame", "row")):
-        parts *= 2
+    parts = lax.axis_size("frame") * lax.axis_size("row")
     padded_width = -(-model_width // parts) * parts
     stats = jnp.pad(stats, ((0, 0), (0, padded_width - model_width)))
-    stats = halving_sum(stats, ("frame",), inner_axis="row")[:, :model_width]
+    stats = exchange_sum(stats, ("frame", "row"))[:, :model_width]
     kv_state, key_total = stats[:HEAD_DIM], stats[HEAD_DIM]
     query_pos = jnp.maximum(query_in, 0).reshape(token_count, HEADS, HEAD_DIM).astype(jnp.float32)
     numerator = jnp.einsum(

time: 197 us -> 197 us (level)
  starting transfers between devices: 23.6 us -> 27.8 us
    ppermute x4 -> x0, waiting for transfers between devices: 13.1 us -> none  [the longest x2 7.45 us: halving_sum(): lax.ppermute(sent, axis, [(i, i ^ bit) for i in range(count)])]
    ppermute x9 -> x15, waiting for transfers between devices: 12.8 us -> 25.6 us  [swap_chunks(): lax.ppermute(sent, axis, [(i, i ^ mask) for i in range(count)])]
    ppermute x9 -> x15, starting transfers between devices: 13.4 us -> 17.2 us  [swap_chunks(): lax.ppermute(sent, axis, [(i, i ^ mask) for i in range(count)])]
  transfers between devices with their start and end apart: 20 -> 22, of which waited for: 16 -> 16; matrix products, arithmetic and copies ran while one was open for 3% -> 2% of each run, Pallas kernels for 0% -> 0%
where the time goes in v13:
time: 197 us
  waiting for transfers between devices  121 us (61%)
  starting transfers between devices  27.8 us (14%)
  between operations  14.5 us (7%)
  local copies, waits for them, and re-layouts  13.5 us (7%)
  other arithmetic  12.5 us (6%)
  matrix products  7.5 us (4%)
    reduce_scatter x1, waiting for transfers between devices, local(): summed = lax.psum_scatter(partial, 'row', scatter_dimension=0, tiled=True)  63.2 us
    ppermute x15, waiting for transfers between devices, swap_chunks(): lax.ppermute(sent, axis, [(i, i ^ mask) for i in range(count)])  25.6 us
    ppermute x4, waiting for transfers between devices, local(): lax.ppermute(pick(row_blocks, frame_at ^ mask), ('frame', 'row'), [(f * r...  24 us
    ppermute x15, starting transfers between devices, swap_chunks(): lax.ppermute(sent, axis, [(i, i ^ mask) for i in range(count)])  17.2 us
    ppermute x4, starting transfers between devices, local(): lax.ppermute(pick(row_blocks, frame_at ^ mask), ('frame', 'row'), [(f * r...  8.85 us
    ppermute x2, waiting for transfers between devices, doubling_gather(): lax.ppermute(jnp.stack([by_mask[key] for key in keys]), axis, [(i, i ^ bi...  7.78 us
    dot_general x1, matrix products, local(): jnp.dot(tokens.reshape(-1, local_depth), weight_flat, preferred_element_t...  4.45 us
  transfers between devices with their start and end apart: 22, of which 16 were waited for; matrix products, arithmetic and copies ran while one was open for 2% of the time, Pallas kernels for 0%

profile of v13, /device:TPU:2, one launch (start us, length us, event | category | flops | bytes accessed | tf_op | source)
XLA Modules:
  0.0 196.5 jit_solution(11233742960926726491)
XLA Ops:
  9.6 1.4 reshape.229
  12.8 1.5 collective-permute-start.1
  14.6 4.2 %collective-permute-done.2 = bf16[113,560]{0,1:T(8,128)(2,1)S(1)} collective-permute-done((bf16[113,560]{0,1:T(8,128)(2,1)S(1)}, bf16[113,560]{0,1:T(8,128)(2,1)S(1)}, u32[]{:S(2)}, u32[]{:S(2)}) %collective-permute-start.2) | collective-permute-done | bytes 126592 | tf_op jit(solution)/shard_map/ppermute | solution.py:81
  18.8 3.1 %collective-permute-done.1 = bf16[113,560]{0,1:T(8,128)(2,1)S(1)} collective-permute-done((bf16[113,560]{0,1:T(8,128)(2,1)S(1)}, bf16[113,560]{0,1:T(8,128)(2,1)S(1)}, u32[]{:S(2)}, u32[]{:S(2)}) %collective-permute-start.1) | collective-permute-done | bytes 126592 | tf_op jit(solution)/shard_map/ppermute | solution.py:81
  22.3 3.7 %collective-permute-start.5 = (bf16[113,140]{0,1:T(8,128)(2,1)S(1)}, bf16[113,140]{0,1:T(8,128)(2,1)S(1)}, u32[]{:S(2)}, u32[]{:S(2)}) collective-permute-start(bf16[113,140]{0,1:T(8,128)(2,1)S(1)} %get-tuple-element.49), channel_id=1, source_target_pairs={{0,3},{1,2},{2,1},{3,0},{4,7},{5,6},{6,5},{7,4},{8,11},{9,10},{10,... | collective-permute-start | bytes 94928 | tf_op jit(solution)/shard_map/ppermute | solution.py:81
  26.8 1.4 collective-permute-done.5
  28.1 2.7 %collective-permute-done.4 = bf16[113,140]{0,1:T(8,128)(2,1)S(1)} collective-permute-done((bf16[113,140]{0,1:T(8,128)(2,1)S(1)}, bf16[113,140]{0,1:T(8,128)(2,1)S(1)}, u32[]{:S(2)}, u32[]{:S(2)}) %collective-permute-start.4) | collective-permute-done | bytes 31672 | tf_op jit(solution)/shard_map/ppermute | solution.py:81
  30.9 1.7 collective-permute-start.8
  33.1 2.3 %collective-permute-start.6 = (bf16[113,140]{0,1:T(8,128)(2,1)S(1)}, bf16[113,140]{0,1:T(8,128)(2,1)S(1)}, u32[]{:S(2)}, u32[]{:S(2)}) collective-permute-start(bf16[113,140]{0,1:T(8,128)(2,1)S(1)} %fusion.30), channel_id=1, source_target_pairs={{0,1},{1,0},{2,3},{3,2},{4,5},{5,4},{6,7},{7,6},{8,9},{9,8},{10,11... | collective-permute-start | bytes 94928 | tf_op jit(solution)/shard_map/ppermute | solution.py:81
  35.4 1.4 collective-permute-done.8
  40.3 3.6 %collective-permute-done.11 = bf16[113,560]{0,1:T(8,128)(2,1)S(1)} collective-permute-done((bf16[113,560]{0,1:T(8,128)(2,1)S(1)}, bf16[113,560]{0,1:T(8,128)(2,1)S(1)}, u32[]{:S(2)}, u32[]{:S(2)}) %collective-permute-start.11) | collective-permute-done | bytes 126592 | tf_op jit(solution)/shard_map/ppermute | solution.py:81
  44.0 1.3 collective-permute-done.10
  49.6 2.4 %collective-permute-start.14 = (bf16[1,1,64,560]{3,2,1,0:T(8,128)(2,1)S(1)}, bf16[1,1,64,560]{3,2,1,0:T(8,128)(2,1)S(1)}, u32[]{:S(2)}, u32[]{:S(2)}) collective-permute-start(bf16[1,1,64,560]{3,2,1,0:T(8,128)(2,1)S(1)} %get-tuple-element.37), channel_id=1, source_target_pairs={{0,3},{1,2},{2,1},{3,0},{4,7},{5,6},{6,5},{7,4},{8,11},{9,10},{10,... | collective-permute-start | bytes 215048 | tf_op jit(solution)/shard_map/ppermute | solution.py:81
  52.7 1.3 collective-permute-start.12
  54.0 2.8 %collective-permute-done.14 = bf16[1,1,64,560]{3,2,1,0:T(8,128)(2,1)S(1)} collective-permute-done((bf16[1,1,64,560]{3,2,1,0:T(8,128)(2,1)S(1)}, bf16[1,1,64,560]{3,2,1,0:T(8,128)(2,1)S(1)}, u32[]{:S(2)}, u32[]{:S(2)}) %collective-permute-start.14) | collective-permute-done | bytes 71712 | tf_op jit(solution)/shard_map/ppermute | solution.py:81
  56.8 4.2 %collective-permute-done.13 = bf16[1,1,64,560]{3,2,1,0:T(8,128)(2,1)S(1)} collective-permute-done((bf16[1,1,64,560]{3,2,1,0:T(8,128)(2,1)S(1)}, bf16[1,1,64,560]{3,2,1,0:T(8,128)(2,1)S(1)}, u32[]{:S(2)}, u32[]{:S(2)}) %collective-permute-start.13) | collective-permute-done | bytes 71712 | tf_op jit(solution)/shard_map/ppermute | solution.py:81
  61.2 1.8 collective-permute-start.15
  63.0 7.8 %collective-permute-done.15 = bf16[1,1,4,64,560]{4,3,2,1,0:T(8,128)(2,1)S(1)} collective-permute-done((bf16[1,1,4,64,560]{4,3,2,1,0:T(8,128)(2,1)S(1)}, bf16[1,1,4,64,560]{4,3,2,1,0:T(8,128)(2,1)S(1)}, u32[]{:S(2)}, u32[]{:S(2)}) %collective-permute-start.15) | collective-permute-done | bytes 286752 | tf_op jit(solution)/shard_map/ppermute | solution.py:92
  71.7 2.5 %reshape.236 = bf16[560,1680]{1,0:T(8,128)(2,1)} reshape(bf16[560,2,840]{2,1,0:T(2,128)(2,1)S(1)} %copy-done) | data formatting | bytes 3763200 | tf_op jit(solution)/shard_map/reshape | solution.py:175
  76.0 1.3 copy-done.1
  77.3 4.5 %convolution_convert_fusion.1 = bf16[1024,1680]{0,1:T(8,128)(2,1)} fusion(bf16[1024,560]{1,0:T(8,128)(2,1)S(1)} %bitcast.152, bf16[560,1680]{1,0:T(8,128)(2,1)S(1)} %copy-done.1), kind=kOutput, calls=%fused_computation.1 | convolution fusion | flops 1928478720 | bytes 6469120 | tf_op jit(solution)/shard_map/dot_general | solution.py:178
  83.2 63.2 %reduce-scatter.2.cloned.1.call-done = bf16[256,1680]{0,1:T(8,128)(2,1)} async-done(((bf16[1024,1680]{0,1:T(8,128)(2,1)}), bf16[256,1680]{0,1:T(8,128)(2,1)}) %reduce-scatter.2.cloned.1.call-update) | async-done | bytes 860176 | tf_op jit(solution)/shard_map/reduce_scatter | solution.py:181
  146.4 1.6 fusion.3
  148.8 2.7 %multiply_add_fusion = f32[1,4,64,1680]{3,2,1,0:T(8,128)S(1)} fusion(bf16[1,4,64,1680]{3,2,1,0:T(8,128)(2,1)S(1)} %bitcast.149, bf16[1,6,64,1680]{3,2,1,0:T(8,128)(2,1)S(1)} %pad.8, f32[1680]{0:T(1024)S(1)} %mul.211, f32[1680]{0:T(1024)S(1)} %mul.208, f32[1680]{0:T(1024)S(1)} %mul.205, f32[1680]{0:T(1024)S(1)} %mul.202, f32[1680]{0:T(1024)S(1)} %mul.199, ...), kind=kLoop, calls=%fused_computation.5 | loop fusion | flops 11182080 | bytes 5922816 | tf_op jit(solution)/shard_map/add | solution.py:126
  151.9 1.8 convolution_convert_fusion
  155.2 1.3 collective-permute-start.20
  156.7 1.7 collective-permute-start.19
  158.6 2.2 %collective-permute-start.18 = (bf16[64,2240]{1,0:T(8,128)(2,1)S(1)}, bf16[64,2240]{1,0:T(8,128)(2,1)S(1)}, u32[]{:S(2)}, u32[]{:S(2)}) collective-permute-start(bf16[64,2240]{1,0:T(8,128)(2,1)S(1)} %bitcast.156), channel_id=1, source_target_pairs={{0,1},{1,5},{2,9},{3,13},{4,0},{5,4},{6,8},{7,12},{8,3},{9,7},{10,... | collective-permute-start | bytes 860168 | tf_op jit(solution)/shard_map/ppermute | solution.py:198
  161.1 3.7 %collective-permute-start.17 = (bf16[64,2240]{1,0:T(8,128)(2,1)S(1)}, bf16[64,2240]{1,0:T(8,128)(2,1)S(1)}, u32[]{:S(2)}, u32[]{:S(2)}) collective-permute-start(bf16[64,2240]{1,0:T(8,128)(2,1)S(1)} %bitcast.157), channel_id=1, source_target_pairs={{0,0},{1,4},{2,8},{3,12},{4,1},{5,5},{6,9},{7,13},{8,2},{9,6},{10,... | collective-permute-start | bytes 860168 | tf_op jit(solution)/shard_map/ppermute | solution.py:198
  164.8 13.1 %collective-permute-done.20 = bf16[64,2240]{1,0:T(8,128)(2,1)S(1)} collective-permute-done((bf16[64,2240]{1,0:T(8,128)(2,1)S(1)}, bf16[64,2240]{1,0:T(8,128)(2,1)S(1)}, u32[]{:S(2)}, u32[]{:S(2)}) %collective-permute-start.20) | collective-permute-done | bytes 286752 | tf_op jit(solution)/shard_map/ppermute | solution.py:198
  177.8 6.6 %collective-permute-done.19 = bf16[64,2240]{1,0:T(8,128)(2,1)S(1)} collective-permute-done((bf16[64,2240]{1,0:T(8,128)(2,1)S(1)}, bf16[64,2240]{1,0:T(8,128)(2,1)S(1)}, u32[]{:S(2)}, u32[]{:S(2)}) %collective-permute-start.19) | collective-permute-done | bytes 286752 | tf_op jit(solution)/shard_map/ppermute | solution.py:198
  184.4 4.3 %collective-permute-done.17 = bf16[64,2240]{1,0:T(8,128)(2,1)S(1)} collective-permute-done((bf16[64,2240]{1,0:T(8,128)(2,1)S(1)}, bf16[64,2240]{1,0:T(8,128)(2,1)S(1)}, u32[]{:S(2)}, u32[]{:S(2)}) %collective-permute-start.17) | collective-permute-done | bytes 286752 | tf_op jit(solution)/shard_map/ppermute | solution.py:198
  (108 shorter events, 23.2 us)
Async XLA Ops:
  7.2 139.2 %reduce-scatter.2.cloned.1.call-start = ((), (), s32[]{:S(2)}) async-start(), calls=%async_computation.1 | async-start | bytes 4300800 | tf_op jit(solution)/shard_map/reduce_scatter | solution.py:181
  12.7 6.1 %collective-permute-start.2 = (bf16[113,560]{0,1:T(8,128)(2,1)S(1)}, bf16[113,560]{0,1:T(8,128)(2,1)S(1)}, u32[]{:S(2)}, u32[]{:S(2)}) collective-permute-start(bf16[113,560]{0,1:T(8,128)(2,1)S(1)} %get-tuple-element.25), channel_id=1, source_target_pairs={{0,12},{4,8},{8,4},{12,0},{1,13},{5,9},{9,5},{13,1},{2,14},{6,10},... | collective-permute-start | bytes 379688 | tf_op jit(solution)/shard_map/ppermute | solution.py:81
  12.8 9.1 %collective-permute-start.1 = (bf16[113,560]{0,1:T(8,128)(2,1)S(1)}, bf16[113,560]{0,1:T(8,128)(2,1)S(1)}, u32[]{:S(2)}, u32[]{:S(2)}) collective-permute-start(bf16[113,560]{0,1:T(8,128)(2,1)S(1)} %get-tuple-element.26), channel_id=1, source_target_pairs={{0,8},{4,12},{8,0},{12,4},{1,9},{5,13},{9,1},{13,5},{2,10},{6,14},... | collective-permute-start | bytes 379688 | tf_op jit(solution)/shard_map/ppermute | solution.py:81
  14.2 7.7 %collective-permute-start = (bf16[113,560]{0,1:T(8,128)(2,1)S(1)}, bf16[113,560]{0,1:T(8,128)(2,1)S(1)}, u32[]{:S(2)}, u32[]{:S(2)}) collective-permute-start(bf16[113,560]{0,1:T(8,128)(2,1)S(1)} %get-tuple-element.27), channel_id=1, source_target_pairs={{0,4},{4,0},{8,12},{12,8},{1,5},{5,1},{9,13},{13,9},{2,6},{6,2},{1... | collective-permute-start | bytes 379688 | tf_op jit(solution)/shard_map/ppermute | solution.py:81
  22.1 17.7 %copy-start.3 = (bf16[1,1,64,2240]{3,2,1,0:T(8,128)(2,1)S(1)}, bf16[1,1,64,2240]{3,2,1,0:T(8,128)(2,1)}, u32[]{:S(2)}) copy-start(bf16[1,1,64,2240]{3,2,1,0:T(8,128)(2,1)} %param.9) | copy-start | bytes 860164
  22.1 17.7 %copy-start.5 = (bf16[2240]{0:T(1024)(128)(2,1)S(1)}, bf16[2240]{0:T(1024)(128)(2,1)}, u32[]{:S(2)}) copy-start(bf16[2240]{0:T(1024)(128)(2,1)} %param.14) | copy-start | bytes 13444
  22.2 18.0 %copy-start.6 = (bf16[2240]{0:T(1024)(128)(2,1)S(1)}, bf16[2240]{0:T(1024)(128)(2,1)}, u32[]{:S(2)}) copy-start(bf16[2240]{0:T(1024)(128)(2,1)} %param.13) | copy-start | bytes 13444
  22.3 5.8 %collective-permute-start.5 = (bf16[113,140]{0,1:T(8,128)(2,1)S(1)}, bf16[113,140]{0,1:T(8,128)(2,1)S(1)}, u32[]{:S(2)}, u32[]{:S(2)}) collective-permute-start(bf16[113,140]{0,1:T(8,128)(2,1)S(1)} %get-tuple-element.49), channel_id=1, source_target_pairs={{0,3},{1,2},{2,1},{3,0},{4,7},{5,6},{6,5},{7,4},{8,11},{9,10},{10,... | collective-permute-start | bytes 94928 | tf_op jit(solution)/shard_map/ppermute | solution.py:81
  26.0 4.9 %collective-permute-start.4 = (bf16[113,140]{0,1:T(8,128)(2,1)S(1)}, bf16[113,140]{0,1:T(8,128)(2,1)S(1)}, u32[]{:S(2)}, u32[]{:S(2)}) collective-permute-start(bf16[113,140]{0,1:T(8,128)(2,1)S(1)} %get-tuple-element.50), channel_id=1, source_target_pairs={{0,2},{1,3},{2,0},{3,1},{4,6},{5,7},{6,4},{7,5},{8,10},{9,11},{10,... | collective-permute-start | bytes 94928 | tf_op jit(solution)/shard_map/ppermute | solution.py:81
  26.0 4.9 %collective-permute-start.3 = (bf16[113,140]{0,1:T(8,128)(2,1)S(1)}, bf16[113,140]{0,1:T(8,128)(2,1)S(1)}, u32[]{:S(2)}, u32[]{:S(2)}) collective-permute-start(bf16[113,140]{0,1:T(8,128)(2,1)S(1)} %get-tuple-element.51), channel_id=1, source_target_pairs={{0,1},{1,0},{2,3},{3,2},{4,5},{5,4},{6,7},{7,6},{8,9},{9,8},{10,11... | collective-permute-start | bytes 94928 | tf_op jit(solution)/shard_map/ppermute | solution.py:81
  30.9 5.8 %collective-permute-start.8 = (bf16[113,140]{0,1:T(8,128)(2,1)S(1)}, bf16[113,140]{0,1:T(8,128)(2,1)S(1)}, u32[]{:S(2)}, u32[]{:S(2)}) collective-permute-start(bf16[113,140]{0,1:T(8,128)(2,1)S(1)} %fusion.30), channel_id=1, source_target_pairs={{0,3},{1,2},{2,1},{3,0},{4,7},{5,6},{6,5},{7,4},{8,11},{9,10},{10,... | collective-permute-start | bytes 94928 | tf_op jit(solution)/shard_map/ppermute | solution.py:81
  32.6 4.9 %collective-permute-start.7 = (bf16[113,140]{0,1:T(8,128)(2,1)S(1)}, bf16[113,140]{0,1:T(8,128)(2,1)S(1)}, u32[]{:S(2)}, u32[]{:S(2)}) collective-permute-start(bf16[113,140]{0,1:T(8,128)(2,1)S(1)} %fusion.30), channel_id=1, source_target_pairs={{0,2},{1,3},{2,0},{3,1},{4,6},{5,7},{6,4},{7,5},{8,10},{9,11},{10,... | collective-permute-start | bytes 94928 | tf_op jit(solution)/shard_map/ppermute | solution.py:81
  33.1 4.6 %collective-permute-start.6 = (bf16[113,140]{0,1:T(8,128)(2,1)S(1)}, bf16[113,140]{0,1:T(8,128)(2,1)S(1)}, u32[]{:S(2)}, u32[]{:S(2)}) collective-permute-start(bf16[113,140]{0,1:T(8,128)(2,1)S(1)} %fusion.30), channel_id=1, source_target_pairs={{0,1},{1,0},{2,3},{3,2},{4,5},{5,4},{6,7},{7,6},{8,9},{9,8},{10,11... | collective-permute-start | bytes 94928 | tf_op jit(solution)/shard_map/ppermute | solution.py:81
  37.8 6.1 %collective-permute-start.11 = (bf16[113,560]{0,1:T(8,128)(2,1)S(1)}, bf16[113,560]{0,1:T(8,128)(2,1)S(1)}, u32[]{:S(2)}, u32[]{:S(2)}) collective-permute-start(bf16[113,560]{0,1:T(8,128)(2,1)S(1)} %pad_maximum_fusion.13), channel_id=1, source_target_pairs={{0,12},{4,8},{8,4},{12,0},{1,13},{5,9},{9,5},{13,1},{2,14},{6,10},... | collective-permute-start | bytes 379688 | tf_op jit(solution)/shard_map/ppermute | solution.py:81
  37.9 7.3 %collective-permute-start.10 = (bf16[113,560]{0,1:T(8,128)(2,1)S(1)}, bf16[113,560]{0,1:T(8,128)(2,1)S(1)}, u32[]{:S(2)}, u32[]{:S(2)}) collective-permute-start(bf16[113,560]{0,1:T(8,128)(2,1)S(1)} %pad_maximum_fusion.13), channel_id=1, source_target_pairs={{0,8},{4,12},{8,0},{12,4},{1,9},{5,13},{9,1},{13,5},{2,10},{6,14},... | collective-permute-start | bytes 379688 | tf_op jit(solution)/shard_map/ppermute | solution.py:81
  38.5 6.7 %collective-permute-start.9 = (bf16[113,560]{0,1:T(8,128)(2,1)S(1)}, bf16[113,560]{0,1:T(8,128)(2,1)S(1)}, u32[]{:S(2)}, u32[]{:S(2)}) collective-permute-start(bf16[113,560]{0,1:T(8,128)(2,1)S(1)} %pad_maximum_fusion.13), channel_id=1, source_target_pairs={{0,4},{4,0},{8,12},{12,8},{1,5},{5,1},{9,13},{13,9},{2,6},{6,2},{1... | collective-permute-start | bytes 379688 | tf_op jit(solution)/shard_map/ppermute | solution.py:81
  47.1 1.0 copy-start.2
  49.5 22.2 %copy-start = (bf16[560,2,840]{2,1,0:T(2,128)(2,1)S(1)}, bf16[560,2,840]{2,1,0:T(2,128)(2,1)}, u32[]{:S(2)}) copy-start(bf16[560,2,840]{2,1,0:T(2,128)(2,1)} %param.15) | copy-start | bytes 5644804
  49.6 7.3 %collective-permute-start.14 = (bf16[1,1,64,560]{3,2,1,0:T(8,128)(2,1)S(1)}, bf16[1,1,64,560]{3,2,1,0:T(8,128)(2,1)S(1)}, u32[]{:S(2)}, u32[]{:S(2)}) collective-permute-start(bf16[1,1,64,560]{3,2,1,0:T(8,128)(2,1)S(1)} %get-tuple-element.37), channel_id=1, source_target_pairs={{0,3},{1,2},{2,1},{3,0},{4,7},{5,6},{6,5},{7,4},{8,11},{9,10},{10,... | collective-permute-start | bytes 215048 | tf_op jit(solution)/shard_map/ppermute | solution.py:81
  52.0 9.0 %collective-permute-start.13 = (bf16[1,1,64,560]{3,2,1,0:T(8,128)(2,1)S(1)}, bf16[1,1,64,560]{3,2,1,0:T(8,128)(2,1)S(1)}, u32[]{:S(2)}, u32[]{:S(2)}) collective-permute-start(bf16[1,1,64,560]{3,2,1,0:T(8,128)(2,1)S(1)} %get-tuple-element.38), channel_id=1, source_target_pairs={{0,2},{1,3},{2,0},{3,1},{4,6},{5,7},{6,4},{7,5},{8,10},{9,11},{10,... | collective-permute-start | bytes 215048 | tf_op jit(solution)/shard_map/ppermute | solution.py:81
  52.7 8.3 %collective-permute-start.12 = (bf16[1,1,64,560]{3,2,1,0:T(8,128)(2,1)S(1)}, bf16[1,1,64,560]{3,2,1,0:T(8,128)(2,1)S(1)}, u32[]{:S(2)}, u32[]{:S(2)}) collective-permute-start(bf16[1,1,64,560]{3,2,1,0:T(8,128)(2,1)S(1)} %get-tuple-element.39), channel_id=1, source_target_pairs={{0,1},{1,0},{2,3},{3,2},{4,5},{5,4},{6,7},{7,6},{8,9},{9,8},{10,11... | collective-permute-start | bytes 215048 | tf_op jit(solution)/shard_map/ppermute | solution.py:81
  61.2 9.5 %collective-permute-start.15 = (bf16[1,1,4,64,560]{4,3,2,1,0:T(8,128)(2,1)S(1)}, bf16[1,1,4,64,560]{4,3,2,1,0:T(8,128)(2,1)S(1)}, u32[]{:S(2)}, u32[]{:S(2)}) collective-permute-start(bf16[1,1,4,64,560]{4,3,2,1,0:T(8,128)(2,1)S(1)} %maximum_bitcast_fusion), channel_id=1, source_target_pairs={{0,8},{4,12},{8,0},{12,4},{1,9},{5,13},{9,1},{13,5},{2,10},{6,14},... | collective-permute-start | bytes 860168 | tf_op jit(solution)/shard_map/ppermute | solution.py:92
  71.7 2.5 %collective-permute-start.16 = (bf16[2,1,4,64,560]{4,3,2,1,0:T(8,128)(2,1)}, bf16[2,1,4,64,560]{4,3,2,1,0:T(8,128)(2,1)}, u32[]{:S(2)}, u32[]{:S(2)}) collective-permute-start(bf16[2,1,4,64,560]{4,3,2,1,0:T(8,128)(2,1)} %pad_maximum_fusion.3), channel_id=1, source_target_pairs={{0,4},{4,0},{8,12},{12,8},{1,5},{5,1},{9,13},{13,9},{2,6},{6,2},{1... | collective-permute-start | bytes 1720328 | tf_op jit(solution)/shard_map/ppermute | solution.py:92
  75.7 1.6 copy-start.1
  81.7 0.8 copy-start.4
  148.8 3.1 %copy-start.7 = (bf16[840,2240]{1,0:T(8,128)(2,1)S(1)}, bf16[840,2240]{1,0:T(8,128)(2,1)}, u32[]{:S(2)}) copy-start(bf16[840,2240]{1,0:T(8,128)(2,1)} %param.17) | copy-start | bytes 11289604
  155.2 22.6 %collective-permute-start.20 = (bf16[64,2240]{1,0:T(8,128)(2,1)S(1)}, bf16[64,2240]{1,0:T(8,128)(2,1)S(1)}, u32[]{:S(2)}, u32[]{:S(2)}) collective-permute-start(bf16[64,2240]{1,0:T(8,128)(2,1)S(1)} %bitcast.154), channel_id=1, source_target_pairs={{0,3},{1,7},{2,11},{3,15},{4,2},{5,6},{6,10},{7,14},{8,1},{9,5},{1... | collective-permute-start | bytes 860168 | tf_op jit(solution)/shard_map/ppermute | solution.py:198
  156.7 27.7 %collective-permute-start.19 = (bf16[64,2240]{1,0:T(8,128)(2,1)S(1)}, bf16[64,2240]{1,0:T(8,128)(2,1)S(1)}, u32[]{:S(2)}, u32[]{:S(2)}) collective-permute-start(bf16[64,2240]{1,0:T(8,128)(2,1)S(1)} %bitcast.155), channel_id=1, source_target_pairs={{0,2},{1,6},{2,10},{3,14},{4,3},{5,7},{6,11},{7,15},{8,0},{9,4},{1... | collective-permute-start | bytes 860168 | tf_op jit(solution)/shard_map/ppermute | solution.py:198
  158.6 25.8 %collective-permute-start.18 = (bf16[64,2240]{1,0:T(8,128)(2,1)S(1)}, bf16[64,2240]{1,0:T(8,128)(2,1)S(1)}, u32[]{:S(2)}, u32[]{:S(2)}) collective-permute-start(bf16[64,2240]{1,0:T(8,128)(2,1)S(1)} %bitcast.156), channel_id=1, source_target_pairs={{0,1},{1,5},{2,9},{3,13},{4,0},{5,4},{6,8},{7,12},{8,3},{9,7},{10,... | collective-permute-start | bytes 860168 | tf_op jit(solution)/shard_map/ppermute | solution.py:198
  161.1 27.7 %collective-permute-start.17 = (bf16[64,2240]{1,0:T(8,128)(2,1)S(1)}, bf16[64,2240]{1,0:T(8,128)(2,1)S(1)}, u32[]{:S(2)}, u32[]{:S(2)}) collective-permute-start(bf16[64,2240]{1,0:T(8,128)(2,1)S(1)} %bitcast.157), channel_id=1, source_target_pairs={{0,0},{1,4},{2,8},{3,12},{4,1},{5,5},{6,9},{7,13},{8,2},{9,6},{10,... | collective-permute-start | bytes 860168 | tf_op jit(solution)/shard_map/ppermute | solution.py:198
Sparse Core Ops, SparseCore 0:
  81.9 64.5 reduce-scatter.1

commit v14 on v11

--- a/solution.py
+++ b/solution.py
@@ -161,7 +161,9 @@
     by_row = jnp.concatenate(swap_chunks(depth_chunks, "row"), axis=1)
     frame_parts = lax.axis_size("frame")
     by_frame = doubling_gather(by_row, "frame")
-    whole_frames = frame_parts == row_parts and frame_count == 1 and row_count == 1
+    whole_frames = (
+        frame_parts == row_parts and frame_parts % 2 == 0 and frame_count == 1 and row_count == 1
+    )
     weight_flat = in_weight.reshape(local_depth, 2 * local_gated)
     if whole_frames:
         tokens = jnp.stack([piece[0] for piece in by_frame])
@@ -180,16 +182,29 @@
         projected = jnp.dot(
             hidden.reshape(-1, local_gated), out_weight, preferred_element_type=jnp.float32
         ).astype(jnp.bfloat16)
-        row_blocks = jnp.split(projected, frame_parts, axis=0)
+        row_blocks = jnp.split(projected, row_parts, axis=0)
         frame_at = lax.axis_index("frame")
+        core_at = frame_at % 2
+        chip_at = frame_at // 2
+        chips = frame_parts // 2
+        core_pairs = [(i, i ^ 1) for i in range(frame_parts)]
+        partner_rows = [pick(row_blocks, (1 - core_at) + 2 * chip) for chip in range(chips)]
+        from_partner = lax.ppermute(jnp.stack(partner_rows), "frame", core_pairs)
+        pair_sums = [
+            (
+                pick(row_blocks, core_at + 2 * chip).astype(jnp.float32)
+                + from_partner[chip].astype(jnp.float32)
+            ).astype(jnp.bfloat16)
+            for chip in range(chips)
+        ]
         arrived = []
-        for mask in range(row_parts):
+        for mask in range(chips):
             arrived.append(
                 lax.ppermute(
-                    pick(row_blocks, frame_at ^ mask),
+                    pick(pair_sums, chip_at ^ mask),
                     ("frame", "row"),
                     [
-                        (f * row_parts + r, r * row_parts + (f ^ mask))
+                        (f * row_parts + r, r * row_parts + (f % 2) + 2 * ((f // 2) ^ mask))
                         for f in range(frame_parts)
                         for r in range(row_parts)
                     ],

time: 197 us -> 192 us (0.975)
  waiting for transfers between devices: 121 us -> 115 us
  starting transfers between devices: 23.6 us -> 19.8 us
  local copies, waits for them, and re-layouts: 14.6 us -> 18.3 us
    ppermute x4 -> x3, waiting for transfers between devices: 23.3 us -> 17.7 us  [the longest x2 15.4 us: local(): lax.ppermute(pick(pair_sums, chip_at ^ mask), ('frame', 'row'), [(f * row...]
    ppermute x4 -> x3, starting transfers between devices: 8.8 us -> 4.6 us  [the longest x2 4.6 us: local(): lax.ppermute(pick(pair_sums, chip_at ^ mask), ('frame', 'row'), [(f * row...]
    unnamed x18 -> x24, local copies, waits for them, and re-layouts: 2.17 us -> 4.9 us
  transfers between devices with their start and end apart: 20 -> 19, of which waited for: 16 -> 16; matrix products, arithmetic and copies ran while one was open for 3% -> 2% of each run, Pallas kernels for 0% -> 0%
where the time goes in v14:
time: 192 us
  waiting for transfers between devices  115 us (60%)
  starting transfers between devices  19.8 us (10%)
  local copies, waits for them, and re-layouts  18.3 us (10%)
  other arithmetic  15.3 us (8%)
  between operations  14.6 us (8%)
  matrix products  8.6 us (4%)
    reduce_scatter x1, waiting for transfers between devices, local(): summed = lax.psum_scatter(partial, 'row', scatter_dimension=0, tiled=True)  64.8 us
    ppermute x2, waiting for transfers between devices, local(): lax.ppermute(pick(pair_sums, chip_at ^ mask), ('frame', 'row'), [(f * row...  15.4 us
    ppermute x9, starting transfers between devices, swap_chunks(): lax.ppermute(sent, axis, [(i, i ^ mask) for i in range(count)])  13.8 us
    ppermute x9, waiting for transfers between devices, swap_chunks(): lax.ppermute(sent, axis, [(i, i ^ mask) for i in range(count)])  12.7 us
    ppermute x2, waiting for transfers between devices, halving_sum(): lax.ppermute(sent, axis, [(i, i ^ bit) for i in range(count)])  7.32 us
    ppermute x2, waiting for transfers between devices, doubling_gather(): lax.ppermute(jnp.stack([by_mask[key] for key in keys]), axis, [(i, i ^ bi...  7.04 us
    ppermute x2, waiting for transfers between devices, halving_sum(): lax.ppermute(block.astype(jnp.bfloat16), axis, [(i, i ^ bit) for i in ran...  5.59 us
    unnamed x24, local copies, waits for them, and re-layouts  4.9 us
  transfers between devices with their start and end apart: 19, of which 16 were waited for; matrix products, arithmetic and copies ran while one was open for 2% of the time, Pallas kernels for 0%

profile of v14, /device:TPU:2, one launch (start us, length us, event | category | flops | bytes accessed | tf_op | source)
XLA Modules:
  0.0 191.8 jit_solution(6641045422094654003)
XLA Ops:
  8.2 1.0 convert_reduce_fusion
  11.6 1.6 collective-permute-done
  13.9 1.2 convert_add_fusion.2
  15.2 5.8 %collective-permute-done.1 = bf16[113,560]{0,1:T(8,128)(2,1)S(1)} collective-permute-done((bf16[113,560]{0,1:T(8,128)(2,1)S(1)}, bf16[113,560]{0,1:T(8,128)(2,1)S(1)}, u32[]{:S(2)}, u32[]{:S(2)}) %collective-permute-start.1) | collective-permute-done | bytes 126592 | tf_op jit(solution)/shard_map/ppermute | solution.py:51
  21.1 3.7 %collective-permute-start.4 = (bf16[113,140]{0,1:T(8,128)(2,1)S(1)}, bf16[113,140]{0,1:T(8,128)(2,1)S(1)}, u32[]{:S(2)}, u32[]{:S(2)}) collective-permute-start(bf16[113,140]{0,1:T(8,128)(2,1)S(1)} %get-tuple-element.45), channel_id=1, source_target_pairs={{0,3},{1,2},{2,1},{3,0},{4,7},{5,6},{6,5},{7,4},{8,11},{9,10},{10,... | collective-permute-start | bytes 94928 | tf_op jit(solution)/shard_map/ppermute | solution.py:81
  25.6 1.5 collective-permute-done.4
  27.1 1.7 collective-permute-done.2
  29.7 2.4 %collective-permute-start.5 = (bf16[113,140]{0,1:T(8,128)(2,1)S(1)}, bf16[113,140]{0,1:T(8,128)(2,1)S(1)}, u32[]{:S(2)}, u32[]{:S(2)}) collective-permute-start(bf16[113,140]{0,1:T(8,128)(2,1)S(1)} %fusion.33), channel_id=1, source_target_pairs={{0,1},{1,0},{2,3},{3,2},{4,5},{5,4},{6,7},{7,6},{8,9},{9,8},{10,11... | collective-permute-start | bytes 94928 | tf_op jit(solution)/shard_map/ppermute | solution.py:81
  32.2 2.4 %collective-permute-start.7 = (bf16[113,140]{0,1:T(8,128)(2,1)S(1)}, bf16[113,140]{0,1:T(8,128)(2,1)S(1)}, u32[]{:S(2)}, u32[]{:S(2)}) collective-permute-start(bf16[113,140]{0,1:T(8,128)(2,1)S(1)} %fusion.33), channel_id=1, source_target_pairs={{0,3},{1,2},{2,1},{3,0},{4,7},{5,6},{6,5},{7,4},{8,11},{9,10},{10,... | collective-permute-start | bytes 94928 | tf_op jit(solution)/shard_map/ppermute | solution.py:81
  34.6 2.4 %collective-permute-done.6 = bf16[113,140]{0,1:T(8,128)(2,1)S(1)} collective-permute-done((bf16[113,140]{0,1:T(8,128)(2,1)S(1)}, bf16[113,140]{0,1:T(8,128)(2,1)S(1)}, u32[]{:S(2)}, u32[]{:S(2)}) %collective-permute-start.6) | collective-permute-done | bytes 31672 | tf_op jit(solution)/shard_map/ppermute | solution.py:81
  38.7 4.6 %collective-permute-done.8 = bf16[113,560]{0,1:T(8,128)(2,1)S(1)} collective-permute-done((bf16[113,560]{0,1:T(8,128)(2,1)S(1)}, bf16[113,560]{0,1:T(8,128)(2,1)S(1)}, u32[]{:S(2)}, u32[]{:S(2)}) %collective-permute-start.8) | collective-permute-done | bytes 126592 | tf_op jit(solution)/shard_map/ppermute | solution.py:61
  45.4 1.0 collective-permute-done.9
  48.0 1.4 multiply_reduce_fusion
  53.1 2.9 %collective-permute-start.11 = (bf16[1,1,64,560]{3,2,1,0:T(8,128)(2,1)S(1)}, bf16[1,1,64,560]{3,2,1,0:T(8,128)(2,1)S(1)}, u32[]{:S(2)}, u32[]{:S(2)}) collective-permute-start(bf16[1,1,64,560]{3,2,1,0:T(8,128)(2,1)S(1)} %get-tuple-element.34), channel_id=1, source_target_pairs={{0,2},{1,3},{2,0},{3,1},{4,6},{5,7},{6,4},{7,5},{8,10},{9,11},{10,... | collective-permute-start | bytes 215048 | tf_op jit(solution)/shard_map/ppermute | solution.py:81
  56.1 1.5 collective-permute-start.12
  57.5 1.3 collective-permute-done.10
  58.9 3.9 %collective-permute-done.11 = bf16[1,1,64,560]{3,2,1,0:T(8,128)(2,1)S(1)} collective-permute-done((bf16[1,1,64,560]{3,2,1,0:T(8,128)(2,1)S(1)}, bf16[1,1,64,560]{3,2,1,0:T(8,128)(2,1)S(1)}, u32[]{:S(2)}, u32[]{:S(2)}) %collective-permute-start.11) | collective-permute-done | bytes 71712 | tf_op jit(solution)/shard_map/ppermute | solution.py:81
  63.6 7.0 %collective-permute-done.13 = bf16[1,1,4,64,560]{4,3,2,1,0:T(8,128)(2,1)S(1)} collective-permute-done((bf16[1,1,4,64,560]{4,3,2,1,0:T(8,128)(2,1)S(1)}, bf16[1,1,4,64,560]{4,3,2,1,0:T(8,128)(2,1)S(1)}, u32[]{:S(2)}, u32[]{:S(2)}) %collective-permute-start.13) | collective-permute-done | bytes 286752 | tf_op jit(solution)/shard_map/ppermute | solution.py:92
  71.5 2.5 %reshape.234 = bf16[560,1680]{1,0:T(8,128)(2,1)} reshape(bf16[560,2,840]{2,1,0:T(2,128)(2,1)S(1)} %copy-done) | data formatting | bytes 3763200 | tf_op jit(solution)/shard_map/reshape | solution.py:167
  74.8 1.3 copy-done.1
  76.1 4.4 %convolution_convert_fusion.1 = bf16[1024,1680]{0,1:T(8,128)(2,1)} fusion(bf16[1024,560]{1,0:T(8,128)(2,1)S(1)} %bitcast.119, bf16[560,1680]{1,0:T(8,128)(2,1)S(1)} %copy-done.1), kind=kOutput, calls=%fused_computation.1 | convolution fusion | flops 1928478720 | bytes 6469120 | tf_op jit(solution)/shard_map/dot_general | solution.py:170
  82.0 64.8 %reduce-scatter.2.cloned.1.call-done = bf16[256,1680]{0,1:T(8,128)(2,1)} async-done(((bf16[1024,1680]{0,1:T(8,128)(2,1)}), bf16[256,1680]{0,1:T(8,128)(2,1)}) %reduce-scatter.2.cloned.1.call-update) | async-done | bytes 860176 | tf_op jit(solution)/shard_map/reduce_scatter | solution.py:173
  146.8 1.6 fusion.3
  149.2 3.0 %multiply_add_fusion = f32[1,4,64,1680]{3,2,1,0:T(8,128)S(1)} fusion(bf16[1,4,64,1680]{3,2,1,0:T(8,128)(2,1)S(1)} %bitcast.117, bf16[1,6,64,1680]{3,2,1,0:T(8,128)(2,1)S(1)} %pad.8, f32[1680]{0:T(1024)S(1)} %mul.211, f32[1680]{0:T(1024)S(1)} %mul.208, f32[1680]{0:T(1024)S(1)} %mul.205, f32[1680]{0:T(1024)S(1)} %mul.202, f32[1680]{0:T(1024)S(1)} %mul.199, ...), kind=kLoop, calls=%fused_computation.5 | loop fusion | flops 11182080 | bytes 5922816 | tf_op jit(solution)/shard_map/add | solution.py:114
  152.5 1.8 convolution_convert_fusion
  155.8 1.3 copy.44
  157.1 2.3 %collective-permute-done.15 = bf16[2,64,2240]{2,1,0:T(8,128)(2,1)} collective-permute-done((bf16[2,64,2240]{2,1,0:T(8,128)(2,1)}, bf16[2,64,2240]{2,1,0:T(8,128)(2,1)}, u32[]{:S(2)}, u32[]{:S(2)}) %collective-permute-start.15) | collective-permute-done | bytes 573472 | tf_op jit(solution)/shard_map/ppermute | solution.py:192
  159.4 1.8 fusion.25
  161.5 1.3 copy.53
  164.0 4.5 %collective-permute-start.16 = (bf16[64,2240]{1,0:T(8,128)(2,1)S(1)}, bf16[64,2240]{1,0:T(8,128)(2,1)S(1)}, u32[]{:S(2)}, u32[]{:S(2)}) collective-permute-start(bf16[64,2240]{1,0:T(8,128)(2,1)S(1)} %bitcast.121), channel_id=1, source_target_pairs={{0,0},{1,4},{2,8},{3,12},{4,1},{5,5},{6,9},{7,13},{8,2},{9,6},{10,... | collective-permute-start | bytes 860168 | tf_op jit(solution)/shard_map/ppermute | solution.py:203
  168.8 14.2 %collective-permute-done.16 = bf16[64,2240]{1,0:T(8,128)(2,1)S(1)} collective-permute-done((bf16[64,2240]{1,0:T(8,128)(2,1)S(1)}, bf16[64,2240]{1,0:T(8,128)(2,1)S(1)}, u32[]{:S(2)}, u32[]{:S(2)}) %collective-permute-start.16) | collective-permute-done | bytes 286752 | tf_op jit(solution)/shard_map/ppermute | solution.py:203
  183.0 1.1 collective-permute-done.17
  (112 shorter events, 24.0 us)
Async XLA Ops:
  7.2 2.5 %copy-start.5 = (bf16[1,1,64,2240]{3,2,1,0:T(8,128)(2,1)S(1)}, bf16[1,1,64,2240]{3,2,1,0:T(8,128)(2,1)}, u32[]{:S(2)}) copy-start(bf16[1,1,64,2240]{3,2,1,0:T(8,128)(2,1)} %param.11) | copy-start | bytes 860164
  7.2 139.6 %reduce-scatter.2.cloned.1.call-start = ((), (), s32[]{:S(2)}) async-start(), calls=%async_computation.1 | async-start | bytes 4300800 | tf_op jit(solution)/shard_map/reduce_scatter | solution.py:173
  11.5 1.6 collective-permute-start
  13.2 0.7 copy-start.6
  15.1 5.9 %collective-permute-start.1 = (bf16[113,560]{0,1:T(8,128)(2,1)S(1)}, bf16[113,560]{0,1:T(8,128)(2,1)S(1)}, u32[]{:S(2)}, u32[]{:S(2)}) collective-permute-start(bf16[113,560]{0,1:T(8,128)(2,1)S(1)} %select_convert_fusion.1), channel_id=1, source_target_pairs={{0,8},{4,12},{8,0},{12,4},{1,9},{5,13},{9,1},{13,5},{2,10},{6,14},... | collective-permute-start | bytes 379688 | tf_op jit(solution)/shard_map/ppermute | solution.py:51
  21.1 5.9 %collective-permute-start.4 = (bf16[113,140]{0,1:T(8,128)(2,1)S(1)}, bf16[113,140]{0,1:T(8,128)(2,1)S(1)}, u32[]{:S(2)}, u32[]{:S(2)}) collective-permute-start(bf16[113,140]{0,1:T(8,128)(2,1)S(1)} %get-tuple-element.45), channel_id=1, source_target_pairs={{0,3},{1,2},{2,1},{3,0},{4,7},{5,6},{6,5},{7,4},{8,11},{9,10},{10,... | collective-permute-start | bytes 94928 | tf_op jit(solution)/shard_map/ppermute | solution.py:81
  24.8 4.0 %collective-permute-start.2 = (bf16[113,140]{0,1:T(8,128)(2,1)S(1)}, bf16[113,140]{0,1:T(8,128)(2,1)S(1)}, u32[]{:S(2)}, u32[]{:S(2)}) collective-permute-start(bf16[113,140]{0,1:T(8,128)(2,1)S(1)} %get-tuple-element.47), channel_id=1, source_target_pairs={{0,1},{1,0},{2,3},{3,2},{4,5},{5,4},{6,7},{7,6},{8,9},{9,8},{10,11... | collective-permute-start | bytes 94928 | tf_op jit(solution)/shard_map/ppermute | solution.py:81
  24.8 4.9 %collective-permute-start.3 = (bf16[113,140]{0,1:T(8,128)(2,1)S(1)}, bf16[113,140]{0,1:T(8,128)(2,1)S(1)}, u32[]{:S(2)}, u32[]{:S(2)}) collective-permute-start(bf16[113,140]{0,1:T(8,128)(2,1)S(1)} %get-tuple-element.46), channel_id=1, source_target_pairs={{0,2},{1,3},{2,0},{3,1},{4,6},{5,7},{6,4},{7,5},{8,10},{9,11},{10,... | collective-permute-start | bytes 94928 | tf_op jit(solution)/shard_map/ppermute | solution.py:81
  29.7 4.9 %collective-permute-start.5 = (bf16[113,140]{0,1:T(8,128)(2,1)S(1)}, bf16[113,140]{0,1:T(8,128)(2,1)S(1)}, u32[]{:S(2)}, u32[]{:S(2)}) collective-permute-start(bf16[113,140]{0,1:T(8,128)(2,1)S(1)} %fusion.33), channel_id=1, source_target_pairs={{0,1},{1,0},{2,3},{3,2},{4,5},{5,4},{6,7},{7,6},{8,9},{9,8},{10,11... | collective-permute-start | bytes 94928 | tf_op jit(solution)/shard_map/ppermute | solution.py:81
  32.2 4.9 %collective-permute-start.6 = (bf16[113,140]{0,1:T(8,128)(2,1)S(1)}, bf16[113,140]{0,1:T(8,128)(2,1)S(1)}, u32[]{:S(2)}, u32[]{:S(2)}) collective-permute-start(bf16[113,140]{0,1:T(8,128)(2,1)S(1)} %fusion.33), channel_id=1, source_target_pairs={{0,2},{1,3},{2,0},{3,1},{4,6},{5,7},{6,4},{7,5},{8,10},{9,11},{10,... | collective-permute-start | bytes 94928 | tf_op jit(solution)/shard_map/ppermute | solution.py:81
  32.2 5.8 %collective-permute-start.7 = (bf16[113,140]{0,1:T(8,128)(2,1)S(1)}, bf16[113,140]{0,1:T(8,128)(2,1)S(1)}, u32[]{:S(2)}, u32[]{:S(2)}) collective-permute-start(bf16[113,140]{0,1:T(8,128)(2,1)S(1)} %fusion.33), channel_id=1, source_target_pairs={{0,3},{1,2},{2,1},{3,0},{4,7},{5,6},{6,5},{7,4},{8,11},{9,10},{10,... | collective-permute-start | bytes 94928 | tf_op jit(solution)/shard_map/ppermute | solution.py:81
  38.1 6.7 %copy-start.4 = (bf16[1,1,64,2240]{3,2,1,0:T(8,128)(2,1)S(1)}, bf16[1,1,64,2240]{3,2,1,0:T(8,128)(2,1)}, u32[]{:S(2)}) copy-start(bf16[1,1,64,2240]{3,2,1,0:T(8,128)(2,1)} %param.9) | copy-start | bytes 860164
  38.1 5.2 %collective-permute-start.8 = (bf16[113,560]{0,1:T(8,128)(2,1)S(1)}, bf16[113,560]{0,1:T(8,128)(2,1)S(1)}, u32[]{:S(2)}, u32[]{:S(2)}) collective-permute-start(bf16[113,560]{0,1:T(8,128)(2,1)S(1)} %pad_maximum_fusion.11), channel_id=1, source_target_pairs={{0,8},{4,12},{8,0},{12,4},{1,9},{5,13},{9,1},{13,5},{2,10},{6,14},... | collective-permute-start | bytes 379688 | tf_op jit(solution)/shard_map/ppermute | solution.py:61
  44.7 0.7 copy-start.8
  44.7 0.7 copy-start.9
  44.8 1.6 collective-permute-start.9
  49.9 1.0 copy-start.2
  53.0 18.5 %copy-start = (bf16[560,2,840]{2,1,0:T(2,128)(2,1)S(1)}, bf16[560,2,840]{2,1,0:T(2,128)(2,1)}, u32[]{:S(2)}) copy-start(bf16[560,2,840]{2,1,0:T(2,128)(2,1)} %param.15) | copy-start | bytes 5644804
  53.1 5.8 %collective-permute-start.10 = (bf16[1,1,64,560]{3,2,1,0:T(8,128)(2,1)S(1)}, bf16[1,1,64,560]{3,2,1,0:T(8,128)(2,1)S(1)}, u32[]{:S(2)}, u32[]{:S(2)}) collective-permute-start(bf16[1,1,64,560]{3,2,1,0:T(8,128)(2,1)S(1)} %get-tuple-element.35), channel_id=1, source_target_pairs={{0,1},{1,0},{2,3},{3,2},{4,5},{5,4},{6,7},{7,6},{8,9},{9,8},{10,11... | collective-permute-start | bytes 215048 | tf_op jit(solution)/shard_map/ppermute | solution.py:81
  53.1 9.6 %collective-permute-start.11 = (bf16[1,1,64,560]{3,2,1,0:T(8,128)(2,1)S(1)}, bf16[1,1,64,560]{3,2,1,0:T(8,128)(2,1)S(1)}, u32[]{:S(2)}, u32[]{:S(2)}) collective-permute-start(bf16[1,1,64,560]{3,2,1,0:T(8,128)(2,1)S(1)} %get-tuple-element.34), channel_id=1, source_target_pairs={{0,2},{1,3},{2,0},{3,1},{4,6},{5,7},{6,4},{7,5},{8,10},{9,11},{10,... | collective-permute-start | bytes 215048 | tf_op jit(solution)/shard_map/ppermute | solution.py:81
  56.1 6.7 %collective-permute-start.12 = (bf16[1,1,64,560]{3,2,1,0:T(8,128)(2,1)S(1)}, bf16[1,1,64,560]{3,2,1,0:T(8,128)(2,1)S(1)}, u32[]{:S(2)}, u32[]{:S(2)}) collective-permute-start(bf16[1,1,64,560]{3,2,1,0:T(8,128)(2,1)S(1)} %get-tuple-element.33), channel_id=1, source_target_pairs={{0,3},{1,2},{2,1},{3,0},{4,7},{5,6},{6,5},{7,4},{8,11},{9,10},{10,... | collective-permute-start | bytes 215048 | tf_op jit(solution)/shard_map/ppermute | solution.py:81
  63.0 7.6 %collective-permute-start.13 = (bf16[1,1,4,64,560]{4,3,2,1,0:T(8,128)(2,1)S(1)}, bf16[1,1,4,64,560]{4,3,2,1,0:T(8,128)(2,1)S(1)}, u32[]{:S(2)}, u32[]{:S(2)}) collective-permute-start(bf16[1,1,4,64,560]{4,3,2,1,0:T(8,128)(2,1)S(1)} %maximum_bitcast_fusion), channel_id=1, source_target_pairs={{0,8},{4,12},{8,0},{12,4},{1,9},{5,13},{9,1},{13,5},{2,10},{6,14},... | collective-permute-start | bytes 860168 | tf_op jit(solution)/shard_map/ppermute | solution.py:92
  71.5 2.5 %collective-permute-start.14 = (bf16[2,1,4,64,560]{4,3,2,1,0:T(8,128)(2,1)}, bf16[2,1,4,64,560]{4,3,2,1,0:T(8,128)(2,1)S(1)}, u32[]{:S(2)}, u32[]{:S(2)}) collective-permute-start(bf16[2,1,4,64,560]{4,3,2,1,0:T(8,128)(2,1)} %pad_maximum_fusion.4), channel_id=1, source_target_pairs={{0,4},{4,0},{8,12},{12,8},{1,5},{5,1},{9,13},{13,9},{2,6},{6,2},{1... | collective-permute-start | bytes 1720328 | tf_op jit(solution)/shard_map/ppermute | solution.py:92
  74.5 1.6 copy-start.1
  80.5 0.8 copy-start.7
  149.2 3.3 %copy-start.10 = (bf16[840,2240]{1,0:T(8,128)(2,1)S(1)}, bf16[840,2240]{1,0:T(8,128)(2,1)}, u32[]{:S(2)}) copy-start(bf16[840,2240]{1,0:T(8,128)(2,1)} %param.17) | copy-start | bytes 11289604
  157.1 2.3 %collective-permute-start.15 = (bf16[2,64,2240]{2,1,0:T(8,128)(2,1)}, bf16[2,64,2240]{2,1,0:T(8,128)(2,1)}, u32[]{:S(2)}, u32[]{:S(2)}) collective-permute-start(bf16[2,64,2240]{2,1,0:T(8,128)(2,1)} %copy.44), channel_id=1, source_target_pairs={{0,4},{4,0},{8,12},{12,8},{1,5},{5,1},{9,13},{13,9},{2,6},{6,2},{1... | collective-permute-start | bytes 1720328 | tf_op jit(solution)/shard_map/ppermute | solution.py:192
  163.1 21.0 %copy-start.3 = (bf16[64,2240]{1,0:T(8,128)(2,1)S(1)}, bf16[64,2240]{1,0:T(8,128)(2,1)}, u32[]{:S(2)}) copy-start(bf16[64,2240]{1,0:T(8,128)(2,1)} %get-tuple-element.5) | copy-start | bytes 860164
  164.0 19.1 %collective-permute-start.16 = (bf16[64,2240]{1,0:T(8,128)(2,1)S(1)}, bf16[64,2240]{1,0:T(8,128)(2,1)S(1)}, u32[]{:S(2)}, u32[]{:S(2)}) collective-permute-start(bf16[64,2240]{1,0:T(8,128)(2,1)S(1)} %bitcast.121), channel_id=1, source_target_pairs={{0,0},{1,4},{2,8},{3,12},{4,1},{5,5},{6,9},{7,13},{8,2},{9,6},{10,... | collective-permute-start | bytes 860168 | tf_op jit(solution)/shard_map/ppermute | solution.py:203
  168.8 15.4 %collective-permute-start.17 = (bf16[64,2240]{1,0:T(8,128)(2,1)S(1)}, bf16[64,2240]{1,0:T(8,128)(2,1)S(1)}, u32[]{:S(2)}, u32[]{:S(2)}) collective-permute-start(bf16[64,2240]{1,0:T(8,128)(2,1)S(1)} %bitcast.122), channel_id=1, source_target_pairs={{0,2},{1,6},{2,10},{3,14},{4,3},{5,7},{6,11},{7,15},{8,0},{9,4},{1... | collective-permute-start | bytes 860168 | tf_op jit(solution)/shard_map/ppermute | solution.py:203
Sparse Core Ops, SparseCore 0:
  80.6 66.1 reduce-scatter.1

commit v15 on v14

--- a/solution.py
+++ b/solution.py
@@ -182,21 +182,19 @@
         projected = jnp.dot(
             hidden.reshape(-1, local_gated), out_weight, preferred_element_type=jnp.float32
         ).astype(jnp.bfloat16)
-        row_blocks = jnp.split(projected, row_parts, axis=0)
         frame_at = lax.axis_index("frame")
         core_at = frame_at % 2
         chip_at = frame_at // 2
         chips = frame_parts // 2
         core_pairs = [(i, i ^ 1) for i in range(frame_parts)]
-        partner_rows = [pick(row_blocks, (1 - core_at) + 2 * chip) for chip in range(chips)]
-        from_partner = lax.ppermute(jnp.stack(partner_rows), "frame", core_pairs)
-        pair_sums = [
-            (
-                pick(row_blocks, core_at + 2 * chip).astype(jnp.float32)
-                + from_partner[chip].astype(jnp.float32)
-            ).astype(jnp.bfloat16)
-            for chip in range(chips)
-        ]
+        by_parity = projected.reshape(chips, 2, -1, model_width)
+        partner_rows = lax.dynamic_index_in_dim(by_parity, 1 - core_at, axis=1, keepdims=False)
+        own_rows = lax.dynamic_index_in_dim(by_parity, core_at, axis=1, keepdims=False)
+        from_partner = lax.ppermute(partner_rows, "frame", core_pairs)
+        pair_sums = (own_rows.astype(jnp.float32) + from_partner.astype(jnp.float32)).astype(
+            jnp.bfloat16
+        )
+        pair_sums = [pair_sums[chip] for chip in range(chips)]
         arrived = []
         for mask in range(chips):
             arrived.append(

time: 192 us -> 185 us (0.964)
  local copies, waits for them, and re-layouts: 18.3 us -> 13.5 us
  other arithmetic: 15.3 us -> 13 us
  waiting for transfers between devices: 115 us -> 113 us
    unnamed x24 -> x18, local copies, waits for them, and re-layouts: 4.9 us -> 2.55 us
where the time goes in v15:
time: 185 us; the launch traced here: 184 us
  waiting for transfers between devices  113 us (61%)
  starting transfers between devices  20.9 us (11%)
  between operations  14.6 us (8%)
  local copies, waits for them, and re-layouts  13.5 us (7%)
  other arithmetic  13 us (7%)
  matrix products  8.6 us (5%)
    reduce_scatter x1, waiting for transfers between devices, local(): summed = lax.psum_scatter(partial, 'row', scatter_dimension=0, tiled=True)  63.6 us
    ppermute x2, waiting for transfers between devices, local(): lax.ppermute(pick(pair_sums, chip_at ^ mask), ('frame', 'row'), [(f * row...  13.6 us
    ppermute x9, starting transfers between devices, swap_chunks(): lax.ppermute(sent, axis, [(i, i ^ mask) for i in range(count)])  13.4 us
    ppermute x9, waiting for transfers between devices, swap_chunks(): lax.ppermute(sent, axis, [(i, i ^ mask) for i in range(count)])  12.8 us
    ppermute x2, waiting for transfers between devices, doubling_gather(): lax.ppermute(jnp.stack([by_mask[key] for key in keys]), axis, [(i, i ^ bi...  8.4 us
    ppermute x2, waiting for transfers between devices, halving_sum(): lax.ppermute(sent, axis, [(i, i ^ bit) for i in range(count)])  7.45 us
    ppermute x2, starting transfers between devices, local(): lax.ppermute(pick(pair_sums, chip_at ^ mask), ('frame', 'row'), [(f * row...  6.04 us
    ppermute x2, waiting for transfers between devices, halving_sum(): lax.ppermute(block.astype(jnp.bfloat16), axis, [(i, i ^ bit) for i in ran...  5.6 us
  transfers between devices with their start and end apart: 19, of which 16 were waited for; matrix products, arithmetic and copies ran while one was open for 2% of the time, Pallas kernels for 0%

profile of v15, /device:TPU:2, one launch (start us, length us, event | category | flops | bytes accessed | tf_op | source)
XLA Modules:
  0.0 184.1 jit_solution(17554187979105360362)
XLA Ops:
  7.2 1.1 convert_reduce_fusion
  8.3 1.0 broadcast_maximum_fusion.1
  11.6 1.7 collective-permute-done
  13.3 1.2 convert_add_fusion.3
  14.6 5.8 %collective-permute-done.1 = bf16[113,560]{0,1:T(8,128)(2,1)S(1)} collective-permute-done((bf16[113,560]{0,1:T(8,128)(2,1)S(1)}, bf16[113,560]{0,1:T(8,128)(2,1)S(1)}, u32[]{:S(2)}, u32[]{:S(2)}) %collective-permute-start.1) | collective-permute-done | bytes 126592 | tf_op jit(solution)/shard_map/ppermute | solution.py:51
  20.5 3.7 %collective-permute-start.4 = (bf16[113,140]{0,1:T(8,128)(2,1)S(1)}, bf16[113,140]{0,1:T(8,128)(2,1)S(1)}, u32[]{:S(2)}, u32[]{:S(2)}) collective-permute-start(bf16[113,140]{0,1:T(8,128)(2,1)S(1)} %get-tuple-element.35), channel_id=1, source_target_pairs={{0,3},{1,2},{2,1},{3,0},{4,7},{5,6},{6,5},{7,4},{8,11},{9,10},{10,... | collective-permute-start | bytes 94928 | tf_op jit(solution)/shard_map/ppermute | solution.py:81
  25.0 1.6 collective-permute-done.4
  26.6 2.5 %collective-permute-done.3 = bf16[113,140]{0,1:T(8,128)(2,1)S(1)} collective-permute-done((bf16[113,140]{0,1:T(8,128)(2,1)S(1)}, bf16[113,140]{0,1:T(8,128)(2,1)S(1)}, u32[]{:S(2)}, u32[]{:S(2)}) %collective-permute-start.3) | collective-permute-done | bytes 31672 | tf_op jit(solution)/shard_map/ppermute | solution.py:81
  29.2 1.5 collective-permute-start.7
  31.3 2.3 %collective-permute-start.5 = (bf16[113,140]{0,1:T(8,128)(2,1)S(1)}, bf16[113,140]{0,1:T(8,128)(2,1)S(1)}, u32[]{:S(2)}, u32[]{:S(2)}) collective-permute-start(bf16[113,140]{0,1:T(8,128)(2,1)S(1)} %fusion.31), channel_id=1, source_target_pairs={{0,1},{1,0},{2,3},{3,2},{4,5},{5,4},{6,7},{7,6},{8,9},{9,8},{10,11... | collective-permute-start | bytes 94928 | tf_op jit(solution)/shard_map/ppermute | solution.py:81
  33.6 1.3 collective-permute-done.7
  36.7 4.6 %collective-permute-done.8 = bf16[113,560]{0,1:T(8,128)(2,1)S(1)} collective-permute-done((bf16[113,560]{0,1:T(8,128)(2,1)S(1)}, bf16[113,560]{0,1:T(8,128)(2,1)S(1)}, u32[]{:S(2)}, u32[]{:S(2)}) %collective-permute-start.8) | collective-permute-done | bytes 126592 | tf_op jit(solution)/shard_map/ppermute | solution.py:61
  43.1 1.0 collective-permute-done.9
  45.8 1.4 multiply_reduce_fusion
  50.1 2.4 %collective-permute-start.12 = (bf16[1,1,64,560]{3,2,1,0:T(8,128)(2,1)S(1)}, bf16[1,1,64,560]{3,2,1,0:T(8,128)(2,1)S(1)}, u32[]{:S(2)}, u32[]{:S(2)}) collective-permute-start(bf16[1,1,64,560]{3,2,1,0:T(8,128)(2,1)S(1)} %get-tuple-element.23), channel_id=1, source_target_pairs={{0,3},{1,2},{2,1},{3,0},{4,7},{5,6},{6,5},{7,4},{8,11},{9,10},{10,... | collective-permute-start | bytes 215048 | tf_op jit(solution)/shard_map/ppermute | solution.py:81
  53.3 1.3 collective-permute-start.10
  54.5 2.8 %collective-permute-done.12 = bf16[1,1,64,560]{3,2,1,0:T(8,128)(2,1)S(1)} collective-permute-done((bf16[1,1,64,560]{3,2,1,0:T(8,128)(2,1)S(1)}, bf16[1,1,64,560]{3,2,1,0:T(8,128)(2,1)S(1)}, u32[]{:S(2)}, u32[]{:S(2)}) %collective-permute-start.12) | collective-permute-done | bytes 71712 | tf_op jit(solution)/shard_map/ppermute | solution.py:81
  57.3 3.6 %collective-permute-done.11 = bf16[1,1,64,560]{3,2,1,0:T(8,128)(2,1)S(1)} collective-permute-done((bf16[1,1,64,560]{3,2,1,0:T(8,128)(2,1)S(1)}, bf16[1,1,64,560]{3,2,1,0:T(8,128)(2,1)S(1)}, u32[]{:S(2)}, u32[]{:S(2)}) %collective-permute-start.11) | collective-permute-done | bytes 71712 | tf_op jit(solution)/shard_map/ppermute | solution.py:81
  61.8 8.4 %collective-permute-done.13 = bf16[1,1,4,64,560]{4,3,2,1,0:T(8,128)(2,1)S(1)} collective-permute-done((bf16[1,1,4,64,560]{4,3,2,1,0:T(8,128)(2,1)S(1)}, bf16[1,1,4,64,560]{4,3,2,1,0:T(8,128)(2,1)S(1)}, u32[]{:S(2)}, u32[]{:S(2)}) %collective-permute-start.13) | collective-permute-done | bytes 286752 | tf_op jit(solution)/shard_map/ppermute | solution.py:92
  70.2 0.9 pad_maximum_fusion.2
  71.1 2.5 %reshape.239 = bf16[560,1680]{1,0:T(8,128)(2,1)} reshape(bf16[560,2,840]{2,1,0:T(2,128)(2,1)S(1)} %copy-done) | data formatting | bytes 3763200 | tf_op jit(solution)/shard_map/reshape | solution.py:167
  73.6 1.1 fusion.23
  75.4 1.3 copy-done.1
  76.7 4.4 %convolution_convert_fusion.1 = bf16[1024,1680]{0,1:T(8,128)(2,1)} fusion(bf16[1024,560]{1,0:T(8,128)(2,1)S(1)} %bitcast.121, bf16[560,1680]{1,0:T(8,128)(2,1)S(1)} %copy-done.1), kind=kOutput, calls=%fused_computation.1 | convolution fusion | flops 1928478720 | bytes 6469120 | tf_op jit(solution)/shard_map/dot_general | solution.py:170
  82.6 63.6 %reduce-scatter.2.cloned.1.call-done = bf16[256,1680]{0,1:T(8,128)(2,1)} async-done(((bf16[1024,1680]{0,1:T(8,128)(2,1)}), bf16[256,1680]{0,1:T(8,128)(2,1)}) %reduce-scatter.2.cloned.1.call-update) | async-done | bytes 860176 | tf_op jit(solution)/shard_map/reduce_scatter | solution.py:173
  146.2 1.6 fusion.3
  148.6 3.0 %multiply_add_fusion = f32[1,4,64,1680]{3,2,1,0:T(8,128)S(1)} fusion(bf16[1,4,64,1680]{3,2,1,0:T(8,128)(2,1)S(1)} %bitcast.117, bf16[1,6,64,1680]{3,2,1,0:T(8,128)(2,1)S(1)} %pad.8, f32[1680]{0:T(1024)S(1)} %mul.211, f32[1680]{0:T(1024)S(1)} %mul.208, f32[1680]{0:T(1024)S(1)} %mul.205, f32[1680]{0:T(1024)S(1)} %mul.202, f32[1680]{0:T(1024)S(1)} %mul.199, ...), kind=kLoop, calls=%fused_computation.4 | loop fusion | flops 11182080 | bytes 5922816 | tf_op jit(solution)/shard_map/add | solution.py:114
  151.9 1.8 convolution_convert_fusion
  154.6 2.0 %collective-permute-done.15 = bf16[2,64,2240]{2,1,0:T(8,128)(2,1)S(1)} collective-permute-done((bf16[2,64,2240]{2,1,0:T(8,128)(2,1)S(1)}, bf16[2,64,2240]{2,1,0:T(8,128)(2,1)S(1)}, u32[]{:S(2)}, u32[]{:S(2)}) %collective-permute-start.15) | collective-permute-done | bytes 573472 | tf_op jit(solution)/shard_map/ppermute | solution.py:193
  157.3 5.4 %collective-permute-start.16 = (bf16[64,2240]{1,0:T(8,128)(2,1)S(1)}, bf16[64,2240]{1,0:T(8,128)(2,1)S(1)}, u32[]{:S(2)}, u32[]{:S(2)}) collective-permute-start(bf16[64,2240]{1,0:T(8,128)(2,1)S(1)} %get-tuple-element.16), channel_id=1, source_target_pairs={{0,0},{1,4},{2,8},{3,12},{4,1},{5,5},{6,9},{7,13},{8,2},{9,6},{10,... | collective-permute-start | bytes 860168 | tf_op jit(solution)/shard_map/ppermute | solution.py:201
  162.8 10.3 %collective-permute-done.17 = bf16[64,2240]{1,0:T(8,128)(2,1)S(1)} collective-permute-done((bf16[64,2240]{1,0:T(8,128)(2,1)S(1)}, bf16[64,2240]{1,0:T(8,128)(2,1)S(1)}, u32[]{:S(2)}, u32[]{:S(2)}) %collective-permute-start.17) | collective-permute-done | bytes 286752 | tf_op jit(solution)/shard_map/ppermute | solution.py:201
  173.0 3.3 %collective-permute-done.16 = bf16[64,2240]{1,0:T(8,128)(2,1)S(1)} collective-permute-done((bf16[64,2240]{1,0:T(8,128)(2,1)S(1)}, bf16[64,2240]{1,0:T(8,128)(2,1)S(1)}, u32[]{:S(2)}, u32[]{:S(2)}) %collective-permute-start.16) | collective-permute-done | bytes 286752 | tf_op jit(solution)/shard_map/ppermute | solution.py:201
  (100 shorter events, 19.1 us)
Async XLA Ops:
  7.2 2.5 %copy-start.4 = (bf16[1,1,64,2240]{3,2,1,0:T(8,128)(2,1)S(1)}, bf16[1,1,64,2240]{3,2,1,0:T(8,128)(2,1)}, u32[]{:S(2)}) copy-start(bf16[1,1,64,2240]{3,2,1,0:T(8,128)(2,1)} %param.11) | copy-start | bytes 860164
  7.2 139.0 %reduce-scatter.2.cloned.1.call-start = ((), (), s32[]{:S(2)}) async-start(), calls=%async_computation.1 | async-start | bytes 4300800 | tf_op jit(solution)/shard_map/reduce_scatter | solution.py:173
  11.5 1.8 collective-permute-start
  14.5 5.9 %collective-permute-start.1 = (bf16[113,560]{0,1:T(8,128)(2,1)S(1)}, bf16[113,560]{0,1:T(8,128)(2,1)S(1)}, u32[]{:S(2)}, u32[]{:S(2)}) collective-permute-start(bf16[113,560]{0,1:T(8,128)(2,1)S(1)} %select_convert_fusion.1), channel_id=1, source_target_pairs={{0,8},{4,12},{8,0},{12,4},{1,9},{5,13},{9,1},{13,5},{2,10},{6,14},... | collective-permute-start | bytes 379688 | tf_op jit(solution)/shard_map/ppermute | solution.py:51
  20.5 6.1 %collective-permute-start.4 = (bf16[113,140]{0,1:T(8,128)(2,1)S(1)}, bf16[113,140]{0,1:T(8,128)(2,1)S(1)}, u32[]{:S(2)}, u32[]{:S(2)}) collective-permute-start(bf16[113,140]{0,1:T(8,128)(2,1)S(1)} %get-tuple-element.35), channel_id=1, source_target_pairs={{0,3},{1,2},{2,1},{3,0},{4,7},{5,6},{6,5},{7,4},{8,11},{9,10},{10,... | collective-permute-start | bytes 94928 | tf_op jit(solution)/shard_map/ppermute | solution.py:81
  24.2 4.9 %collective-permute-start.3 = (bf16[113,140]{0,1:T(8,128)(2,1)S(1)}, bf16[113,140]{0,1:T(8,128)(2,1)S(1)}, u32[]{:S(2)}, u32[]{:S(2)}) collective-permute-start(bf16[113,140]{0,1:T(8,128)(2,1)S(1)} %get-tuple-element.36), channel_id=1, source_target_pairs={{0,2},{1,3},{2,0},{3,1},{4,6},{5,7},{6,4},{7,5},{8,10},{9,11},{10,... | collective-permute-start | bytes 94928 | tf_op jit(solution)/shard_map/ppermute | solution.py:81
  24.2 4.9 %collective-permute-start.2 = (bf16[113,140]{0,1:T(8,128)(2,1)S(1)}, bf16[113,140]{0,1:T(8,128)(2,1)S(1)}, u32[]{:S(2)}, u32[]{:S(2)}) collective-permute-start(bf16[113,140]{0,1:T(8,128)(2,1)S(1)} %get-tuple-element.37), channel_id=1, source_target_pairs={{0,1},{1,0},{2,3},{3,2},{4,5},{5,4},{6,7},{7,6},{8,9},{9,8},{10,11... | collective-permute-start | bytes 94928 | tf_op jit(solution)/shard_map/ppermute | solution.py:81
  29.2 5.8 %collective-permute-start.7 = (bf16[113,140]{0,1:T(8,128)(2,1)S(1)}, bf16[113,140]{0,1:T(8,128)(2,1)S(1)}, u32[]{:S(2)}, u32[]{:S(2)}) collective-permute-start(bf16[113,140]{0,1:T(8,128)(2,1)S(1)} %fusion.31), channel_id=1, source_target_pairs={{0,3},{1,2},{2,1},{3,0},{4,7},{5,6},{6,5},{7,4},{8,11},{9,10},{10,... | collective-permute-start | bytes 94928 | tf_op jit(solution)/shard_map/ppermute | solution.py:81
  30.7 4.9 %collective-permute-start.6 = (bf16[113,140]{0,1:T(8,128)(2,1)S(1)}, bf16[113,140]{0,1:T(8,128)(2,1)S(1)}, u32[]{:S(2)}, u32[]{:S(2)}) collective-permute-start(bf16[113,140]{0,1:T(8,128)(2,1)S(1)} %fusion.31), channel_id=1, source_target_pairs={{0,2},{1,3},{2,0},{3,1},{4,6},{5,7},{6,4},{7,5},{8,10},{9,11},{10,... | collective-permute-start | bytes 94928 | tf_op jit(solution)/shard_map/ppermute | solution.py:81
  31.3 4.6 %collective-permute-start.5 = (bf16[113,140]{0,1:T(8,128)(2,1)S(1)}, bf16[113,140]{0,1:T(8,128)(2,1)S(1)}, u32[]{:S(2)}, u32[]{:S(2)}) collective-permute-start(bf16[113,140]{0,1:T(8,128)(2,1)S(1)} %fusion.31), channel_id=1, source_target_pairs={{0,1},{1,0},{2,3},{3,2},{4,5},{5,4},{6,7},{7,6},{8,9},{9,8},{10,11... | collective-permute-start | bytes 94928 | tf_op jit(solution)/shard_map/ppermute | solution.py:81
  36.1 6.5 %copy-start.3 = (bf16[1,1,64,2240]{3,2,1,0:T(8,128)(2,1)S(1)}, bf16[1,1,64,2240]{3,2,1,0:T(8,128)(2,1)}, u32[]{:S(2)}) copy-start(bf16[1,1,64,2240]{3,2,1,0:T(8,128)(2,1)} %param.9) | copy-start | bytes 860164
  36.1 5.2 %collective-permute-start.8 = (bf16[113,560]{0,1:T(8,128)(2,1)S(1)}, bf16[113,560]{0,1:T(8,128)(2,1)S(1)}, u32[]{:S(2)}, u32[]{:S(2)}) collective-permute-start(bf16[113,560]{0,1:T(8,128)(2,1)S(1)} %pad_maximum_fusion.9), channel_id=1, source_target_pairs={{0,8},{4,12},{8,0},{12,4},{1,9},{5,13},{9,1},{13,5},{2,10},{6,14},... | collective-permute-start | bytes 379688 | tf_op jit(solution)/shard_map/ppermute | solution.py:61
  41.9 0.8 copy-start.6
  42.4 0.7 copy-start.7
  42.5 1.6 collective-permute-start.9
  47.6 1.0 copy-start.2
  50.1 21.0 %copy-start = (bf16[560,2,840]{2,1,0:T(2,128)(2,1)S(1)}, bf16[560,2,840]{2,1,0:T(2,128)(2,1)}, u32[]{:S(2)}) copy-start(bf16[560,2,840]{2,1,0:T(2,128)(2,1)} %param.15) | copy-start | bytes 5644804
  50.1 7.3 %collective-permute-start.12 = (bf16[1,1,64,560]{3,2,1,0:T(8,128)(2,1)S(1)}, bf16[1,1,64,560]{3,2,1,0:T(8,128)(2,1)S(1)}, u32[]{:S(2)}, u32[]{:S(2)}) collective-permute-start(bf16[1,1,64,560]{3,2,1,0:T(8,128)(2,1)S(1)} %get-tuple-element.23), channel_id=1, source_target_pairs={{0,3},{1,2},{2,1},{3,0},{4,7},{5,6},{6,5},{7,4},{8,11},{9,10},{10,... | collective-permute-start | bytes 215048 | tf_op jit(solution)/shard_map/ppermute | solution.py:81
  52.5 8.5 %collective-permute-start.11 = (bf16[1,1,64,560]{3,2,1,0:T(8,128)(2,1)S(1)}, bf16[1,1,64,560]{3,2,1,0:T(8,128)(2,1)S(1)}, u32[]{:S(2)}, u32[]{:S(2)}) collective-permute-start(bf16[1,1,64,560]{3,2,1,0:T(8,128)(2,1)S(1)} %get-tuple-element.24), channel_id=1, source_target_pairs={{0,2},{1,3},{2,0},{3,1},{4,6},{5,7},{6,4},{7,5},{8,10},{9,11},{10,... | collective-permute-start | bytes 215048 | tf_op jit(solution)/shard_map/ppermute | solution.py:81
  53.3 7.7 %collective-permute-start.10 = (bf16[1,1,64,560]{3,2,1,0:T(8,128)(2,1)S(1)}, bf16[1,1,64,560]{3,2,1,0:T(8,128)(2,1)S(1)}, u32[]{:S(2)}, u32[]{:S(2)}) collective-permute-start(bf16[1,1,64,560]{3,2,1,0:T(8,128)(2,1)S(1)} %get-tuple-element.25), channel_id=1, source_target_pairs={{0,1},{1,0},{2,3},{3,2},{4,5},{5,4},{6,7},{7,6},{8,9},{9,8},{10,11... | collective-permute-start | bytes 215048 | tf_op jit(solution)/shard_map/ppermute | solution.py:81
  61.2 9.0 %collective-permute-start.13 = (bf16[1,1,4,64,560]{4,3,2,1,0:T(8,128)(2,1)S(1)}, bf16[1,1,4,64,560]{4,3,2,1,0:T(8,128)(2,1)S(1)}, u32[]{:S(2)}, u32[]{:S(2)}) collective-permute-start(bf16[1,1,4,64,560]{4,3,2,1,0:T(8,128)(2,1)S(1)} %maximum_bitcast_fusion), channel_id=1, source_target_pairs={{0,8},{4,12},{8,0},{12,4},{1,9},{5,13},{9,1},{13,5},{2,10},{6,14},... | collective-permute-start | bytes 860168 | tf_op jit(solution)/shard_map/ppermute | solution.py:92
  71.1 2.5 %collective-permute-start.14 = (bf16[2,1,4,64,560]{4,3,2,1,0:T(8,128)(2,1)}, bf16[2,1,4,64,560]{4,3,2,1,0:T(8,128)(2,1)}, u32[]{:S(2)}, u32[]{:S(2)}) collective-permute-start(bf16[2,1,4,64,560]{4,3,2,1,0:T(8,128)(2,1)} %pad_maximum_fusion.2), channel_id=1, source_target_pairs={{0,4},{4,0},{8,12},{12,8},{1,5},{5,1},{9,13},{13,9},{2,6},{6,2},{1... | collective-permute-start | bytes 1720328 | tf_op jit(solution)/shard_map/ppermute | solution.py:92
  75.1 1.6 copy-start.1
  81.1 0.8 copy-start.5
  148.6 3.3 %copy-start.8 = (bf16[840,2240]{1,0:T(8,128)(2,1)S(1)}, bf16[840,2240]{1,0:T(8,128)(2,1)}, u32[]{:S(2)}) copy-start(bf16[840,2240]{1,0:T(8,128)(2,1)} %param.17) | copy-start | bytes 11289604
  154.5 2.1 %collective-permute-start.15 = (bf16[2,64,2240]{2,1,0:T(8,128)(2,1)S(1)}, bf16[2,64,2240]{2,1,0:T(8,128)(2,1)S(1)}, u32[]{:S(2)}, u32[]{:S(2)}) collective-permute-start(bf16[2,64,2240]{2,1,0:T(8,128)(2,1)S(1)} %dynamic-slice_bitcast_fusion), channel_id=1, source_target_pairs={{0,4},{4,0},{8,12},{12,8},{1,5},{5,1},{9,13},{13,9},{2,6},{6,2},{1... | collective-permute-start | bytes 1720328 | tf_op jit(solution)/shard_map/ppermute | solution.py:193
  156.7 16.3 %collective-permute-start.17 = (bf16[64,2240]{1,0:T(8,128)(2,1)S(1)}, bf16[64,2240]{1,0:T(8,128)(2,1)S(1)}, u32[]{:S(2)}, u32[]{:S(2)}) collective-permute-start(bf16[64,2240]{1,0:T(8,128)(2,1)S(1)} %get-tuple-element.17), channel_id=1, source_target_pairs={{0,2},{1,6},{2,10},{3,14},{4,3},{5,7},{6,11},{7,15},{8,0},{9,4},{1... | collective-permute-start | bytes 860168 | tf_op jit(solution)/shard_map/ppermute | solution.py:201
  157.3 19.0 %collective-permute-start.16 = (bf16[64,2240]{1,0:T(8,128)(2,1)S(1)}, bf16[64,2240]{1,0:T(8,128)(2,1)S(1)}, u32[]{:S(2)}, u32[]{:S(2)}) collective-permute-start(bf16[64,2240]{1,0:T(8,128)(2,1)S(1)} %get-tuple-element.16), channel_id=1, source_target_pairs={{0,0},{1,4},{2,8},{3,12},{4,1},{5,5},{6,9},{7,13},{8,2},{9,6},{10,... | collective-permute-start | bytes 860168 | tf_op jit(solution)/shard_map/ppermute | solution.py:201
Sparse Core Ops, SparseCore 0:
  81.3 64.8 reduce-scatter.1

commit v16 on v15

--- a/solution.py
+++ b/solution.py
@@ -72,14 +72,19 @@
     return lax.dynamic_index_in_dim(stacked, index, axis=0, keepdims=False)
 
 
-def swap_chunks(chunks, axis):
+def swap_stacked(stacked, axis):
     count = lax.axis_size(axis)
     own = lax.axis_index(axis)
-    by_mask = [pick(chunks, own)]
+    by_mask = [lax.dynamic_index_in_dim(stacked, own, axis=0, keepdims=False)]
     for mask in range(1, count):
-        sent = pick(chunks, own ^ mask)
+        sent = lax.dynamic_index_in_dim(stacked, own ^ mask, axis=0, keepdims=False)
         by_mask.append(lax.ppermute(sent, axis, [(i, i ^ mask) for i in range(count)]))
-    return [pick(by_mask, own ^ source) for source in range(count)]
+    return jnp.take(jnp.stack(by_mask), own ^ jnp.arange(count), axis=0)
+
+
+def swap_chunks(chunks, axis):
+    arrived = swap_stacked(jnp.stack(chunks), axis)
+    return [arrived[source] for source in range(len(chunks))]
 
 
 def doubling_gather(block, axis):
@@ -95,8 +100,10 @@
         for at, key in enumerate(keys):
             by_mask[key ^ bit] = received[at]
         bit //= 2
-    ordered = [by_mask[mask] for mask in range(count)]
-    return [pick(ordered, own ^ source) for source in range(count)]
+    ordered = jnp.take(
+        jnp.stack([by_mask[mask] for mask in range(count)]), own ^ jnp.arange(count), axis=0
+    )
+    return [ordered[source] for source in range(count)]
 
 
 def rms_norm(features):
@@ -155,10 +162,10 @@
     conv_taps = conv_weight.reshape(9, 2 * local_gated).astype(jnp.float32)
     row_parts = lax.axis_size("row")
     local_depth = in_weight.shape[0]
-    depth_chunks = [
-        normed_grid[..., part * local_depth : (part + 1) * local_depth] for part in range(row_parts)
-    ]
-    by_row = jnp.concatenate(swap_chunks(depth_chunks, "row"), axis=1)
+    depth_split = jnp.moveaxis(
+        normed_grid.reshape(frame_count, row_count, col_count, row_parts, local_depth), 3, 0
+    )
+    by_row = jnp.concatenate(list(swap_stacked(depth_split, "row")), axis=1)
     frame_parts = lax.axis_size("frame")
     by_frame = doubling_gather(by_row, "frame")
     whole_frames = (
@@ -194,12 +201,11 @@
         pair_sums = (own_rows.astype(jnp.float32) + from_partner.astype(jnp.float32)).astype(
             jnp.bfloat16
         )
-        pair_sums = [pair_sums[chip] for chip in range(chips)]
         arrived = []
         for mask in range(chips):
             arrived.append(
                 lax.ppermute(
-                    pick(pair_sums, chip_at ^ mask),
+                    lax.dynamic_index_in_dim(pair_sums, chip_at ^ mask, axis=0, keepdims=False),
                     ("frame", "row"),
                     [
                         (f * row_parts + r, r * row_parts + (f % 2) + 2 * ((f // 2) ^ mask))

time: 185 us -> 190 us (1.027)
  local copies, waits for them, and re-layouts: 13.5 us -> 18.4 us
  other arithmetic: 13 us -> 15.9 us
  waiting for transfers between devices: 113 us -> 111 us
    gather x0 -> x4, local copies, waits for them, and re-layouts: none -> 2.55 us  [the longest x3 1.76 us: swap_stacked(): return jnp.take(jnp.stack(by_mask), own ^ jnp.arange(count), axis=0)]
  transfers between devices with their start and end apart: 19 -> 19, of which waited for: 16 -> 15; matrix products, arithmetic and copies ran while one was open for 2% -> 3% of each run, Pallas kernels for 0% -> 0%
where the time goes in v16:
time: 190 us
  waiting for transfers between devices  111 us (58%)
  starting transfers between devices  21.1 us (11%)
  local copies, waits for them, and re-layouts  18.4 us (10%)
  other arithmetic  15.9 us (8%)
  between operations  14.8 us (8%)
  matrix products  8.62 us (5%)
    reduce_scatter x1, waiting for transfers between devices, local(): summed = lax.psum_scatter(partial, 'row', scatter_dimension=0, tiled=True)  63.6 us
    ppermute x9, starting transfers between devices, swap_stacked(): lax.ppermute(sent, axis, [(i, i ^ mask) for i in range(count)])  13.5 us
    ppermute x2, waiting for transfers between devices, local(): lax.ppermute(lax.dynamic_index_in_dim(pair_sums, chip_at ^ mask, axis=0,...  12.7 us
    ppermute x9, waiting for transfers between devices, swap_stacked(): lax.ppermute(sent, axis, [(i, i ^ mask) for i in range(count)])  12.5 us
    ppermute x2, waiting for transfers between devices, doubling_gather(): lax.ppermute(jnp.stack([by_mask[key] for key in keys]), axis, [(i, i ^ bi...  8.39 us
    ppermute x2, waiting for transfers between devices, halving_sum(): lax.ppermute(sent, axis, [(i, i ^ bit) for i in range(count)])  7.42 us
    ppermute x2, starting transfers between devices, local(): lax.ppermute(lax.dynamic_index_in_dim(pair_sums, chip_at ^ mask, axis=0,...  6.06 us
    ppermute x2, waiting for transfers between devices, halving_sum(): lax.ppermute(block.astype(jnp.bfloat16), axis, [(i, i ^ bit) for i in ran...  4.57 us
  transfers between devices with their start and end apart: 19, of which 15 were waited for; matrix products, arithmetic and copies ran while one was open for 3% of the time, Pallas kernels for 0%

profile of v16, /device:TPU:2, one launch (start us, length us, event | category | flops | bytes accessed | tf_op | source)
XLA Modules:
  0.0 189.8 jit_solution(5932525855702492630)
XLA Ops:
  7.2 1.1 convert_reduce_fusion
  8.3 1.0 broadcast_maximum_fusion.1
  11.6 1.7 collective-permute-done
  13.3 1.2 convert_add_fusion.2
  14.6 5.7 %collective-permute-done.1 = bf16[113,560]{0,1:T(8,128)(2,1)S(1)} collective-permute-done((bf16[113,560]{0,1:T(8,128)(2,1)S(1)}, bf16[113,560]{0,1:T(8,128)(2,1)S(1)}, u32[]{:S(2)}, u32[]{:S(2)}) %collective-permute-start.1) | collective-permute-done | bytes 126592 | tf_op jit(solution)/shard_map/ppermute | solution.py:51
  20.5 3.7 %collective-permute-start.4 = (bf16[113,140]{0,1:T(8,128)(2,1)S(1)}, bf16[113,140]{0,1:T(8,128)(2,1)S(1)}, u32[]{:S(2)}, u32[]{:S(2)}) collective-permute-start(bf16[113,140]{0,1:T(8,128)(2,1)S(1)} %get-tuple-element.32), channel_id=1, source_target_pairs={{0,3},{1,2},{2,1},{3,0},{4,7},{5,6},{6,5},{7,4},{8,11},{9,10},{10,... | collective-permute-start | bytes 94928 | tf_op jit(solution)/shard_map/ppermute | solution.py:81
  25.0 1.6 collective-permute-done.4
  26.6 2.5 %collective-permute-done.3 = bf16[113,140]{0,1:T(8,128)(2,1)S(1)} collective-permute-done((bf16[113,140]{0,1:T(8,128)(2,1)S(1)}, bf16[113,140]{0,1:T(8,128)(2,1)S(1)}, u32[]{:S(2)}, u32[]{:S(2)}) %collective-permute-start.3) | collective-permute-done | bytes 31672 | tf_op jit(solution)/shard_map/ppermute | solution.py:81
  29.8 1.5 collective-permute-start.7
  32.0 2.3 %collective-permute-start.5 = (bf16[113,140]{0,1:T(8,128)(2,1)S(1)}, bf16[113,140]{0,1:T(8,128)(2,1)S(1)}, u32[]{:S(2)}, u32[]{:S(2)}) collective-permute-start(bf16[113,140]{0,1:T(8,128)(2,1)S(1)} %fusion.36), channel_id=1, source_target_pairs={{0,1},{1,0},{2,3},{3,2},{4,5},{5,4},{6,7},{7,6},{8,9},{9,8},{10,11... | collective-permute-start | bytes 94928 | tf_op jit(solution)/shard_map/ppermute | solution.py:81
  34.3 1.3 collective-permute-done.7
  38.0 4.6 %collective-permute-done.8 = bf16[113,560]{0,1:T(8,128)(2,1)S(1)} collective-permute-done((bf16[113,560]{0,1:T(8,128)(2,1)S(1)}, bf16[113,560]{0,1:T(8,128)(2,1)S(1)}, u32[]{:S(2)}, u32[]{:S(2)}) %collective-permute-start.8) | collective-permute-done | bytes 126592 | tf_op jit(solution)/shard_map/ppermute | solution.py:61
  47.2 1.4 multiply_reduce_fusion
  49.7 1.0 fusion.7
  51.8 2.4 %collective-permute-start.12 = (bf16[1,1,64,560]{3,2,1,0:T(8,128)(2,1)S(1)}, bf16[1,1,64,560]{3,2,1,0:T(8,128)(2,1)S(1)}, u32[]{:S(2)}, u32[]{:S(2)}) collective-permute-start(bf16[1,1,64,560]{3,2,1,0:T(8,128)(2,1)S(1)} %bitcast.157), channel_id=1, source_target_pairs={{0,3},{1,2},{2,1},{3,0},{4,7},{5,6},{6,5},{7,4},{8,11},{9,10},{10,... | collective-permute-start | bytes 215048 | tf_op jit(solution)/shard_map/ppermute | solution.py:81
  55.1 1.4 collective-permute-start.10
  56.4 2.6 %collective-permute-done.12 = bf16[1,1,64,560]{3,2,1,0:T(8,128)(2,1)S(1)} collective-permute-done((bf16[1,1,64,560]{3,2,1,0:T(8,128)(2,1)S(1)}, bf16[1,1,64,560]{3,2,1,0:T(8,128)(2,1)S(1)}, u32[]{:S(2)}, u32[]{:S(2)}) %collective-permute-start.12) | collective-permute-done | bytes 71712 | tf_op jit(solution)/shard_map/ppermute | solution.py:81
  59.1 3.6 %collective-permute-done.11 = bf16[1,1,64,560]{3,2,1,0:T(8,128)(2,1)S(1)} collective-permute-done((bf16[1,1,64,560]{3,2,1,0:T(8,128)(2,1)S(1)}, bf16[1,1,64,560]{3,2,1,0:T(8,128)(2,1)S(1)}, u32[]{:S(2)}, u32[]{:S(2)}) %collective-permute-start.11) | collective-permute-done | bytes 71712 | tf_op jit(solution)/shard_map/ppermute | solution.py:81
  64.3 8.4 %collective-permute-done.13 = bf16[1,1,4,64,560]{4,3,2,1,0:T(8,128)(2,1)S(1)} collective-permute-done((bf16[1,1,4,64,560]{4,3,2,1,0:T(8,128)(2,1)S(1)}, bf16[1,1,4,64,560]{4,3,2,1,0:T(8,128)(2,1)S(1)}, u32[]{:S(2)}, u32[]{:S(2)}) %collective-permute-start.13) | collective-permute-done | bytes 286752 | tf_op jit(solution)/shard_map/ppermute | solution.py:97
  74.4 2.4 %reshape.354 = bf16[560,1680]{1,0:T(8,128)(2,1)} reshape(bf16[560,2,840]{2,1,0:T(2,128)(2,1)S(1)} %copy-done.2) | data formatting | bytes 3763200 | tf_op jit(solution)/shard_map/reshape | solution.py:174
  76.8 1.2 fusion.26
  79.9 1.3 copy-done.3
  81.2 4.5 %convolution_convert_fusion.1 = bf16[1024,1680]{0,1:T(8,128)(2,1)} fusion(bf16[1024,560]{1,0:T(8,128)(2,1)S(1)} %bitcast.151, bf16[560,1680]{1,0:T(8,128)(2,1)S(1)} %copy-done.3), kind=kOutput, calls=%fused_computation.5 | convolution fusion | flops 1928478720 | bytes 6469120 | tf_op jit(solution)/shard_map/dot_general | solution.py:177
  87.2 63.6 %reduce-scatter.2.cloned.1.call-done = bf16[256,1680]{0,1:T(8,128)(2,1)} async-done(((bf16[1024,1680]{0,1:T(8,128)(2,1)}), bf16[256,1680]{0,1:T(8,128)(2,1)}) %reduce-scatter.2.cloned.1.call-update) | async-done | bytes 860176 | tf_op jit(solution)/shard_map/reduce_scatter | solution.py:180
  150.7 1.6 fusion.3
  153.1 3.0 %multiply_add_fusion = f32[1,4,64,1680]{3,2,1,0:T(8,128)S(1)} fusion(bf16[1,4,64,1680]{3,2,1,0:T(8,128)(2,1)S(1)} %bitcast.147, bf16[1,6,64,1680]{3,2,1,0:T(8,128)(2,1)S(1)} %pad.8, f32[1680]{0:T(1024)S(1)} %mul.256, f32[1680]{0:T(1024)S(1)} %mul.253, f32[1680]{0:T(1024)S(1)} %mul.250, f32[1680]{0:T(1024)S(1)} %mul.247, f32[1680]{0:T(1024)S(1)} %mul.244, ...), kind=kLoop, calls=%fused_computation.8 | loop fusion | flops 11182080 | bytes 5922816 | tf_op jit(solution)/shard_map/add | solution.py:121
  156.4 1.8 convolution_convert_fusion
  159.4 1.8 collective-permute-done.15
  161.2 1.2 fusion.5
  163.1 5.4 %collective-permute-start.16 = (bf16[64,2240]{1,0:T(8,128)(2,1)S(1)}, bf16[64,2240]{1,0:T(8,128)(2,1)S(1)}, u32[]{:S(2)}, u32[]{:S(2)}) collective-permute-start(bf16[64,2240]{1,0:T(8,128)(2,1)S(1)} %get-tuple-element.14), channel_id=1, source_target_pairs={{0,0},{1,4},{2,8},{3,12},{4,1},{5,5},{6,9},{7,13},{8,2},{9,6},{10,... | collective-permute-start | bytes 860168 | tf_op jit(solution)/shard_map/ppermute | solution.py:207
  169.4 9.4 %collective-permute-done.17 = bf16[64,2240]{1,0:T(8,128)(2,1)S(1)} collective-permute-done((bf16[64,2240]{1,0:T(8,128)(2,1)S(1)}, bf16[64,2240]{1,0:T(8,128)(2,1)S(1)}, u32[]{:S(2)}, u32[]{:S(2)}) %collective-permute-start.17) | collective-permute-done | bytes 286752 | tf_op jit(solution)/shard_map/ppermute | solution.py:207
  178.8 3.3 %collective-permute-done.16 = bf16[64,2240]{1,0:T(8,128)(2,1)S(1)} collective-permute-done((bf16[64,2240]{1,0:T(8,128)(2,1)S(1)}, bf16[64,2240]{1,0:T(8,128)(2,1)S(1)}, u32[]{:S(2)}, u32[]{:S(2)}) %collective-permute-start.16) | collective-permute-done | bytes 286752 | tf_op jit(solution)/shard_map/ppermute | solution.py:207
  (134 shorter events, 25.7 us)
Async XLA Ops:
  7.2 2.5 %copy-start.8 = (bf16[1,1,64,2240]{3,2,1,0:T(8,128)(2,1)S(1)}, bf16[1,1,64,2240]{3,2,1,0:T(8,128)(2,1)}, u32[]{:S(2)}) copy-start(bf16[1,1,64,2240]{3,2,1,0:T(8,128)(2,1)} %param.13) | copy-start | bytes 860164
  7.2 143.5 %reduce-scatter.2.cloned.1.call-start = ((), (), s32[]{:S(2)}) async-start(), calls=%async_computation.1 | async-start | bytes 4300800 | tf_op jit(solution)/shard_map/reduce_scatter | solution.py:180
  11.5 1.8 collective-permute-start
  14.5 5.9 %collective-permute-start.1 = (bf16[113,560]{0,1:T(8,128)(2,1)S(1)}, bf16[113,560]{0,1:T(8,128)(2,1)S(1)}, u32[]{:S(2)}, u32[]{:S(2)}) collective-permute-start(bf16[113,560]{0,1:T(8,128)(2,1)S(1)} %select_convert_fusion.1), channel_id=1, source_target_pairs={{0,8},{4,12},{8,0},{12,4},{1,9},{5,13},{9,1},{13,5},{2,10},{6,14},... | collective-permute-start | bytes 379688 | tf_op jit(solution)/shard_map/ppermute | solution.py:51
  20.5 6.1 %collective-permute-start.4 = (bf16[113,140]{0,1:T(8,128)(2,1)S(1)}, bf16[113,140]{0,1:T(8,128)(2,1)S(1)}, u32[]{:S(2)}, u32[]{:S(2)}) collective-permute-start(bf16[113,140]{0,1:T(8,128)(2,1)S(1)} %get-tuple-element.32), channel_id=1, source_target_pairs={{0,3},{1,2},{2,1},{3,0},{4,7},{5,6},{6,5},{7,4},{8,11},{9,10},{10,... | collective-permute-start | bytes 94928 | tf_op jit(solution)/shard_map/ppermute | solution.py:81
  24.2 4.9 %collective-permute-start.3 = (bf16[113,140]{0,1:T(8,128)(2,1)S(1)}, bf16[113,140]{0,1:T(8,128)(2,1)S(1)}, u32[]{:S(2)}, u32[]{:S(2)}) collective-permute-start(bf16[113,140]{0,1:T(8,128)(2,1)S(1)} %get-tuple-element.33), channel_id=1, source_target_pairs={{0,2},{1,3},{2,0},{3,1},{4,6},{5,7},{6,4},{7,5},{8,10},{9,11},{10,... | collective-permute-start | bytes 94928 | tf_op jit(solution)/shard_map/ppermute | solution.py:81
  24.2 4.9 %collective-permute-start.2 = (bf16[113,140]{0,1:T(8,128)(2,1)S(1)}, bf16[113,140]{0,1:T(8,128)(2,1)S(1)}, u32[]{:S(2)}, u32[]{:S(2)}) collective-permute-start(bf16[113,140]{0,1:T(8,128)(2,1)S(1)} %get-tuple-element.34), channel_id=1, source_target_pairs={{0,1},{1,0},{2,3},{3,2},{4,5},{5,4},{6,7},{7,6},{8,9},{9,8},{10,11... | collective-permute-start | bytes 94928 | tf_op jit(solution)/shard_map/ppermute | solution.py:81
  29.8 5.8 %collective-permute-start.7 = (bf16[113,140]{0,1:T(8,128)(2,1)S(1)}, bf16[113,140]{0,1:T(8,128)(2,1)S(1)}, u32[]{:S(2)}, u32[]{:S(2)}) collective-permute-start(bf16[113,140]{0,1:T(8,128)(2,1)S(1)} %fusion.36), channel_id=1, source_target_pairs={{0,3},{1,2},{2,1},{3,0},{4,7},{5,6},{6,5},{7,4},{8,11},{9,10},{10,... | collective-permute-start | bytes 94928 | tf_op jit(solution)/shard_map/ppermute | solution.py:81
  31.3 4.9 %collective-permute-start.6 = (bf16[113,140]{0,1:T(8,128)(2,1)S(1)}, bf16[113,140]{0,1:T(8,128)(2,1)S(1)}, u32[]{:S(2)}, u32[]{:S(2)}) collective-permute-start(bf16[113,140]{0,1:T(8,128)(2,1)S(1)} %fusion.36), channel_id=1, source_target_pairs={{0,2},{1,3},{2,0},{3,1},{4,6},{5,7},{6,4},{7,5},{8,10},{9,11},{10,... | collective-permute-start | bytes 94928 | tf_op jit(solution)/shard_map/ppermute | solution.py:81
  32.0 4.6 %collective-permute-start.5 = (bf16[113,140]{0,1:T(8,128)(2,1)S(1)}, bf16[113,140]{0,1:T(8,128)(2,1)S(1)}, u32[]{:S(2)}, u32[]{:S(2)}) collective-permute-start(bf16[113,140]{0,1:T(8,128)(2,1)S(1)} %fusion.36), channel_id=1, source_target_pairs={{0,1},{1,0},{2,3},{3,2},{4,5},{5,4},{6,7},{7,6},{8,9},{9,8},{10,11... | collective-permute-start | bytes 94928 | tf_op jit(solution)/shard_map/ppermute | solution.py:81
  37.4 5.2 %collective-permute-start.8 = (bf16[113,560]{0,1:T(8,128)(2,1)S(1)}, bf16[113,560]{0,1:T(8,128)(2,1)S(1)}, u32[]{:S(2)}, u32[]{:S(2)}) collective-permute-start(bf16[113,560]{0,1:T(8,128)(2,1)S(1)} %pad_maximum_fusion.6), channel_id=1, source_target_pairs={{0,8},{4,12},{8,0},{12,4},{1,9},{5,13},{9,1},{13,5},{2,10},{6,14},... | collective-permute-start | bytes 379688 | tf_op jit(solution)/shard_map/ppermute | solution.py:61
  43.2 1.0 copy-start.7
  43.7 0.7 copy-start.10
  43.7 1.2 copy-start
  43.8 1.6 copy-start.11
  43.9 1.7 collective-permute-start.9
  51.8 7.3 %collective-permute-start.12 = (bf16[1,1,64,560]{3,2,1,0:T(8,128)(2,1)S(1)}, bf16[1,1,64,560]{3,2,1,0:T(8,128)(2,1)S(1)}, u32[]{:S(2)}, u32[]{:S(2)}) collective-permute-start(bf16[1,1,64,560]{3,2,1,0:T(8,128)(2,1)S(1)} %bitcast.157), channel_id=1, source_target_pairs={{0,3},{1,2},{2,1},{3,0},{4,7},{5,6},{6,5},{7,4},{8,11},{9,10},{10,... | collective-permute-start | bytes 215048 | tf_op jit(solution)/shard_map/ppermute | solution.py:81
  54.3 8.4 %collective-permute-start.11 = (bf16[1,1,64,560]{3,2,1,0:T(8,128)(2,1)S(1)}, bf16[1,1,64,560]{3,2,1,0:T(8,128)(2,1)S(1)}, u32[]{:S(2)}, u32[]{:S(2)}) collective-permute-start(bf16[1,1,64,560]{3,2,1,0:T(8,128)(2,1)S(1)} %bitcast.158), channel_id=1, source_target_pairs={{0,2},{1,3},{2,0},{3,1},{4,6},{5,7},{6,4},{7,5},{8,10},{9,11},{10,... | collective-permute-start | bytes 215048 | tf_op jit(solution)/shard_map/ppermute | solution.py:81
  55.1 7.6 %collective-permute-start.10 = (bf16[1,1,64,560]{3,2,1,0:T(8,128)(2,1)S(1)}, bf16[1,1,64,560]{3,2,1,0:T(8,128)(2,1)S(1)}, u32[]{:S(2)}, u32[]{:S(2)}) collective-permute-start(bf16[1,1,64,560]{3,2,1,0:T(8,128)(2,1)S(1)} %bitcast.159), channel_id=1, source_target_pairs={{0,1},{1,0},{2,3},{3,2},{4,5},{5,4},{6,7},{7,6},{8,9},{9,8},{10,11... | collective-permute-start | bytes 215048 | tf_op jit(solution)/shard_map/ppermute | solution.py:81
  63.5 10.8 %copy-start.2 = (bf16[560,2,840]{2,1,0:T(2,128)(2,1)S(1)}, bf16[560,2,840]{2,1,0:T(2,128)(2,1)}, u32[]{:S(2)}) copy-start(bf16[560,2,840]{2,1,0:T(2,128)(2,1)} %param.17) | copy-start | bytes 5644804
  63.7 9.0 %collective-permute-start.13 = (bf16[1,1,4,64,560]{4,3,2,1,0:T(8,128)(2,1)S(1)}, bf16[1,1,4,64,560]{4,3,2,1,0:T(8,128)(2,1)S(1)}, u32[]{:S(2)}, u32[]{:S(2)}) collective-permute-start(bf16[1,1,4,64,560]{4,3,2,1,0:T(8,128)(2,1)S(1)} %maximum_bitcast_fusion.2), channel_id=1, source_target_pairs={{0,8},{4,12},{8,0},{12,4},{1,9},{5,13},{9,1},{13,5},{2,10},{6,14},... | collective-permute-start | bytes 860168 | tf_op jit(solution)/shard_map/ppermute | solution.py:97
  72.7 0.7 copy-start.4
  74.4 2.5 %collective-permute-start.14 = (bf16[2,1,4,64,560]{4,3,2,1,0:T(8,128)(2,1)}, bf16[2,1,4,64,560]{4,3,2,1,0:T(8,128)(2,1)}, u32[]{:S(2)}, u32[]{:S(2)}) collective-permute-start(bf16[2,1,4,64,560]{4,3,2,1,0:T(8,128)(2,1)} %pad_maximum_fusion.1), channel_id=1, source_target_pairs={{0,4},{4,0},{8,12},{12,8},{1,5},{5,1},{9,13},{13,9},{2,6},{6,2},{1... | collective-permute-start | bytes 1720328 | tf_op jit(solution)/shard_map/ppermute | solution.py:97
  76.8 1.2 copy-start.5
  79.6 1.6 copy-start.3
  85.7 0.8 copy-start.9
  153.1 3.3 %copy-start.12 = (bf16[840,2240]{1,0:T(8,128)(2,1)S(1)}, bf16[840,2240]{1,0:T(8,128)(2,1)}, u32[]{:S(2)}) copy-start(bf16[840,2240]{1,0:T(8,128)(2,1)} %param.19) | copy-start | bytes 11289604
  159.0 2.2 %collective-permute-start.15 = (bf16[2,64,2240]{2,1,0:T(8,128)(2,1)S(1)}, bf16[2,64,2240]{2,1,0:T(8,128)(2,1)}, u32[]{:S(2)}, u32[]{:S(2)}) collective-permute-start(bf16[2,64,2240]{2,1,0:T(8,128)(2,1)S(1)} %dynamic-slice_bitcast_fusion), channel_id=1, source_target_pairs={{0,4},{4,0},{8,12},{12,8},{1,5},{5,1},{9,13},{13,9},{2,6},{6,2},{1... | collective-permute-start | bytes 1720328 | tf_op jit(solution)/shard_map/ppermute | solution.py:200
  159.4 9.2 %copy-start.1 = (bf16[1,1,64,2240]{3,2,1,0:T(8,128)(2,1)S(1)}, bf16[1,1,64,2240]{3,2,1,0:T(8,128)(2,1)}, u32[]{:S(2)}) copy-start(bf16[1,1,64,2240]{3,2,1,0:T(8,128)(2,1)} %param.14) | copy-start | bytes 860164
  162.4 19.7 %copy-start.6 = (bf16[64,2240]{1,0:T(8,128)(2,1)S(1)}, bf16[64,2240]{1,0:T(8,128)(2,1)}, u32[]{:S(2)}) copy-start(bf16[64,2240]{1,0:T(8,128)(2,1)} %get-tuple-element.4) | copy-start | bytes 860164
  162.5 16.3 %collective-permute-start.17 = (bf16[64,2240]{1,0:T(8,128)(2,1)S(1)}, bf16[64,2240]{1,0:T(8,128)(2,1)S(1)}, u32[]{:S(2)}, u32[]{:S(2)}) collective-permute-start(bf16[64,2240]{1,0:T(8,128)(2,1)S(1)} %get-tuple-element.15), channel_id=1, source_target_pairs={{0,2},{1,6},{2,10},{3,14},{4,3},{5,7},{6,11},{7,15},{8,0},{9,4},{1... | collective-permute-start | bytes 860168 | tf_op jit(solution)/shard_map/ppermute | solution.py:207
  163.1 19.0 %collective-permute-start.16 = (bf16[64,2240]{1,0:T(8,128)(2,1)S(1)}, bf16[64,2240]{1,0:T(8,128)(2,1)S(1)}, u32[]{:S(2)}, u32[]{:S(2)}) collective-permute-start(bf16[64,2240]{1,0:T(8,128)(2,1)S(1)} %get-tuple-element.14), channel_id=1, source_target_pairs={{0,0},{1,4},{2,8},{3,12},{4,1},{5,5},{6,9},{7,13},{8,2},{9,6},{10,... | collective-permute-start | bytes 860168 | tf_op jit(solution)/shard_map/ppermute | solution.py:207
Sparse Core Ops, SparseCore 0:
  85.8 64.8 reduce-scatter.1

commit v17 on v15

--- a/solution.py
+++ b/solution.py
@@ -82,21 +82,22 @@
     return [pick(by_mask, own ^ source) for source in range(count)]
 
 
-def doubling_gather(block, axis):
+def doubling_gather(block, axis, rider):
     count = lax.axis_size(axis)
     own = lax.axis_index(axis)
     by_mask = {0: block}
     bit = count // 2
     while bit >= 1:
         keys = sorted(by_mask)
-        received = lax.ppermute(
-            jnp.stack([by_mask[key] for key in keys]), axis, [(i, i ^ bit) for i in range(count)]
-        )
+        outgoing = jnp.stack([by_mask[key] for key in keys])
+        if bit == 1:
+            outgoing, rider = lax.optimization_barrier((outgoing, rider))
+        received = lax.ppermute(outgoing, axis, [(i, i ^ bit) for i in range(count)])
         for at, key in enumerate(keys):
             by_mask[key ^ bit] = received[at]
         bit //= 2
     ordered = [by_mask[mask] for mask in range(count)]
-    return [pick(ordered, own ^ source) for source in range(count)]
+    return [pick(ordered, own ^ source) for source in range(count)], rider
 
 
 def rms_norm(features):
@@ -160,11 +161,11 @@
     ]
     by_row = jnp.concatenate(swap_chunks(depth_chunks, "row"), axis=1)
     frame_parts = lax.axis_size("frame")
-    by_frame = doubling_gather(by_row, "frame")
+    by_frame, weight_late = doubling_gather(by_row, "frame", in_weight)
     whole_frames = (
         frame_parts == row_parts and frame_parts % 2 == 0 and frame_count == 1 and row_count == 1
     )
-    weight_flat = in_weight.reshape(local_depth, 2 * local_gated)
+    weight_flat = weight_late.reshape(local_depth, 2 * local_gated)
     if whole_frames:
         tokens = jnp.stack([piece[0] for piece in by_frame])
         partial = jnp.dot(

time: 185 us -> 185 us (level)
  no operation moved by 1% of the time
where the time goes in v17:
time: 185 us; the launch traced here: 184 us
  waiting for transfers between devices  113 us (61%)
  starting transfers between devices  20.9 us (11%)
  between operations  14.6 us (8%)
  local copies, waits for them, and re-layouts  13.5 us (7%)
  other arithmetic  13 us (7%)
  matrix products  8.6 us (5%)
    reduce_scatter x1, waiting for transfers between devices, local(): summed = lax.psum_scatter(partial, 'row', scatter_dimension=0, tiled=True)  63.6 us
    ppermute x2, waiting for transfers between devices, local(): lax.ppermute(pick(pair_sums, chip_at ^ mask), ('frame', 'row'), [(f * row...  13.6 us
    ppermute x9, starting transfers between devices, swap_chunks(): lax.ppermute(sent, axis, [(i, i ^ mask) for i in range(count)])  13.4 us
    ppermute x9, waiting for transfers between devices, swap_chunks(): lax.ppermute(sent, axis, [(i, i ^ mask) for i in range(count)])  12.8 us
    ppermute x2, waiting for transfers between devices, doubling_gather(): lax.ppermute(outgoing, axis, [(i, i ^ bit) for i in range(count)])  8.4 us
    ppermute x2, waiting for transfers between devices, halving_sum(): lax.ppermute(sent, axis, [(i, i ^ bit) for i in range(count)])  7.45 us
    ppermute x2, starting transfers between devices, local(): lax.ppermute(pick(pair_sums, chip_at ^ mask), ('frame', 'row'), [(f * row...  6.04 us
    ppermute x2, waiting for transfers between devices, halving_sum(): lax.ppermute(block.astype(jnp.bfloat16), axis, [(i, i ^ bit) for i in ran...  5.6 us
  transfers between devices with their start and end apart: 19, of which 16 were waited for; matrix products, arithmetic and copies ran while one was open for 2% of the time, Pallas kernels for 0%

profile of v17, /device:TPU:2, one launch (start us, length us, event | category | flops | bytes accessed | tf_op | source)
XLA Modules:
  0.0 184.1 jit_solution(17835043015405754555)
XLA Ops:
  7.2 1.1 convert_reduce_fusion
  8.3 1.0 broadcast_maximum_fusion.1
  11.6 1.7 collective-permute-done
  13.3 1.2 convert_add_fusion.3
  14.6 5.8 %collective-permute-done.1 = bf16[113,560]{0,1:T(8,128)(2,1)S(1)} collective-permute-done((bf16[113,560]{0,1:T(8,128)(2,1)S(1)}, bf16[113,560]{0,1:T(8,128)(2,1)S(1)}, u32[]{:S(2)}, u32[]{:S(2)}) %collective-permute-start.1) | collective-permute-done | bytes 126592 | tf_op jit(solution)/shard_map/ppermute | solution.py:51
  20.5 3.7 %collective-permute-start.4 = (bf16[113,140]{0,1:T(8,128)(2,1)S(1)}, bf16[113,140]{0,1:T(8,128)(2,1)S(1)}, u32[]{:S(2)}, u32[]{:S(2)}) collective-permute-start(bf16[113,140]{0,1:T(8,128)(2,1)S(1)} %get-tuple-element.39), channel_id=1, source_target_pairs={{0,3},{1,2},{2,1},{3,0},{4,7},{5,6},{6,5},{7,4},{8,11},{9,10},{10,... | collective-permute-start | bytes 94928 | tf_op jit(solution)/shard_map/ppermute | solution.py:81
  25.0 1.6 collective-permute-done.4
  26.6 2.5 %collective-permute-done.3 = bf16[113,140]{0,1:T(8,128)(2,1)S(1)} collective-permute-done((bf16[113,140]{0,1:T(8,128)(2,1)S(1)}, bf16[113,140]{0,1:T(8,128)(2,1)S(1)}, u32[]{:S(2)}, u32[]{:S(2)}) %collective-permute-start.3) | collective-permute-done | bytes 31672 | tf_op jit(solution)/shard_map/ppermute | solution.py:81
  29.2 1.5 collective-permute-start.7
  31.3 2.3 %collective-permute-start.5 = (bf16[113,140]{0,1:T(8,128)(2,1)S(1)}, bf16[113,140]{0,1:T(8,128)(2,1)S(1)}, u32[]{:S(2)}, u32[]{:S(2)}) collective-permute-start(bf16[113,140]{0,1:T(8,128)(2,1)S(1)} %fusion.31), channel_id=1, source_target_pairs={{0,1},{1,0},{2,3},{3,2},{4,5},{5,4},{6,7},{7,6},{8,9},{9,8},{10,11... | collective-permute-start | bytes 94928 | tf_op jit(solution)/shard_map/ppermute | solution.py:81
  33.6 1.3 collective-permute-done.7
  36.7 4.6 %collective-permute-done.8 = bf16[113,560]{0,1:T(8,128)(2,1)S(1)} collective-permute-done((bf16[113,560]{0,1:T(8,128)(2,1)S(1)}, bf16[113,560]{0,1:T(8,128)(2,1)S(1)}, u32[]{:S(2)}, u32[]{:S(2)}) %collective-permute-start.8) | collective-permute-done | bytes 126592 | tf_op jit(solution)/shard_map/ppermute | solution.py:61
  43.1 1.0 collective-permute-done.9
  45.8 1.4 multiply_reduce_fusion
  50.1 2.4 %collective-permute-start.12 = (bf16[1,1,64,560]{3,2,1,0:T(8,128)(2,1)S(1)}, bf16[1,1,64,560]{3,2,1,0:T(8,128)(2,1)S(1)}, u32[]{:S(2)}, u32[]{:S(2)}) collective-permute-start(bf16[1,1,64,560]{3,2,1,0:T(8,128)(2,1)S(1)} %get-tuple-element.27), channel_id=1, source_target_pairs={{0,3},{1,2},{2,1},{3,0},{4,7},{5,6},{6,5},{7,4},{8,11},{9,10},{10,... | collective-permute-start | bytes 215048 | tf_op jit(solution)/shard_map/ppermute | solution.py:81
  53.3 1.3 collective-permute-start.10
  54.5 2.8 %collective-permute-done.12 = bf16[1,1,64,560]{3,2,1,0:T(8,128)(2,1)S(1)} collective-permute-done((bf16[1,1,64,560]{3,2,1,0:T(8,128)(2,1)S(1)}, bf16[1,1,64,560]{3,2,1,0:T(8,128)(2,1)S(1)}, u32[]{:S(2)}, u32[]{:S(2)}) %collective-permute-start.12) | collective-permute-done | bytes 71712 | tf_op jit(solution)/shard_map/ppermute | solution.py:81
  57.3 3.6 %collective-permute-done.11 = bf16[1,1,64,560]{3,2,1,0:T(8,128)(2,1)S(1)} collective-permute-done((bf16[1,1,64,560]{3,2,1,0:T(8,128)(2,1)S(1)}, bf16[1,1,64,560]{3,2,1,0:T(8,128)(2,1)S(1)}, u32[]{:S(2)}, u32[]{:S(2)}) %collective-permute-start.11) | collective-permute-done | bytes 71712 | tf_op jit(solution)/shard_map/ppermute | solution.py:81
  61.8 8.4 %collective-permute-done.13 = bf16[1,1,4,64,560]{4,3,2,1,0:T(8,128)(2,1)S(1)} collective-permute-done((bf16[1,1,4,64,560]{4,3,2,1,0:T(8,128)(2,1)S(1)}, bf16[1,1,4,64,560]{4,3,2,1,0:T(8,128)(2,1)S(1)}, u32[]{:S(2)}, u32[]{:S(2)}) %collective-permute-start.13) | collective-permute-done | bytes 286752 | tf_op jit(solution)/shard_map/ppermute | solution.py:95
  70.2 0.9 pad_maximum_fusion.2
  71.1 2.5 %reshape.239 = bf16[560,1680]{1,0:T(8,128)(2,1)} reshape(bf16[560,2,840]{2,1,0:T(2,128)(2,1)S(1)} %copy-done) | data formatting | bytes 3763200 | tf_op jit(solution)/shard_map/reshape | solution.py:168
  73.6 1.1 fusion.23
  75.4 1.3 copy-done.1
  76.7 4.4 %convolution_convert_fusion.1 = bf16[1024,1680]{0,1:T(8,128)(2,1)} fusion(bf16[1024,560]{1,0:T(8,128)(2,1)S(1)} %bitcast.121, bf16[560,1680]{1,0:T(8,128)(2,1)S(1)} %copy-done.1), kind=kOutput, calls=%fused_computation.1 | convolution fusion | flops 1928478720 | bytes 6469120 | tf_op jit(solution)/shard_map/dot_general | solution.py:171
  82.6 63.6 %reduce-scatter.2.cloned.1.call-done = bf16[256,1680]{0,1:T(8,128)(2,1)} async-done(((bf16[1024,1680]{0,1:T(8,128)(2,1)}), bf16[256,1680]{0,1:T(8,128)(2,1)}) %reduce-scatter.2.cloned.1.call-update) | async-done | bytes 860176 | tf_op jit(solution)/shard_map/reduce_scatter | solution.py:174
  146.2 1.6 fusion.3
  148.6 3.0 %multiply_add_fusion = f32[1,4,64,1680]{3,2,1,0:T(8,128)S(1)} fusion(bf16[1,4,64,1680]{3,2,1,0:T(8,128)(2,1)S(1)} %bitcast.117, bf16[1,6,64,1680]{3,2,1,0:T(8,128)(2,1)S(1)} %pad.8, f32[1680]{0:T(1024)S(1)} %mul.211, f32[1680]{0:T(1024)S(1)} %mul.208, f32[1680]{0:T(1024)S(1)} %mul.205, f32[1680]{0:T(1024)S(1)} %mul.202, f32[1680]{0:T(1024)S(1)} %mul.199, ...), kind=kLoop, calls=%fused_computation.4 | loop fusion | flops 11182080 | bytes 5922816 | tf_op jit(solution)/shard_map/add | solution.py:115
  151.9 1.8 convolution_convert_fusion
  154.6 2.0 %collective-permute-done.15 = bf16[2,64,2240]{2,1,0:T(8,128)(2,1)S(1)} collective-permute-done((bf16[2,64,2240]{2,1,0:T(8,128)(2,1)S(1)}, bf16[2,64,2240]{2,1,0:T(8,128)(2,1)S(1)}, u32[]{:S(2)}, u32[]{:S(2)}) %collective-permute-start.15) | collective-permute-done | bytes 573472 | tf_op jit(solution)/shard_map/ppermute | solution.py:194
  157.3 5.4 %collective-permute-start.16 = (bf16[64,2240]{1,0:T(8,128)(2,1)S(1)}, bf16[64,2240]{1,0:T(8,128)(2,1)S(1)}, u32[]{:S(2)}, u32[]{:S(2)}) collective-permute-start(bf16[64,2240]{1,0:T(8,128)(2,1)S(1)} %get-tuple-element.20), channel_id=1, source_target_pairs={{0,0},{1,4},{2,8},{3,12},{4,1},{5,5},{6,9},{7,13},{8,2},{9,6},{10,... | collective-permute-start | bytes 860168 | tf_op jit(solution)/shard_map/ppermute | solution.py:202
  162.8 10.3 %collective-permute-done.17 = bf16[64,2240]{1,0:T(8,128)(2,1)S(1)} collective-permute-done((bf16[64,2240]{1,0:T(8,128)(2,1)S(1)}, bf16[64,2240]{1,0:T(8,128)(2,1)S(1)}, u32[]{:S(2)}, u32[]{:S(2)}) %collective-permute-start.17) | collective-permute-done | bytes 286752 | tf_op jit(solution)/shard_map/ppermute | solution.py:202
  173.0 3.3 %collective-permute-done.16 = bf16[64,2240]{1,0:T(8,128)(2,1)S(1)} collective-permute-done((bf16[64,2240]{1,0:T(8,128)(2,1)S(1)}, bf16[64,2240]{1,0:T(8,128)(2,1)S(1)}, u32[]{:S(2)}, u32[]{:S(2)}) %collective-permute-start.16) | collective-permute-done | bytes 286752 | tf_op jit(solution)/shard_map/ppermute | solution.py:202
  (100 shorter events, 19.1 us)
Async XLA Ops:
  7.2 2.5 %copy-start.4 = (bf16[1,1,64,2240]{3,2,1,0:T(8,128)(2,1)S(1)}, bf16[1,1,64,2240]{3,2,1,0:T(8,128)(2,1)}, u32[]{:S(2)}) copy-start(bf16[1,1,64,2240]{3,2,1,0:T(8,128)(2,1)} %param.11) | copy-start | bytes 860164
  7.2 139.0 %reduce-scatter.2.cloned.1.call-start = ((), (), s32[]{:S(2)}) async-start(), calls=%async_computation.1 | async-start | bytes 4300800 | tf_op jit(solution)/shard_map/reduce_scatter | solution.py:174
  11.5 1.8 collective-permute-start
  14.5 5.9 %collective-permute-start.1 = (bf16[113,560]{0,1:T(8,128)(2,1)S(1)}, bf16[113,560]{0,1:T(8,128)(2,1)S(1)}, u32[]{:S(2)}, u32[]{:S(2)}) collective-permute-start(bf16[113,560]{0,1:T(8,128)(2,1)S(1)} %select_convert_fusion.1), channel_id=1, source_target_pairs={{0,8},{4,12},{8,0},{12,4},{1,9},{5,13},{9,1},{13,5},{2,10},{6,14},... | collective-permute-start | bytes 379688 | tf_op jit(solution)/shard_map/ppermute | solution.py:51
  20.5 6.1 %collective-permute-start.4 = (bf16[113,140]{0,1:T(8,128)(2,1)S(1)}, bf16[113,140]{0,1:T(8,128)(2,1)S(1)}, u32[]{:S(2)}, u32[]{:S(2)}) collective-permute-start(bf16[113,140]{0,1:T(8,128)(2,1)S(1)} %get-tuple-element.39), channel_id=1, source_target_pairs={{0,3},{1,2},{2,1},{3,0},{4,7},{5,6},{6,5},{7,4},{8,11},{9,10},{10,... | collective-permute-start | bytes 94928 | tf_op jit(solution)/shard_map/ppermute | solution.py:81
  24.2 4.9 %collective-permute-start.3 = (bf16[113,140]{0,1:T(8,128)(2,1)S(1)}, bf16[113,140]{0,1:T(8,128)(2,1)S(1)}, u32[]{:S(2)}, u32[]{:S(2)}) collective-permute-start(bf16[113,140]{0,1:T(8,128)(2,1)S(1)} %get-tuple-element.40), channel_id=1, source_target_pairs={{0,2},{1,3},{2,0},{3,1},{4,6},{5,7},{6,4},{7,5},{8,10},{9,11},{10,... | collective-permute-start | bytes 94928 | tf_op jit(solution)/shard_map/ppermute | solution.py:81
  24.2 4.9 %collective-permute-start.2 = (bf16[113,140]{0,1:T(8,128)(2,1)S(1)}, bf16[113,140]{0,1:T(8,128)(2,1)S(1)}, u32[]{:S(2)}, u32[]{:S(2)}) collective-permute-start(bf16[113,140]{0,1:T(8,128)(2,1)S(1)} %get-tuple-element.41), channel_id=1, source_target_pairs={{0,1},{1,0},{2,3},{3,2},{4,5},{5,4},{6,7},{7,6},{8,9},{9,8},{10,11... | collective-permute-start | bytes 94928 | tf_op jit(solution)/shard_map/ppermute | solution.py:81
  29.2 5.8 %collective-permute-start.7 = (bf16[113,140]{0,1:T(8,128)(2,1)S(1)}, bf16[113,140]{0,1:T(8,128)(2,1)S(1)}, u32[]{:S(2)}, u32[]{:S(2)}) collective-permute-start(bf16[113,140]{0,1:T(8,128)(2,1)S(1)} %fusion.31), channel_id=1, source_target_pairs={{0,3},{1,2},{2,1},{3,0},{4,7},{5,6},{6,5},{7,4},{8,11},{9,10},{10,... | collective-permute-start | bytes 94928 | tf_op jit(solution)/shard_map/ppermute | solution.py:81
  30.7 4.9 %collective-permute-start.6 = (bf16[113,140]{0,1:T(8,128)(2,1)S(1)}, bf16[113,140]{0,1:T(8,128)(2,1)S(1)}, u32[]{:S(2)}, u32[]{:S(2)}) collective-permute-start(bf16[113,140]{0,1:T(8,128)(2,1)S(1)} %fusion.31), channel_id=1, source_target_pairs={{0,2},{1,3},{2,0},{3,1},{4,6},{5,7},{6,4},{7,5},{8,10},{9,11},{10,... | collective-permute-start | bytes 94928 | tf_op jit(solution)/shard_map/ppermute | solution.py:81
  31.3 4.6 %collective-permute-start.5 = (bf16[113,140]{0,1:T(8,128)(2,1)S(1)}, bf16[113,140]{0,1:T(8,128)(2,1)S(1)}, u32[]{:S(2)}, u32[]{:S(2)}) collective-permute-start(bf16[113,140]{0,1:T(8,128)(2,1)S(1)} %fusion.31), channel_id=1, source_target_pairs={{0,1},{1,0},{2,3},{3,2},{4,5},{5,4},{6,7},{7,6},{8,9},{9,8},{10,11... | collective-permute-start | bytes 94928 | tf_op jit(solution)/shard_map/ppermute | solution.py:81
  36.1 6.5 %copy-start.3 = (bf16[1,1,64,2240]{3,2,1,0:T(8,128)(2,1)S(1)}, bf16[1,1,64,2240]{3,2,1,0:T(8,128)(2,1)}, u32[]{:S(2)}) copy-start(bf16[1,1,64,2240]{3,2,1,0:T(8,128)(2,1)} %param.9) | copy-start | bytes 860164
  36.1 5.2 %collective-permute-start.8 = (bf16[113,560]{0,1:T(8,128)(2,1)S(1)}, bf16[113,560]{0,1:T(8,128)(2,1)S(1)}, u32[]{:S(2)}, u32[]{:S(2)}) collective-permute-start(bf16[113,560]{0,1:T(8,128)(2,1)S(1)} %pad_maximum_fusion.9), channel_id=1, source_target_pairs={{0,8},{4,12},{8,0},{12,4},{1,9},{5,13},{9,1},{13,5},{2,10},{6,14},... | collective-permute-start | bytes 379688 | tf_op jit(solution)/shard_map/ppermute | solution.py:61
  41.9 0.8 copy-start.6
  42.4 0.7 copy-start.7
  42.5 1.6 collective-permute-start.9
  47.6 1.0 copy-start.2
  50.1 21.0 %copy-start = (bf16[560,2,840]{2,1,0:T(2,128)(2,1)S(1)}, bf16[560,2,840]{2,1,0:T(2,128)(2,1)}, u32[]{:S(2)}) copy-start(bf16[560,2,840]{2,1,0:T(2,128)(2,1)} %param.15) | copy-start | bytes 5644804
  50.1 7.3 %collective-permute-start.12 = (bf16[1,1,64,560]{3,2,1,0:T(8,128)(2,1)S(1)}, bf16[1,1,64,560]{3,2,1,0:T(8,128)(2,1)S(1)}, u32[]{:S(2)}, u32[]{:S(2)}) collective-permute-start(bf16[1,1,64,560]{3,2,1,0:T(8,128)(2,1)S(1)} %get-tuple-element.27), channel_id=1, source_target_pairs={{0,3},{1,2},{2,1},{3,0},{4,7},{5,6},{6,5},{7,4},{8,11},{9,10},{10,... | collective-permute-start | bytes 215048 | tf_op jit(solution)/shard_map/ppermute | solution.py:81
  52.5 8.5 %collective-permute-start.11 = (bf16[1,1,64,560]{3,2,1,0:T(8,128)(2,1)S(1)}, bf16[1,1,64,560]{3,2,1,0:T(8,128)(2,1)S(1)}, u32[]{:S(2)}, u32[]{:S(2)}) collective-permute-start(bf16[1,1,64,560]{3,2,1,0:T(8,128)(2,1)S(1)} %get-tuple-element.28), channel_id=1, source_target_pairs={{0,2},{1,3},{2,0},{3,1},{4,6},{5,7},{6,4},{7,5},{8,10},{9,11},{10,... | collective-permute-start | bytes 215048 | tf_op jit(solution)/shard_map/ppermute | solution.py:81
  53.3 7.7 %collective-permute-start.10 = (bf16[1,1,64,560]{3,2,1,0:T(8,128)(2,1)S(1)}, bf16[1,1,64,560]{3,2,1,0:T(8,128)(2,1)S(1)}, u32[]{:S(2)}, u32[]{:S(2)}) collective-permute-start(bf16[1,1,64,560]{3,2,1,0:T(8,128)(2,1)S(1)} %get-tuple-element.29), channel_id=1, source_target_pairs={{0,1},{1,0},{2,3},{3,2},{4,5},{5,4},{6,7},{7,6},{8,9},{9,8},{10,11... | collective-permute-start | bytes 215048 | tf_op jit(solution)/shard_map/ppermute | solution.py:81
  61.2 9.0 %collective-permute-start.13 = (bf16[1,1,4,64,560]{4,3,2,1,0:T(8,128)(2,1)S(1)}, bf16[1,1,4,64,560]{4,3,2,1,0:T(8,128)(2,1)S(1)}, u32[]{:S(2)}, u32[]{:S(2)}) collective-permute-start(bf16[1,1,4,64,560]{4,3,2,1,0:T(8,128)(2,1)S(1)} %maximum_bitcast_fusion), channel_id=1, source_target_pairs={{0,8},{4,12},{8,0},{12,4},{1,9},{5,13},{9,1},{13,5},{2,10},{6,14},... | collective-permute-start | bytes 860168 | tf_op jit(solution)/shard_map/ppermute | solution.py:95
  71.1 2.5 %collective-permute-start.14 = (bf16[2,1,4,64,560]{4,3,2,1,0:T(8,128)(2,1)}, bf16[2,1,4,64,560]{4,3,2,1,0:T(8,128)(2,1)}, u32[]{:S(2)}, u32[]{:S(2)}) collective-permute-start(bf16[2,1,4,64,560]{4,3,2,1,0:T(8,128)(2,1)} %pad_maximum_fusion.2), channel_id=1, source_target_pairs={{0,4},{4,0},{8,12},{12,8},{1,5},{5,1},{9,13},{13,9},{2,6},{6,2},{1... | collective-permute-start | bytes 1720328 | tf_op jit(solution)/shard_map/ppermute | solution.py:95
  75.1 1.6 copy-start.1
  81.1 0.8 copy-start.5
  148.6 3.3 %copy-start.8 = (bf16[840,2240]{1,0:T(8,128)(2,1)S(1)}, bf16[840,2240]{1,0:T(8,128)(2,1)}, u32[]{:S(2)}) copy-start(bf16[840,2240]{1,0:T(8,128)(2,1)} %param.17) | copy-start | bytes 11289604
  154.5 2.1 %collective-permute-start.15 = (bf16[2,64,2240]{2,1,0:T(8,128)(2,1)S(1)}, bf16[2,64,2240]{2,1,0:T(8,128)(2,1)S(1)}, u32[]{:S(2)}, u32[]{:S(2)}) collective-permute-start(bf16[2,64,2240]{2,1,0:T(8,128)(2,1)S(1)} %dynamic-slice_bitcast_fusion), channel_id=1, source_target_pairs={{0,4},{4,0},{8,12},{12,8},{1,5},{5,1},{9,13},{13,9},{2,6},{6,2},{1... | collective-permute-start | bytes 1720328 | tf_op jit(solution)/shard_map/ppermute | solution.py:194
  156.7 16.3 %collective-permute-start.17 = (bf16[64,2240]{1,0:T(8,128)(2,1)S(1)}, bf16[64,2240]{1,0:T(8,128)(2,1)S(1)}, u32[]{:S(2)}, u32[]{:S(2)}) collective-permute-start(bf16[64,2240]{1,0:T(8,128)(2,1)S(1)} %get-tuple-element.21), channel_id=1, source_target_pairs={{0,2},{1,6},{2,10},{3,14},{4,3},{5,7},{6,11},{7,15},{8,0},{9,4},{1... | collective-permute-start | bytes 860168 | tf_op jit(solution)/shard_map/ppermute | solution.py:202
  157.3 19.0 %collective-permute-start.16 = (bf16[64,2240]{1,0:T(8,128)(2,1)S(1)}, bf16[64,2240]{1,0:T(8,128)(2,1)S(1)}, u32[]{:S(2)}, u32[]{:S(2)}) collective-permute-start(bf16[64,2240]{1,0:T(8,128)(2,1)S(1)} %get-tuple-element.20), channel_id=1, source_target_pairs={{0,0},{1,4},{2,8},{3,12},{4,1},{5,5},{6,9},{7,13},{8,2},{9,6},{10,... | collective-permute-start | bytes 860168 | tf_op jit(solution)/shard_map/ppermute | solution.py:202
Sparse Core Ops, SparseCore 0:
  81.3 64.8 reduce-scatter.1

commit v18 on v15

--- a/solution.py
+++ b/solution.py
@@ -133,7 +133,8 @@
     for axis, count, bit in exchange_steps(("frame", "row")):
         parts *= 2
     padded_width = -(-model_width // parts) * parts
-    stats = jnp.pad(stats, ((0, 0), (0, padded_width - model_width)))
+    stat_rows = -(-stats.shape[0] // 16) * 16
+    stats = jnp.pad(stats, ((0, stat_rows - stats.shape[0]), (0, padded_width - model_width)))
     stats = halving_sum(stats, ("frame",), inner_axis="row")[:, :model_width]
     kv_state, key_total = stats[:HEAD_DIM], stats[HEAD_DIM]
     query_pos = jnp.maximum(query_in, 0).reshape(token_count, HEADS, HEAD_DIM).astype(jnp.float32)

time: 185 us -> 183 us (0.989)
  no operation moved by 1% of the time
where the time goes in v18:
time: 183 us
  waiting for transfers between devices  113 us (62%)
  starting transfers between devices  20.9 us (11%)
  between operations  14.6 us (8%)
  local copies, waits for them, and re-layouts  14 us (8%)
  other arithmetic  11.9 us (7%)
  matrix products  8.6 us (5%)
    reduce_scatter x1, waiting for transfers between devices, local(): summed = lax.psum_scatter(partial, 'row', scatter_dimension=0, tiled=True)  63.6 us
    ppermute x2, waiting for transfers between devices, local(): lax.ppermute(pick(pair_sums, chip_at ^ mask), ('frame', 'row'), [(f * row...  13.6 us
    ppermute x9, starting transfers between devices, swap_chunks(): lax.ppermute(sent, axis, [(i, i ^ mask) for i in range(count)])  13.4 us
    ppermute x9, waiting for transfers between devices, swap_chunks(): lax.ppermute(sent, axis, [(i, i ^ mask) for i in range(count)])  12.8 us
    ppermute x2, waiting for transfers between devices, doubling_gather(): lax.ppermute(jnp.stack([by_mask[key] for key in keys]), axis, [(i, i ^ bi...  8.4 us
    ppermute x2, waiting for transfers between devices, halving_sum(): lax.ppermute(sent, axis, [(i, i ^ bit) for i in range(count)])  7.32 us
    ppermute x2, starting transfers between devices, local(): lax.ppermute(pick(pair_sums, chip_at ^ mask), ('frame', 'row'), [(f * row...  6.03 us
    ppermute x2, waiting for transfers between devices, halving_sum(): lax.ppermute(block.astype(jnp.bfloat16), axis, [(i, i ^ bit) for i in ran...  5.15 us
  transfers between devices with their start and end apart: 19, of which 16 were waited for; matrix products, arithmetic and copies ran while one was open for 2% of the time, Pallas kernels for 0%

profile of v18, /device:TPU:2, one launch (start us, length us, event | category | flops | bytes accessed | tf_op | source)
XLA Modules:
  0.0 182.9 jit_solution(13465412411749931860)
XLA Ops:
  7.2 1.1 convert_reduce_fusion
  8.3 1.0 broadcast_maximum_fusion.1
  11.7 1.6 collective-permute-done
  13.5 5.8 %collective-permute-done.1 = bf16[128,560]{0,1:T(8,128)(2,1)S(1)} collective-permute-done((bf16[128,560]{0,1:T(8,128)(2,1)S(1)}, bf16[128,560]{0,1:T(8,128)(2,1)S(1)}, u32[]{:S(2)}, u32[]{:S(2)}) %collective-permute-start.1) | collective-permute-done | bytes 143392 | tf_op jit(solution)/shard_map/ppermute | solution.py:51
  19.4 3.7 %collective-permute-start.4 = (bf16[128,140]{0,1:T(8,128)(2,1)S(1)}, bf16[128,140]{0,1:T(8,128)(2,1)S(1)}, u32[]{:S(2)}, u32[]{:S(2)}) collective-permute-start(bf16[128,140]{0,1:T(8,128)(2,1)S(1)} %get-tuple-element.33), channel_id=1, source_target_pairs={{0,3},{1,2},{2,1},{3,0},{4,7},{5,6},{6,5},{7,4},{8,11},{9,10},{10,... | collective-permute-start | bytes 107528 | tf_op jit(solution)/shard_map/ppermute | solution.py:81
  23.9 1.6 collective-permute-done.4
  25.5 2.5 %collective-permute-done.3 = bf16[128,140]{0,1:T(8,128)(2,1)S(1)} collective-permute-done((bf16[128,140]{0,1:T(8,128)(2,1)S(1)}, bf16[128,140]{0,1:T(8,128)(2,1)S(1)}, u32[]{:S(2)}, u32[]{:S(2)}) %collective-permute-start.3) | collective-permute-done | bytes 35872 | tf_op jit(solution)/shard_map/ppermute | solution.py:81
  28.0 1.5 collective-permute-start.7
  30.2 2.3 %collective-permute-start.5 = (bf16[128,140]{0,1:T(8,128)(2,1)S(1)}, bf16[128,140]{0,1:T(8,128)(2,1)S(1)}, u32[]{:S(2)}, u32[]{:S(2)}) collective-permute-start(bf16[128,140]{0,1:T(8,128)(2,1)S(1)} %fusion.30), channel_id=1, source_target_pairs={{0,1},{1,0},{2,3},{3,2},{4,5},{5,4},{6,7},{7,6},{8,9},{9,8},{10,11... | collective-permute-start | bytes 107528 | tf_op jit(solution)/shard_map/ppermute | solution.py:81
  32.5 1.3 collective-permute-done.7
  35.5 4.6 %collective-permute-done.8 = bf16[128,560]{0,1:T(8,128)(2,1)S(1)} collective-permute-done((bf16[128,560]{0,1:T(8,128)(2,1)S(1)}, bf16[128,560]{0,1:T(8,128)(2,1)S(1)}, u32[]{:S(2)}, u32[]{:S(2)}) %collective-permute-start.8) | collective-permute-done | bytes 143392 | tf_op jit(solution)/shard_map/ppermute | solution.py:61
  44.6 1.4 multiply_reduce_fusion
  47.7 0.9 multiply_convert_fusion
  48.9 2.4 %collective-permute-start.12 = (bf16[1,1,64,560]{3,2,1,0:T(8,128)(2,1)S(1)}, bf16[1,1,64,560]{3,2,1,0:T(8,128)(2,1)S(1)}, u32[]{:S(2)}, u32[]{:S(2)}) collective-permute-start(bf16[1,1,64,560]{3,2,1,0:T(8,128)(2,1)S(1)} %get-tuple-element.21), channel_id=1, source_target_pairs={{0,3},{1,2},{2,1},{3,0},{4,7},{5,6},{6,5},{7,4},{8,11},{9,10},{10,... | collective-permute-start | bytes 215048 | tf_op jit(solution)/shard_map/ppermute | solution.py:81
  52.0 1.3 collective-permute-start.10
  53.3 2.8 %collective-permute-done.12 = bf16[1,1,64,560]{3,2,1,0:T(8,128)(2,1)S(1)} collective-permute-done((bf16[1,1,64,560]{3,2,1,0:T(8,128)(2,1)S(1)}, bf16[1,1,64,560]{3,2,1,0:T(8,128)(2,1)S(1)}, u32[]{:S(2)}, u32[]{:S(2)}) %collective-permute-start.12) | collective-permute-done | bytes 71712 | tf_op jit(solution)/shard_map/ppermute | solution.py:81
  56.1 3.6 %collective-permute-done.11 = bf16[1,1,64,560]{3,2,1,0:T(8,128)(2,1)S(1)} collective-permute-done((bf16[1,1,64,560]{3,2,1,0:T(8,128)(2,1)S(1)}, bf16[1,1,64,560]{3,2,1,0:T(8,128)(2,1)S(1)}, u32[]{:S(2)}, u32[]{:S(2)}) %collective-permute-start.11) | collective-permute-done | bytes 71712 | tf_op jit(solution)/shard_map/ppermute | solution.py:81
  60.6 8.4 %collective-permute-done.13 = bf16[1,1,4,64,560]{4,3,2,1,0:T(8,128)(2,1)S(1)} collective-permute-done((bf16[1,1,4,64,560]{4,3,2,1,0:T(8,128)(2,1)S(1)}, bf16[1,1,4,64,560]{4,3,2,1,0:T(8,128)(2,1)S(1)}, u32[]{:S(2)}, u32[]{:S(2)}) %collective-permute-start.13) | collective-permute-done | bytes 286752 | tf_op jit(solution)/shard_map/ppermute | solution.py:92
  69.0 1.0 pad_maximum_fusion.2
  69.9 2.5 %reshape.239 = bf16[560,1680]{1,0:T(8,128)(2,1)} reshape(bf16[560,2,840]{2,1,0:T(2,128)(2,1)S(1)} %copy-done) | data formatting | bytes 3763200 | tf_op jit(solution)/shard_map/reshape | solution.py:168
  72.4 1.1 fusion.22
  74.2 1.3 copy-done.1
  75.5 4.4 %convolution_convert_fusion.1 = bf16[1024,1680]{0,1:T(8,128)(2,1)} fusion(bf16[1024,560]{1,0:T(8,128)(2,1)S(1)} %bitcast.120, bf16[560,1680]{1,0:T(8,128)(2,1)S(1)} %copy-done.1), kind=kOutput, calls=%fused_computation.1 | convolution fusion | flops 1928478720 | bytes 6469120 | tf_op jit(solution)/shard_map/dot_general | solution.py:171
  81.4 63.6 %reduce-scatter.2.cloned.1.call-done = bf16[256,1680]{0,1:T(8,128)(2,1)} async-done(((bf16[1024,1680]{0,1:T(8,128)(2,1)}), bf16[256,1680]{0,1:T(8,128)(2,1)}) %reduce-scatter.2.cloned.1.call-update) | async-done | bytes 860176 | tf_op jit(solution)/shard_map/reduce_scatter | solution.py:174
  145.0 1.6 fusion.3
  147.4 3.0 %multiply_add_fusion = f32[1,4,64,1680]{3,2,1,0:T(8,128)S(1)} fusion(bf16[1,4,64,1680]{3,2,1,0:T(8,128)(2,1)S(1)} %bitcast.115, bf16[1,6,64,1680]{3,2,1,0:T(8,128)(2,1)S(1)} %pad.13, f32[1680]{0:T(1024)S(1)} %mul.211, f32[1680]{0:T(1024)S(1)} %mul.208, f32[1680]{0:T(1024)S(1)} %mul.205, f32[1680]{0:T(1024)S(1)} %mul.202, f32[1680]{0:T(1024)S(1)} %mul.199, ...), kind=kLoop, calls=%fused_computation.4 | loop fusion | flops 11182080 | bytes 5922816 | tf_op jit(solution)/shard_map/add | solution.py:114
  150.7 1.8 convolution_convert_fusion
  153.4 2.0 %collective-permute-done.15 = bf16[2,64,2240]{2,1,0:T(8,128)(2,1)S(1)} collective-permute-done((bf16[2,64,2240]{2,1,0:T(8,128)(2,1)S(1)}, bf16[2,64,2240]{2,1,0:T(8,128)(2,1)S(1)}, u32[]{:S(2)}, u32[]{:S(2)}) %collective-permute-start.15) | collective-permute-done | bytes 573472 | tf_op jit(solution)/shard_map/ppermute | solution.py:194
  156.1 5.4 %collective-permute-start.16 = (bf16[64,2240]{1,0:T(8,128)(2,1)S(1)}, bf16[64,2240]{1,0:T(8,128)(2,1)S(1)}, u32[]{:S(2)}, u32[]{:S(2)}) collective-permute-start(bf16[64,2240]{1,0:T(8,128)(2,1)S(1)} %get-tuple-element.14), channel_id=1, source_target_pairs={{0,0},{1,4},{2,8},{3,12},{4,1},{5,5},{6,9},{7,13},{8,2},{9,6},{10,... | collective-permute-start | bytes 860168 | tf_op jit(solution)/shard_map/ppermute | solution.py:202
  161.6 10.3 %collective-permute-done.17 = bf16[64,2240]{1,0:T(8,128)(2,1)S(1)} collective-permute-done((bf16[64,2240]{1,0:T(8,128)(2,1)S(1)}, bf16[64,2240]{1,0:T(8,128)(2,1)S(1)}, u32[]{:S(2)}, u32[]{:S(2)}) %collective-permute-start.17) | collective-permute-done | bytes 286752 | tf_op jit(solution)/shard_map/ppermute | solution.py:202
  171.9 3.3 %collective-permute-done.16 = bf16[64,2240]{1,0:T(8,128)(2,1)S(1)} collective-permute-done((bf16[64,2240]{1,0:T(8,128)(2,1)S(1)}, bf16[64,2240]{1,0:T(8,128)(2,1)S(1)}, u32[]{:S(2)}, u32[]{:S(2)}) %collective-permute-start.16) | collective-permute-done | bytes 286752 | tf_op jit(solution)/shard_map/ppermute | solution.py:202
  175.2 0.8 fusion.14
  (101 shorter events, 18.5 us)
Async XLA Ops:
  7.2 2.5 %copy-start.4 = (bf16[1,1,64,2240]{3,2,1,0:T(8,128)(2,1)S(1)}, bf16[1,1,64,2240]{3,2,1,0:T(8,128)(2,1)}, u32[]{:S(2)}) copy-start(bf16[1,1,64,2240]{3,2,1,0:T(8,128)(2,1)} %param.11) | copy-start | bytes 860164
  7.2 137.8 %reduce-scatter.2.cloned.1.call-start = ((), (), s32[]{:S(2)}) async-start(), calls=%async_computation.1 | async-start | bytes 4300800 | tf_op jit(solution)/shard_map/reduce_scatter | solution.py:174
  11.7 1.6 collective-permute-start
  13.4 5.9 %collective-permute-start.1 = (bf16[128,560]{0,1:T(8,128)(2,1)S(1)}, bf16[128,560]{0,1:T(8,128)(2,1)S(1)}, u32[]{:S(2)}, u32[]{:S(2)}) collective-permute-start(bf16[128,560]{0,1:T(8,128)(2,1)S(1)} %select_convert_fusion.1), channel_id=1, source_target_pairs={{0,8},{4,12},{8,0},{12,4},{1,9},{5,13},{9,1},{13,5},{2,10},{6,14},... | collective-permute-start | bytes 430088 | tf_op jit(solution)/shard_map/ppermute | solution.py:51
  19.4 6.1 %collective-permute-start.4 = (bf16[128,140]{0,1:T(8,128)(2,1)S(1)}, bf16[128,140]{0,1:T(8,128)(2,1)S(1)}, u32[]{:S(2)}, u32[]{:S(2)}) collective-permute-start(bf16[128,140]{0,1:T(8,128)(2,1)S(1)} %get-tuple-element.33), channel_id=1, source_target_pairs={{0,3},{1,2},{2,1},{3,0},{4,7},{5,6},{6,5},{7,4},{8,11},{9,10},{10,... | collective-permute-start | bytes 107528 | tf_op jit(solution)/shard_map/ppermute | solution.py:81
  23.1 4.9 %collective-permute-start.3 = (bf16[128,140]{0,1:T(8,128)(2,1)S(1)}, bf16[128,140]{0,1:T(8,128)(2,1)S(1)}, u32[]{:S(2)}, u32[]{:S(2)}) collective-permute-start(bf16[128,140]{0,1:T(8,128)(2,1)S(1)} %get-tuple-element.34), channel_id=1, source_target_pairs={{0,2},{1,3},{2,0},{3,1},{4,6},{5,7},{6,4},{7,5},{8,10},{9,11},{10,... | collective-permute-start | bytes 107528 | tf_op jit(solution)/shard_map/ppermute | solution.py:81
  23.1 4.9 %collective-permute-start.2 = (bf16[128,140]{0,1:T(8,128)(2,1)S(1)}, bf16[128,140]{0,1:T(8,128)(2,1)S(1)}, u32[]{:S(2)}, u32[]{:S(2)}) collective-permute-start(bf16[128,140]{0,1:T(8,128)(2,1)S(1)} %get-tuple-element.35), channel_id=1, source_target_pairs={{0,1},{1,0},{2,3},{3,2},{4,5},{5,4},{6,7},{7,6},{8,9},{9,8},{10,11... | collective-permute-start | bytes 107528 | tf_op jit(solution)/shard_map/ppermute | solution.py:81
  28.0 5.8 %collective-permute-start.7 = (bf16[128,140]{0,1:T(8,128)(2,1)S(1)}, bf16[128,140]{0,1:T(8,128)(2,1)S(1)}, u32[]{:S(2)}, u32[]{:S(2)}) collective-permute-start(bf16[128,140]{0,1:T(8,128)(2,1)S(1)} %fusion.30), channel_id=1, source_target_pairs={{0,3},{1,2},{2,1},{3,0},{4,7},{5,6},{6,5},{7,4},{8,11},{9,10},{10,... | collective-permute-start | bytes 107528 | tf_op jit(solution)/shard_map/ppermute | solution.py:81
  29.5 4.9 %collective-permute-start.6 = (bf16[128,140]{0,1:T(8,128)(2,1)S(1)}, bf16[128,140]{0,1:T(8,128)(2,1)S(1)}, u32[]{:S(2)}, u32[]{:S(2)}) collective-permute-start(bf16[128,140]{0,1:T(8,128)(2,1)S(1)} %fusion.30), channel_id=1, source_target_pairs={{0,2},{1,3},{2,0},{3,1},{4,6},{5,7},{6,4},{7,5},{8,10},{9,11},{10,... | collective-permute-start | bytes 107528 | tf_op jit(solution)/shard_map/ppermute | solution.py:81
  30.2 4.6 %collective-permute-start.5 = (bf16[128,140]{0,1:T(8,128)(2,1)S(1)}, bf16[128,140]{0,1:T(8,128)(2,1)S(1)}, u32[]{:S(2)}, u32[]{:S(2)}) collective-permute-start(bf16[128,140]{0,1:T(8,128)(2,1)S(1)} %fusion.30), channel_id=1, source_target_pairs={{0,1},{1,0},{2,3},{3,2},{4,5},{5,4},{6,7},{7,6},{8,9},{9,8},{10,11... | collective-permute-start | bytes 107528 | tf_op jit(solution)/shard_map/ppermute | solution.py:81
  34.9 5.2 %collective-permute-start.8 = (bf16[128,560]{0,1:T(8,128)(2,1)S(1)}, bf16[128,560]{0,1:T(8,128)(2,1)S(1)}, u32[]{:S(2)}, u32[]{:S(2)}) collective-permute-start(bf16[128,560]{0,1:T(8,128)(2,1)S(1)} %pad_maximum_fusion.8), channel_id=1, source_target_pairs={{0,8},{4,12},{8,0},{12,4},{1,9},{5,13},{9,1},{13,5},{2,10},{6,14},... | collective-permute-start | bytes 430088 | tf_op jit(solution)/shard_map/ppermute | solution.py:61
  40.7 1.0 copy-start.3
  41.2 0.7 copy-start.6
  41.3 1.1 copy-start.7
  41.4 1.6 collective-permute-start.9
  46.4 1.0 copy-start.2
  48.9 7.3 %collective-permute-start.12 = (bf16[1,1,64,560]{3,2,1,0:T(8,128)(2,1)S(1)}, bf16[1,1,64,560]{3,2,1,0:T(8,128)(2,1)S(1)}, u32[]{:S(2)}, u32[]{:S(2)}) collective-permute-start(bf16[1,1,64,560]{3,2,1,0:T(8,128)(2,1)S(1)} %get-tuple-element.21), channel_id=1, source_target_pairs={{0,3},{1,2},{2,1},{3,0},{4,7},{5,6},{6,5},{7,4},{8,11},{9,10},{10,... | collective-permute-start | bytes 215048 | tf_op jit(solution)/shard_map/ppermute | solution.py:81
  51.3 8.5 %collective-permute-start.11 = (bf16[1,1,64,560]{3,2,1,0:T(8,128)(2,1)S(1)}, bf16[1,1,64,560]{3,2,1,0:T(8,128)(2,1)S(1)}, u32[]{:S(2)}, u32[]{:S(2)}) collective-permute-start(bf16[1,1,64,560]{3,2,1,0:T(8,128)(2,1)S(1)} %get-tuple-element.22), channel_id=1, source_target_pairs={{0,2},{1,3},{2,0},{3,1},{4,6},{5,7},{6,4},{7,5},{8,10},{9,11},{10,... | collective-permute-start | bytes 215048 | tf_op jit(solution)/shard_map/ppermute | solution.py:81
  52.0 7.7 %collective-permute-start.10 = (bf16[1,1,64,560]{3,2,1,0:T(8,128)(2,1)S(1)}, bf16[1,1,64,560]{3,2,1,0:T(8,128)(2,1)S(1)}, u32[]{:S(2)}, u32[]{:S(2)}) collective-permute-start(bf16[1,1,64,560]{3,2,1,0:T(8,128)(2,1)S(1)} %get-tuple-element.23), channel_id=1, source_target_pairs={{0,1},{1,0},{2,3},{3,2},{4,5},{5,4},{6,7},{7,6},{8,9},{9,8},{10,11... | collective-permute-start | bytes 215048 | tf_op jit(solution)/shard_map/ppermute | solution.py:81
  59.8 10.1 %copy-start = (bf16[560,2,840]{2,1,0:T(2,128)(2,1)S(1)}, bf16[560,2,840]{2,1,0:T(2,128)(2,1)}, u32[]{:S(2)}) copy-start(bf16[560,2,840]{2,1,0:T(2,128)(2,1)} %param.15) | copy-start | bytes 5644804
  60.0 9.0 %collective-permute-start.13 = (bf16[1,1,4,64,560]{4,3,2,1,0:T(8,128)(2,1)S(1)}, bf16[1,1,4,64,560]{4,3,2,1,0:T(8,128)(2,1)S(1)}, u32[]{:S(2)}, u32[]{:S(2)}) collective-permute-start(bf16[1,1,4,64,560]{4,3,2,1,0:T(8,128)(2,1)S(1)} %maximum_bitcast_fusion), channel_id=1, source_target_pairs={{0,8},{4,12},{8,0},{12,4},{1,9},{5,13},{9,1},{13,5},{2,10},{6,14},... | collective-permute-start | bytes 860168 | tf_op jit(solution)/shard_map/ppermute | solution.py:92
  69.9 2.5 %collective-permute-start.14 = (bf16[2,1,4,64,560]{4,3,2,1,0:T(8,128)(2,1)}, bf16[2,1,4,64,560]{4,3,2,1,0:T(8,128)(2,1)}, u32[]{:S(2)}, u32[]{:S(2)}) collective-permute-start(bf16[2,1,4,64,560]{4,3,2,1,0:T(8,128)(2,1)} %pad_maximum_fusion.2), channel_id=1, source_target_pairs={{0,4},{4,0},{8,12},{12,8},{1,5},{5,1},{9,13},{13,9},{2,6},{6,2},{1... | collective-permute-start | bytes 1720328 | tf_op jit(solution)/shard_map/ppermute | solution.py:92
  73.9 1.6 copy-start.1
  79.9 0.8 copy-start.5
  147.4 3.3 %copy-start.8 = (bf16[840,2240]{1,0:T(8,128)(2,1)S(1)}, bf16[840,2240]{1,0:T(8,128)(2,1)}, u32[]{:S(2)}) copy-start(bf16[840,2240]{1,0:T(8,128)(2,1)} %param.17) | copy-start | bytes 11289604
  153.3 2.1 %collective-permute-start.15 = (bf16[2,64,2240]{2,1,0:T(8,128)(2,1)S(1)}, bf16[2,64,2240]{2,1,0:T(8,128)(2,1)S(1)}, u32[]{:S(2)}, u32[]{:S(2)}) collective-permute-start(bf16[2,64,2240]{2,1,0:T(8,128)(2,1)S(1)} %dynamic-slice_bitcast_fusion), channel_id=1, source_target_pairs={{0,4},{4,0},{8,12},{12,8},{1,5},{5,1},{9,13},{13,9},{2,6},{6,2},{1... | collective-permute-start | bytes 1720328 | tf_op jit(solution)/shard_map/ppermute | solution.py:194
  155.6 16.3 %collective-permute-start.17 = (bf16[64,2240]{1,0:T(8,128)(2,1)S(1)}, bf16[64,2240]{1,0:T(8,128)(2,1)S(1)}, u32[]{:S(2)}, u32[]{:S(2)}) collective-permute-start(bf16[64,2240]{1,0:T(8,128)(2,1)S(1)} %get-tuple-element.15), channel_id=1, source_target_pairs={{0,2},{1,6},{2,10},{3,14},{4,3},{5,7},{6,11},{7,15},{8,0},{9,4},{1... | collective-permute-start | bytes 860168 | tf_op jit(solution)/shard_map/ppermute | solution.py:202
  156.1 19.0 %collective-permute-start.16 = (bf16[64,2240]{1,0:T(8,128)(2,1)S(1)}, bf16[64,2240]{1,0:T(8,128)(2,1)S(1)}, u32[]{:S(2)}, u32[]{:S(2)}) collective-permute-start(bf16[64,2240]{1,0:T(8,128)(2,1)S(1)} %get-tuple-element.14), channel_id=1, source_target_pairs={{0,0},{1,4},{2,8},{3,12},{4,1},{5,5},{6,9},{7,13},{8,2},{9,6},{10,... | collective-permute-start | bytes 860168 | tf_op jit(solution)/shard_map/ppermute | solution.py:202
Sparse Core Ops, SparseCore 0:
  80.1 64.8 reduce-scatter.1

commit v19 on v18

--- a/solution.py
+++ b/solution.py
@@ -156,8 +156,13 @@
     conv_taps = conv_weight.reshape(9, 2 * local_gated).astype(jnp.float32)
     row_parts = lax.axis_size("row")
     local_depth = in_weight.shape[0]
+    lane_depth = -(-local_depth // 128) * 128
     depth_chunks = [
-        normed_grid[..., part * local_depth : (part + 1) * local_depth] for part in range(row_parts)
+        jnp.pad(
+            normed_grid[..., part * local_depth : (part + 1) * local_depth],
+            ((0, 0), (0, 0), (0, 0), (0, lane_depth - local_depth)),
+        )
+        for part in range(row_parts)
     ]
     by_row = jnp.concatenate(swap_chunks(depth_chunks, "row"), axis=1)
     frame_parts = lax.axis_size("frame")
@@ -165,11 +170,13 @@
     whole_frames = (
         frame_parts == row_parts and frame_parts % 2 == 0 and frame_count == 1 and row_count == 1
     )
-    weight_flat = in_weight.reshape(local_depth, 2 * local_gated)
+    weight_flat = jnp.pad(
+        in_weight.reshape(local_depth, 2 * local_gated), ((0, lane_depth - local_depth), (0, 0))
+    )
     if whole_frames:
         tokens = jnp.stack([piece[0] for piece in by_frame])
         partial = jnp.dot(
-            tokens.reshape(-1, local_depth), weight_flat, preferred_element_type=jnp.float32
+            tokens.reshape(-1, lane_depth), weight_flat, preferred_element_type=jnp.float32
         ).astype(jnp.bfloat16)
         summed = lax.psum_scatter(partial, "row", scatter_dimension=0, tiled=True)
         frame_rows = tokens.shape[1]
@@ -216,7 +223,7 @@
     tokens = jnp.stack([piece.transpose(1, 0, 2, 3) for piece in by_frame], axis=1)
     piece_frames = tokens.shape[1] * tokens.shape[2]
     partial = jnp.dot(
-        tokens.reshape(-1, local_depth), weight_flat, preferred_element_type=jnp.float32
+        tokens.reshape(-1, lane_depth), weight_flat, preferred_element_type=jnp.float32
     ).astype(jnp.bfloat16)
     summed = lax.psum_scatter(partial, "row", scatter_dimension=0, tiled=True).reshape(
         piece_frames, row_count, col_count, 2 * local_gated

time: 183 us -> 183 us (level)
  no operation moved by 1% of the time
where the time goes in v19:
time: 183 us
  waiting for transfers between devices  113 us (62%)
  starting transfers between devices  20.9 us (11%)
  between operations  14.6 us (8%)
  local copies, waits for them, and re-layouts  14.1 us (8%)
  other arithmetic  11.7 us (6%)
  matrix products  8.62 us (5%)
    reduce_scatter x1, waiting for transfers between devices, local(): summed = lax.psum_scatter(partial, 'row', scatter_dimension=0, tiled=True)  63.6 us
    ppermute x2, waiting for transfers between devices, local(): lax.ppermute(pick(pair_sums, chip_at ^ mask), ('frame', 'row'), [(f * row...  13.6 us
    ppermute x9, starting transfers between devices, swap_chunks(): lax.ppermute(sent, axis, [(i, i ^ mask) for i in range(count)])  13.4 us
    ppermute x9, waiting for transfers between devices, swap_chunks(): lax.ppermute(sent, axis, [(i, i ^ mask) for i in range(count)])  12.8 us
    ppermute x2, waiting for transfers between devices, doubling_gather(): lax.ppermute(jnp.stack([by_mask[key] for key in keys]), axis, [(i, i ^ bi...  8.4 us
    ppermute x2, waiting for transfers between devices, halving_sum(): lax.ppermute(sent, axis, [(i, i ^ bit) for i in range(count)])  7.32 us
    ppermute x2, starting transfers between devices, local(): lax.ppermute(pick(pair_sums, chip_at ^ mask), ('frame', 'row'), [(f * row...  6.03 us
    ppermute x2, waiting for transfers between devices, halving_sum(): lax.ppermute(block.astype(jnp.bfloat16), axis, [(i, i ^ bit) for i in ran...  5.15 us
  transfers between devices with their start and end apart: 19, of which 16 were waited for; matrix products, arithmetic and copies ran while one was open for 2% of the time, Pallas kernels for 0%

profile of v19, /device:TPU:2, one launch (start us, length us, event | category | flops | bytes accessed | tf_op | source)
XLA Modules:
  0.0 182.8 jit_solution(10703582922854195035)
XLA Ops:
  7.2 1.1 convert_reduce_fusion
  8.3 1.0 broadcast_maximum_fusion.1
  11.7 1.6 collective-permute-done
  13.5 5.8 %collective-permute-done.1 = bf16[128,560]{0,1:T(8,128)(2,1)S(1)} collective-permute-done((bf16[128,560]{0,1:T(8,128)(2,1)S(1)}, bf16[128,560]{0,1:T(8,128)(2,1)S(1)}, u32[]{:S(2)}, u32[]{:S(2)}) %collective-permute-start.1) | collective-permute-done | bytes 143392 | tf_op jit(solution)/shard_map/ppermute | solution.py:51
  19.4 3.7 %collective-permute-start.4 = (bf16[128,140]{0,1:T(8,128)(2,1)S(1)}, bf16[128,140]{0,1:T(8,128)(2,1)S(1)}, u32[]{:S(2)}, u32[]{:S(2)}) collective-permute-start(bf16[128,140]{0,1:T(8,128)(2,1)S(1)} %get-tuple-element.32), channel_id=1, source_target_pairs={{0,3},{1,2},{2,1},{3,0},{4,7},{5,6},{6,5},{7,4},{8,11},{9,10},{10,... | collective-permute-start | bytes 107528 | tf_op jit(solution)/shard_map/ppermute | solution.py:81
  23.9 1.6 collective-permute-done.4
  25.5 2.5 %collective-permute-done.3 = bf16[128,140]{0,1:T(8,128)(2,1)S(1)} collective-permute-done((bf16[128,140]{0,1:T(8,128)(2,1)S(1)}, bf16[128,140]{0,1:T(8,128)(2,1)S(1)}, u32[]{:S(2)}, u32[]{:S(2)}) %collective-permute-start.3) | collective-permute-done | bytes 35872 | tf_op jit(solution)/shard_map/ppermute | solution.py:81
  28.0 1.5 collective-permute-start.7
  30.2 2.3 %collective-permute-start.5 = (bf16[128,140]{0,1:T(8,128)(2,1)S(1)}, bf16[128,140]{0,1:T(8,128)(2,1)S(1)}, u32[]{:S(2)}, u32[]{:S(2)}) collective-permute-start(bf16[128,140]{0,1:T(8,128)(2,1)S(1)} %fusion.33), channel_id=1, source_target_pairs={{0,1},{1,0},{2,3},{3,2},{4,5},{5,4},{6,7},{7,6},{8,9},{9,8},{10,11... | collective-permute-start | bytes 107528 | tf_op jit(solution)/shard_map/ppermute | solution.py:81
  32.5 1.3 collective-permute-done.7
  35.5 4.6 %collective-permute-done.8 = bf16[128,560]{0,1:T(8,128)(2,1)S(1)} collective-permute-done((bf16[128,560]{0,1:T(8,128)(2,1)S(1)}, bf16[128,560]{0,1:T(8,128)(2,1)S(1)}, u32[]{:S(2)}, u32[]{:S(2)}) %collective-permute-start.8) | collective-permute-done | bytes 143392 | tf_op jit(solution)/shard_map/ppermute | solution.py:61
  44.6 1.4 multiply_reduce_fusion
  47.7 0.9 multiply_convert_fusion
  48.9 2.4 %collective-permute-start.12 = (bf16[1,1,64,640]{3,2,1,0:T(8,128)(2,1)S(1)}, bf16[1,1,64,640]{3,2,1,0:T(8,128)(2,1)S(1)}, u32[]{:S(2)}, u32[]{:S(2)}) collective-permute-start(bf16[1,1,64,640]{3,2,1,0:T(8,128)(2,1)S(1)} %get-tuple-element.21), channel_id=1, source_target_pairs={{0,3},{1,2},{2,1},{3,0},{4,7},{5,6},{6,5},{7,4},{8,11},{9,10},{10,... | collective-permute-start | bytes 245768 | tf_op jit(solution)/shard_map/ppermute | solution.py:81
  52.1 1.3 collective-permute-start.10
  53.4 2.8 %collective-permute-done.12 = bf16[1,1,64,640]{3,2,1,0:T(8,128)(2,1)S(1)} collective-permute-done((bf16[1,1,64,640]{3,2,1,0:T(8,128)(2,1)S(1)}, bf16[1,1,64,640]{3,2,1,0:T(8,128)(2,1)S(1)}, u32[]{:S(2)}, u32[]{:S(2)}) %collective-permute-start.12) | collective-permute-done | bytes 81952 | tf_op jit(solution)/shard_map/ppermute | solution.py:81
  56.2 3.6 %collective-permute-done.11 = bf16[1,1,64,640]{3,2,1,0:T(8,128)(2,1)S(1)} collective-permute-done((bf16[1,1,64,640]{3,2,1,0:T(8,128)(2,1)S(1)}, bf16[1,1,64,640]{3,2,1,0:T(8,128)(2,1)S(1)}, u32[]{:S(2)}, u32[]{:S(2)}) %collective-permute-start.11) | collective-permute-done | bytes 81952 | tf_op jit(solution)/shard_map/ppermute | solution.py:81
  60.6 8.4 %collective-permute-done.13 = bf16[1,1,4,64,640]{4,3,2,1,0:T(8,128)(2,1)S(1)} collective-permute-done((bf16[1,1,4,64,640]{4,3,2,1,0:T(8,128)(2,1)S(1)}, bf16[1,1,4,64,640]{4,3,2,1,0:T(8,128)(2,1)S(1)}, u32[]{:S(2)}, u32[]{:S(2)}) %collective-permute-start.13) | collective-permute-done | bytes 327712 | tf_op jit(solution)/shard_map/ppermute | solution.py:92
  69.0 0.9 pad_maximum_fusion.2
  69.9 2.4 %reshape.239 = bf16[560,1680]{1,0:T(8,128)(2,1)} reshape(bf16[560,2,840]{2,1,0:T(2,128)(2,1)S(1)} %copy-done) | data formatting | bytes 3763200 | tf_op jit(solution)/shard_map/reshape | solution.py:174
  72.4 1.1 fusion.25
  74.1 1.3 copy-done.1
  75.4 4.5 %convolution_convert_fusion.1 = bf16[1024,1680]{0,1:T(8,128)(2,1)} fusion(bf16[1024,640]{1,0:T(8,128)(2,1)S(1)} %bitcast.119, bf16[560,1680]{1,0:T(8,128)(2,1)S(1)} %copy-done.1), kind=kOutput, calls=%fused_computation.1 | convolution fusion | flops 2203729920 | bytes 6632960 | tf_op jit(solution)/shard_map/dot_general | solution.py:178
  81.4 63.6 %reduce-scatter.2.cloned.1.call-done = bf16[256,1680]{0,1:T(8,128)(2,1)} async-done(((bf16[1024,1680]{0,1:T(8,128)(2,1)}), bf16[256,1680]{0,1:T(8,128)(2,1)}) %reduce-scatter.2.cloned.1.call-update) | async-done | bytes 860176 | tf_op jit(solution)/shard_map/reduce_scatter | solution.py:181
  144.9 1.6 fusion.4
  147.3 3.0 %multiply_add_fusion = f32[1,4,64,1680]{3,2,1,0:T(8,128)S(1)} fusion(bf16[1,4,64,1680]{3,2,1,0:T(8,128)(2,1)S(1)} %bitcast.114, bf16[1,6,64,1680]{3,2,1,0:T(8,128)(2,1)S(1)} %pad.35, f32[1680]{0:T(1024)S(1)} %mul.211, f32[1680]{0:T(1024)S(1)} %mul.208, f32[1680]{0:T(1024)S(1)} %mul.205, f32[1680]{0:T(1024)S(1)} %mul.202, f32[1680]{0:T(1024)S(1)} %mul.199, ...), kind=kLoop, calls=%fused_computation.5 | loop fusion | flops 11182080 | bytes 5922816 | tf_op jit(solution)/shard_map/add | solution.py:114
  150.6 1.8 convolution_convert_fusion
  153.3 2.0 %collective-permute-done.15 = bf16[2,64,2240]{2,1,0:T(8,128)(2,1)S(1)} collective-permute-done((bf16[2,64,2240]{2,1,0:T(8,128)(2,1)S(1)}, bf16[2,64,2240]{2,1,0:T(8,128)(2,1)S(1)}, u32[]{:S(2)}, u32[]{:S(2)}) %collective-permute-start.15) | collective-permute-done | bytes 573472 | tf_op jit(solution)/shard_map/ppermute | solution.py:201
  156.1 5.4 %collective-permute-start.16 = (bf16[64,2240]{1,0:T(8,128)(2,1)S(1)}, bf16[64,2240]{1,0:T(8,128)(2,1)S(1)}, u32[]{:S(2)}, u32[]{:S(2)}) collective-permute-start(bf16[64,2240]{1,0:T(8,128)(2,1)S(1)} %get-tuple-element.14), channel_id=1, source_target_pairs={{0,0},{1,4},{2,8},{3,12},{4,1},{5,5},{6,9},{7,13},{8,2},{9,6},{10,... | collective-permute-start | bytes 860168 | tf_op jit(solution)/shard_map/ppermute | solution.py:209
  161.5 10.3 %collective-permute-done.17 = bf16[64,2240]{1,0:T(8,128)(2,1)S(1)} collective-permute-done((bf16[64,2240]{1,0:T(8,128)(2,1)S(1)}, bf16[64,2240]{1,0:T(8,128)(2,1)S(1)}, u32[]{:S(2)}, u32[]{:S(2)}) %collective-permute-start.17) | collective-permute-done | bytes 286752 | tf_op jit(solution)/shard_map/ppermute | solution.py:209
  171.8 3.3 %collective-permute-done.16 = bf16[64,2240]{1,0:T(8,128)(2,1)S(1)} collective-permute-done((bf16[64,2240]{1,0:T(8,128)(2,1)S(1)}, bf16[64,2240]{1,0:T(8,128)(2,1)S(1)}, u32[]{:S(2)}, u32[]{:S(2)}) %collective-permute-start.16) | collective-permute-done | bytes 286752 | tf_op jit(solution)/shard_map/ppermute | solution.py:209
  175.1 0.8 fusion.15
  (105 shorter events, 18.4 us)
Async XLA Ops:
  7.2 2.5 %copy-start.4 = (bf16[1,1,64,2240]{3,2,1,0:T(8,128)(2,1)S(1)}, bf16[1,1,64,2240]{3,2,1,0:T(8,128)(2,1)}, u32[]{:S(2)}) copy-start(bf16[1,1,64,2240]{3,2,1,0:T(8,128)(2,1)} %param.11) | copy-start | bytes 860164
  7.2 137.8 %reduce-scatter.2.cloned.1.call-start = ((), (), s32[]{:S(2)}) async-start(), calls=%async_computation.1 | async-start | bytes 4300800 | tf_op jit(solution)/shard_map/reduce_scatter | solution.py:181
  11.7 1.6 collective-permute-start
  13.4 5.9 %collective-permute-start.1 = (bf16[128,560]{0,1:T(8,128)(2,1)S(1)}, bf16[128,560]{0,1:T(8,128)(2,1)S(1)}, u32[]{:S(2)}, u32[]{:S(2)}) collective-permute-start(bf16[128,560]{0,1:T(8,128)(2,1)S(1)} %select_convert_fusion.1), channel_id=1, source_target_pairs={{0,8},{4,12},{8,0},{12,4},{1,9},{5,13},{9,1},{13,5},{2,10},{6,14},... | collective-permute-start | bytes 430088 | tf_op jit(solution)/shard_map/ppermute | solution.py:51
  19.4 6.1 %collective-permute-start.4 = (bf16[128,140]{0,1:T(8,128)(2,1)S(1)}, bf16[128,140]{0,1:T(8,128)(2,1)S(1)}, u32[]{:S(2)}, u32[]{:S(2)}) collective-permute-start(bf16[128,140]{0,1:T(8,128)(2,1)S(1)} %get-tuple-element.32), channel_id=1, source_target_pairs={{0,3},{1,2},{2,1},{3,0},{4,7},{5,6},{6,5},{7,4},{8,11},{9,10},{10,... | collective-permute-start | bytes 107528 | tf_op jit(solution)/shard_map/ppermute | solution.py:81
  23.1 4.9 %collective-permute-start.3 = (bf16[128,140]{0,1:T(8,128)(2,1)S(1)}, bf16[128,140]{0,1:T(8,128)(2,1)S(1)}, u32[]{:S(2)}, u32[]{:S(2)}) collective-permute-start(bf16[128,140]{0,1:T(8,128)(2,1)S(1)} %get-tuple-element.33), channel_id=1, source_target_pairs={{0,2},{1,3},{2,0},{3,1},{4,6},{5,7},{6,4},{7,5},{8,10},{9,11},{10,... | collective-permute-start | bytes 107528 | tf_op jit(solution)/shard_map/ppermute | solution.py:81
  23.1 4.9 %collective-permute-start.2 = (bf16[128,140]{0,1:T(8,128)(2,1)S(1)}, bf16[128,140]{0,1:T(8,128)(2,1)S(1)}, u32[]{:S(2)}, u32[]{:S(2)}) collective-permute-start(bf16[128,140]{0,1:T(8,128)(2,1)S(1)} %get-tuple-element.34), channel_id=1, source_target_pairs={{0,1},{1,0},{2,3},{3,2},{4,5},{5,4},{6,7},{7,6},{8,9},{9,8},{10,11... | collective-permute-start | bytes 107528 | tf_op jit(solution)/shard_map/ppermute | solution.py:81
  28.0 5.8 %collective-permute-start.7 = (bf16[128,140]{0,1:T(8,128)(2,1)S(1)}, bf16[128,140]{0,1:T(8,128)(2,1)S(1)}, u32[]{:S(2)}, u32[]{:S(2)}) collective-permute-start(bf16[128,140]{0,1:T(8,128)(2,1)S(1)} %fusion.33), channel_id=1, source_target_pairs={{0,3},{1,2},{2,1},{3,0},{4,7},{5,6},{6,5},{7,4},{8,11},{9,10},{10,... | collective-permute-start | bytes 107528 | tf_op jit(solution)/shard_map/ppermute | solution.py:81
  29.5 4.9 %collective-permute-start.6 = (bf16[128,140]{0,1:T(8,128)(2,1)S(1)}, bf16[128,140]{0,1:T(8,128)(2,1)S(1)}, u32[]{:S(2)}, u32[]{:S(2)}) collective-permute-start(bf16[128,140]{0,1:T(8,128)(2,1)S(1)} %fusion.33), channel_id=1, source_target_pairs={{0,2},{1,3},{2,0},{3,1},{4,6},{5,7},{6,4},{7,5},{8,10},{9,11},{10,... | collective-permute-start | bytes 107528 | tf_op jit(solution)/shard_map/ppermute | solution.py:81
  30.2 4.6 %collective-permute-start.5 = (bf16[128,140]{0,1:T(8,128)(2,1)S(1)}, bf16[128,140]{0,1:T(8,128)(2,1)S(1)}, u32[]{:S(2)}, u32[]{:S(2)}) collective-permute-start(bf16[128,140]{0,1:T(8,128)(2,1)S(1)} %fusion.33), channel_id=1, source_target_pairs={{0,1},{1,0},{2,3},{3,2},{4,5},{5,4},{6,7},{7,6},{8,9},{9,8},{10,11... | collective-permute-start | bytes 107528 | tf_op jit(solution)/shard_map/ppermute | solution.py:81
  34.9 5.2 %collective-permute-start.8 = (bf16[128,560]{0,1:T(8,128)(2,1)S(1)}, bf16[128,560]{0,1:T(8,128)(2,1)S(1)}, u32[]{:S(2)}, u32[]{:S(2)}) collective-permute-start(bf16[128,560]{0,1:T(8,128)(2,1)S(1)} %pad_maximum_fusion.8), channel_id=1, source_target_pairs={{0,8},{4,12},{8,0},{12,4},{1,9},{5,13},{9,1},{13,5},{2,10},{6,14},... | collective-permute-start | bytes 430088 | tf_op jit(solution)/shard_map/ppermute | solution.py:61
  40.7 1.0 copy-start.3
  41.2 0.7 copy-start.6
  41.3 1.1 copy-start.7
  41.4 1.6 collective-permute-start.9
  46.4 1.0 copy-start.2
  47.7 1.1 copy-start.8
  48.9 7.3 %collective-permute-start.12 = (bf16[1,1,64,640]{3,2,1,0:T(8,128)(2,1)S(1)}, bf16[1,1,64,640]{3,2,1,0:T(8,128)(2,1)S(1)}, u32[]{:S(2)}, u32[]{:S(2)}) collective-permute-start(bf16[1,1,64,640]{3,2,1,0:T(8,128)(2,1)S(1)} %get-tuple-element.21), channel_id=1, source_target_pairs={{0,3},{1,2},{2,1},{3,0},{4,7},{5,6},{6,5},{7,4},{8,11},{9,10},{10,... | collective-permute-start | bytes 245768 | tf_op jit(solution)/shard_map/ppermute | solution.py:81
  51.3 8.5 %collective-permute-start.11 = (bf16[1,1,64,640]{3,2,1,0:T(8,128)(2,1)S(1)}, bf16[1,1,64,640]{3,2,1,0:T(8,128)(2,1)S(1)}, u32[]{:S(2)}, u32[]{:S(2)}) collective-permute-start(bf16[1,1,64,640]{3,2,1,0:T(8,128)(2,1)S(1)} %get-tuple-element.22), channel_id=1, source_target_pairs={{0,2},{1,3},{2,0},{3,1},{4,6},{5,7},{6,4},{7,5},{8,10},{9,11},{10,... | collective-permute-start | bytes 245768 | tf_op jit(solution)/shard_map/ppermute | solution.py:81
  52.1 7.7 %collective-permute-start.10 = (bf16[1,1,64,640]{3,2,1,0:T(8,128)(2,1)S(1)}, bf16[1,1,64,640]{3,2,1,0:T(8,128)(2,1)S(1)}, u32[]{:S(2)}, u32[]{:S(2)}) collective-permute-start(bf16[1,1,64,640]{3,2,1,0:T(8,128)(2,1)S(1)} %get-tuple-element.23), channel_id=1, source_target_pairs={{0,1},{1,0},{2,3},{3,2},{4,5},{5,4},{6,7},{7,6},{8,9},{9,8},{10,11... | collective-permute-start | bytes 245768 | tf_op jit(solution)/shard_map/ppermute | solution.py:81
  59.9 10.1 %copy-start = (bf16[560,2,840]{2,1,0:T(2,128)(2,1)S(1)}, bf16[560,2,840]{2,1,0:T(2,128)(2,1)}, u32[]{:S(2)}) copy-start(bf16[560,2,840]{2,1,0:T(2,128)(2,1)} %param.15) | copy-start | bytes 5644804
  60.0 9.0 %collective-permute-start.13 = (bf16[1,1,4,64,640]{4,3,2,1,0:T(8,128)(2,1)S(1)}, bf16[1,1,4,64,640]{4,3,2,1,0:T(8,128)(2,1)S(1)}, u32[]{:S(2)}, u32[]{:S(2)}) collective-permute-start(bf16[1,1,4,64,640]{4,3,2,1,0:T(8,128)(2,1)S(1)} %maximum_bitcast_fusion), channel_id=1, source_target_pairs={{0,8},{4,12},{8,0},{12,4},{1,9},{5,13},{9,1},{13,5},{2,10},{6,14},... | collective-permute-start | bytes 983048 | tf_op jit(solution)/shard_map/ppermute | solution.py:92
  69.9 2.5 %collective-permute-start.14 = (bf16[2,1,4,64,640]{4,3,2,1,0:T(8,128)(2,1)}, bf16[2,1,4,64,640]{4,3,2,1,0:T(8,128)(2,1)}, u32[]{:S(2)}, u32[]{:S(2)}) collective-permute-start(bf16[2,1,4,64,640]{4,3,2,1,0:T(8,128)(2,1)} %pad_maximum_fusion.2), channel_id=1, source_target_pairs={{0,4},{4,0},{8,12},{12,8},{1,5},{5,1},{9,13},{13,9},{2,6},{6,2},{1... | collective-permute-start | bytes 1966088 | tf_op jit(solution)/shard_map/ppermute | solution.py:92
  73.8 1.6 copy-start.1
  79.9 0.8 copy-start.5
  147.3 3.3 %copy-start.9 = (bf16[840,2240]{1,0:T(8,128)(2,1)S(1)}, bf16[840,2240]{1,0:T(8,128)(2,1)}, u32[]{:S(2)}) copy-start(bf16[840,2240]{1,0:T(8,128)(2,1)} %param.17) | copy-start | bytes 11289604
  153.2 2.1 %collective-permute-start.15 = (bf16[2,64,2240]{2,1,0:T(8,128)(2,1)S(1)}, bf16[2,64,2240]{2,1,0:T(8,128)(2,1)S(1)}, u32[]{:S(2)}, u32[]{:S(2)}) collective-permute-start(bf16[2,64,2240]{2,1,0:T(8,128)(2,1)S(1)} %dynamic-slice_bitcast_fusion), channel_id=1, source_target_pairs={{0,4},{4,0},{8,12},{12,8},{1,5},{5,1},{9,13},{13,9},{2,6},{6,2},{1... | collective-permute-start | bytes 1720328 | tf_op jit(solution)/shard_map/ppermute | solution.py:201
  155.5 16.3 %collective-permute-start.17 = (bf16[64,2240]{1,0:T(8,128)(2,1)S(1)}, bf16[64,2240]{1,0:T(8,128)(2,1)S(1)}, u32[]{:S(2)}, u32[]{:S(2)}) collective-permute-start(bf16[64,2240]{1,0:T(8,128)(2,1)S(1)} %get-tuple-element.15), channel_id=1, source_target_pairs={{0,2},{1,6},{2,10},{3,14},{4,3},{5,7},{6,11},{7,15},{8,0},{9,4},{1... | collective-permute-start | bytes 860168 | tf_op jit(solution)/shard_map/ppermute | solution.py:209
  156.1 19.0 %collective-permute-start.16 = (bf16[64,2240]{1,0:T(8,128)(2,1)S(1)}, bf16[64,2240]{1,0:T(8,128)(2,1)S(1)}, u32[]{:S(2)}, u32[]{:S(2)}) collective-permute-start(bf16[64,2240]{1,0:T(8,128)(2,1)S(1)} %get-tuple-element.14), channel_id=1, source_target_pairs={{0,0},{1,4},{2,8},{3,12},{4,1},{5,5},{6,9},{7,13},{8,2},{9,6},{10,... | collective-permute-start | bytes 860168 | tf_op jit(solution)/shard_map/ppermute | solution.py:209
Sparse Core Ops, SparseCore 0:
  80.0 64.8 reduce-scatter.1

commit v20 on v18

--- a/solution.py
+++ b/solution.py
@@ -138,11 +138,18 @@
     stats = halving_sum(stats, ("frame",), inner_axis="row")[:, :model_width]
     kv_state, key_total = stats[:HEAD_DIM], stats[HEAD_DIM]
     query_pos = jnp.maximum(query_in, 0).reshape(token_count, HEADS, HEAD_DIM).astype(jnp.float32)
+    query_narrow = query_pos.astype(jnp.bfloat16)
     numerator = jnp.einsum(
-        "thi,ihj->thj", query_pos, kv_state.reshape(HEAD_DIM, HEADS, HEAD_DIM), precision=highest
+        "thi,ihj->thj",
+        query_narrow,
+        kv_state.astype(jnp.bfloat16).reshape(HEAD_DIM, HEADS, HEAD_DIM),
+        preferred_element_type=jnp.float32,
     )
     denominator = jnp.einsum(
-        "thi,hi->th", query_pos, key_total.reshape(HEADS, HEAD_DIM), precision=highest
+        "thi,hi->th",
+        query_narrow,
+        key_total.astype(jnp.bfloat16).reshape(HEADS, HEAD_DIM),
+        preferred_element_type=jnp.float32,
     )
     attended = (numerator / (denominator[:, :, None] + SHARE_EPS)).reshape(token_count, model_width)
     stream_flat = stream_in.reshape(token_count, model_width).astype(jnp.float32)

time: 183 us -> 182 us (level)
  no operation moved by 1% of the time
where the time goes in v20:
time: 182 us; the launch traced here: 181 us
  waiting for transfers between devices  113 us (62%)
  starting transfers between devices  20.9 us (11%)
  between operations  14.6 us (8%)
  local copies, waits for them, and re-layouts  13.3 us (7%)
  other arithmetic  11.6 us (6%)
  matrix products  7.5 us (4%)
    reduce_scatter x1, waiting for transfers between devices, local(): summed = lax.psum_scatter(partial, 'row', scatter_dimension=0, tiled=True)  63.5 us
    ppermute x2, waiting for transfers between devices, local(): lax.ppermute(pick(pair_sums, chip_at ^ mask), ('frame', 'row'), [(f * row...  13.6 us
    ppermute x9, starting transfers between devices, swap_chunks(): lax.ppermute(sent, axis, [(i, i ^ mask) for i in range(count)])  13.4 us
    ppermute x9, waiting for transfers between devices, swap_chunks(): lax.ppermute(sent, axis, [(i, i ^ mask) for i in range(count)])  12.8 us
    ppermute x2, waiting for transfers between devices, doubling_gather(): lax.ppermute(jnp.stack([by_mask[key] for key in keys]), axis, [(i, i ^ bi...  8.4 us
    ppermute x2, waiting for transfers between devices, halving_sum(): lax.ppermute(sent, axis, [(i, i ^ bit) for i in range(count)])  7.32 us
    ppermute x2, starting transfers between devices, local(): lax.ppermute(pick(pair_sums, chip_at ^ mask), ('frame', 'row'), [(f * row...  6.05 us
    ppermute x2, waiting for transfers between devices, halving_sum(): lax.ppermute(block.astype(jnp.bfloat16), axis, [(i, i ^ bit) for i in ran...  5.62 us
  transfers between devices with their start and end apart: 19, of which 16 were waited for; matrix products, arithmetic and copies ran while one was open for 2% of the time, Pallas kernels for 0%

profile of v20, /device:TPU:2, one launch (start us, length us, event | category | flops | bytes accessed | tf_op | source)
XLA Modules:
  0.0 181.2 jit_solution(14107459700575711000)
XLA Ops:
  7.2 1.1 convert_reduce_fusion
  8.3 1.0 broadcast_maximum_fusion.1
  11.7 1.6 collective-permute-done
  13.5 5.8 %collective-permute-done.1 = bf16[128,560]{0,1:T(8,128)(2,1)S(1)} collective-permute-done((bf16[128,560]{0,1:T(8,128)(2,1)S(1)}, bf16[128,560]{0,1:T(8,128)(2,1)S(1)}, u32[]{:S(2)}, u32[]{:S(2)}) %collective-permute-start.1) | collective-permute-done | bytes 143392 | tf_op jit(solution)/shard_map/ppermute | solution.py:51
  19.4 3.7 %collective-permute-start.4 = (bf16[128,140]{0,1:T(8,128)(2,1)S(1)}, bf16[128,140]{0,1:T(8,128)(2,1)S(1)}, u32[]{:S(2)}, u32[]{:S(2)}) collective-permute-start(bf16[128,140]{0,1:T(8,128)(2,1)S(1)} %get-tuple-element.31), channel_id=1, source_target_pairs={{0,3},{1,2},{2,1},{3,0},{4,7},{5,6},{6,5},{7,4},{8,11},{9,10},{10,... | collective-permute-start | bytes 107528 | tf_op jit(solution)/shard_map/ppermute | solution.py:81
  23.9 1.6 collective-permute-done.4
  25.5 2.5 %collective-permute-done.3 = bf16[128,140]{0,1:T(8,128)(2,1)S(1)} collective-permute-done((bf16[128,140]{0,1:T(8,128)(2,1)S(1)}, bf16[128,140]{0,1:T(8,128)(2,1)S(1)}, u32[]{:S(2)}, u32[]{:S(2)}) %collective-permute-start.3) | collective-permute-done | bytes 35872 | tf_op jit(solution)/shard_map/ppermute | solution.py:81
  28.0 1.5 collective-permute-start.7
  30.2 2.3 %collective-permute-start.5 = (bf16[128,140]{0,1:T(8,128)(2,1)S(1)}, bf16[128,140]{0,1:T(8,128)(2,1)S(1)}, u32[]{:S(2)}, u32[]{:S(2)}) collective-permute-start(bf16[128,140]{0,1:T(8,128)(2,1)S(1)} %fusion.30), channel_id=1, source_target_pairs={{0,1},{1,0},{2,3},{3,2},{4,5},{5,4},{6,7},{7,6},{8,9},{9,8},{10,11... | collective-permute-start | bytes 107528 | tf_op jit(solution)/shard_map/ppermute | solution.py:81
  32.5 1.3 collective-permute-done.7
  35.5 4.6 %collective-permute-done.8 = bf16[128,560]{0,1:T(8,128)(2,1)S(1)} collective-permute-done((bf16[128,560]{0,1:T(8,128)(2,1)S(1)}, bf16[128,560]{0,1:T(8,128)(2,1)S(1)}, u32[]{:S(2)}, u32[]{:S(2)}) %collective-permute-start.8) | collective-permute-done | bytes 143392 | tf_op jit(solution)/shard_map/ppermute | solution.py:61
  41.9 1.1 collective-permute-done.9
  46.3 0.9 multiply_convert_fusion
  47.5 2.4 %collective-permute-start.12 = (bf16[1,1,64,560]{3,2,1,0:T(8,128)(2,1)S(1)}, bf16[1,1,64,560]{3,2,1,0:T(8,128)(2,1)S(1)}, u32[]{:S(2)}, u32[]{:S(2)}) collective-permute-start(bf16[1,1,64,560]{3,2,1,0:T(8,128)(2,1)S(1)} %get-tuple-element.19), channel_id=1, source_target_pairs={{0,3},{1,2},{2,1},{3,0},{4,7},{5,6},{6,5},{7,4},{8,11},{9,10},{10,... | collective-permute-start | bytes 215048 | tf_op jit(solution)/shard_map/ppermute | solution.py:81
  50.6 1.3 collective-permute-start.10
  51.9 2.8 %collective-permute-done.12 = bf16[1,1,64,560]{3,2,1,0:T(8,128)(2,1)S(1)} collective-permute-done((bf16[1,1,64,560]{3,2,1,0:T(8,128)(2,1)S(1)}, bf16[1,1,64,560]{3,2,1,0:T(8,128)(2,1)S(1)}, u32[]{:S(2)}, u32[]{:S(2)}) %collective-permute-start.12) | collective-permute-done | bytes 71712 | tf_op jit(solution)/shard_map/ppermute | solution.py:81
  54.7 3.6 %collective-permute-done.11 = bf16[1,1,64,560]{3,2,1,0:T(8,128)(2,1)S(1)} collective-permute-done((bf16[1,1,64,560]{3,2,1,0:T(8,128)(2,1)S(1)}, bf16[1,1,64,560]{3,2,1,0:T(8,128)(2,1)S(1)}, u32[]{:S(2)}, u32[]{:S(2)}) %collective-permute-start.11) | collective-permute-done | bytes 71712 | tf_op jit(solution)/shard_map/ppermute | solution.py:81
  59.1 8.4 %collective-permute-done.13 = bf16[1,1,4,64,560]{4,3,2,1,0:T(8,128)(2,1)S(1)} collective-permute-done((bf16[1,1,4,64,560]{4,3,2,1,0:T(8,128)(2,1)S(1)}, bf16[1,1,4,64,560]{4,3,2,1,0:T(8,128)(2,1)S(1)}, u32[]{:S(2)}, u32[]{:S(2)}) %collective-permute-start.13) | collective-permute-done | bytes 286752 | tf_op jit(solution)/shard_map/ppermute | solution.py:92
  67.5 1.0 pad_maximum_fusion.2
  68.5 2.5 %reshape.242 = bf16[560,1680]{1,0:T(8,128)(2,1)} reshape(bf16[560,2,840]{2,1,0:T(2,128)(2,1)S(1)} %copy-done) | data formatting | bytes 3763200 | tf_op jit(solution)/shard_map/reshape | solution.py:175
  71.0 1.1 fusion.22
  72.8 1.3 copy-done.1
  74.1 4.4 %convolution_convert_fusion.1 = bf16[1024,1680]{0,1:T(8,128)(2,1)} fusion(bf16[1024,560]{1,0:T(8,128)(2,1)S(1)} %bitcast.120, bf16[560,1680]{1,0:T(8,128)(2,1)S(1)} %copy-done.1), kind=kOutput, calls=%fused_computation.1 | convolution fusion | flops 1928478720 | bytes 6469120 | tf_op jit(solution)/shard_map/dot_general | solution.py:178
  80.0 63.5 %reduce-scatter.2.cloned.1.call-done = bf16[256,1680]{0,1:T(8,128)(2,1)} async-done(((bf16[1024,1680]{0,1:T(8,128)(2,1)}), bf16[256,1680]{0,1:T(8,128)(2,1)}) %reduce-scatter.2.cloned.1.call-update) | async-done | bytes 860176 | tf_op jit(solution)/shard_map/reduce_scatter | solution.py:181
  143.6 1.6 fusion.3
  145.9 2.7 %multiply_add_fusion = f32[1,4,64,1680]{3,2,1,0:T(8,128)S(1)} fusion(bf16[1,4,64,1680]{3,2,1,0:T(8,128)(2,1)S(1)} %bitcast.115, bf16[1,6,64,1680]{3,2,1,0:T(8,128)(2,1)S(1)} %pad.13, f32[1680]{0:T(1024)S(1)} %mul.211, f32[1680]{0:T(1024)S(1)} %mul.208, f32[1680]{0:T(1024)S(1)} %mul.205, f32[1680]{0:T(1024)S(1)} %mul.202, f32[1680]{0:T(1024)S(1)} %mul.199, ...), kind=kLoop, calls=%fused_computation.4 | loop fusion | flops 11182080 | bytes 5922816 | tf_op jit(solution)/shard_map/add | solution.py:114
  149.0 1.8 convolution_convert_fusion
  151.7 2.0 %collective-permute-done.15 = bf16[2,64,2240]{2,1,0:T(8,128)(2,1)S(1)} collective-permute-done((bf16[2,64,2240]{2,1,0:T(8,128)(2,1)S(1)}, bf16[2,64,2240]{2,1,0:T(8,128)(2,1)S(1)}, u32[]{:S(2)}, u32[]{:S(2)}) %collective-permute-start.15) | collective-permute-done | bytes 573472 | tf_op jit(solution)/shard_map/ppermute | solution.py:201
  154.5 5.4 %collective-permute-start.16 = (bf16[64,2240]{1,0:T(8,128)(2,1)S(1)}, bf16[64,2240]{1,0:T(8,128)(2,1)S(1)}, u32[]{:S(2)}, u32[]{:S(2)}) collective-permute-start(bf16[64,2240]{1,0:T(8,128)(2,1)S(1)} %get-tuple-element.12), channel_id=1, source_target_pairs={{0,0},{1,4},{2,8},{3,12},{4,1},{5,5},{6,9},{7,13},{8,2},{9,6},{10,... | collective-permute-start | bytes 860168 | tf_op jit(solution)/shard_map/ppermute | solution.py:209
  159.9 10.3 %collective-permute-done.17 = bf16[64,2240]{1,0:T(8,128)(2,1)S(1)} collective-permute-done((bf16[64,2240]{1,0:T(8,128)(2,1)S(1)}, bf16[64,2240]{1,0:T(8,128)(2,1)S(1)}, u32[]{:S(2)}, u32[]{:S(2)}) %collective-permute-start.17) | collective-permute-done | bytes 286752 | tf_op jit(solution)/shard_map/ppermute | solution.py:209
  170.2 3.3 %collective-permute-done.16 = bf16[64,2240]{1,0:T(8,128)(2,1)S(1)} collective-permute-done((bf16[64,2240]{1,0:T(8,128)(2,1)S(1)}, bf16[64,2240]{1,0:T(8,128)(2,1)S(1)}, u32[]{:S(2)}, u32[]{:S(2)}) %collective-permute-start.16) | collective-permute-done | bytes 286752 | tf_op jit(solution)/shard_map/ppermute | solution.py:209
  173.6 0.8 fusion.15
  (100 shorter events, 17.4 us)
Async XLA Ops:
  7.2 2.5 %copy-start.4 = (bf16[1,1,64,2240]{3,2,1,0:T(8,128)(2,1)S(1)}, bf16[1,1,64,2240]{3,2,1,0:T(8,128)(2,1)}, u32[]{:S(2)}) copy-start(bf16[1,1,64,2240]{3,2,1,0:T(8,128)(2,1)} %param.11) | copy-start | bytes 860164
  7.2 136.4 %reduce-scatter.2.cloned.1.call-start = ((), (), s32[]{:S(2)}) async-start(), calls=%async_computation.1 | async-start | bytes 4300800 | tf_op jit(solution)/shard_map/reduce_scatter | solution.py:181
  11.7 1.6 collective-permute-start
  13.4 5.9 %collective-permute-start.1 = (bf16[128,560]{0,1:T(8,128)(2,1)S(1)}, bf16[128,560]{0,1:T(8,128)(2,1)S(1)}, u32[]{:S(2)}, u32[]{:S(2)}) collective-permute-start(bf16[128,560]{0,1:T(8,128)(2,1)S(1)} %select_convert_fusion.1), channel_id=1, source_target_pairs={{0,8},{4,12},{8,0},{12,4},{1,9},{5,13},{9,1},{13,5},{2,10},{6,14},... | collective-permute-start | bytes 430088 | tf_op jit(solution)/shard_map/ppermute | solution.py:51
  19.4 6.1 %collective-permute-start.4 = (bf16[128,140]{0,1:T(8,128)(2,1)S(1)}, bf16[128,140]{0,1:T(8,128)(2,1)S(1)}, u32[]{:S(2)}, u32[]{:S(2)}) collective-permute-start(bf16[128,140]{0,1:T(8,128)(2,1)S(1)} %get-tuple-element.31), channel_id=1, source_target_pairs={{0,3},{1,2},{2,1},{3,0},{4,7},{5,6},{6,5},{7,4},{8,11},{9,10},{10,... | collective-permute-start | bytes 107528 | tf_op jit(solution)/shard_map/ppermute | solution.py:81
  23.1 4.9 %collective-permute-start.3 = (bf16[128,140]{0,1:T(8,128)(2,1)S(1)}, bf16[128,140]{0,1:T(8,128)(2,1)S(1)}, u32[]{:S(2)}, u32[]{:S(2)}) collective-permute-start(bf16[128,140]{0,1:T(8,128)(2,1)S(1)} %get-tuple-element.32), channel_id=1, source_target_pairs={{0,2},{1,3},{2,0},{3,1},{4,6},{5,7},{6,4},{7,5},{8,10},{9,11},{10,... | collective-permute-start | bytes 107528 | tf_op jit(solution)/shard_map/ppermute | solution.py:81
  23.1 4.9 %collective-permute-start.2 = (bf16[128,140]{0,1:T(8,128)(2,1)S(1)}, bf16[128,140]{0,1:T(8,128)(2,1)S(1)}, u32[]{:S(2)}, u32[]{:S(2)}) collective-permute-start(bf16[128,140]{0,1:T(8,128)(2,1)S(1)} %get-tuple-element.33), channel_id=1, source_target_pairs={{0,1},{1,0},{2,3},{3,2},{4,5},{5,4},{6,7},{7,6},{8,9},{9,8},{10,11... | collective-permute-start | bytes 107528 | tf_op jit(solution)/shard_map/ppermute | solution.py:81
  27.9 13.5 %copy-start.3 = (bf16[1,1,64,2240]{3,2,1,0:T(8,128)(2,1)S(1)}, bf16[1,1,64,2240]{3,2,1,0:T(8,128)(2,1)}, u32[]{:S(2)}) copy-start(bf16[1,1,64,2240]{3,2,1,0:T(8,128)(2,1)} %param.9) | copy-start | bytes 860164
  28.0 5.8 %collective-permute-start.7 = (bf16[128,140]{0,1:T(8,128)(2,1)S(1)}, bf16[128,140]{0,1:T(8,128)(2,1)S(1)}, u32[]{:S(2)}, u32[]{:S(2)}) collective-permute-start(bf16[128,140]{0,1:T(8,128)(2,1)S(1)} %fusion.30), channel_id=1, source_target_pairs={{0,3},{1,2},{2,1},{3,0},{4,7},{5,6},{6,5},{7,4},{8,11},{9,10},{10,... | collective-permute-start | bytes 107528 | tf_op jit(solution)/shard_map/ppermute | solution.py:81
  29.5 4.9 %collective-permute-start.6 = (bf16[128,140]{0,1:T(8,128)(2,1)S(1)}, bf16[128,140]{0,1:T(8,128)(2,1)S(1)}, u32[]{:S(2)}, u32[]{:S(2)}) collective-permute-start(bf16[128,140]{0,1:T(8,128)(2,1)S(1)} %fusion.30), channel_id=1, source_target_pairs={{0,2},{1,3},{2,0},{3,1},{4,6},{5,7},{6,4},{7,5},{8,10},{9,11},{10,... | collective-permute-start | bytes 107528 | tf_op jit(solution)/shard_map/ppermute | solution.py:81
  30.2 4.6 %collective-permute-start.5 = (bf16[128,140]{0,1:T(8,128)(2,1)S(1)}, bf16[128,140]{0,1:T(8,128)(2,1)S(1)}, u32[]{:S(2)}, u32[]{:S(2)}) collective-permute-start(bf16[128,140]{0,1:T(8,128)(2,1)S(1)} %fusion.30), channel_id=1, source_target_pairs={{0,1},{1,0},{2,3},{3,2},{4,5},{5,4},{6,7},{7,6},{8,9},{9,8},{10,11... | collective-permute-start | bytes 107528 | tf_op jit(solution)/shard_map/ppermute | solution.py:81
  34.8 6.6 %copy-start.6 = (bf16[2240]{0:T(1024)(128)(2,1)S(1)}, bf16[2240]{0:T(1024)(128)(2,1)}, u32[]{:S(2)}) copy-start(bf16[2240]{0:T(1024)(128)(2,1)} %param.14) | copy-start | bytes 13444
  34.9 7.0 %copy-start.7 = (bf16[2240]{0:T(1024)(128)(2,1)S(1)}, bf16[2240]{0:T(1024)(128)(2,1)}, u32[]{:S(2)}) copy-start(bf16[2240]{0:T(1024)(128)(2,1)} %param.13) | copy-start | bytes 13444
  34.9 5.2 %collective-permute-start.8 = (bf16[128,560]{0,1:T(8,128)(2,1)S(1)}, bf16[128,560]{0,1:T(8,128)(2,1)S(1)}, u32[]{:S(2)}, u32[]{:S(2)}) collective-permute-start(bf16[128,560]{0,1:T(8,128)(2,1)S(1)} %pad_maximum_fusion.8), channel_id=1, source_target_pairs={{0,8},{4,12},{8,0},{12,4},{1,9},{5,13},{9,1},{13,5},{2,10},{6,14},... | collective-permute-start | bytes 430088 | tf_op jit(solution)/shard_map/ppermute | solution.py:61
  41.3 1.6 collective-permute-start.9
  45.0 1.0 copy-start.2
  47.5 21.1 %copy-start = (bf16[560,2,840]{2,1,0:T(2,128)(2,1)S(1)}, bf16[560,2,840]{2,1,0:T(2,128)(2,1)}, u32[]{:S(2)}) copy-start(bf16[560,2,840]{2,1,0:T(2,128)(2,1)} %param.15) | copy-start | bytes 5644804
  47.5 7.3 %collective-permute-start.12 = (bf16[1,1,64,560]{3,2,1,0:T(8,128)(2,1)S(1)}, bf16[1,1,64,560]{3,2,1,0:T(8,128)(2,1)S(1)}, u32[]{:S(2)}, u32[]{:S(2)}) collective-permute-start(bf16[1,1,64,560]{3,2,1,0:T(8,128)(2,1)S(1)} %get-tuple-element.19), channel_id=1, source_target_pairs={{0,3},{1,2},{2,1},{3,0},{4,7},{5,6},{6,5},{7,4},{8,11},{9,10},{10,... | collective-permute-start | bytes 215048 | tf_op jit(solution)/shard_map/ppermute | solution.py:81
  49.9 8.5 %collective-permute-start.11 = (bf16[1,1,64,560]{3,2,1,0:T(8,128)(2,1)S(1)}, bf16[1,1,64,560]{3,2,1,0:T(8,128)(2,1)S(1)}, u32[]{:S(2)}, u32[]{:S(2)}) collective-permute-start(bf16[1,1,64,560]{3,2,1,0:T(8,128)(2,1)S(1)} %get-tuple-element.20), channel_id=1, source_target_pairs={{0,2},{1,3},{2,0},{3,1},{4,6},{5,7},{6,4},{7,5},{8,10},{9,11},{10,... | collective-permute-start | bytes 215048 | tf_op jit(solution)/shard_map/ppermute | solution.py:81
  50.6 7.7 %collective-permute-start.10 = (bf16[1,1,64,560]{3,2,1,0:T(8,128)(2,1)S(1)}, bf16[1,1,64,560]{3,2,1,0:T(8,128)(2,1)S(1)}, u32[]{:S(2)}, u32[]{:S(2)}) collective-permute-start(bf16[1,1,64,560]{3,2,1,0:T(8,128)(2,1)S(1)} %get-tuple-element.21), channel_id=1, source_target_pairs={{0,1},{1,0},{2,3},{3,2},{4,5},{5,4},{6,7},{7,6},{8,9},{9,8},{10,11... | collective-permute-start | bytes 215048 | tf_op jit(solution)/shard_map/ppermute | solution.py:81
  58.5 9.0 %collective-permute-start.13 = (bf16[1,1,4,64,560]{4,3,2,1,0:T(8,128)(2,1)S(1)}, bf16[1,1,4,64,560]{4,3,2,1,0:T(8,128)(2,1)S(1)}, u32[]{:S(2)}, u32[]{:S(2)}) collective-permute-start(bf16[1,1,4,64,560]{4,3,2,1,0:T(8,128)(2,1)S(1)} %maximum_bitcast_fusion), channel_id=1, source_target_pairs={{0,8},{4,12},{8,0},{12,4},{1,9},{5,13},{9,1},{13,5},{2,10},{6,14},... | collective-permute-start | bytes 860168 | tf_op jit(solution)/shard_map/ppermute | solution.py:92
  68.5 2.5 %collective-permute-start.14 = (bf16[2,1,4,64,560]{4,3,2,1,0:T(8,128)(2,1)}, bf16[2,1,4,64,560]{4,3,2,1,0:T(8,128)(2,1)}, u32[]{:S(2)}, u32[]{:S(2)}) collective-permute-start(bf16[2,1,4,64,560]{4,3,2,1,0:T(8,128)(2,1)} %pad_maximum_fusion.2), channel_id=1, source_target_pairs={{0,4},{4,0},{8,12},{12,8},{1,5},{5,1},{9,13},{13,9},{2,6},{6,2},{1... | collective-permute-start | bytes 1720328 | tf_op jit(solution)/shard_map/ppermute | solution.py:92
  72.5 1.6 copy-start.1
  78.5 0.8 copy-start.5
  145.9 3.1 %copy-start.8 = (bf16[840,2240]{1,0:T(8,128)(2,1)S(1)}, bf16[840,2240]{1,0:T(8,128)(2,1)}, u32[]{:S(2)}) copy-start(bf16[840,2240]{1,0:T(8,128)(2,1)} %param.17) | copy-start | bytes 11289604
  151.6 2.1 %collective-permute-start.15 = (bf16[2,64,2240]{2,1,0:T(8,128)(2,1)S(1)}, bf16[2,64,2240]{2,1,0:T(8,128)(2,1)S(1)}, u32[]{:S(2)}, u32[]{:S(2)}) collective-permute-start(bf16[2,64,2240]{2,1,0:T(8,128)(2,1)S(1)} %dynamic-slice_bitcast_fusion), channel_id=1, source_target_pairs={{0,4},{4,0},{8,12},{12,8},{1,5},{5,1},{9,13},{13,9},{2,6},{6,2},{1... | collective-permute-start | bytes 1720328 | tf_op jit(solution)/shard_map/ppermute | solution.py:201
  153.9 16.3 %collective-permute-start.17 = (bf16[64,2240]{1,0:T(8,128)(2,1)S(1)}, bf16[64,2240]{1,0:T(8,128)(2,1)S(1)}, u32[]{:S(2)}, u32[]{:S(2)}) collective-permute-start(bf16[64,2240]{1,0:T(8,128)(2,1)S(1)} %get-tuple-element.13), channel_id=1, source_target_pairs={{0,2},{1,6},{2,10},{3,14},{4,3},{5,7},{6,11},{7,15},{8,0},{9,4},{1... | collective-permute-start | bytes 860168 | tf_op jit(solution)/shard_map/ppermute | solution.py:209
  154.5 19.0 %collective-permute-start.16 = (bf16[64,2240]{1,0:T(8,128)(2,1)S(1)}, bf16[64,2240]{1,0:T(8,128)(2,1)S(1)}, u32[]{:S(2)}, u32[]{:S(2)}) collective-permute-start(bf16[64,2240]{1,0:T(8,128)(2,1)S(1)} %get-tuple-element.12), channel_id=1, source_target_pairs={{0,0},{1,4},{2,8},{3,12},{4,1},{5,5},{6,9},{7,13},{8,2},{9,6},{10,... | collective-permute-start | bytes 860168 | tf_op jit(solution)/shard_map/ppermute | solution.py:209
Sparse Core Ops, SparseCore 0:
  78.7 64.8 reduce-scatter.1

commit v21 on v20

--- a/solution.py
+++ b/solution.py
@@ -127,8 +127,12 @@
     local_state = jnp.einsum(
         "thi,thj->ihj", key_pos, value_heads, preferred_element_type=jnp.float32
     ).reshape(HEAD_DIM, model_width)
-    local_total = jnp.sum(key_pos.reshape(token_count, model_width), axis=0, dtype=jnp.float32)
-    stats = jnp.concatenate([local_state, local_total[None, :]], axis=0)
+    local_total = jnp.dot(
+        jnp.ones((1, token_count), key_pos.dtype),
+        key_pos.reshape(token_count, model_width),
+        preferred_element_type=jnp.float32,
+    )
+    stats = jnp.concatenate([local_state, local_total], axis=0)
     parts = 1
     for axis, count, bit in exchange_steps(("frame", "row")):
         parts *= 2

time: 182 us -> 182 us (level)
  no operation moved by 1% of the time
where the time goes in v21:
time: 182 us; the launch traced here: 181 us
  waiting for transfers between devices  113 us (62%)
  starting transfers between devices  20.9 us (11%)
  between operations  14.6 us (8%)
  local copies, waits for them, and re-layouts  13.3 us (7%)
  other arithmetic  10.6 us (6%)
  matrix products  8.66 us (5%)
    reduce_scatter x1, waiting for transfers between devices, local(): summed = lax.psum_scatter(partial, 'row', scatter_dimension=0, tiled=True)  63.5 us
    ppermute x2, waiting for transfers between devices, local(): lax.ppermute(pick(pair_sums, chip_at ^ mask), ('frame', 'row'), [(f * row...  13.6 us
    ppermute x9, starting transfers between devices, swap_chunks(): lax.ppermute(sent, axis, [(i, i ^ mask) for i in range(count)])  13.4 us
    ppermute x9, waiting for transfers between devices, swap_chunks(): lax.ppermute(sent, axis, [(i, i ^ mask) for i in range(count)])  12.8 us
    ppermute x2, waiting for transfers between devices, doubling_gather(): lax.ppermute(jnp.stack([by_mask[key] for key in keys]), axis, [(i, i ^ bi...  8.4 us
    ppermute x2, waiting for transfers between devices, halving_sum(): lax.ppermute(sent, axis, [(i, i ^ bit) for i in range(count)])  7.32 us
    ppermute x2, starting transfers between devices, local(): lax.ppermute(pick(pair_sums, chip_at ^ mask), ('frame', 'row'), [(f * row...  6.05 us
    ppermute x2, waiting for transfers between devices, halving_sum(): lax.ppermute(block.astype(jnp.bfloat16), axis, [(i, i ^ bit) for i in ran...  5.62 us
  transfers between devices with their start and end apart: 19, of which 16 were waited for; matrix products, arithmetic and copies ran while one was open for 2% of the time, Pallas kernels for 0%

profile of v21, /device:TPU:2, one launch (start us, length us, event | category | flops | bytes accessed | tf_op | source)
XLA Modules:
  0.0 181.3 jit_solution(10143566207563210295)
XLA Ops:
  7.2 1.2 convolution_reduce_fusion
  8.4 1.0 broadcast_maximum_fusion.1
  11.8 1.6 collective-permute-done
  13.6 5.8 %collective-permute-done.1 = bf16[128,560]{0,1:T(8,128)(2,1)S(1)} collective-permute-done((bf16[128,560]{0,1:T(8,128)(2,1)S(1)}, bf16[128,560]{0,1:T(8,128)(2,1)S(1)}, u32[]{:S(2)}, u32[]{:S(2)}) %collective-permute-start.1) | collective-permute-done | bytes 143392 | tf_op jit(solution)/shard_map/ppermute | solution.py:51
  19.5 3.7 %collective-permute-start.4 = (bf16[128,140]{0,1:T(8,128)(2,1)S(1)}, bf16[128,140]{0,1:T(8,128)(2,1)S(1)}, u32[]{:S(2)}, u32[]{:S(2)}) collective-permute-start(bf16[128,140]{0,1:T(8,128)(2,1)S(1)} %get-tuple-element.31), channel_id=1, source_target_pairs={{0,3},{1,2},{2,1},{3,0},{4,7},{5,6},{6,5},{7,4},{8,11},{9,10},{10,... | collective-permute-start | bytes 107528 | tf_op jit(solution)/shard_map/ppermute | solution.py:81
  24.0 1.6 collective-permute-done.4
  25.6 2.5 %collective-permute-done.3 = bf16[128,140]{0,1:T(8,128)(2,1)S(1)} collective-permute-done((bf16[128,140]{0,1:T(8,128)(2,1)S(1)}, bf16[128,140]{0,1:T(8,128)(2,1)S(1)}, u32[]{:S(2)}, u32[]{:S(2)}) %collective-permute-start.3) | collective-permute-done | bytes 35872 | tf_op jit(solution)/shard_map/ppermute | solution.py:81
  28.1 1.5 collective-permute-start.7
  30.3 2.3 %collective-permute-start.5 = (bf16[128,140]{0,1:T(8,128)(2,1)S(1)}, bf16[128,140]{0,1:T(8,128)(2,1)S(1)}, u32[]{:S(2)}, u32[]{:S(2)}) collective-permute-start(bf16[128,140]{0,1:T(8,128)(2,1)S(1)} %fusion.33), channel_id=1, source_target_pairs={{0,1},{1,0},{2,3},{3,2},{4,5},{5,4},{6,7},{7,6},{8,9},{9,8},{10,11... | collective-permute-start | bytes 107528 | tf_op jit(solution)/shard_map/ppermute | solution.py:81
  32.6 1.3 collective-permute-done.7
  35.6 4.6 %collective-permute-done.8 = bf16[128,560]{0,1:T(8,128)(2,1)S(1)} collective-permute-done((bf16[128,560]{0,1:T(8,128)(2,1)S(1)}, bf16[128,560]{0,1:T(8,128)(2,1)S(1)}, u32[]{:S(2)}, u32[]{:S(2)}) %collective-permute-start.8) | collective-permute-done | bytes 143392 | tf_op jit(solution)/shard_map/ppermute | solution.py:61
  42.0 1.1 collective-permute-done.9
  46.3 0.9 multiply_convert_fusion
  47.5 2.4 %collective-permute-start.12 = (bf16[1,1,64,560]{3,2,1,0:T(8,128)(2,1)S(1)}, bf16[1,1,64,560]{3,2,1,0:T(8,128)(2,1)S(1)}, u32[]{:S(2)}, u32[]{:S(2)}) collective-permute-start(bf16[1,1,64,560]{3,2,1,0:T(8,128)(2,1)S(1)} %get-tuple-element.19), channel_id=1, source_target_pairs={{0,3},{1,2},{2,1},{3,0},{4,7},{5,6},{6,5},{7,4},{8,11},{9,10},{10,... | collective-permute-start | bytes 215048 | tf_op jit(solution)/shard_map/ppermute | solution.py:81
  50.7 1.3 collective-permute-start.10
  52.0 2.8 %collective-permute-done.12 = bf16[1,1,64,560]{3,2,1,0:T(8,128)(2,1)S(1)} collective-permute-done((bf16[1,1,64,560]{3,2,1,0:T(8,128)(2,1)S(1)}, bf16[1,1,64,560]{3,2,1,0:T(8,128)(2,1)S(1)}, u32[]{:S(2)}, u32[]{:S(2)}) %collective-permute-start.12) | collective-permute-done | bytes 71712 | tf_op jit(solution)/shard_map/ppermute | solution.py:81
  54.8 3.6 %collective-permute-done.11 = bf16[1,1,64,560]{3,2,1,0:T(8,128)(2,1)S(1)} collective-permute-done((bf16[1,1,64,560]{3,2,1,0:T(8,128)(2,1)S(1)}, bf16[1,1,64,560]{3,2,1,0:T(8,128)(2,1)S(1)}, u32[]{:S(2)}, u32[]{:S(2)}) %collective-permute-start.11) | collective-permute-done | bytes 71712 | tf_op jit(solution)/shard_map/ppermute | solution.py:81
  59.2 8.4 %collective-permute-done.13 = bf16[1,1,4,64,560]{4,3,2,1,0:T(8,128)(2,1)S(1)} collective-permute-done((bf16[1,1,4,64,560]{4,3,2,1,0:T(8,128)(2,1)S(1)}, bf16[1,1,4,64,560]{4,3,2,1,0:T(8,128)(2,1)S(1)}, u32[]{:S(2)}, u32[]{:S(2)}) %collective-permute-start.13) | collective-permute-done | bytes 286752 | tf_op jit(solution)/shard_map/ppermute | solution.py:92
  67.6 1.0 pad_maximum_fusion.2
  68.6 2.5 %reshape.243 = bf16[560,1680]{1,0:T(8,128)(2,1)} reshape(bf16[560,2,840]{2,1,0:T(2,128)(2,1)S(1)} %copy-done) | data formatting | bytes 3763200 | tf_op jit(solution)/shard_map/reshape | solution.py:179
  71.1 1.1 fusion.25
  72.9 1.3 copy-done.1
  74.2 4.4 %convolution_convert_fusion.1 = bf16[1024,1680]{0,1:T(8,128)(2,1)} fusion(bf16[1024,560]{1,0:T(8,128)(2,1)S(1)} %bitcast.123, bf16[560,1680]{1,0:T(8,128)(2,1)S(1)} %copy-done.1), kind=kOutput, calls=%fused_computation.1 | convolution fusion | flops 1928478720 | bytes 6469120 | tf_op jit(solution)/shard_map/dot_general | solution.py:182
  80.1 63.5 %reduce-scatter.2.cloned.1.call-done = bf16[256,1680]{0,1:T(8,128)(2,1)} async-done(((bf16[1024,1680]{0,1:T(8,128)(2,1)}), bf16[256,1680]{0,1:T(8,128)(2,1)}) %reduce-scatter.2.cloned.1.call-update) | async-done | bytes 860176 | tf_op jit(solution)/shard_map/reduce_scatter | solution.py:185
  143.6 1.6 fusion.3
  146.0 2.7 %multiply_add_fusion = f32[1,4,64,1680]{3,2,1,0:T(8,128)S(1)} fusion(bf16[1,4,64,1680]{3,2,1,0:T(8,128)(2,1)S(1)} %bitcast.118, bf16[1,6,64,1680]{3,2,1,0:T(8,128)(2,1)S(1)} %pad.13, f32[1680]{0:T(1024)S(1)} %mul.211, f32[1680]{0:T(1024)S(1)} %mul.208, f32[1680]{0:T(1024)S(1)} %mul.205, f32[1680]{0:T(1024)S(1)} %mul.202, f32[1680]{0:T(1024)S(1)} %mul.199, ...), kind=kLoop, calls=%fused_computation.4 | loop fusion | flops 11182080 | bytes 5922816 | tf_op jit(solution)/shard_map/add | solution.py:114
  149.1 1.8 convolution_convert_fusion
  151.8 2.0 %collective-permute-done.15 = bf16[2,64,2240]{2,1,0:T(8,128)(2,1)S(1)} collective-permute-done((bf16[2,64,2240]{2,1,0:T(8,128)(2,1)S(1)}, bf16[2,64,2240]{2,1,0:T(8,128)(2,1)S(1)}, u32[]{:S(2)}, u32[]{:S(2)}) %collective-permute-start.15) | collective-permute-done | bytes 573472 | tf_op jit(solution)/shard_map/ppermute | solution.py:205
  154.6 5.4 %collective-permute-start.16 = (bf16[64,2240]{1,0:T(8,128)(2,1)S(1)}, bf16[64,2240]{1,0:T(8,128)(2,1)S(1)}, u32[]{:S(2)}, u32[]{:S(2)}) collective-permute-start(bf16[64,2240]{1,0:T(8,128)(2,1)S(1)} %get-tuple-element.12), channel_id=1, source_target_pairs={{0,0},{1,4},{2,8},{3,12},{4,1},{5,5},{6,9},{7,13},{8,2},{9,6},{10,... | collective-permute-start | bytes 860168 | tf_op jit(solution)/shard_map/ppermute | solution.py:213
  160.0 10.3 %collective-permute-done.17 = bf16[64,2240]{1,0:T(8,128)(2,1)S(1)} collective-permute-done((bf16[64,2240]{1,0:T(8,128)(2,1)S(1)}, bf16[64,2240]{1,0:T(8,128)(2,1)S(1)}, u32[]{:S(2)}, u32[]{:S(2)}) %collective-permute-start.17) | collective-permute-done | bytes 286752 | tf_op jit(solution)/shard_map/ppermute | solution.py:213
  170.3 3.3 %collective-permute-done.16 = bf16[64,2240]{1,0:T(8,128)(2,1)S(1)} collective-permute-done((bf16[64,2240]{1,0:T(8,128)(2,1)S(1)}, bf16[64,2240]{1,0:T(8,128)(2,1)S(1)}, u32[]{:S(2)}, u32[]{:S(2)}) %collective-permute-start.16) | collective-permute-done | bytes 286752 | tf_op jit(solution)/shard_map/ppermute | solution.py:213
  173.6 0.8 fusion.15
  (100 shorter events, 17.4 us)
Async XLA Ops:
  7.2 2.6 %copy-start.4 = (bf16[1,1,64,2240]{3,2,1,0:T(8,128)(2,1)S(1)}, bf16[1,1,64,2240]{3,2,1,0:T(8,128)(2,1)}, u32[]{:S(2)}) copy-start(bf16[1,1,64,2240]{3,2,1,0:T(8,128)(2,1)} %param.11) | copy-start | bytes 860164
  7.2 136.5 %reduce-scatter.2.cloned.1.call-start = ((), (), s32[]{:S(2)}) async-start(), calls=%async_computation.1 | async-start | bytes 4300800 | tf_op jit(solution)/shard_map/reduce_scatter | solution.py:185
  11.7 1.6 collective-permute-start
  13.5 5.9 %collective-permute-start.1 = (bf16[128,560]{0,1:T(8,128)(2,1)S(1)}, bf16[128,560]{0,1:T(8,128)(2,1)S(1)}, u32[]{:S(2)}, u32[]{:S(2)}) collective-permute-start(bf16[128,560]{0,1:T(8,128)(2,1)S(1)} %select_convert_fusion.1), channel_id=1, source_target_pairs={{0,8},{4,12},{8,0},{12,4},{1,9},{5,13},{9,1},{13,5},{2,10},{6,14},... | collective-permute-start | bytes 430088 | tf_op jit(solution)/shard_map/ppermute | solution.py:51
  19.5 6.1 %collective-permute-start.4 = (bf16[128,140]{0,1:T(8,128)(2,1)S(1)}, bf16[128,140]{0,1:T(8,128)(2,1)S(1)}, u32[]{:S(2)}, u32[]{:S(2)}) collective-permute-start(bf16[128,140]{0,1:T(8,128)(2,1)S(1)} %get-tuple-element.31), channel_id=1, source_target_pairs={{0,3},{1,2},{2,1},{3,0},{4,7},{5,6},{6,5},{7,4},{8,11},{9,10},{10,... | collective-permute-start | bytes 107528 | tf_op jit(solution)/shard_map/ppermute | solution.py:81
  23.2 4.9 %collective-permute-start.3 = (bf16[128,140]{0,1:T(8,128)(2,1)S(1)}, bf16[128,140]{0,1:T(8,128)(2,1)S(1)}, u32[]{:S(2)}, u32[]{:S(2)}) collective-permute-start(bf16[128,140]{0,1:T(8,128)(2,1)S(1)} %get-tuple-element.32), channel_id=1, source_target_pairs={{0,2},{1,3},{2,0},{3,1},{4,6},{5,7},{6,4},{7,5},{8,10},{9,11},{10,... | collective-permute-start | bytes 107528 | tf_op jit(solution)/shard_map/ppermute | solution.py:81
  23.2 4.9 %collective-permute-start.2 = (bf16[128,140]{0,1:T(8,128)(2,1)S(1)}, bf16[128,140]{0,1:T(8,128)(2,1)S(1)}, u32[]{:S(2)}, u32[]{:S(2)}) collective-permute-start(bf16[128,140]{0,1:T(8,128)(2,1)S(1)} %get-tuple-element.33), channel_id=1, source_target_pairs={{0,1},{1,0},{2,3},{3,2},{4,5},{5,4},{6,7},{7,6},{8,9},{9,8},{10,11... | collective-permute-start | bytes 107528 | tf_op jit(solution)/shard_map/ppermute | solution.py:81
  28.0 13.5 %copy-start.3 = (bf16[1,1,64,2240]{3,2,1,0:T(8,128)(2,1)S(1)}, bf16[1,1,64,2240]{3,2,1,0:T(8,128)(2,1)}, u32[]{:S(2)}) copy-start(bf16[1,1,64,2240]{3,2,1,0:T(8,128)(2,1)} %param.9) | copy-start | bytes 860164
  28.1 5.8 %collective-permute-start.7 = (bf16[128,140]{0,1:T(8,128)(2,1)S(1)}, bf16[128,140]{0,1:T(8,128)(2,1)S(1)}, u32[]{:S(2)}, u32[]{:S(2)}) collective-permute-start(bf16[128,140]{0,1:T(8,128)(2,1)S(1)} %fusion.33), channel_id=1, source_target_pairs={{0,3},{1,2},{2,1},{3,0},{4,7},{5,6},{6,5},{7,4},{8,11},{9,10},{10,... | collective-permute-start | bytes 107528 | tf_op jit(solution)/shard_map/ppermute | solution.py:81
  29.6 4.9 %collective-permute-start.6 = (bf16[128,140]{0,1:T(8,128)(2,1)S(1)}, bf16[128,140]{0,1:T(8,128)(2,1)S(1)}, u32[]{:S(2)}, u32[]{:S(2)}) collective-permute-start(bf16[128,140]{0,1:T(8,128)(2,1)S(1)} %fusion.33), channel_id=1, source_target_pairs={{0,2},{1,3},{2,0},{3,1},{4,6},{5,7},{6,4},{7,5},{8,10},{9,11},{10,... | collective-permute-start | bytes 107528 | tf_op jit(solution)/shard_map/ppermute | solution.py:81
  30.3 4.6 %collective-permute-start.5 = (bf16[128,140]{0,1:T(8,128)(2,1)S(1)}, bf16[128,140]{0,1:T(8,128)(2,1)S(1)}, u32[]{:S(2)}, u32[]{:S(2)}) collective-permute-start(bf16[128,140]{0,1:T(8,128)(2,1)S(1)} %fusion.33), channel_id=1, source_target_pairs={{0,1},{1,0},{2,3},{3,2},{4,5},{5,4},{6,7},{7,6},{8,9},{9,8},{10,11... | collective-permute-start | bytes 107528 | tf_op jit(solution)/shard_map/ppermute | solution.py:81
  34.9 6.6 %copy-start.6 = (bf16[2240]{0:T(1024)(128)(2,1)S(1)}, bf16[2240]{0:T(1024)(128)(2,1)}, u32[]{:S(2)}) copy-start(bf16[2240]{0:T(1024)(128)(2,1)} %param.14) | copy-start | bytes 13444
  35.0 7.0 %copy-start.7 = (bf16[2240]{0:T(1024)(128)(2,1)S(1)}, bf16[2240]{0:T(1024)(128)(2,1)}, u32[]{:S(2)}) copy-start(bf16[2240]{0:T(1024)(128)(2,1)} %param.13) | copy-start | bytes 13444
  35.0 5.2 %collective-permute-start.8 = (bf16[128,560]{0,1:T(8,128)(2,1)S(1)}, bf16[128,560]{0,1:T(8,128)(2,1)S(1)}, u32[]{:S(2)}, u32[]{:S(2)}) collective-permute-start(bf16[128,560]{0,1:T(8,128)(2,1)S(1)} %pad_maximum_fusion.8), channel_id=1, source_target_pairs={{0,8},{4,12},{8,0},{12,4},{1,9},{5,13},{9,1},{13,5},{2,10},{6,14},... | collective-permute-start | bytes 430088 | tf_op jit(solution)/shard_map/ppermute | solution.py:61
  41.4 1.6 collective-permute-start.9
  45.1 1.0 copy-start.2
  47.5 21.1 %copy-start = (bf16[560,2,840]{2,1,0:T(2,128)(2,1)S(1)}, bf16[560,2,840]{2,1,0:T(2,128)(2,1)}, u32[]{:S(2)}) copy-start(bf16[560,2,840]{2,1,0:T(2,128)(2,1)} %param.15) | copy-start | bytes 5644804
  47.5 7.3 %collective-permute-start.12 = (bf16[1,1,64,560]{3,2,1,0:T(8,128)(2,1)S(1)}, bf16[1,1,64,560]{3,2,1,0:T(8,128)(2,1)S(1)}, u32[]{:S(2)}, u32[]{:S(2)}) collective-permute-start(bf16[1,1,64,560]{3,2,1,0:T(8,128)(2,1)S(1)} %get-tuple-element.19), channel_id=1, source_target_pairs={{0,3},{1,2},{2,1},{3,0},{4,7},{5,6},{6,5},{7,4},{8,11},{9,10},{10,... | collective-permute-start | bytes 215048 | tf_op jit(solution)/shard_map/ppermute | solution.py:81
  50.0 8.5 %collective-permute-start.11 = (bf16[1,1,64,560]{3,2,1,0:T(8,128)(2,1)S(1)}, bf16[1,1,64,560]{3,2,1,0:T(8,128)(2,1)S(1)}, u32[]{:S(2)}, u32[]{:S(2)}) collective-permute-start(bf16[1,1,64,560]{3,2,1,0:T(8,128)(2,1)S(1)} %get-tuple-element.20), channel_id=1, source_target_pairs={{0,2},{1,3},{2,0},{3,1},{4,6},{5,7},{6,4},{7,5},{8,10},{9,11},{10,... | collective-permute-start | bytes 215048 | tf_op jit(solution)/shard_map/ppermute | solution.py:81
  50.7 7.7 %collective-permute-start.10 = (bf16[1,1,64,560]{3,2,1,0:T(8,128)(2,1)S(1)}, bf16[1,1,64,560]{3,2,1,0:T(8,128)(2,1)S(1)}, u32[]{:S(2)}, u32[]{:S(2)}) collective-permute-start(bf16[1,1,64,560]{3,2,1,0:T(8,128)(2,1)S(1)} %get-tuple-element.21), channel_id=1, source_target_pairs={{0,1},{1,0},{2,3},{3,2},{4,5},{5,4},{6,7},{7,6},{8,9},{9,8},{10,11... | collective-permute-start | bytes 215048 | tf_op jit(solution)/shard_map/ppermute | solution.py:81
  58.6 9.0 %collective-permute-start.13 = (bf16[1,1,4,64,560]{4,3,2,1,0:T(8,128)(2,1)S(1)}, bf16[1,1,4,64,560]{4,3,2,1,0:T(8,128)(2,1)S(1)}, u32[]{:S(2)}, u32[]{:S(2)}) collective-permute-start(bf16[1,1,4,64,560]{4,3,2,1,0:T(8,128)(2,1)S(1)} %maximum_bitcast_fusion), channel_id=1, source_target_pairs={{0,8},{4,12},{8,0},{12,4},{1,9},{5,13},{9,1},{13,5},{2,10},{6,14},... | collective-permute-start | bytes 860168 | tf_op jit(solution)/shard_map/ppermute | solution.py:92
  68.6 2.5 %collective-permute-start.14 = (bf16[2,1,4,64,560]{4,3,2,1,0:T(8,128)(2,1)}, bf16[2,1,4,64,560]{4,3,2,1,0:T(8,128)(2,1)}, u32[]{:S(2)}, u32[]{:S(2)}) collective-permute-start(bf16[2,1,4,64,560]{4,3,2,1,0:T(8,128)(2,1)} %pad_maximum_fusion.2), channel_id=1, source_target_pairs={{0,4},{4,0},{8,12},{12,8},{1,5},{5,1},{9,13},{13,9},{2,6},{6,2},{1... | collective-permute-start | bytes 1720328 | tf_op jit(solution)/shard_map/ppermute | solution.py:92
  72.6 1.6 copy-start.1
  78.6 0.8 copy-start.5
  146.0 3.1 %copy-start.8 = (bf16[840,2240]{1,0:T(8,128)(2,1)S(1)}, bf16[840,2240]{1,0:T(8,128)(2,1)}, u32[]{:S(2)}) copy-start(bf16[840,2240]{1,0:T(8,128)(2,1)} %param.17) | copy-start | bytes 11289604
  151.7 2.1 %collective-permute-start.15 = (bf16[2,64,2240]{2,1,0:T(8,128)(2,1)S(1)}, bf16[2,64,2240]{2,1,0:T(8,128)(2,1)S(1)}, u32[]{:S(2)}, u32[]{:S(2)}) collective-permute-start(bf16[2,64,2240]{2,1,0:T(8,128)(2,1)S(1)} %dynamic-slice_bitcast_fusion), channel_id=1, source_target_pairs={{0,4},{4,0},{8,12},{12,8},{1,5},{5,1},{9,13},{13,9},{2,6},{6,2},{1... | collective-permute-start | bytes 1720328 | tf_op jit(solution)/shard_map/ppermute | solution.py:205
  154.0 16.3 %collective-permute-start.17 = (bf16[64,2240]{1,0:T(8,128)(2,1)S(1)}, bf16[64,2240]{1,0:T(8,128)(2,1)S(1)}, u32[]{:S(2)}, u32[]{:S(2)}) collective-permute-start(bf16[64,2240]{1,0:T(8,128)(2,1)S(1)} %get-tuple-element.13), channel_id=1, source_target_pairs={{0,2},{1,6},{2,10},{3,14},{4,3},{5,7},{6,11},{7,15},{8,0},{9,4},{1... | collective-permute-start | bytes 860168 | tf_op jit(solution)/shard_map/ppermute | solution.py:213
  154.6 19.0 %collective-permute-start.16 = (bf16[64,2240]{1,0:T(8,128)(2,1)S(1)}, bf16[64,2240]{1,0:T(8,128)(2,1)S(1)}, u32[]{:S(2)}, u32[]{:S(2)}) collective-permute-start(bf16[64,2240]{1,0:T(8,128)(2,1)S(1)} %get-tuple-element.12), channel_id=1, source_target_pairs={{0,0},{1,4},{2,8},{3,12},{4,1},{5,5},{6,9},{7,13},{8,2},{9,6},{10,... | collective-permute-start | bytes 860168 | tf_op jit(solution)/shard_map/ppermute | solution.py:213
Sparse Core Ops, SparseCore 0:
  78.8 64.8 reduce-scatter.1

commit v22 on v20

--- a/solution.py
+++ b/solution.py
@@ -185,7 +185,7 @@
             .astype(jnp.bfloat16)
             .reshape(1, frame_rows, col_count, 2 * local_gated)
         )
-        padded_expanded = jnp.pad(expanded, ((0, 0), (1, 1), (0, 0), (0, 0)))
+        padded_expanded = jnp.pad(expanded.astype(jnp.float32), ((0, 0), (1, 1), (0, 0), (0, 0)))
         hidden = depthwise(padded_expanded, conv_taps, frame_rows, col_count, local_gated)
         projected = jnp.dot(
             hidden.reshape(-1, local_gated), out_weight, preferred_element_type=jnp.float32

time: 182 us -> 182 us (level)
  local copies, waits for them, and re-layouts: 13.3 us -> 18.4 us
  waiting for transfers between devices: 113 us -> 108 us
    mul x9, local copies, waits for them, and re-layouts: 0.71 us -> 6.08 us  [depthwise(): summed = summed + window * conv_taps[row_off * 3 + col_off]]
    reduce_scatter x1, waiting for transfers between devices: 63.5 us -> 58.2 us  [local(): summed = lax.psum_scatter(partial, 'row', scatter_dimension=0, tiled=True)]
  transfers between devices with their start and end apart: 19 -> 19, of which waited for: 16 -> 16; matrix products, arithmetic and copies ran while one was open for 2% -> 5% of each run, Pallas kernels for 0% -> 0%
where the time goes in v22:
time: 182 us; the launch traced here: 181 us
  waiting for transfers between devices  108 us (59%)
  starting transfers between devices  20.9 us (11%)
  local copies, waits for them, and re-layouts  18.4 us (10%)
  between operations  14.7 us (8%)
  other arithmetic  11.7 us (6%)
  matrix products  7.54 us (4%)
    reduce_scatter x1, waiting for transfers between devices, local(): summed = lax.psum_scatter(partial, 'row', scatter_dimension=0, tiled=True)  58.2 us
    ppermute x2, waiting for transfers between devices, local(): lax.ppermute(pick(pair_sums, chip_at ^ mask), ('frame', 'row'), [(f * row...  13.6 us
    ppermute x9, starting transfers between devices, swap_chunks(): lax.ppermute(sent, axis, [(i, i ^ mask) for i in range(count)])  13.4 us
    ppermute x9, waiting for transfers between devices, swap_chunks(): lax.ppermute(sent, axis, [(i, i ^ mask) for i in range(count)])  12.8 us
    ppermute x2, waiting for transfers between devices, doubling_gather(): lax.ppermute(jnp.stack([by_mask[key] for key in keys]), axis, [(i, i ^ bi...  8.4 us
    ppermute x2, waiting for transfers between devices, halving_sum(): lax.ppermute(sent, axis, [(i, i ^ bit) for i in range(count)])  7.32 us
    mul x9, local copies, waits for them, and re-layouts, depthwise(): summed = summed + window * conv_taps[row_off * 3 + col_off]  6.08 us
    ppermute x2, starting transfers between devices, local(): lax.ppermute(pick(pair_sums, chip_at ^ mask), ('frame', 'row'), [(f * row...  6.05 us
  transfers between devices with their start and end apart: 19, of which 16 were waited for; matrix products, arithmetic and copies ran while one was open for 5% of the time, Pallas kernels for 0%

profile of v22, /device:TPU:2, one launch (start us, length us, event | category | flops | bytes accessed | tf_op | source)
XLA Modules:
  0.0 181.2 jit_solution(18274982452206985171)
XLA Ops:
  7.2 1.1 convert_reduce_fusion
  8.3 1.0 broadcast_maximum_fusion.1
  11.7 1.6 collective-permute-done
  13.5 5.8 %collective-permute-done.1 = bf16[128,560]{0,1:T(8,128)(2,1)S(1)} collective-permute-done((bf16[128,560]{0,1:T(8,128)(2,1)S(1)}, bf16[128,560]{0,1:T(8,128)(2,1)S(1)}, u32[]{:S(2)}, u32[]{:S(2)}) %collective-permute-start.1) | collective-permute-done | bytes 143392 | tf_op jit(solution)/shard_map/ppermute | solution.py:51
  19.4 3.7 %collective-permute-start.4 = (bf16[128,140]{0,1:T(8,128)(2,1)S(1)}, bf16[128,140]{0,1:T(8,128)(2,1)S(1)}, u32[]{:S(2)}, u32[]{:S(2)}) collective-permute-start(bf16[128,140]{0,1:T(8,128)(2,1)S(1)} %get-tuple-element.31), channel_id=1, source_target_pairs={{0,3},{1,2},{2,1},{3,0},{4,7},{5,6},{6,5},{7,4},{8,11},{9,10},{10,... | collective-permute-start | bytes 107528 | tf_op jit(solution)/shard_map/ppermute | solution.py:81
  23.9 1.6 collective-permute-done.4
  25.5 2.5 %collective-permute-done.3 = bf16[128,140]{0,1:T(8,128)(2,1)S(1)} collective-permute-done((bf16[128,140]{0,1:T(8,128)(2,1)S(1)}, bf16[128,140]{0,1:T(8,128)(2,1)S(1)}, u32[]{:S(2)}, u32[]{:S(2)}) %collective-permute-start.3) | collective-permute-done | bytes 35872 | tf_op jit(solution)/shard_map/ppermute | solution.py:81
  28.0 1.5 collective-permute-start.7
  30.2 2.3 %collective-permute-start.5 = (bf16[128,140]{0,1:T(8,128)(2,1)S(1)}, bf16[128,140]{0,1:T(8,128)(2,1)S(1)}, u32[]{:S(2)}, u32[]{:S(2)}) collective-permute-start(bf16[128,140]{0,1:T(8,128)(2,1)S(1)} %fusion.45), channel_id=1, source_target_pairs={{0,1},{1,0},{2,3},{3,2},{4,5},{5,4},{6,7},{7,6},{8,9},{9,8},{10,11... | collective-permute-start | bytes 107528 | tf_op jit(solution)/shard_map/ppermute | solution.py:81
  32.5 1.3 collective-permute-done.7
  35.5 4.6 %collective-permute-done.8 = bf16[128,560]{0,1:T(8,128)(2,1)S(1)} collective-permute-done((bf16[128,560]{0,1:T(8,128)(2,1)S(1)}, bf16[128,560]{0,1:T(8,128)(2,1)S(1)}, u32[]{:S(2)}, u32[]{:S(2)}) %collective-permute-start.8) | collective-permute-done | bytes 143392 | tf_op jit(solution)/shard_map/ppermute | solution.py:61
  41.9 1.1 collective-permute-done.9
  46.0 1.0 fusion.26
  47.0 0.9 multiply_convert_fusion
  48.2 2.4 %collective-permute-start.12 = (bf16[1,1,64,560]{3,2,1,0:T(8,128)(2,1)S(1)}, bf16[1,1,64,560]{3,2,1,0:T(8,128)(2,1)S(1)}, u32[]{:S(2)}, u32[]{:S(2)}) collective-permute-start(bf16[1,1,64,560]{3,2,1,0:T(8,128)(2,1)S(1)} %get-tuple-element.19), channel_id=1, source_target_pairs={{0,3},{1,2},{2,1},{3,0},{4,7},{5,6},{6,5},{7,4},{8,11},{9,10},{10,... | collective-permute-start | bytes 215048 | tf_op jit(solution)/shard_map/ppermute | solution.py:81
  51.3 1.3 collective-permute-start.10
  52.6 2.8 %collective-permute-done.12 = bf16[1,1,64,560]{3,2,1,0:T(8,128)(2,1)S(1)} collective-permute-done((bf16[1,1,64,560]{3,2,1,0:T(8,128)(2,1)S(1)}, bf16[1,1,64,560]{3,2,1,0:T(8,128)(2,1)S(1)}, u32[]{:S(2)}, u32[]{:S(2)}) %collective-permute-start.12) | collective-permute-done | bytes 71712 | tf_op jit(solution)/shard_map/ppermute | solution.py:81
  55.4 3.6 %collective-permute-done.11 = bf16[1,1,64,560]{3,2,1,0:T(8,128)(2,1)S(1)} collective-permute-done((bf16[1,1,64,560]{3,2,1,0:T(8,128)(2,1)S(1)}, bf16[1,1,64,560]{3,2,1,0:T(8,128)(2,1)S(1)}, u32[]{:S(2)}, u32[]{:S(2)}) %collective-permute-start.11) | collective-permute-done | bytes 71712 | tf_op jit(solution)/shard_map/ppermute | solution.py:81
  59.9 8.4 %collective-permute-done.13 = bf16[1,1,4,64,560]{4,3,2,1,0:T(8,128)(2,1)S(1)} collective-permute-done((bf16[1,1,4,64,560]{4,3,2,1,0:T(8,128)(2,1)S(1)}, bf16[1,1,4,64,560]{4,3,2,1,0:T(8,128)(2,1)S(1)}, u32[]{:S(2)}, u32[]{:S(2)}) %collective-permute-start.13) | collective-permute-done | bytes 286752 | tf_op jit(solution)/shard_map/ppermute | solution.py:92
  68.3 0.9 pad_maximum_fusion.2
  69.2 2.5 %reshape.248 = bf16[560,1680]{1,0:T(8,128)(2,1)} reshape(bf16[560,2,840]{2,1,0:T(2,128)(2,1)S(1)} %copy-done) | data formatting | bytes 3763200 | tf_op jit(solution)/shard_map/reshape | solution.py:175
  72.4 1.3 copy-done.1
  73.7 4.4 %convolution_convert_fusion.1 = bf16[1024,1680]{0,1:T(8,128)(2,1)} fusion(bf16[1024,560]{1,0:T(8,128)(2,1)S(1)} %bitcast.120, bf16[560,1680]{1,0:T(8,128)(2,1)S(1)} %copy-done.1), kind=kOutput, calls=%fused_computation.1 | convolution fusion | flops 1928478720 | bytes 6469120 | tf_op jit(solution)/shard_map/dot_general | solution.py:178
  85.0 58.2 %reduce-scatter.2.cloned.1.call-done = bf16[256,1680]{0,1:T(8,128)(2,1)} async-done(((bf16[1024,1680]{0,1:T(8,128)(2,1)}), bf16[256,1680]{0,1:T(8,128)(2,1)}) %reduce-scatter.2.cloned.1.call-update) | async-done | bytes 860176 | tf_op jit(solution)/shard_map/reduce_scatter | solution.py:181
  143.2 1.6 fusion.22
  146.4 2.2 %fusion.8 = f32[1,4,64,1680]{3,2,1,0:T(8,128)S(1)} fusion(f32[1,6,64,1680]{3,2,1,0:T(8,128)S(1)} %pad.13, f32[1,4,64,1680]{3,2,1,0:T(8,128)S(1)} %bitcast.115, f32[1680]{0:T(1024)S(1)} %copy-done.7, f32[1680]{0:T(1024)S(1)} %copy-done.8, f32[1680]{0:T(1024)S(1)} %copy-done.9, f32[1680]{0:T(1024)S(1)} %copy-done.10, f32[1680]{0:T(1024)S(1)} %copy-done.11, ...), kind=kLoop, calls=%fused_computation.18 | loop fusion | flops 7311360 | bytes 10051584 | tf_op jit(solution)/shard_map/add | solution.py:114
  149.0 1.8 %convolution_convert_fusion = bf16[256,2240]{0,1:T(8,128)(2,1)S(1)} fusion(bf16[256,840]{1,0:T(8,128)(2,1)S(1)} %bitcast.121, bf16[840,2240]{1,0:T(8,128)(2,1)S(1)} %copy-done.18), kind=kOutput, calls=%fused_computation | convolution fusion | flops 963952640 | bytes 5340160 | tf_op jit(solution)/shard_map/dot_general | solution.py:190
  151.7 2.0 %collective-permute-done.15 = bf16[2,64,2240]{2,1,0:T(8,128)(2,1)S(1)} collective-permute-done((bf16[2,64,2240]{2,1,0:T(8,128)(2,1)S(1)}, bf16[2,64,2240]{2,1,0:T(8,128)(2,1)S(1)}, u32[]{:S(2)}, u32[]{:S(2)}) %collective-permute-start.15) | collective-permute-done | bytes 573472 | tf_op jit(solution)/shard_map/ppermute | solution.py:201
  154.5 5.5 %collective-permute-start.16 = (bf16[64,2240]{1,0:T(8,128)(2,1)S(1)}, bf16[64,2240]{1,0:T(8,128)(2,1)S(1)}, u32[]{:S(2)}, u32[]{:S(2)}) collective-permute-start(bf16[64,2240]{1,0:T(8,128)(2,1)S(1)} %get-tuple-element.12), channel_id=1, source_target_pairs={{0,0},{1,4},{2,8},{3,12},{4,1},{5,5},{6,9},{7,13},{8,2},{9,6},{10,... | collective-permute-start | bytes 860168 | tf_op jit(solution)/shard_map/ppermute | solution.py:209
  160.0 10.3 %collective-permute-done.17 = bf16[64,2240]{1,0:T(8,128)(2,1)S(1)} collective-permute-done((bf16[64,2240]{1,0:T(8,128)(2,1)S(1)}, bf16[64,2240]{1,0:T(8,128)(2,1)S(1)}, u32[]{:S(2)}, u32[]{:S(2)}) %collective-permute-start.17) | collective-permute-done | bytes 286752 | tf_op jit(solution)/shard_map/ppermute | solution.py:209
  170.2 3.3 %collective-permute-done.16 = bf16[64,2240]{1,0:T(8,128)(2,1)S(1)} collective-permute-done((bf16[64,2240]{1,0:T(8,128)(2,1)S(1)}, bf16[64,2240]{1,0:T(8,128)(2,1)S(1)}, u32[]{:S(2)}, u32[]{:S(2)}) %collective-permute-start.16) | collective-permute-done | bytes 286752 | tf_op jit(solution)/shard_map/ppermute | solution.py:209
  173.5 0.8 fusion.30
  (120 shorter events, 23.4 us)
Async XLA Ops:
  7.2 2.5 %copy-start.5 = (bf16[1,1,64,2240]{3,2,1,0:T(8,128)(2,1)S(1)}, bf16[1,1,64,2240]{3,2,1,0:T(8,128)(2,1)}, u32[]{:S(2)}) copy-start(bf16[1,1,64,2240]{3,2,1,0:T(8,128)(2,1)} %param.11) | copy-start | bytes 860164
  7.2 136.1 %reduce-scatter.2.cloned.1.call-start = ((), (), s32[]{:S(2)}) async-start(), calls=%async_computation.1 | async-start | bytes 4300800 | tf_op jit(solution)/shard_map/reduce_scatter | solution.py:181
  11.7 1.6 collective-permute-start
  13.4 5.9 %collective-permute-start.1 = (bf16[128,560]{0,1:T(8,128)(2,1)S(1)}, bf16[128,560]{0,1:T(8,128)(2,1)S(1)}, u32[]{:S(2)}, u32[]{:S(2)}) collective-permute-start(bf16[128,560]{0,1:T(8,128)(2,1)S(1)} %select_convert_fusion.1), channel_id=1, source_target_pairs={{0,8},{4,12},{8,0},{12,4},{1,9},{5,13},{9,1},{13,5},{2,10},{6,14},... | collective-permute-start | bytes 430088 | tf_op jit(solution)/shard_map/ppermute | solution.py:51
  19.4 6.1 %collective-permute-start.4 = (bf16[128,140]{0,1:T(8,128)(2,1)S(1)}, bf16[128,140]{0,1:T(8,128)(2,1)S(1)}, u32[]{:S(2)}, u32[]{:S(2)}) collective-permute-start(bf16[128,140]{0,1:T(8,128)(2,1)S(1)} %get-tuple-element.31), channel_id=1, source_target_pairs={{0,3},{1,2},{2,1},{3,0},{4,7},{5,6},{6,5},{7,4},{8,11},{9,10},{10,... | collective-permute-start | bytes 107528 | tf_op jit(solution)/shard_map/ppermute | solution.py:81
  23.1 4.9 %collective-permute-start.3 = (bf16[128,140]{0,1:T(8,128)(2,1)S(1)}, bf16[128,140]{0,1:T(8,128)(2,1)S(1)}, u32[]{:S(2)}, u32[]{:S(2)}) collective-permute-start(bf16[128,140]{0,1:T(8,128)(2,1)S(1)} %get-tuple-element.32), channel_id=1, source_target_pairs={{0,2},{1,3},{2,0},{3,1},{4,6},{5,7},{6,4},{7,5},{8,10},{9,11},{10,... | collective-permute-start | bytes 107528 | tf_op jit(solution)/shard_map/ppermute | solution.py:81
  23.1 4.9 %collective-permute-start.2 = (bf16[128,140]{0,1:T(8,128)(2,1)S(1)}, bf16[128,140]{0,1:T(8,128)(2,1)S(1)}, u32[]{:S(2)}, u32[]{:S(2)}) collective-permute-start(bf16[128,140]{0,1:T(8,128)(2,1)S(1)} %get-tuple-element.33), channel_id=1, source_target_pairs={{0,1},{1,0},{2,3},{3,2},{4,5},{5,4},{6,7},{7,6},{8,9},{9,8},{10,11... | collective-permute-start | bytes 107528 | tf_op jit(solution)/shard_map/ppermute | solution.py:81
  27.9 13.5 %copy-start.4 = (bf16[1,1,64,2240]{3,2,1,0:T(8,128)(2,1)S(1)}, bf16[1,1,64,2240]{3,2,1,0:T(8,128)(2,1)}, u32[]{:S(2)}) copy-start(bf16[1,1,64,2240]{3,2,1,0:T(8,128)(2,1)} %param.9) | copy-start | bytes 860164
  28.0 5.8 %collective-permute-start.7 = (bf16[128,140]{0,1:T(8,128)(2,1)S(1)}, bf16[128,140]{0,1:T(8,128)(2,1)S(1)}, u32[]{:S(2)}, u32[]{:S(2)}) collective-permute-start(bf16[128,140]{0,1:T(8,128)(2,1)S(1)} %fusion.45), channel_id=1, source_target_pairs={{0,3},{1,2},{2,1},{3,0},{4,7},{5,6},{6,5},{7,4},{8,11},{9,10},{10,... | collective-permute-start | bytes 107528 | tf_op jit(solution)/shard_map/ppermute | solution.py:81
  29.5 4.9 %collective-permute-start.6 = (bf16[128,140]{0,1:T(8,128)(2,1)S(1)}, bf16[128,140]{0,1:T(8,128)(2,1)S(1)}, u32[]{:S(2)}, u32[]{:S(2)}) collective-permute-start(bf16[128,140]{0,1:T(8,128)(2,1)S(1)} %fusion.45), channel_id=1, source_target_pairs={{0,2},{1,3},{2,0},{3,1},{4,6},{5,7},{6,4},{7,5},{8,10},{9,11},{10,... | collective-permute-start | bytes 107528 | tf_op jit(solution)/shard_map/ppermute | solution.py:81
  30.2 4.6 %collective-permute-start.5 = (bf16[128,140]{0,1:T(8,128)(2,1)S(1)}, bf16[128,140]{0,1:T(8,128)(2,1)S(1)}, u32[]{:S(2)}, u32[]{:S(2)}) collective-permute-start(bf16[128,140]{0,1:T(8,128)(2,1)S(1)} %fusion.45), channel_id=1, source_target_pairs={{0,1},{1,0},{2,3},{3,2},{4,5},{5,4},{6,7},{7,6},{8,9},{9,8},{10,11... | collective-permute-start | bytes 107528 | tf_op jit(solution)/shard_map/ppermute | solution.py:81
  34.8 6.6 %copy-start.16 = (bf16[2240]{0:T(1024)(128)(2,1)S(1)}, bf16[2240]{0:T(1024)(128)(2,1)}, u32[]{:S(2)}) copy-start(bf16[2240]{0:T(1024)(128)(2,1)} %param.14) | copy-start | bytes 13444
  34.9 7.0 %copy-start.17 = (bf16[2240]{0:T(1024)(128)(2,1)S(1)}, bf16[2240]{0:T(1024)(128)(2,1)}, u32[]{:S(2)}) copy-start(bf16[2240]{0:T(1024)(128)(2,1)} %param.13) | copy-start | bytes 13444
  34.9 5.2 %collective-permute-start.8 = (bf16[128,560]{0,1:T(8,128)(2,1)S(1)}, bf16[128,560]{0,1:T(8,128)(2,1)S(1)}, u32[]{:S(2)}, u32[]{:S(2)}) collective-permute-start(bf16[128,560]{0,1:T(8,128)(2,1)S(1)} %pad_maximum_fusion.8), channel_id=1, source_target_pairs={{0,8},{4,12},{8,0},{12,4},{1,9},{5,13},{9,1},{13,5},{2,10},{6,14},... | collective-permute-start | bytes 430088 | tf_op jit(solution)/shard_map/ppermute | solution.py:61
  41.3 1.6 collective-permute-start.9
  45.0 1.0 copy-start.2
  48.2 21.0 %copy-start = (bf16[560,2,840]{2,1,0:T(2,128)(2,1)S(1)}, bf16[560,2,840]{2,1,0:T(2,128)(2,1)}, u32[]{:S(2)}) copy-start(bf16[560,2,840]{2,1,0:T(2,128)(2,1)} %param.15) | copy-start | bytes 5644804
  48.2 7.3 %collective-permute-start.12 = (bf16[1,1,64,560]{3,2,1,0:T(8,128)(2,1)S(1)}, bf16[1,1,64,560]{3,2,1,0:T(8,128)(2,1)S(1)}, u32[]{:S(2)}, u32[]{:S(2)}) collective-permute-start(bf16[1,1,64,560]{3,2,1,0:T(8,128)(2,1)S(1)} %get-tuple-element.19), channel_id=1, source_target_pairs={{0,3},{1,2},{2,1},{3,0},{4,7},{5,6},{6,5},{7,4},{8,11},{9,10},{10,... | collective-permute-start | bytes 215048 | tf_op jit(solution)/shard_map/ppermute | solution.py:81
  50.6 8.5 %collective-permute-start.11 = (bf16[1,1,64,560]{3,2,1,0:T(8,128)(2,1)S(1)}, bf16[1,1,64,560]{3,2,1,0:T(8,128)(2,1)S(1)}, u32[]{:S(2)}, u32[]{:S(2)}) collective-permute-start(bf16[1,1,64,560]{3,2,1,0:T(8,128)(2,1)S(1)} %get-tuple-element.20), channel_id=1, source_target_pairs={{0,2},{1,3},{2,0},{3,1},{4,6},{5,7},{6,4},{7,5},{8,10},{9,11},{10,... | collective-permute-start | bytes 215048 | tf_op jit(solution)/shard_map/ppermute | solution.py:81
  51.3 7.7 %collective-permute-start.10 = (bf16[1,1,64,560]{3,2,1,0:T(8,128)(2,1)S(1)}, bf16[1,1,64,560]{3,2,1,0:T(8,128)(2,1)S(1)}, u32[]{:S(2)}, u32[]{:S(2)}) collective-permute-start(bf16[1,1,64,560]{3,2,1,0:T(8,128)(2,1)S(1)} %get-tuple-element.21), channel_id=1, source_target_pairs={{0,1},{1,0},{2,3},{3,2},{4,5},{5,4},{6,7},{7,6},{8,9},{9,8},{10,11... | collective-permute-start | bytes 215048 | tf_op jit(solution)/shard_map/ppermute | solution.py:81
  59.3 9.0 %collective-permute-start.13 = (bf16[1,1,4,64,560]{4,3,2,1,0:T(8,128)(2,1)S(1)}, bf16[1,1,4,64,560]{4,3,2,1,0:T(8,128)(2,1)S(1)}, u32[]{:S(2)}, u32[]{:S(2)}) collective-permute-start(bf16[1,1,4,64,560]{4,3,2,1,0:T(8,128)(2,1)S(1)} %maximum_bitcast_fusion), channel_id=1, source_target_pairs={{0,8},{4,12},{8,0},{12,4},{1,9},{5,13},{9,1},{13,5},{2,10},{6,14},... | collective-permute-start | bytes 860168 | tf_op jit(solution)/shard_map/ppermute | solution.py:92
  69.2 2.5 %collective-permute-start.14 = (bf16[2,1,4,64,560]{4,3,2,1,0:T(8,128)(2,1)}, bf16[2,1,4,64,560]{4,3,2,1,0:T(8,128)(2,1)S(1)}, u32[]{:S(2)}, u32[]{:S(2)}) collective-permute-start(bf16[2,1,4,64,560]{4,3,2,1,0:T(8,128)(2,1)} %pad_maximum_fusion.2), channel_id=1, source_target_pairs={{0,4},{4,0},{8,12},{12,8},{1,5},{5,1},{9,13},{13,9},{2,6},{6,2},{1... | collective-permute-start | bytes 1720328 | tf_op jit(solution)/shard_map/ppermute | solution.py:92
  72.2 1.6 copy-start.1
  78.2 0.8 copy-start.6
  145.7 0.7 copy-start.13
  145.7 0.7 copy-start.14
  145.7 0.7 copy-start.15
  146.4 2.5 %copy-start.18 = (bf16[840,2240]{1,0:T(8,128)(2,1)S(1)}, bf16[840,2240]{1,0:T(8,128)(2,1)}, u32[]{:S(2)}) copy-start(bf16[840,2240]{1,0:T(8,128)(2,1)} %param.17) | copy-start | bytes 11289604
  151.6 21.9 %copy-start.3 = (bf16[64,2240]{1,0:T(8,128)(2,1)S(1)}, bf16[64,2240]{1,0:T(8,128)(2,1)}, u32[]{:S(2)}) copy-start(bf16[64,2240]{1,0:T(8,128)(2,1)} %get-tuple-element.5) | copy-start | bytes 860164
  151.6 2.1 %collective-permute-start.15 = (bf16[2,64,2240]{2,1,0:T(8,128)(2,1)S(1)}, bf16[2,64,2240]{2,1,0:T(8,128)(2,1)S(1)}, u32[]{:S(2)}, u32[]{:S(2)}) collective-permute-start(bf16[2,64,2240]{2,1,0:T(8,128)(2,1)S(1)} %dynamic-slice_bitcast_fusion), channel_id=1, source_target_pairs={{0,4},{4,0},{8,12},{12,8},{1,5},{5,1},{9,13},{13,9},{2,6},{6,2},{1... | collective-permute-start | bytes 1720328 | tf_op jit(solution)/shard_map/ppermute | solution.py:201
  153.9 16.3 %collective-permute-start.17 = (bf16[64,2240]{1,0:T(8,128)(2,1)S(1)}, bf16[64,2240]{1,0:T(8,128)(2,1)S(1)}, u32[]{:S(2)}, u32[]{:S(2)}) collective-permute-start(bf16[64,2240]{1,0:T(8,128)(2,1)S(1)} %get-tuple-element.13), channel_id=1, source_target_pairs={{0,2},{1,6},{2,10},{3,14},{4,3},{5,7},{6,11},{7,15},{8,0},{9,4},{1... | collective-permute-start | bytes 860168 | tf_op jit(solution)/shard_map/ppermute | solution.py:209
  154.5 19.0 %collective-permute-start.16 = (bf16[64,2240]{1,0:T(8,128)(2,1)S(1)}, bf16[64,2240]{1,0:T(8,128)(2,1)S(1)}, u32[]{:S(2)}, u32[]{:S(2)}) collective-permute-start(bf16[64,2240]{1,0:T(8,128)(2,1)S(1)} %get-tuple-element.12), channel_id=1, source_target_pairs={{0,0},{1,4},{2,8},{3,12},{4,1},{5,5},{6,9},{7,13},{8,2},{9,6},{10,... | collective-permute-start | bytes 860168 | tf_op jit(solution)/shard_map/ppermute | solution.py:209
  (6 other events, 4.3 us)
Sparse Core Ops, SparseCore 0:
  78.3 64.8 reduce-scatter.1
